TPU v7x, 1024 devices: a whole 4x4x32 slice. The times are simulated.
1024 devices in a mesh: frames: 64 (over z, core), rows: 16 (over y, x).
Axes of the slice: x: 4, y: 4, z: 32, core: 2. Of those that a mesh axis runs over, the one named last changes fastest.
Arguments:
- images: float32 [128, 32, 96, 128], P('frames', 'rows'), may hold values from -6 to 6
- spatial_weight: float32 [3, 3, 128, 128], replicated, may hold values from -0.1875 to 0.1875
- temporal_weight: float32 [3, 128, 128], replicated, may hold values from -0.3125 to 0.3125
- cotangent: float32 [128, 32, 96, 128], P('frames', 'rows'), may hold values from -6 to 6
Outputs:
- block_out: float32 [128, 32, 96, 128], P('frames', 'rows')
- grad_images: float32 [128, 32, 96, 128], P('frames', 'rows')
- grad_spatial: float32 [3, 3, 128, 128], P(None, None, None, 'rows')
- grad_temporal: float32 [3, 128, 128], P(None, None, 'rows')
All inputs are finite; a program needn't handle non-finite values.
Results may differ from a plain program's by a relative error of at most 0.0003.
Values sent between devices are 32-bit elements; how exact they have to be, the bound alone decides.
No kernel may reach another device: no remote copies, remote signals or barrier semaphores. Data moves between devices by JAX's collectives and lax.ppermute only.
A program may use at most 32 MiB of HBM per device.

v0:
```python
import math

import jax
import jax.numpy as jnp
from jax import lax
from jax.sharding import PartitionSpec as P

HIGH = lax.Precision.HIGHEST


def padded_2(value, sides, width):
    for axis, dim in sides:
        count, length = (lax.axis_size(axis), value.shape[dim])
        up = [(i, (i + 1) % count) for i in range(count - 1)]
        down = [(j, i) for i, j in up]
        last = lax.slice_in_dim(value, length - width, length, axis=dim)
        leading = lax.slice_in_dim(value, 0, width, axis=dim)
        before = lax.ppermute(last, axis, up)
        after = lax.ppermute(leading, axis, down)
        value = jnp.concatenate([before, value, after], axis=dim)
    return value


def passed_along(value, axis, by):
    count = lax.axis_size(axis)
    pairs = [(i, i + by) for i in range(count) if 0 <= i + by < count]
    return lax.ppermute(value, axis, pairs)


def widen(array):
    return jnp.pad(array, ((0, 0), (0, 0), (1, 1), (0, 0)))


def convolve(source, kernel, height, width):
    total = jnp.zeros((source.shape[0], height, width, kernel.shape[3]), jnp.float32)
    for i in range(3):
        for j in range(3):
            total = total + jnp.einsum(
                "frwc,cd->frwd",
                source[:, i : i + height, j : j + width],
                kernel[i, j],
                precision=HIGH,
            )
    return total


def temporal_back(grad_long, temporal_weight, nframes):
    dact = jnp.zeros((nframes,) + grad_long.shape[1:], jnp.float32)
    for k in range(3):
        dact = dact + jnp.einsum(
            "frwd,cd->frwc", grad_long[k : k + nframes], temporal_weight[k], precision=HIGH
        )
    return dact


def per_device(images, spatial_weight, temporal_weight, cotangent):
    nframes, strip, width, chans = images.shape
    padded = widen(padded_2(images, (("rows", 1),), 1))
    pre = convolve(padded, spatial_weight, strip, width)
    sig = jax.nn.sigmoid(pre)
    later = passed_along(cotangent, "frames", -1)
    grad_long = jnp.concatenate([cotangent, later], axis=0)
    dact = temporal_back(grad_long, temporal_weight, nframes)
    dpre = dact * sig * (1.0 + pre * (1.0 - sig))
    dpre_wide = widen(padded_2(dpre, (("rows", 1),), 1))
    act = pre * sig
    earlier = passed_along(act, "frames", 1)
    longer = jnp.concatenate([earlier, act], axis=0)
    mixed = jnp.zeros(images.shape, jnp.float32)
    for k in range(3):
        mixed = mixed + jnp.einsum(
            "frwc,cd->frwd", longer[2 - k : 2 - k + nframes], temporal_weight[k], precision=HIGH
        )
    block_out = images + mixed
    grad_images = cotangent
    for i in range(3):
        for j in range(3):
            grad_images = grad_images + jnp.einsum(
                "frwd,cd->frwc",
                dpre_wide[:, 2 - i : 2 - i + strip, 2 - j : 2 - j + width],
                spatial_weight[i, j],
                precision=HIGH,
            )
    total_cells = nframes * lax.axis_size("frames") * strip * lax.axis_size("rows") * width
    factor = 1.0 / math.sqrt(total_cells)
    rows_out = []
    for i in range(3):
        cols_out = []
        for j in range(3):
            cols_out.append(
                jnp.einsum(
                    "frwc,frwd->cd", padded[:, i : i + strip, j : j + width], dpre, precision=HIGH
                )
            )
        rows_out.append(jnp.stack(cols_out))
    spatial_terms = jnp.stack(rows_out).reshape(9, chans, chans) * factor
    temporal_terms = (
        jnp.stack(
            [
                jnp.einsum(
                    "frwc,frwd->cd", longer[2 - k : 2 - k + nframes], cotangent, precision=HIGH
                )
                for k in range(3)
            ]
        )
        * factor
    )
    all_terms = jnp.concatenate([spatial_terms, temporal_terms], axis=0)
    shares = lax.psum_scatter(all_terms, "rows", scatter_dimension=2, tiled=True)
    summed = lax.psum(shares, "frames")
    grad_spatial = summed[:9].reshape(3, 3, chans, summed.shape[2])
    grad_temporal = summed[9:]
    return (block_out, grad_images, grad_spatial, grad_temporal)


def solution(mesh):
    return jax.shard_map(
        per_device,
        mesh=mesh,
        in_specs=(P("frames", "rows", None, None), P(), P(), P("frames", "rows", None, None)),
        out_specs=(
            P("frames", "rows", None, None),
            P("frames", "rows", None, None),
            P(None, None, None, "rows"),
            P(None, None, "rows"),
        ),
        check_vma=False,
    )
```

profile of v0, /device:TPU:1, one launch (start us, length us, event | category | flops | bytes accessed | tf_op | source)
XLA Modules:
  0.0 354.7 jit_solution(4782858804251511893)
XLA Ops:
  7.2 1.1 fusion.109
  8.3 4.0 %collective-permute-start = (f32[2,1,96,128]{3,2,1,0:T(8,128)S(1)}, f32[2,1,96,128]{3,2,1,0:T(8,128)S(1)}, u32[]{:S(2)}, u32[]{:S(2)}) collective-permute-start(f32[2,1,96,128]{3,2,1,0:T(8,128)S(1)} %get-tuple-element.8), channel_id=1, source_target_pairs={{0,1},{1,2},{2,3},{3,4},{4,5},{5,6},{6,7},{7,8},{8,9},{9,10},{10,1... | collective-permute-start | bytes 294920 | tf_op jit(solution)/shard_map/ppermute | solution.py:18
  12.3 1.3 collective-permute-start.1
  13.6 13.4 %collective-permute-start.3 = (f32[2,2,96,128]{3,2,1,0:T(8,128)S(1)}, f32[2,2,96,128]{3,2,1,0:T(8,128)S(1)}, u32[]{:S(2)}, u32[]{:S(2)}) collective-permute-start(f32[2,2,96,128]{3,2,1,0:T(8,128)S(1)} %copy-done.1), channel_id=1, source_target_pairs={{16,0},{32,16},{48,32},{64,48},{80,64},{96,80},{112,96},{128,112},... | collective-permute-start | bytes 589832 | tf_op jit(solution)/shard_map/ppermute | solution.py:27
  27.0 0.3 fusion.73
  27.4 0.9 copy-done
  28.9 0.3 fusion.35
  29.2 0.3 convolution_add_fusion.11
  30.5 0.3 convolution_add_fusion.7
  31.1 0.3 fusion.33
  31.5 1.9 collective-permute-start.2
  33.4 0.5 convolution_bitcast_fusion.4
  33.9 1.0 fusion.75
  34.9 0.3 fusion.67
  35.3 0.4 fusion.6
  35.6 0.5 convolution_bitcast_fusion.2
  36.1 0.5 convolution_bitcast_fusion.10
  36.6 0.5 convolution_bitcast_fusion.11
  37.1 0.5 convolution_bitcast_fusion.7
  37.6 0.5 convolution_bitcast_fusion.9
  38.1 0.5 convolution_bitcast_fusion.8
  38.6 0.5 convolution_bitcast_fusion.1
  39.1 0.5 convolution_bitcast_fusion.5
  39.6 0.5 convolution_bitcast_fusion.6
  40.2 0.7 fusion.108
  40.8 0.3 fusion.55
  41.2 4.3 %collective-permute-start.4 = (f32[2,1,96,128]{3,2,1,0:T(8,128)}, f32[2,1,96,128]{3,2,1,0:T(8,128)S(1)}, u32[]{:S(2)}, u32[]{:S(2)}) collective-permute-start(f32[2,1,96,128]{3,2,1,0:T(8,128)} %get-tuple-element.4), channel_id=1, source_target_pairs={{0,1},{1,2},{2,3},{3,4},{4,5},{5,6},{6,7},{7,8},{8,9},{9,10},{10,1... | collective-permute-start | bytes 294920 | tf_op jit(solution)/shard_map/ppermute | solution.py:18
  45.5 1.5 collective-permute-start.5
  47.4 3.7 %collective-permute-done.5 = f32[2,1,96,128]{3,2,1,0:T(8,128)} collective-permute-done((f32[2,1,96,128]{3,2,1,0:T(8,128)}, f32[2,1,96,128]{3,2,1,0:T(8,128)}, u32[]{:S(2)}, u32[]{:S(2)}) %collective-permute-start.5) | collective-permute-done | bytes 98336 | tf_op jit(solution)/shard_map/ppermute | solution.py:19
  51.1 0.9 select_maximum_fusion
  52.1 0.3 fusion.24
  52.4 1.0 fusion.26
  53.4 1.0 fusion.28
  54.4 0.5 convolution_bitcast_fusion
  54.9 0.5 convolution_bitcast_fusion.3
  55.6 1.0 pad_maximum_fusion
  56.5 0.3 fusion.30
  56.9 0.3 fusion.22
  57.2 0.6 copy-done.6
  58.2 0.3 convolution_add_fusion.5
  58.5 0.6 copy-done.3
  59.2 1.3 fusion.11
  60.4 1.0 fusion
  61.5 1.0 fusion.8
  62.5 103.4 %reduce-scatter.2.cloned.1.call-done = f32[12,128,8]{1,2,0:T(8,128)} async-done(((f32[12,128,128]{1,2,0:T(8,128)}), f32[12,128,8]{1,2,0:T(8,128)}) %reduce-scatter.2.cloned.1.call-update) | async-done | bytes 49168 | tf_op jit(solution)/shard_map/reduce_scatter | solution.py:109
  165.9 180.8 %psum.7 = f32[12,128,8]{1,2,0:T(8,128)S(1)} all-reduce(f32[12,128,8]{1,2,0:T(8,128)} %reduce-scatter.2.cloned.1.call-done), channel_id=1, replica_groups=mesh['frames'=64,'rows'=16] {'frames'}, use_global_device_ids=true, to_apply=%region_1.2 | all-reduce | flops 12288 | bytes 98304 | tf_op jit(solution)/shard_map/psum | solution.py:110
  346.6 0.6 slice.192
  347.3 0.6 slice.193
  (36 shorter events, 2.9 us)
Async XLA Ops:
  7.2 6.4 %copy-start.1 = (f32[2,2,96,128]{3,2,1,0:T(8,128)S(1)}, f32[2,2,96,128]{3,2,1,0:T(8,128)}, u32[]{:S(2)}) copy-start(f32[2,2,96,128]{3,2,1,0:T(8,128)} %param.7) | copy-start | bytes 589828
  7.2 19.8 %copy-start.5 = (f32[3,128,128]{2,1,0:T(8,128)S(1)}, f32[3,128,128]{2,1,0:T(8,128)}, u32[]{:S(2)}) copy-start(f32[3,128,128]{2,1,0:T(8,128)} %param.6) | copy-start | bytes 589828
  7.2 158.7 %reduce-scatter.2.cloned.1.call-start = ((), (), s32[]{:S(2)}) async-start(), calls=%async_computation.1 | async-start | bytes 835584 | tf_op jit(solution)/shard_map/reduce_scatter | solution.py:109
  8.3 19.1 %collective-permute-start = (f32[2,1,96,128]{3,2,1,0:T(8,128)S(1)}, f32[2,1,96,128]{3,2,1,0:T(8,128)S(1)}, u32[]{:S(2)}, u32[]{:S(2)}) collective-permute-start(f32[2,1,96,128]{3,2,1,0:T(8,128)S(1)} %get-tuple-element.8), channel_id=1, source_target_pairs={{0,1},{1,2},{2,3},{3,4},{4,5},{5,6},{6,7},{7,8},{8,9},{9,10},{10,1... | collective-permute-start | bytes 294920 | tf_op jit(solution)/shard_map/ppermute | solution.py:18
  12.3 16.6 %collective-permute-start.1 = (f32[2,1,96,128]{3,2,1,0:T(8,128)S(1)}, f32[2,1,96,128]{3,2,1,0:T(8,128)S(1)}, u32[]{:S(2)}, u32[]{:S(2)}) collective-permute-start(f32[2,1,96,128]{3,2,1,0:T(8,128)S(1)} %get-tuple-element.9), channel_id=1, source_target_pairs={{1,0},{2,1},{3,2},{4,3},{5,4},{6,5},{7,6},{8,7},{9,8},{10,9},{11,1... | collective-permute-start | bytes 294920 | tf_op jit(solution)/shard_map/ppermute | solution.py:19
  13.6 21.4 %collective-permute-start.3 = (f32[2,2,96,128]{3,2,1,0:T(8,128)S(1)}, f32[2,2,96,128]{3,2,1,0:T(8,128)S(1)}, u32[]{:S(2)}, u32[]{:S(2)}) collective-permute-start(f32[2,2,96,128]{3,2,1,0:T(8,128)S(1)} %copy-done.1), channel_id=1, source_target_pairs={{16,0},{32,16},{48,32},{64,48},{80,64},{96,80},{112,96},{128,112},... | collective-permute-start | bytes 589832 | tf_op jit(solution)/shard_map/ppermute | solution.py:27
  27.3 0.9 copy-start
  27.3 1.2 copy-start.2
  31.5 22.9 %collective-permute-start.2 = (f32[2,2,96,128]{3,2,1,0:T(8,128)S(1)}, f32[2,2,96,128]{3,2,1,0:T(8,128)S(1)}, u32[]{:S(2)}, u32[]{:S(2)}) collective-permute-start(f32[2,2,96,128]{3,2,1,0:T(8,128)S(1)} %get-tuple-element.10), channel_id=1, source_target_pairs={{0,16},{16,32},{32,48},{48,64},{64,80},{80,96},{96,112},{112,128},... | collective-permute-start | bytes 589832 | tf_op jit(solution)/shard_map/ppermute | solution.py:27
  41.2 6.2 %collective-permute-start.4 = (f32[2,1,96,128]{3,2,1,0:T(8,128)}, f32[2,1,96,128]{3,2,1,0:T(8,128)S(1)}, u32[]{:S(2)}, u32[]{:S(2)}) collective-permute-start(f32[2,1,96,128]{3,2,1,0:T(8,128)} %get-tuple-element.4), channel_id=1, source_target_pairs={{0,1},{1,2},{2,3},{3,4},{4,5},{5,6},{6,7},{7,8},{8,9},{9,10},{10,1... | collective-permute-start | bytes 294920 | tf_op jit(solution)/shard_map/ppermute | solution.py:18
  45.5 5.7 %collective-permute-start.5 = (f32[2,1,96,128]{3,2,1,0:T(8,128)}, f32[2,1,96,128]{3,2,1,0:T(8,128)}, u32[]{:S(2)}, u32[]{:S(2)}) collective-permute-start(f32[2,1,96,128]{3,2,1,0:T(8,128)} %get-tuple-element.5), channel_id=1, source_target_pairs={{1,0},{2,1},{3,2},{4,3},{5,4},{6,5},{7,6},{8,7},{9,8},{10,9},{11,1... | collective-permute-start | bytes 294920 | tf_op jit(solution)/shard_map/ppermute | solution.py:19
  56.9 0.9 copy-start.6
  58.1 0.9 copy-start.3
  58.1 1.0 copy-start.4
  60.4 1.0 copy-start.7
Sparse Core Ops, SparseCore 0:
  56.7 109.1 reduce-scatter.1
where the time goes:
time: 356 us; the launch traced here: 355 us
  blocking collectives  181 us (51%)
  waiting for transfers between devices  107 us (30%)
  starting transfers between devices  26.4 us (7%)
  matrix products  18 us (5%)
  between operations  14.5 us (4%)
  local copies, waits for them, and re-layouts  5.76 us (2%)
    psum x1, blocking collectives, per_device(): summed = lax.psum(shares, 'frames')  181 us
    reduce_scatter x1, waiting for transfers between devices, per_device(): lax.psum_scatter(all_terms, 'rows', scatter_dimension=2, tiled=True)  103 us
    ppermute x2, starting transfers between devices, passed_along(): return lax.ppermute(value, axis, pairs)  15.3 us
    ppermute x2, starting transfers between devices, padded_2(): before = lax.ppermute(last, axis, up)  8.22 us
  transfers between devices with their start and end apart: 7, of which 3 were waited for; matrix products, arithmetic and copies ran while one was open for 5% of the time, Pallas kernels for 0%

commit v1 on v0

--- a/solution.py
+++ b/solution.py
@@ -53,6 +53,31 @@
     return dact
 
 
+def halving_scatter(blocks, axis):
+    count = blocks.shape[0]
+    me = lax.axis_index(axis)
+    mask = count // 2
+    while mask >= 1:
+        half = blocks.shape[0] // 2
+        bit = (me // mask) % 2
+        keep = lax.dynamic_slice_in_dim(blocks, bit * half, half, axis=0)
+        give = lax.dynamic_slice_in_dim(blocks, (1 - bit) * half, half, axis=0)
+        pairs = [(i, i ^ mask) for i in range(count)]
+        blocks = keep + lax.ppermute(give, axis, pairs)
+        mask //= 2
+    return blocks
+
+
+def doubling_sum(value, axis):
+    count = lax.axis_size(axis)
+    mask = 1
+    while mask < count:
+        pairs = [(i, i ^ mask) for i in range(count)]
+        value = value + lax.ppermute(value, axis, pairs)
+        mask *= 2
+    return value
+
+
 def per_device(images, spatial_weight, temporal_weight, cotangent):
     nframes, strip, width, chans = images.shape
     padded = widen(padded_2(images, (("rows", 1),), 1))
@@ -83,31 +108,24 @@
             )
     total_cells = nframes * lax.axis_size("frames") * strip * lax.axis_size("rows") * width
     factor = 1.0 / math.sqrt(total_cells)
-    rows_out = []
+    taps = []
     for i in range(3):
-        cols_out = []
         for j in range(3):
-            cols_out.append(
+            taps.append(
                 jnp.einsum(
-                    "frwc,frwd->cd", padded[:, i : i + strip, j : j + width], dpre, precision=HIGH
+                    "frwc,frwd->dc", padded[:, i : i + strip, j : j + width], dpre, precision=HIGH
                 )
             )
-        rows_out.append(jnp.stack(cols_out))
-    spatial_terms = jnp.stack(rows_out).reshape(9, chans, chans) * factor
-    temporal_terms = (
-        jnp.stack(
-            [
-                jnp.einsum(
-                    "frwc,frwd->cd", longer[2 - k : 2 - k + nframes], cotangent, precision=HIGH
-                )
-                for k in range(3)
-            ]
+    for k in range(3):
+        taps.append(
+            jnp.einsum("frwc,frwd->dc", longer[2 - k : 2 - k + nframes], cotangent, precision=HIGH)
         )
-        * factor
-    )
-    all_terms = jnp.concatenate([spatial_terms, temporal_terms], axis=0)
-    shares = lax.psum_scatter(all_terms, "rows", scatter_dimension=2, tiled=True)
-    summed = lax.psum(shares, "frames")
+    nrows = lax.axis_size("rows")
+    terms = jnp.stack(taps, axis=1) * factor
+    terms = terms.reshape(nrows, chans // nrows, len(taps), chans)
+    summed = halving_scatter(terms, "rows")[0]
+    summed = doubling_sum(summed, "frames")
+    summed = jnp.transpose(summed, (1, 2, 0))
     grad_spatial = summed[:9].reshape(3, 3, chans, summed.shape[2])
     grad_temporal = summed[9:]
     return (block_out, grad_images, grad_spatial, grad_temporal)

time: 356 us -> 149 us (0.42)
  the two profiles are of different devices: /device:TPU:1 before, /device:TPU:24 now
where the time goes in v1:
time: 149 us; the launch traced here: 148 us
  starting transfers between devices  96.2 us (65%)
  waiting for transfers between devices  32.4 us (22%)
  matrix products  15.1 us (10%)
  local copies, waits for them, and re-layouts  3.17 us (2%)
    ppermute x6, starting transfers between devices, doubling_sum(): value = value + lax.ppermute(value, axis, pairs)  62.2 us
    ppermute x4, waiting for transfers between devices, halving_scatter(): blocks = keep + lax.ppermute(give, axis, pairs)  22.6 us
    ppermute x4, starting transfers between devices, halving_scatter(): blocks = keep + lax.ppermute(give, axis, pairs)  13.8 us
    ppermute x2, starting transfers between devices, padded_2(): after = lax.ppermute(leading, axis, down)  10.6 us
    ppermute x6, waiting for transfers between devices, doubling_sum(): value = value + lax.ppermute(value, axis, pairs)  9.75 us
    ppermute x2, starting transfers between devices, padded_2(): before = lax.ppermute(last, axis, up)  5.32 us
    dot_general x9, matrix products, per_device(): jnp.einsum('frwc,frwd->dc', padded[:, i:i + strip, j:j + width], dpre, pr...  4.42 us
    ppermute x2, starting transfers between devices, passed_along(): return lax.ppermute(value, axis, pairs)  4.34 us
  transfers between devices with their start and end apart: 16, of which 10 were waited for; matrix products, arithmetic and copies ran while one was open for 10% of the time, Pallas kernels for 0%

profile of v1, /device:TPU:24, one launch (start us, length us, event | category | flops | bytes accessed | tf_op | source)
XLA Modules:
  0.0 148.5 jit_solution(309068326391361572)
XLA Ops:
  0.7 1.0 fusion.123
  1.7 3.4 %collective-permute-start = (f32[2,1,96,128]{3,2,1,0:T(8,128)S(1)}, f32[2,1,96,128]{3,2,1,0:T(8,128)S(1)}, u32[]{:S(2)}, u32[]{:S(2)}) collective-permute-start(f32[2,1,96,128]{3,2,1,0:T(8,128)S(1)} %get-tuple-element.8), channel_id=1, source_target_pairs={{0,1},{1,2},{2,3},{3,4},{4,5},{5,6},{6,7},{7,8},{8,9},{9,10},{10,1... | collective-permute-start | bytes 294920 | tf_op jit(solution)/shard_map/ppermute | solution.py:18
  5.1 4.6 %collective-permute-start.1 = (f32[2,1,96,128]{3,2,1,0:T(8,128)S(1)}, f32[2,1,96,128]{3,2,1,0:T(8,128)S(1)}, u32[]{:S(2)}, u32[]{:S(2)}) collective-permute-start(f32[2,1,96,128]{3,2,1,0:T(8,128)S(1)} %get-tuple-element.9), channel_id=1, source_target_pairs={{1,0},{2,1},{3,2},{4,3},{5,4},{6,5},{7,6},{8,7},{9,8},{10,9},{11,1... | collective-permute-start | bytes 294920 | tf_op jit(solution)/shard_map/ppermute | solution.py:19
  9.6 1.3 collective-permute-start.3
  11.5 0.8 copy-done
  14.9 0.3 fusion.47
  15.3 3.0 %collective-permute-start.2 = (f32[2,2,96,128]{3,2,1,0:T(8,128)S(1)}, f32[2,2,96,128]{3,2,1,0:T(8,128)S(1)}, u32[]{:S(2)}, u32[]{:S(2)}) collective-permute-start(f32[2,2,96,128]{3,2,1,0:T(8,128)S(1)} %get-tuple-element.10), channel_id=1, source_target_pairs={{0,16},{16,32},{32,48},{48,64},{64,80},{80,96},{96,112},{112,128},... | collective-permute-start | bytes 589832 | tf_op jit(solution)/shard_map/ppermute | solution.py:27
  18.3 0.3 fusion.89
  19.0 0.4 fusion.6
  19.4 0.5 fusion.23
  19.9 0.5 fusion.22
  20.4 0.5 fusion.21
  20.9 0.5 fusion.20
  21.4 0.5 fusion.19
  21.9 0.5 fusion.18
  22.4 0.5 fusion.17
  22.9 0.5 fusion.16
  23.4 0.5 fusion.15
  23.9 1.9 %collective-permute-start.4 = (f32[2,1,96,128]{3,2,1,0:T(8,128)S(1)}, f32[2,1,96,128]{3,2,1,0:T(8,128)S(1)}, u32[]{:S(2)}, u32[]{:S(2)}) collective-permute-start(f32[2,1,96,128]{3,2,1,0:T(8,128)S(1)} %get-tuple-element.4), channel_id=1, source_target_pairs={{0,1},{1,2},{2,3},{3,4},{4,5},{5,6},{6,7},{7,8},{8,9},{9,10},{10,1... | collective-permute-start | bytes 294920 | tf_op jit(solution)/shard_map/ppermute | solution.py:18
  25.8 6.0 %collective-permute-start.5 = (f32[2,1,96,128]{3,2,1,0:T(8,128)S(1)}, f32[2,1,96,128]{3,2,1,0:T(8,128)S(1)}, u32[]{:S(2)}, u32[]{:S(2)}) collective-permute-start(f32[2,1,96,128]{3,2,1,0:T(8,128)S(1)} %get-tuple-element.5), channel_id=1, source_target_pairs={{1,0},{2,1},{3,2},{4,3},{5,4},{6,5},{7,6},{8,7},{9,8},{10,9},{11,1... | collective-permute-start | bytes 294920 | tf_op jit(solution)/shard_map/ppermute | solution.py:19
  31.8 0.5 fusion.14
  32.3 0.5 fusion.12
  32.8 0.5 fusion.13
  33.5 3.1 %collective-permute-start.6 = (f32[8,8,12,128]{3,1,2,0:T(8,128)S(1)}, f32[8,8,12,128]{3,1,2,0:T(8,128)S(1)}, u32[]{:S(2)}, u32[]{:S(2)}) collective-permute-start(f32[8,8,12,128]{3,1,2,0:T(8,128)S(1)} %constant_dynamic-slice_fusion.3), channel_id=1, source_target_pairs={{0,8},{1,9},{2,10},{3,11},{4,12},{5,13},{6,14},{7,15},{8,0},{9,1},... | collective-permute-start | bytes 1179656 | tf_op jit(solution)/shard_map/ppermute | solution.py:66
  37.4 11.5 %collective-permute-done.6 = f32[8,8,12,128]{3,1,2,0:T(8,128)S(1)} collective-permute-done((f32[8,8,12,128]{3,1,2,0:T(8,128)S(1)}, f32[8,8,12,128]{3,1,2,0:T(8,128)S(1)}, u32[]{:S(2)}, u32[]{:S(2)}) %collective-permute-start.6) | collective-permute-done | bytes 393248 | tf_op jit(solution)/shard_map/ppermute | solution.py:66
  48.9 3.7 %collective-permute-start.7 = (f32[4,8,12,128]{3,1,2,0:T(8,128)S(1)}, f32[4,8,12,128]{3,1,2,0:T(8,128)S(1)}, u32[]{:S(2)}, u32[]{:S(2)}) collective-permute-start(f32[4,8,12,128]{3,1,2,0:T(8,128)S(1)} %constant_dynamic-slice_fusion.2), channel_id=1, source_target_pairs={{0,4},{1,5},{2,6},{3,7},{4,0},{5,1},{6,2},{7,3},{8,12},{9,13},{10,... | collective-permute-start | bytes 589832 | tf_op jit(solution)/shard_map/ppermute | solution.py:66
  53.0 4.8 %collective-permute-done.7 = f32[4,8,12,128]{3,1,2,0:T(8,128)S(1)} collective-permute-done((f32[4,8,12,128]{3,1,2,0:T(8,128)S(1)}, f32[4,8,12,128]{3,1,2,0:T(8,128)S(1)}, u32[]{:S(2)}, u32[]{:S(2)}) %collective-permute-start.7) | collective-permute-done | bytes 196640 | tf_op jit(solution)/shard_map/ppermute | solution.py:66
  57.8 3.7 %collective-permute-start.8 = (f32[2,8,12,128]{3,1,2,0:T(8,128)S(1)}, f32[2,8,12,128]{3,1,2,0:T(8,128)S(1)}, u32[]{:S(2)}, u32[]{:S(2)}) collective-permute-start(f32[2,8,12,128]{3,1,2,0:T(8,128)S(1)} %constant_dynamic-slice_fusion.1), channel_id=1, source_target_pairs={{0,2},{1,3},{2,0},{3,1},{4,6},{5,7},{6,4},{7,5},{8,10},{9,11},{10,... | collective-permute-start | bytes 294920 | tf_op jit(solution)/shard_map/ppermute | solution.py:66
  61.8 4.0 %collective-permute-done.8 = f32[2,8,12,128]{3,1,2,0:T(8,128)S(1)} collective-permute-done((f32[2,8,12,128]{3,1,2,0:T(8,128)S(1)}, f32[2,8,12,128]{3,1,2,0:T(8,128)S(1)}, u32[]{:S(2)}, u32[]{:S(2)}) %collective-permute-start.8) | collective-permute-done | bytes 98336 | tf_op jit(solution)/shard_map/ppermute | solution.py:66
  65.8 3.2 %collective-permute-start.9 = (f32[1,8,12,128]{3,1,2,0:T(8,128)S(1)}, f32[1,8,12,128]{3,1,2,0:T(8,128)S(1)}, u32[]{:S(2)}, u32[]{:S(2)}) collective-permute-start(f32[1,8,12,128]{3,1,2,0:T(8,128)S(1)} %constant_dynamic-slice_fusion), channel_id=1, source_target_pairs={{0,1},{1,0},{2,3},{3,2},{4,5},{5,4},{6,7},{7,6},{8,9},{9,8},{10,11... | collective-permute-start | bytes 147464 | tf_op jit(solution)/shard_map/ppermute | solution.py:66
  69.4 2.4 %collective-permute-done.9 = f32[1,8,12,128]{3,1,2,0:T(8,128)S(1)} collective-permute-done((f32[1,8,12,128]{3,1,2,0:T(8,128)S(1)}, f32[1,8,12,128]{3,1,2,0:T(8,128)S(1)}, u32[]{:S(2)}, u32[]{:S(2)}) %collective-permute-start.9) | collective-permute-done | bytes 49184 | tf_op jit(solution)/shard_map/ppermute | solution.py:66
  71.8 1.9 %collective-permute-start.10 = (f32[8,12,128]{2,0,1:T(8,128)S(1)}, f32[8,12,128]{2,0,1:T(8,128)S(1)}, u32[]{:S(2)}, u32[]{:S(2)}) collective-permute-start(f32[8,12,128]{2,0,1:T(8,128)S(1)} %add_bitcast_fusion.1), channel_id=1, source_target_pairs={{0,16},{16,0},{32,48},{48,32},{64,80},{80,64},{96,112},{112,96},{1... | collective-permute-start | bytes 147464 | tf_op jit(solution)/shard_map/ppermute | solution.py:76
  74.1 0.9 collective-permute-done.10
  75.0 3.8 %collective-permute-start.11 = (f32[8,12,128]{2,0,1:T(8,128)S(1)}, f32[8,12,128]{2,0,1:T(8,128)S(1)}, u32[]{:S(2)}, u32[]{:S(2)}) collective-permute-start(f32[8,12,128]{2,0,1:T(8,128)S(1)} %add.188), channel_id=1, source_target_pairs={{0,32},{16,48},{32,0},{48,16},{64,96},{80,112},{96,64},{112,80},{1... | collective-permute-start | bytes 147464 | tf_op jit(solution)/shard_map/ppermute | solution.py:76
  78.8 0.4 fusion.11
  79.1 1.8 %collective-permute-done.11 = f32[8,12,128]{2,0,1:T(8,128)S(1)} collective-permute-done((f32[8,12,128]{2,0,1:T(8,128)S(1)}, f32[8,12,128]{2,0,1:T(8,128)S(1)}, u32[]{:S(2)}, u32[]{:S(2)}) %collective-permute-start.11) | collective-permute-done | bytes 49184 | tf_op jit(solution)/shard_map/ppermute | solution.py:76
  80.9 5.1 %collective-permute-start.12 = (f32[8,12,128]{2,0,1:T(8,128)S(1)}, f32[8,12,128]{2,0,1:T(8,128)S(1)}, u32[]{:S(2)}, u32[]{:S(2)}) collective-permute-start(f32[8,12,128]{2,0,1:T(8,128)S(1)} %add.189), channel_id=1, source_target_pairs={{0,64},{16,80},{32,96},{48,112},{64,0},{80,16},{96,32},{112,48},{1... | collective-permute-start | bytes 147464 | tf_op jit(solution)/shard_map/ppermute | solution.py:76
  86.4 1.7 %collective-permute-done.12 = f32[8,12,128]{2,0,1:T(8,128)S(1)} collective-permute-done((f32[8,12,128]{2,0,1:T(8,128)S(1)}, f32[8,12,128]{2,0,1:T(8,128)S(1)}, u32[]{:S(2)}, u32[]{:S(2)}) %collective-permute-start.12) | collective-permute-done | bytes 49184 | tf_op jit(solution)/shard_map/ppermute | solution.py:76
  88.2 9.1 %collective-permute-start.13 = (f32[8,12,128]{2,0,1:T(8,128)S(1)}, f32[8,12,128]{2,0,1:T(8,128)S(1)}, u32[]{:S(2)}, u32[]{:S(2)}) collective-permute-start(f32[8,12,128]{2,0,1:T(8,128)S(1)} %add.190), channel_id=1, source_target_pairs={{0,128},{16,144},{32,160},{48,176},{64,192},{80,208},{96,224},{112... | collective-permute-start | bytes 147464 | tf_op jit(solution)/shard_map/ppermute | solution.py:76
  97.3 1.0 fusion.8
  98.3 1.1 collective-permute-done.13
  99.4 15.7 %collective-permute-start.14 = (f32[8,12,128]{2,0,1:T(8,128)S(1)}, f32[8,12,128]{2,0,1:T(8,128)S(1)}, u32[]{:S(2)}, u32[]{:S(2)}) collective-permute-start(f32[8,12,128]{2,0,1:T(8,128)S(1)} %add.191), channel_id=1, source_target_pairs={{0,256},{16,272},{32,288},{48,304},{64,320},{80,336},{96,352},{112... | collective-permute-start | bytes 147464 | tf_op jit(solution)/shard_map/ppermute | solution.py:76
  115.5 2.2 %collective-permute-done.14 = f32[8,12,128]{2,0,1:T(8,128)S(1)} collective-permute-done((f32[8,12,128]{2,0,1:T(8,128)S(1)}, f32[8,12,128]{2,0,1:T(8,128)S(1)}, u32[]{:S(2)}, u32[]{:S(2)}) %collective-permute-start.14) | collective-permute-done | bytes 49184 | tf_op jit(solution)/shard_map/ppermute | solution.py:76
  117.7 26.5 %collective-permute-start.15 = (f32[8,12,128]{2,0,1:T(8,128)S(1)}, f32[8,12,128]{2,0,1:T(8,128)S(1)}, u32[]{:S(2)}, u32[]{:S(2)}) collective-permute-start(f32[8,12,128]{2,0,1:T(8,128)S(1)} %add.192), channel_id=1, source_target_pairs={{0,512},{16,528},{32,544},{48,560},{64,576},{80,592},{96,608},{112... | collective-permute-start | bytes 147464 | tf_op jit(solution)/shard_map/ppermute | solution.py:76
  144.3 1.0 fusion
  145.3 2.0 %collective-permute-done.15 = f32[8,12,128]{2,0,1:T(8,128)S(1)} collective-permute-done((f32[8,12,128]{2,0,1:T(8,128)S(1)}, f32[8,12,128]{2,0,1:T(8,128)S(1)}, u32[]{:S(2)}, u32[]{:S(2)}) %collective-permute-start.15) | collective-permute-done | bytes 49184 | tf_op jit(solution)/shard_map/ppermute | solution.py:76
  147.3 0.6 slice.194
  147.9 0.6 slice.195
  (52 shorter events, 6.2 us)
Async XLA Ops:
  0.6 9.0 %copy-start.1 = (f32[2,2,96,128]{3,2,1,0:T(8,128)S(1)}, f32[2,2,96,128]{3,2,1,0:T(8,128)}, u32[]{:S(2)}) copy-start(f32[2,2,96,128]{3,2,1,0:T(8,128)} %param.7) | copy-start | bytes 589828
  0.6 10.3 %copy-start.3 = (f32[3,128,128]{2,1,0:T(8,128)S(1)}, f32[3,128,128]{2,1,0:T(8,128)}, u32[]{:S(2)}) copy-start(f32[3,128,128]{2,1,0:T(8,128)} %param.6) | copy-start | bytes 589828
  1.7 9.8 %collective-permute-start = (f32[2,1,96,128]{3,2,1,0:T(8,128)S(1)}, f32[2,1,96,128]{3,2,1,0:T(8,128)S(1)}, u32[]{:S(2)}, u32[]{:S(2)}) collective-permute-start(f32[2,1,96,128]{3,2,1,0:T(8,128)S(1)} %get-tuple-element.8), channel_id=1, source_target_pairs={{0,1},{1,2},{2,3},{3,4},{4,5},{5,6},{6,7},{7,8},{8,9},{9,10},{10,1... | collective-permute-start | bytes 294920 | tf_op jit(solution)/shard_map/ppermute | solution.py:18
  5.1 7.5 %collective-permute-start.1 = (f32[2,1,96,128]{3,2,1,0:T(8,128)S(1)}, f32[2,1,96,128]{3,2,1,0:T(8,128)S(1)}, u32[]{:S(2)}, u32[]{:S(2)}) collective-permute-start(f32[2,1,96,128]{3,2,1,0:T(8,128)S(1)} %get-tuple-element.9), channel_id=1, source_target_pairs={{1,0},{2,1},{3,2},{4,3},{5,4},{6,5},{7,6},{8,7},{9,8},{10,9},{11,1... | collective-permute-start | bytes 294920 | tf_op jit(solution)/shard_map/ppermute | solution.py:19
  9.6 9.0 %collective-permute-start.3 = (f32[2,2,96,128]{3,2,1,0:T(8,128)S(1)}, f32[2,2,96,128]{3,2,1,0:T(8,128)S(1)}, u32[]{:S(2)}, u32[]{:S(2)}) collective-permute-start(f32[2,2,96,128]{3,2,1,0:T(8,128)S(1)} %copy-done.1), channel_id=1, source_target_pairs={{16,0},{32,16},{48,32},{64,48},{80,64},{96,80},{112,96},{128,112},... | collective-permute-start | bytes 589832 | tf_op jit(solution)/shard_map/ppermute | solution.py:27
  11.0 1.3 copy-start.2
  11.3 0.9 copy-start
  15.3 17.1 %collective-permute-start.2 = (f32[2,2,96,128]{3,2,1,0:T(8,128)S(1)}, f32[2,2,96,128]{3,2,1,0:T(8,128)S(1)}, u32[]{:S(2)}, u32[]{:S(2)}) collective-permute-start(f32[2,2,96,128]{3,2,1,0:T(8,128)S(1)} %get-tuple-element.10), channel_id=1, source_target_pairs={{0,16},{16,32},{32,48},{48,64},{64,80},{80,96},{96,112},{112,128},... | collective-permute-start | bytes 589832 | tf_op jit(solution)/shard_map/ppermute | solution.py:27
  23.9 13.1 %collective-permute-start.4 = (f32[2,1,96,128]{3,2,1,0:T(8,128)S(1)}, f32[2,1,96,128]{3,2,1,0:T(8,128)S(1)}, u32[]{:S(2)}, u32[]{:S(2)}) collective-permute-start(f32[2,1,96,128]{3,2,1,0:T(8,128)S(1)} %get-tuple-element.4), channel_id=1, source_target_pairs={{0,1},{1,2},{2,3},{3,4},{4,5},{5,6},{6,7},{7,8},{8,9},{9,10},{10,1... | collective-permute-start | bytes 294920 | tf_op jit(solution)/shard_map/ppermute | solution.py:18
  25.8 11.2 %collective-permute-start.5 = (f32[2,1,96,128]{3,2,1,0:T(8,128)S(1)}, f32[2,1,96,128]{3,2,1,0:T(8,128)S(1)}, u32[]{:S(2)}, u32[]{:S(2)}) collective-permute-start(f32[2,1,96,128]{3,2,1,0:T(8,128)S(1)} %get-tuple-element.5), channel_id=1, source_target_pairs={{1,0},{2,1},{3,2},{4,3},{5,4},{6,5},{7,6},{8,7},{9,8},{10,9},{11,1... | collective-permute-start | bytes 294920 | tf_op jit(solution)/shard_map/ppermute | solution.py:19
  33.5 15.4 %collective-permute-start.6 = (f32[8,8,12,128]{3,1,2,0:T(8,128)S(1)}, f32[8,8,12,128]{3,1,2,0:T(8,128)S(1)}, u32[]{:S(2)}, u32[]{:S(2)}) collective-permute-start(f32[8,8,12,128]{3,1,2,0:T(8,128)S(1)} %constant_dynamic-slice_fusion.3), channel_id=1, source_target_pairs={{0,8},{1,9},{2,10},{3,11},{4,12},{5,13},{6,14},{7,15},{8,0},{9,1},... | collective-permute-start | bytes 1179656 | tf_op jit(solution)/shard_map/ppermute | solution.py:66
  48.9 8.8 %collective-permute-start.7 = (f32[4,8,12,128]{3,1,2,0:T(8,128)S(1)}, f32[4,8,12,128]{3,1,2,0:T(8,128)S(1)}, u32[]{:S(2)}, u32[]{:S(2)}) collective-permute-start(f32[4,8,12,128]{3,1,2,0:T(8,128)S(1)} %constant_dynamic-slice_fusion.2), channel_id=1, source_target_pairs={{0,4},{1,5},{2,6},{3,7},{4,0},{5,1},{6,2},{7,3},{8,12},{9,13},{10,... | collective-permute-start | bytes 589832 | tf_op jit(solution)/shard_map/ppermute | solution.py:66
  57.8 8.0 %collective-permute-start.8 = (f32[2,8,12,128]{3,1,2,0:T(8,128)S(1)}, f32[2,8,12,128]{3,1,2,0:T(8,128)S(1)}, u32[]{:S(2)}, u32[]{:S(2)}) collective-permute-start(f32[2,8,12,128]{3,1,2,0:T(8,128)S(1)} %constant_dynamic-slice_fusion.1), channel_id=1, source_target_pairs={{0,2},{1,3},{2,0},{3,1},{4,6},{5,7},{6,4},{7,5},{8,10},{9,11},{10,... | collective-permute-start | bytes 294920 | tf_op jit(solution)/shard_map/ppermute | solution.py:66
  65.8 6.0 %collective-permute-start.9 = (f32[1,8,12,128]{3,1,2,0:T(8,128)S(1)}, f32[1,8,12,128]{3,1,2,0:T(8,128)S(1)}, u32[]{:S(2)}, u32[]{:S(2)}) collective-permute-start(f32[1,8,12,128]{3,1,2,0:T(8,128)S(1)} %constant_dynamic-slice_fusion), channel_id=1, source_target_pairs={{0,1},{1,0},{2,3},{3,2},{4,5},{5,4},{6,7},{7,6},{8,9},{9,8},{10,11... | collective-permute-start | bytes 147464 | tf_op jit(solution)/shard_map/ppermute | solution.py:66
  71.8 3.1 %collective-permute-start.10 = (f32[8,12,128]{2,0,1:T(8,128)S(1)}, f32[8,12,128]{2,0,1:T(8,128)S(1)}, u32[]{:S(2)}, u32[]{:S(2)}) collective-permute-start(f32[8,12,128]{2,0,1:T(8,128)S(1)} %add_bitcast_fusion.1), channel_id=1, source_target_pairs={{0,16},{16,0},{32,48},{48,32},{64,80},{80,64},{96,112},{112,96},{1... | collective-permute-start | bytes 147464 | tf_op jit(solution)/shard_map/ppermute | solution.py:76
  75.0 6.0 %collective-permute-start.11 = (f32[8,12,128]{2,0,1:T(8,128)S(1)}, f32[8,12,128]{2,0,1:T(8,128)S(1)}, u32[]{:S(2)}, u32[]{:S(2)}) collective-permute-start(f32[8,12,128]{2,0,1:T(8,128)S(1)} %add.188), channel_id=1, source_target_pairs={{0,32},{16,48},{32,0},{48,16},{64,96},{80,112},{96,64},{112,80},{1... | collective-permute-start | bytes 147464 | tf_op jit(solution)/shard_map/ppermute | solution.py:76
  80.9 7.2 %collective-permute-start.12 = (f32[8,12,128]{2,0,1:T(8,128)S(1)}, f32[8,12,128]{2,0,1:T(8,128)S(1)}, u32[]{:S(2)}, u32[]{:S(2)}) collective-permute-start(f32[8,12,128]{2,0,1:T(8,128)S(1)} %add.189), channel_id=1, source_target_pairs={{0,64},{16,80},{32,96},{48,112},{64,0},{80,16},{96,32},{112,48},{1... | collective-permute-start | bytes 147464 | tf_op jit(solution)/shard_map/ppermute | solution.py:76
  88.2 11.2 %collective-permute-start.13 = (f32[8,12,128]{2,0,1:T(8,128)S(1)}, f32[8,12,128]{2,0,1:T(8,128)S(1)}, u32[]{:S(2)}, u32[]{:S(2)}) collective-permute-start(f32[8,12,128]{2,0,1:T(8,128)S(1)} %add.190), channel_id=1, source_target_pairs={{0,128},{16,144},{32,160},{48,176},{64,192},{80,208},{96,224},{112... | collective-permute-start | bytes 147464 | tf_op jit(solution)/shard_map/ppermute | solution.py:76
  99.4 18.3 %collective-permute-start.14 = (f32[8,12,128]{2,0,1:T(8,128)S(1)}, f32[8,12,128]{2,0,1:T(8,128)S(1)}, u32[]{:S(2)}, u32[]{:S(2)}) collective-permute-start(f32[8,12,128]{2,0,1:T(8,128)S(1)} %add.191), channel_id=1, source_target_pairs={{0,256},{16,272},{32,288},{48,304},{64,320},{80,336},{96,352},{112... | collective-permute-start | bytes 147464 | tf_op jit(solution)/shard_map/ppermute | solution.py:76
  117.7 29.5 %collective-permute-start.15 = (f32[8,12,128]{2,0,1:T(8,128)S(1)}, f32[8,12,128]{2,0,1:T(8,128)S(1)}, u32[]{:S(2)}, u32[]{:S(2)}) collective-permute-start(f32[8,12,128]{2,0,1:T(8,128)S(1)} %add.192), channel_id=1, source_target_pairs={{0,512},{16,528},{32,544},{48,560},{64,576},{80,592},{96,608},{112... | collective-permute-start | bytes 147464 | tf_op jit(solution)/shard_map/ppermute | solution.py:76

commit v2 on v1

--- a/solution.py
+++ b/solution.py
@@ -53,29 +53,37 @@
     return dact
 
 
-def halving_scatter(blocks, axis):
-    count = blocks.shape[0]
+def halving_scatter(blocks, axis, order):
+    count = lax.axis_size(axis)
+    bits = count.bit_length() - 1
     me = lax.axis_index(axis)
-    mask = count // 2
-    while mask >= 1:
-        half = blocks.shape[0] // 2
+    rest = blocks.shape[1:]
+    blocks = blocks.reshape((2,) * bits + rest)
+    for mask in order:
+        dim = bits - mask.bit_length()
         bit = (me // mask) % 2
-        keep = lax.dynamic_slice_in_dim(blocks, bit * half, half, axis=0)
-        give = lax.dynamic_slice_in_dim(blocks, (1 - bit) * half, half, axis=0)
+        keep = lax.dynamic_slice_in_dim(blocks, bit, 1, axis=dim)
+        give = lax.dynamic_slice_in_dim(blocks, 1 - bit, 1, axis=dim)
         pairs = [(i, i ^ mask) for i in range(count)]
         blocks = keep + lax.ppermute(give, axis, pairs)
-        mask //= 2
-    return blocks
+    return blocks.reshape(rest)
 
 
-def doubling_sum(value, axis):
+def doubling_sum(value, axis, first):
     count = lax.axis_size(axis)
-    mask = 1
+    mask = first
     while mask < count:
         pairs = [(i, i ^ mask) for i in range(count)]
         value = value + lax.ppermute(value, axis, pairs)
         mask *= 2
     return value
+
+
+def pair_gather(value, axis):
+    count = lax.axis_size(axis)
+    low = lax.axis_index(axis) % 2 == 0
+    other = lax.ppermute(value, axis, [(i, i ^ 1) for i in range(count)])
+    return jnp.where(low, jnp.concatenate([value, other]), jnp.concatenate([other, value]))
 
 
 def per_device(images, spatial_weight, temporal_weight, cotangent):
@@ -122,9 +130,15 @@
         )
     nrows = lax.axis_size("rows")
     terms = jnp.stack(taps, axis=1) * factor
-    terms = terms.reshape(nrows, chans // nrows, len(taps), chans)
-    summed = halving_scatter(terms, "rows")[0]
-    summed = doubling_sum(summed, "frames")
+    terms = terms.reshape(nrows, 2, chans // nrows // 2, len(taps), chans)
+    parity = lax.axis_index("frames") % 2
+    keep = lax.dynamic_index_in_dim(terms, parity, axis=1, keepdims=False)
+    give = lax.dynamic_index_in_dim(terms, 1 - parity, axis=1, keepdims=False)
+    nframes_all = lax.axis_size("frames")
+    terms = keep + lax.ppermute(give, "frames", [(i, i ^ 1) for i in range(nframes_all)])
+    order = [nrows // 4, 1, nrows // 2, 2] if nrows == 16 else [nrows >> k for k in range(1, 5)]
+    terms = halving_scatter(terms, "rows", [m for m in order if m >= 1])
+    summed = pair_gather(doubling_sum(terms, "frames", 2), "frames")
     summed = jnp.transpose(summed, (1, 2, 0))
     grad_spatial = summed[:9].reshape(3, 3, chans, summed.shape[2])
     grad_temporal = summed[9:]

time: 149 us -> 144 us (0.966)
  the two profiles are of different devices: /device:TPU:24 before, /device:TPU:1 now
where the time goes in v2:
time: 144 us; the launch traced here: 143 us
  starting transfers between devices  88 us (61%)
  waiting for transfers between devices  34.6 us (24%)
  matrix products  15.1 us (10%)
  local copies, waits for them, and re-layouts  3.6 us (2%)
  between operations  1.49 us (1%)
    ppermute x5, starting transfers between devices, doubling_sum(): value = value + lax.ppermute(value, axis, pairs)  37.9 us
    ppermute x5, waiting for transfers between devices, doubling_sum(): value = value + lax.ppermute(value, axis, pairs)  15.4 us
    ppermute x2, starting transfers between devices, passed_along(): return lax.ppermute(value, axis, pairs)  15.3 us
    ppermute x4, waiting for transfers between devices, halving_scatter(): blocks = keep + lax.ppermute(give, axis, pairs)  14.8 us
    ppermute x1, starting transfers between devices, pair_gather(): other = lax.ppermute(value, axis, [(i, i ^ 1) for i in range(count)])  12.8 us
    ppermute x4, starting transfers between devices, halving_scatter(): blocks = keep + lax.ppermute(give, axis, pairs)  8.79 us
    ppermute x2, starting transfers between devices, padded_2(): before = lax.ppermute(last, axis, up)  7.73 us
    dot_general x9, matrix products, per_device(): jnp.einsum('frwc,frwd->dc', padded[:, i:i + strip, j:j + width], dpre, pr...  4.43 us
  transfers between devices with their start and end apart: 17, of which 11 were waited for; matrix products, arithmetic and copies ran while one was open for 10% of the time, Pallas kernels for 0%

profile of v2, /device:TPU:1, one launch (start us, length us, event | category | flops | bytes accessed | tf_op | source)
XLA Modules:
  0.0 143.2 jit_solution(10344594785469216402)
XLA Ops:
  0.7 1.0 fusion.122
  1.7 4.0 %collective-permute-start = (f32[2,1,96,128]{3,2,1,0:T(8,128)S(1)}, f32[2,1,96,128]{3,2,1,0:T(8,128)S(1)}, u32[]{:S(2)}, u32[]{:S(2)}) collective-permute-start(f32[2,1,96,128]{3,2,1,0:T(8,128)S(1)} %get-tuple-element.10), channel_id=1, source_target_pairs={{0,1},{1,2},{2,3},{3,4},{4,5},{5,6},{6,7},{7,8},{8,9},{9,10},{10,1... | collective-permute-start | bytes 294920 | tf_op jit(solution)/shard_map/ppermute | solution.py:18
  5.6 1.3 collective-permute-start.1
  6.9 13.4 %collective-permute-start.3 = (f32[2,2,96,128]{3,2,1,0:T(8,128)S(1)}, f32[2,2,96,128]{3,2,1,0:T(8,128)S(1)}, u32[]{:S(2)}, u32[]{:S(2)}) collective-permute-start(f32[2,2,96,128]{3,2,1,0:T(8,128)S(1)} %copy-done.1), channel_id=1, source_target_pairs={{16,0},{32,16},{48,32},{64,48},{80,64},{96,80},{112,96},{128,112},... | collective-permute-start | bytes 589832 | tf_op jit(solution)/shard_map/ppermute | solution.py:27
  20.9 0.8 copy-done
  24.7 0.5 fusion.118
  25.2 1.9 %collective-permute-start.2 = (f32[2,2,96,128]{3,2,1,0:T(8,128)S(1)}, f32[2,2,96,128]{3,2,1,0:T(8,128)S(1)}, u32[]{:S(2)}, u32[]{:S(2)}) collective-permute-start(f32[2,2,96,128]{3,2,1,0:T(8,128)S(1)} %get-tuple-element.12), channel_id=1, source_target_pairs={{0,16},{16,32},{32,48},{48,64},{64,80},{80,96},{96,112},{112,128},... | collective-permute-start | bytes 589832 | tf_op jit(solution)/shard_map/ppermute | solution.py:27
  27.8 0.4 fusion.6
  28.1 0.5 fusion.55
  28.6 0.5 fusion.25
  29.1 0.5 fusion.52
  29.6 0.5 fusion.49
  30.1 0.5 fusion.123
  30.6 0.5 fusion.46
  31.1 0.5 fusion.43
  31.6 0.5 fusion.23
  32.1 0.5 fusion.39
  32.9 0.5 fusion.16
  33.4 0.5 fusion.124
  34.0 2.9 %collective-permute-start.6 = (f32[16,4,12,128]{3,0,2,1:T(8,128)S(1)}, f32[16,4,12,128]{3,0,2,1:T(8,128)S(1)}, u32[]{:S(2)}, u32[]{:S(2)}) collective-permute-start(f32[16,4,12,128]{3,0,2,1:T(8,128)S(1)} %dynamic-slice_bitcast_fusion), channel_id=1, source_target_pairs={{0,16},{16,0},{32,48},{48,32},{64,80},{80,64},{96,112},{112,96},{1... | collective-permute-start | bytes 1179656 | tf_op jit(solution)/shard_map/ppermute | solution.py:138
  37.0 3.8 %collective-permute-start.4 = (f32[2,1,96,128]{3,2,1,0:T(8,128)S(1)}, f32[2,1,96,128]{3,2,1,0:T(8,128)S(1)}, u32[]{:S(2)}, u32[]{:S(2)}) collective-permute-start(f32[2,1,96,128]{3,2,1,0:T(8,128)S(1)} %get-tuple-element.6), channel_id=1, source_target_pairs={{0,1},{1,2},{2,3},{3,4},{4,5},{5,6},{6,7},{7,8},{8,9},{9,10},{10,1... | collective-permute-start | bytes 294920 | tf_op jit(solution)/shard_map/ppermute | solution.py:18
  40.7 1.3 collective-permute-start.5
  42.4 0.6 collective-permute-done.4
  42.9 3.8 %collective-permute-done.5 = f32[2,1,96,128]{3,2,1,0:T(8,128)S(1)} collective-permute-done((f32[2,1,96,128]{3,2,1,0:T(8,128)S(1)}, f32[2,1,96,128]{3,2,1,0:T(8,128)S(1)}, u32[]{:S(2)}, u32[]{:S(2)}) %collective-permute-start.5) | collective-permute-done | bytes 98336 | tf_op jit(solution)/shard_map/ppermute | solution.py:19
  47.1 1.9 %collective-permute-start.7 = (f32[2,1,2,2,4,12,128]{6,4,5,3,2,1,0:T(4,128)S(1)}, f32[2,1,2,2,4,12,128]{6,4,5,3,2,1,0:T(4,128)S(1)}, u32[]{:S(2)}, u32[]{:S(2)}) collective-permute-start(f32[2,1,2,2,4,12,128]{6,4,5,3,2,1,0:T(4,128)S(1)} %copy.47), channel_id=1, source_target_pairs={{0,4},{1,5},{2,6},{3,7},{4,0},{5,1},{6,2},{7,3},{8,12},{9,13},{10,... | collective-permute-start | bytes 589832 | tf_op jit(solution)/shard_map/ppermute | solution.py:68
  49.4 4.9 %collective-permute-done.7 = f32[2,1,2,2,4,12,128]{6,4,5,3,2,1,0:T(4,128)S(1)} collective-permute-done((f32[2,1,2,2,4,12,128]{6,4,5,3,2,1,0:T(4,128)S(1)}, f32[2,1,2,2,4,12,128]{6,4,5,3,2,1,0:T(4,128)S(1)}, u32[]{:S(2)}, u32[]{:S(2)}) %collective-permute-start.7) | collective-permute-done | bytes 196640 | tf_op jit(solution)/shard_map/ppermute | solution.py:68
  54.5 2.8 %collective-permute-start.8 = (f32[2,1,2,1,4,12,128]{6,4,5,3,2,1,0:T(4,128)S(1)}, f32[2,1,2,1,4,12,128]{6,4,5,3,2,1,0:T(4,128)S(1)}, u32[]{:S(2)}, u32[]{:S(2)}) collective-permute-start(f32[2,1,2,1,4,12,128]{6,4,5,3,2,1,0:T(4,128)S(1)} %constant_dynamic-slice_fusion.2), channel_id=1, source_target_pairs={{0,1},{1,0},{2,3},{3,2},{4,5},{5,4},{6,7},{7,6},{8,9},{9,8},{10,11... | collective-permute-start | bytes 294920 | tf_op jit(solution)/shard_map/ppermute | solution.py:68
  57.6 2.3 %collective-permute-done.8 = f32[2,1,2,1,4,12,128]{6,4,5,3,2,1,0:T(4,128)S(1)} collective-permute-done((f32[2,1,2,1,4,12,128]{6,4,5,3,2,1,0:T(4,128)S(1)}, f32[2,1,2,1,4,12,128]{6,4,5,3,2,1,0:T(4,128)S(1)}, u32[]{:S(2)}, u32[]{:S(2)}) %collective-permute-start.8) | collective-permute-done | bytes 98336 | tf_op jit(solution)/shard_map/ppermute | solution.py:68
  59.9 1.9 %collective-permute-start.9 = (f32[1,1,2,1,4,12,128]{6,4,5,3,2,1,0:T(4,128)S(1)}, f32[1,1,2,1,4,12,128]{6,4,5,3,2,1,0:T(4,128)S(1)}, u32[]{:S(2)}, u32[]{:S(2)}) collective-permute-start(f32[1,1,2,1,4,12,128]{6,4,5,3,2,1,0:T(4,128)S(1)} %constant_dynamic-slice_fusion.1), channel_id=1, source_target_pairs={{0,8},{1,9},{2,10},{3,11},{4,12},{5,13},{6,14},{7,15},{8,0},{9,1},... | collective-permute-start | bytes 147464 | tf_op jit(solution)/shard_map/ppermute | solution.py:68
  62.2 4.1 %collective-permute-done.9 = f32[1,1,2,1,4,12,128]{6,4,5,3,2,1,0:T(4,128)S(1)} collective-permute-done((f32[1,1,2,1,4,12,128]{6,4,5,3,2,1,0:T(4,128)S(1)}, f32[1,1,2,1,4,12,128]{6,4,5,3,2,1,0:T(4,128)S(1)}, u32[]{:S(2)}, u32[]{:S(2)}) %collective-permute-start.9) | collective-permute-done | bytes 49184 | tf_op jit(solution)/shard_map/ppermute | solution.py:68
  66.3 2.2 %collective-permute-start.10 = (f32[1,1,1,1,4,12,128]{6,4,5,3,2,1,0:T(4,128)S(1)}, f32[1,1,1,1,4,12,128]{6,4,5,3,2,1,0:T(4,128)S(1)}, u32[]{:S(2)}, u32[]{:S(2)}) collective-permute-start(f32[1,1,1,1,4,12,128]{6,4,5,3,2,1,0:T(4,128)S(1)} %constant_dynamic-slice_fusion), channel_id=1, source_target_pairs={{0,2},{1,3},{2,0},{3,1},{4,6},{5,7},{6,4},{7,5},{8,10},{9,11},{10,... | collective-permute-start | bytes 73736 | tf_op jit(solution)/shard_map/ppermute | solution.py:68
  68.8 3.6 %collective-permute-done.10 = f32[1,1,1,1,4,12,128]{6,4,5,3,2,1,0:T(4,128)S(1)} collective-permute-done((f32[1,1,1,1,4,12,128]{6,4,5,3,2,1,0:T(4,128)S(1)}, f32[1,1,1,1,4,12,128]{6,4,5,3,2,1,0:T(4,128)S(1)}, u32[]{:S(2)}, u32[]{:S(2)}) %collective-permute-start.10) | collective-permute-done | bytes 24608 | tf_op jit(solution)/shard_map/ppermute | solution.py:68
  72.4 1.9 %collective-permute-start.11 = (f32[4,12,128]{2,0,1:T(4,128)S(1)}, f32[4,12,128]{2,0,1:T(4,128)S(1)}, u32[]{:S(2)}, u32[]{:S(2)}) collective-permute-start(f32[4,12,128]{2,0,1:T(4,128)S(1)} %add_bitcast_fusion), channel_id=1, source_target_pairs={{0,32},{16,48},{32,0},{48,16},{64,96},{80,112},{96,64},{112,80},{1... | collective-permute-start | bytes 73736 | tf_op jit(solution)/shard_map/ppermute | solution.py:77
  74.6 2.6 %collective-permute-done.11 = f32[4,12,128]{2,0,1:T(4,128)S(1)} collective-permute-done((f32[4,12,128]{2,0,1:T(4,128)S(1)}, f32[4,12,128]{2,0,1:T(4,128)S(1)}, u32[]{:S(2)}, u32[]{:S(2)}) %collective-permute-start.11) | collective-permute-done | bytes 24608 | tf_op jit(solution)/shard_map/ppermute | solution.py:77
  77.3 1.9 %collective-permute-start.12 = (f32[4,12,128]{2,0,1:T(4,128)S(1)}, f32[4,12,128]{2,0,1:T(4,128)S(1)}, u32[]{:S(2)}, u32[]{:S(2)}) collective-permute-start(f32[4,12,128]{2,0,1:T(4,128)S(1)} %add.207), channel_id=1, source_target_pairs={{0,64},{16,80},{32,96},{48,112},{64,0},{80,16},{96,32},{112,48},{1... | collective-permute-start | bytes 73736 | tf_op jit(solution)/shard_map/ppermute | solution.py:77
  79.2 0.4 fusion.11
  79.5 3.2 %collective-permute-done.12 = f32[4,12,128]{2,0,1:T(4,128)S(1)} collective-permute-done((f32[4,12,128]{2,0,1:T(4,128)S(1)}, f32[4,12,128]{2,0,1:T(4,128)S(1)}, u32[]{:S(2)}, u32[]{:S(2)}) %collective-permute-start.12) | collective-permute-done | bytes 24608 | tf_op jit(solution)/shard_map/ppermute | solution.py:77
  82.7 3.1 %collective-permute-start.13 = (f32[4,12,128]{2,0,1:T(4,128)S(1)}, f32[4,12,128]{2,0,1:T(4,128)S(1)}, u32[]{:S(2)}, u32[]{:S(2)}) collective-permute-start(f32[4,12,128]{2,0,1:T(4,128)S(1)} %add.208), channel_id=1, source_target_pairs={{0,128},{16,144},{32,160},{48,176},{64,192},{80,208},{96,224},{112... | collective-permute-start | bytes 73736 | tf_op jit(solution)/shard_map/ppermute | solution.py:77
  86.2 5.4 %collective-permute-done.13 = f32[4,12,128]{2,0,1:T(4,128)S(1)} collective-permute-done((f32[4,12,128]{2,0,1:T(4,128)S(1)}, f32[4,12,128]{2,0,1:T(4,128)S(1)}, u32[]{:S(2)}, u32[]{:S(2)}) %collective-permute-start.13) | collective-permute-done | bytes 24608 | tf_op jit(solution)/shard_map/ppermute | solution.py:77
  91.6 10.9 %collective-permute-start.14 = (f32[4,12,128]{2,0,1:T(4,128)S(1)}, f32[4,12,128]{2,0,1:T(4,128)S(1)}, u32[]{:S(2)}, u32[]{:S(2)}) collective-permute-start(f32[4,12,128]{2,0,1:T(4,128)S(1)} %add.209), channel_id=1, source_target_pairs={{0,256},{16,272},{32,288},{48,304},{64,320},{80,336},{96,352},{112... | collective-permute-start | bytes 73736 | tf_op jit(solution)/shard_map/ppermute | solution.py:77
  102.5 1.0 fusion.8
  103.5 1.4 collective-permute-done.14
  104.9 20.0 %collective-permute-start.15 = (f32[4,12,128]{2,0,1:T(4,128)S(1)}, f32[4,12,128]{2,0,1:T(4,128)S(1)}, u32[]{:S(2)}, u32[]{:S(2)}) collective-permute-start(f32[4,12,128]{2,0,1:T(4,128)S(1)} %add.210), channel_id=1, source_target_pairs={{0,512},{16,528},{32,544},{48,560},{64,576},{80,592},{96,608},{112... | collective-permute-start | bytes 73736 | tf_op jit(solution)/shard_map/ppermute | solution.py:77
  125.2 2.9 %collective-permute-done.15 = f32[4,12,128]{2,0,1:T(4,128)S(1)} collective-permute-done((f32[4,12,128]{2,0,1:T(4,128)S(1)}, f32[4,12,128]{2,0,1:T(4,128)S(1)}, u32[]{:S(2)}, u32[]{:S(2)}) %collective-permute-start.15) | collective-permute-done | bytes 24608 | tf_op jit(solution)/shard_map/ppermute | solution.py:77
  128.1 12.8 %collective-permute-start.16 = (f32[4,12,128]{2,0,1:T(4,128)S(1)}, f32[4,12,128]{2,0,1:T(4,128)S(1)}, u32[]{:S(2)}, u32[]{:S(2)}) collective-permute-start(f32[4,12,128]{2,0,1:T(4,128)S(1)} %add.211), channel_id=1, source_target_pairs={{0,16},{16,0},{32,48},{48,32},{64,80},{80,64},{96,112},{112,96},{1... | collective-permute-start | bytes 73736 | tf_op jit(solution)/shard_map/ppermute | solution.py:85
  140.9 1.0 fusion
  142.0 0.6 slice.194
  142.6 0.6 slice.195
  (69 shorter events, 7.5 us)
Async XLA Ops:
  0.6 6.3 %copy-start.1 = (f32[2,2,96,128]{3,2,1,0:T(8,128)S(1)}, f32[2,2,96,128]{3,2,1,0:T(8,128)}, u32[]{:S(2)}) copy-start(f32[2,2,96,128]{3,2,1,0:T(8,128)} %param.7) | copy-start | bytes 589828
  0.6 19.7 %copy-start.3 = (f32[3,128,128]{2,1,0:T(8,128)S(1)}, f32[3,128,128]{2,1,0:T(8,128)}, u32[]{:S(2)}) copy-start(f32[3,128,128]{2,1,0:T(8,128)} %param.6) | copy-start | bytes 589828
  1.7 19.2 %collective-permute-start = (f32[2,1,96,128]{3,2,1,0:T(8,128)S(1)}, f32[2,1,96,128]{3,2,1,0:T(8,128)S(1)}, u32[]{:S(2)}, u32[]{:S(2)}) collective-permute-start(f32[2,1,96,128]{3,2,1,0:T(8,128)S(1)} %get-tuple-element.10), channel_id=1, source_target_pairs={{0,1},{1,2},{2,3},{3,4},{4,5},{5,6},{6,7},{7,8},{8,9},{9,10},{10,1... | collective-permute-start | bytes 294920 | tf_op jit(solution)/shard_map/ppermute | solution.py:18
  5.6 16.4 %collective-permute-start.1 = (f32[2,1,96,128]{3,2,1,0:T(8,128)S(1)}, f32[2,1,96,128]{3,2,1,0:T(8,128)S(1)}, u32[]{:S(2)}, u32[]{:S(2)}) collective-permute-start(f32[2,1,96,128]{3,2,1,0:T(8,128)S(1)} %get-tuple-element.11), channel_id=1, source_target_pairs={{1,0},{2,1},{3,2},{4,3},{5,4},{6,5},{7,6},{8,7},{9,8},{10,9},{11,1... | collective-permute-start | bytes 294920 | tf_op jit(solution)/shard_map/ppermute | solution.py:19
  6.9 20.5 %collective-permute-start.3 = (f32[2,2,96,128]{3,2,1,0:T(8,128)S(1)}, f32[2,2,96,128]{3,2,1,0:T(8,128)S(1)}, u32[]{:S(2)}, u32[]{:S(2)}) collective-permute-start(f32[2,2,96,128]{3,2,1,0:T(8,128)S(1)} %copy-done.1), channel_id=1, source_target_pairs={{16,0},{32,16},{48,32},{64,48},{80,64},{96,80},{112,96},{128,112},... | collective-permute-start | bytes 589832 | tf_op jit(solution)/shard_map/ppermute | solution.py:27
  20.4 1.3 copy-start.2
  20.7 0.9 copy-start
  25.2 7.7 %collective-permute-start.2 = (f32[2,2,96,128]{3,2,1,0:T(8,128)S(1)}, f32[2,2,96,128]{3,2,1,0:T(8,128)S(1)}, u32[]{:S(2)}, u32[]{:S(2)}) collective-permute-start(f32[2,2,96,128]{3,2,1,0:T(8,128)S(1)} %get-tuple-element.12), channel_id=1, source_target_pairs={{0,16},{16,32},{32,48},{48,64},{64,80},{80,96},{96,112},{112,128},... | collective-permute-start | bytes 589832 | tf_op jit(solution)/shard_map/ppermute | solution.py:27
  34.0 12.8 %collective-permute-start.6 = (f32[16,4,12,128]{3,0,2,1:T(8,128)S(1)}, f32[16,4,12,128]{3,0,2,1:T(8,128)S(1)}, u32[]{:S(2)}, u32[]{:S(2)}) collective-permute-start(f32[16,4,12,128]{3,0,2,1:T(8,128)S(1)} %dynamic-slice_bitcast_fusion), channel_id=1, source_target_pairs={{0,16},{16,0},{32,48},{48,32},{64,80},{80,64},{96,112},{112,96},{1... | collective-permute-start | bytes 1179656 | tf_op jit(solution)/shard_map/ppermute | solution.py:138
  37.0 6.0 %collective-permute-start.4 = (f32[2,1,96,128]{3,2,1,0:T(8,128)S(1)}, f32[2,1,96,128]{3,2,1,0:T(8,128)S(1)}, u32[]{:S(2)}, u32[]{:S(2)}) collective-permute-start(f32[2,1,96,128]{3,2,1,0:T(8,128)S(1)} %get-tuple-element.6), channel_id=1, source_target_pairs={{0,1},{1,2},{2,3},{3,4},{4,5},{5,6},{6,7},{7,8},{8,9},{9,10},{10,1... | collective-permute-start | bytes 294920 | tf_op jit(solution)/shard_map/ppermute | solution.py:18
  40.7 6.0 %collective-permute-start.5 = (f32[2,1,96,128]{3,2,1,0:T(8,128)S(1)}, f32[2,1,96,128]{3,2,1,0:T(8,128)S(1)}, u32[]{:S(2)}, u32[]{:S(2)}) collective-permute-start(f32[2,1,96,128]{3,2,1,0:T(8,128)S(1)} %get-tuple-element.7), channel_id=1, source_target_pairs={{1,0},{2,1},{3,2},{4,3},{5,4},{6,5},{7,6},{8,7},{9,8},{10,9},{11,1... | collective-permute-start | bytes 294920 | tf_op jit(solution)/shard_map/ppermute | solution.py:19
  47.1 7.2 %collective-permute-start.7 = (f32[2,1,2,2,4,12,128]{6,4,5,3,2,1,0:T(4,128)S(1)}, f32[2,1,2,2,4,12,128]{6,4,5,3,2,1,0:T(4,128)S(1)}, u32[]{:S(2)}, u32[]{:S(2)}) collective-permute-start(f32[2,1,2,2,4,12,128]{6,4,5,3,2,1,0:T(4,128)S(1)} %copy.47), channel_id=1, source_target_pairs={{0,4},{1,5},{2,6},{3,7},{4,0},{5,1},{6,2},{7,3},{8,12},{9,13},{10,... | collective-permute-start | bytes 589832 | tf_op jit(solution)/shard_map/ppermute | solution.py:68
  54.5 5.4 %collective-permute-start.8 = (f32[2,1,2,1,4,12,128]{6,4,5,3,2,1,0:T(4,128)S(1)}, f32[2,1,2,1,4,12,128]{6,4,5,3,2,1,0:T(4,128)S(1)}, u32[]{:S(2)}, u32[]{:S(2)}) collective-permute-start(f32[2,1,2,1,4,12,128]{6,4,5,3,2,1,0:T(4,128)S(1)} %constant_dynamic-slice_fusion.2), channel_id=1, source_target_pairs={{0,1},{1,0},{2,3},{3,2},{4,5},{5,4},{6,7},{7,6},{8,9},{9,8},{10,11... | collective-permute-start | bytes 294920 | tf_op jit(solution)/shard_map/ppermute | solution.py:68
  59.9 6.3 %collective-permute-start.9 = (f32[1,1,2,1,4,12,128]{6,4,5,3,2,1,0:T(4,128)S(1)}, f32[1,1,2,1,4,12,128]{6,4,5,3,2,1,0:T(4,128)S(1)}, u32[]{:S(2)}, u32[]{:S(2)}) collective-permute-start(f32[1,1,2,1,4,12,128]{6,4,5,3,2,1,0:T(4,128)S(1)} %constant_dynamic-slice_fusion.1), channel_id=1, source_target_pairs={{0,8},{1,9},{2,10},{3,11},{4,12},{5,13},{6,14},{7,15},{8,0},{9,1},... | collective-permute-start | bytes 147464 | tf_op jit(solution)/shard_map/ppermute | solution.py:68
  66.3 6.1 %collective-permute-start.10 = (f32[1,1,1,1,4,12,128]{6,4,5,3,2,1,0:T(4,128)S(1)}, f32[1,1,1,1,4,12,128]{6,4,5,3,2,1,0:T(4,128)S(1)}, u32[]{:S(2)}, u32[]{:S(2)}) collective-permute-start(f32[1,1,1,1,4,12,128]{6,4,5,3,2,1,0:T(4,128)S(1)} %constant_dynamic-slice_fusion), channel_id=1, source_target_pairs={{0,2},{1,3},{2,0},{3,1},{4,6},{5,7},{6,4},{7,5},{8,10},{9,11},{10,... | collective-permute-start | bytes 73736 | tf_op jit(solution)/shard_map/ppermute | solution.py:68
  72.4 4.9 %collective-permute-start.11 = (f32[4,12,128]{2,0,1:T(4,128)S(1)}, f32[4,12,128]{2,0,1:T(4,128)S(1)}, u32[]{:S(2)}, u32[]{:S(2)}) collective-permute-start(f32[4,12,128]{2,0,1:T(4,128)S(1)} %add_bitcast_fusion), channel_id=1, source_target_pairs={{0,32},{16,48},{32,0},{48,16},{64,96},{80,112},{96,64},{112,80},{1... | collective-permute-start | bytes 73736 | tf_op jit(solution)/shard_map/ppermute | solution.py:77
  77.3 5.5 %collective-permute-start.12 = (f32[4,12,128]{2,0,1:T(4,128)S(1)}, f32[4,12,128]{2,0,1:T(4,128)S(1)}, u32[]{:S(2)}, u32[]{:S(2)}) collective-permute-start(f32[4,12,128]{2,0,1:T(4,128)S(1)} %add.207), channel_id=1, source_target_pairs={{0,64},{16,80},{32,96},{48,112},{64,0},{80,16},{96,32},{112,48},{1... | collective-permute-start | bytes 73736 | tf_op jit(solution)/shard_map/ppermute | solution.py:77
  82.7 8.8 %collective-permute-start.13 = (f32[4,12,128]{2,0,1:T(4,128)S(1)}, f32[4,12,128]{2,0,1:T(4,128)S(1)}, u32[]{:S(2)}, u32[]{:S(2)}) collective-permute-start(f32[4,12,128]{2,0,1:T(4,128)S(1)} %add.208), channel_id=1, source_target_pairs={{0,128},{16,144},{32,160},{48,176},{64,192},{80,208},{96,224},{112... | collective-permute-start | bytes 73736 | tf_op jit(solution)/shard_map/ppermute | solution.py:77
  91.6 13.3 %collective-permute-start.14 = (f32[4,12,128]{2,0,1:T(4,128)S(1)}, f32[4,12,128]{2,0,1:T(4,128)S(1)}, u32[]{:S(2)}, u32[]{:S(2)}) collective-permute-start(f32[4,12,128]{2,0,1:T(4,128)S(1)} %add.209), channel_id=1, source_target_pairs={{0,256},{16,272},{32,288},{48,304},{64,320},{80,336},{96,352},{112... | collective-permute-start | bytes 73736 | tf_op jit(solution)/shard_map/ppermute | solution.py:77
  104.9 23.2 %collective-permute-start.15 = (f32[4,12,128]{2,0,1:T(4,128)S(1)}, f32[4,12,128]{2,0,1:T(4,128)S(1)}, u32[]{:S(2)}, u32[]{:S(2)}) collective-permute-start(f32[4,12,128]{2,0,1:T(4,128)S(1)} %add.210), channel_id=1, source_target_pairs={{0,512},{16,528},{32,544},{48,560},{64,576},{80,592},{96,608},{112... | collective-permute-start | bytes 73736 | tf_op jit(solution)/shard_map/ppermute | solution.py:77
  128.1 13.9 %collective-permute-start.16 = (f32[4,12,128]{2,0,1:T(4,128)S(1)}, f32[4,12,128]{2,0,1:T(4,128)S(1)}, u32[]{:S(2)}, u32[]{:S(2)}) collective-permute-start(f32[4,12,128]{2,0,1:T(4,128)S(1)} %add.211), channel_id=1, source_target_pairs={{0,16},{16,0},{32,48},{48,32},{64,80},{80,64},{96,112},{112,96},{1... | collective-permute-start | bytes 73736 | tf_op jit(solution)/shard_map/ppermute | solution.py:85

commit v3 on v2

--- a/solution.py
+++ b/solution.py
@@ -72,11 +72,12 @@
 def doubling_sum(value, axis, first):
     count = lax.axis_size(axis)
     mask = first
-    while mask < count:
+    while mask < count // 2:
         pairs = [(i, i ^ mask) for i in range(count)]
         value = value + lax.ppermute(value, axis, pairs)
         mask *= 2
-    return value
+    pairs = [(i, count - first * (i // first + 1) + i % first) for i in range(count)]
+    return value + lax.ppermute(value, axis, pairs)
 
 
 def pair_gather(value, axis):
@@ -136,8 +137,7 @@
     give = lax.dynamic_index_in_dim(terms, 1 - parity, axis=1, keepdims=False)
     nframes_all = lax.axis_size("frames")
     terms = keep + lax.ppermute(give, "frames", [(i, i ^ 1) for i in range(nframes_all)])
-    order = [nrows // 4, 1, nrows // 2, 2] if nrows == 16 else [nrows >> k for k in range(1, 5)]
-    terms = halving_scatter(terms, "rows", [m for m in order if m >= 1])
+    terms = lax.all_to_all(terms, "rows", 0, 0, tiled=True).sum(axis=0)
     summed = pair_gather(doubling_sum(terms, "frames", 2), "frames")
     summed = jnp.transpose(summed, (1, 2, 0))
     grad_spatial = summed[:9].reshape(3, 3, chans, summed.shape[2])

time: 144 us -> 125 us (0.87)
  the two profiles are of different devices: /device:TPU:1 before, /device:TPU:225 now
where the time goes in v3:
time: 125 us; the launch traced here: 124 us
  starting transfers between devices  70.6 us (56%)
  waiting for transfers between devices  31 us (25%)
  matrix products  15.7 us (13%)
  local copies, waits for them, and re-layouts  4.42 us (4%)
  between operations  1.3 us (1%)
  other arithmetic  1.27 us (1%)
    ppermute x4, starting transfers between devices, doubling_sum(): value = value + lax.ppermute(value, axis, pairs)  21.5 us
    ppermute x4, waiting for transfers between devices, doubling_sum(): value = value + lax.ppermute(value, axis, pairs)  12.5 us
    ppermute x1, starting transfers between devices, doubling_sum(): return value + lax.ppermute(value, axis, pairs)  12.2 us
    all_to_all x1, starting transfers between devices, per_device(): terms = lax.all_to_all(terms, 'rows', 0, 0, tiled=True).sum(axis=0)  9.96 us
    all_to_all x1, waiting for transfers between devices, per_device(): terms = lax.all_to_all(terms, 'rows', 0, 0, tiled=True).sum(axis=0)  9.87 us
    ppermute x2, starting transfers between devices, passed_along(): return lax.ppermute(value, axis, pairs)  8.93 us
    ppermute x1, waiting for transfers between devices, doubling_sum(): return value + lax.ppermute(value, axis, pairs)  8.32 us
    ppermute x1, starting transfers between devices, pair_gather(): other = lax.ppermute(value, axis, [(i, i ^ 1) for i in range(count)])  7.24 us
  transfers between devices with their start and end apart: 14, of which 8 were waited for; matrix products, arithmetic and copies ran while one was open for 13% of the time, Pallas kernels for 0%

profile of v3, /device:TPU:225, one launch (start us, length us, event | category | flops | bytes accessed | tf_op | source)
XLA Modules:
  0.0 124.3 jit_solution(9244201720006605232)
XLA Ops:
  0.7 1.0 fusion.122
  1.7 3.1 %collective-permute-start = (f32[2,1,96,128]{3,2,1,0:T(8,128)S(1)}, f32[2,1,96,128]{3,2,1,0:T(8,128)S(1)}, u32[]{:S(2)}, u32[]{:S(2)}) collective-permute-start(f32[2,1,96,128]{3,2,1,0:T(8,128)S(1)} %get-tuple-element.10), channel_id=1, source_target_pairs={{0,1},{1,2},{2,3},{3,4},{4,5},{5,6},{6,7},{7,8},{8,9},{9,10},{10,1... | collective-permute-start | bytes 294920 | tf_op jit(solution)/shard_map/ppermute | solution.py:18
  4.8 1.3 %collective-permute-start.1 = (f32[2,1,96,128]{3,2,1,0:T(8,128)S(1)}, f32[2,1,96,128]{3,2,1,0:T(8,128)S(1)}, u32[]{:S(2)}, u32[]{:S(2)}) collective-permute-start(f32[2,1,96,128]{3,2,1,0:T(8,128)S(1)} %get-tuple-element.11), channel_id=1, source_target_pairs={{1,0},{2,1},{3,2},{4,3},{5,4},{6,5},{7,6},{8,7},{9,8},{10,9},{11,1... | collective-permute-start | bytes 294920 | tf_op jit(solution)/shard_map/ppermute | solution.py:19
  6.1 2.9 %collective-permute-start.3 = (f32[2,2,96,128]{3,2,1,0:T(8,128)S(1)}, f32[2,2,96,128]{3,2,1,0:T(8,128)S(1)}, u32[]{:S(2)}, u32[]{:S(2)}) collective-permute-start(f32[2,2,96,128]{3,2,1,0:T(8,128)S(1)} %copy-done.1), channel_id=1, source_target_pairs={{16,0},{32,16},{48,32},{64,48},{80,64},{96,80},{112,96},{128,112},... | collective-permute-start | bytes 589832 | tf_op jit(solution)/shard_map/ppermute | solution.py:27
  9.0 0.3 fusion.84
  9.4 0.9 copy-done
  13.1 0.3 fusion.38
  13.5 0.5 fusion.118
  14.0 6.1 %collective-permute-start.2 = (f32[2,2,96,128]{3,2,1,0:T(8,128)S(1)}, f32[2,2,96,128]{3,2,1,0:T(8,128)S(1)}, u32[]{:S(2)}, u32[]{:S(2)}) collective-permute-start(f32[2,2,96,128]{3,2,1,0:T(8,128)S(1)} %get-tuple-element.12), channel_id=1, source_target_pairs={{0,16},{16,32},{32,48},{48,64},{64,80},{80,96},{96,112},{112,128},... | collective-permute-start | bytes 589832 | tf_op jit(solution)/shard_map/ppermute | solution.py:27
  20.1 1.0 fusion.86
  21.4 0.3 fusion.6
  21.8 0.5 fusion.55
  22.3 0.5 fusion.25
  22.8 0.5 fusion.52
  23.3 0.5 fusion.49
  23.8 0.5 fusion.123
  24.3 0.5 fusion.46
  24.8 0.5 fusion.43
  25.3 0.5 fusion.23
  25.8 0.5 fusion.39
  26.3 3.1 %collective-permute-start.4 = (f32[2,1,96,128]{3,2,1,0:T(8,128)S(1)}, f32[2,1,96,128]{3,2,1,0:T(8,128)S(1)}, u32[]{:S(2)}, u32[]{:S(2)}) collective-permute-start(f32[2,1,96,128]{3,2,1,0:T(8,128)S(1)} %get-tuple-element.6), channel_id=1, source_target_pairs={{0,1},{1,2},{2,3},{3,4},{4,5},{5,6},{6,7},{7,8},{8,9},{9,10},{10,1... | collective-permute-start | bytes 294920 | tf_op jit(solution)/shard_map/ppermute | solution.py:18
  29.4 1.3 %collective-permute-start.5 = (f32[2,1,96,128]{3,2,1,0:T(8,128)S(1)}, f32[2,1,96,128]{3,2,1,0:T(8,128)S(1)}, u32[]{:S(2)}, u32[]{:S(2)}) collective-permute-start(f32[2,1,96,128]{3,2,1,0:T(8,128)S(1)} %get-tuple-element.7), channel_id=1, source_target_pairs={{1,0},{2,1},{3,2},{4,3},{5,4},{6,5},{7,6},{8,7},{9,8},{10,9},{11,1... | collective-permute-start | bytes 294920 | tf_op jit(solution)/shard_map/ppermute | solution.py:19
  30.9 0.3 fusion.66
  31.2 0.5 fusion.16
  31.8 0.5 fusion.124
  32.7 1.9 %collective-permute-start.6 = (f32[16,4,12,128]{3,1,2,0:T(4,128)S(1)}, f32[16,4,12,128]{3,1,2,0:T(4,128)S(1)}, u32[]{:S(2)}, u32[]{:S(2)}) collective-permute-start(f32[16,4,12,128]{3,1,2,0:T(4,128)S(1)} %bitcast.205), channel_id=1, source_target_pairs={{0,16},{16,0},{32,48},{48,32},{64,80},{80,64},{96,112},{112,96},{1... | collective-permute-start | bytes 1179656 | tf_op jit(solution)/shard_map/ppermute | solution.py:139
  34.8 0.6 copy-done.3
  35.5 0.3 fusion.29
  35.8 0.3 fusion.31
  36.3 0.8 bitcast_add_fusion
  37.2 10.0 %all-to-all-start = ((f32[16,4,12,128]{3,1,2,0:T(4,128)}), f32[16,4,12,128]{3,1,2,0:T(4,128)S(1)}, u32[]{:S(2)}, u32[]{:S(2)}) async-start(f32[16,4,12,128]{3,1,2,0:T(4,128)} %bitcast_add_fusion), calls=%async_computation | async-start | bytes 786432 | tf_op jit(solution)/shard_map/all_to_all | solution.py:140
  47.8 9.9 %all-to-all-done = f32[16,4,12,128]{3,1,2,0:T(4,128)S(1)} async-done(((f32[16,4,12,128]{3,1,2,0:T(4,128)}), f32[16,4,12,128]{3,1,2,0:T(4,128)S(1)}, u32[]{:S(2)}, u32[]{:S(2)}) %all-to-all-start) | async-done | bytes 393248 | tf_op jit(solution)/shard_map/all_to_all | solution.py:140
  57.8 1.9 %collective-permute-start.7 = (f32[4,12,128]{2,0,1:T(4,128)S(1)}, f32[4,12,128]{2,0,1:T(4,128)S(1)}, u32[]{:S(2)}, u32[]{:S(2)}) collective-permute-start(f32[4,12,128]{2,0,1:T(4,128)S(1)} %reduce_sum.9), channel_id=1, source_target_pairs={{0,32},{16,48},{32,0},{48,16},{64,96},{80,112},{96,64},{112,80},{1... | collective-permute-start | bytes 73736 | tf_op jit(solution)/shard_map/ppermute | solution.py:77
  60.0 2.3 %collective-permute-done.7 = f32[4,12,128]{2,0,1:T(4,128)S(1)} collective-permute-done((f32[4,12,128]{2,0,1:T(4,128)S(1)}, f32[4,12,128]{2,0,1:T(4,128)S(1)}, u32[]{:S(2)}, u32[]{:S(2)}) %collective-permute-start.7) | collective-permute-done | bytes 24608 | tf_op jit(solution)/shard_map/ppermute | solution.py:77
  62.3 2.1 %collective-permute-start.8 = (f32[4,12,128]{2,0,1:T(4,128)S(1)}, f32[4,12,128]{2,0,1:T(4,128)S(1)}, u32[]{:S(2)}, u32[]{:S(2)}) collective-permute-start(f32[4,12,128]{2,0,1:T(4,128)S(1)} %add.135), channel_id=1, source_target_pairs={{0,64},{16,80},{32,96},{48,112},{64,0},{80,16},{96,32},{112,48},{1... | collective-permute-start | bytes 73736 | tf_op jit(solution)/shard_map/ppermute | solution.py:77
  64.4 0.3 fusion.11
  64.8 3.2 %collective-permute-done.8 = f32[4,12,128]{2,0,1:T(4,128)S(1)} collective-permute-done((f32[4,12,128]{2,0,1:T(4,128)S(1)}, f32[4,12,128]{2,0,1:T(4,128)S(1)}, u32[]{:S(2)}, u32[]{:S(2)}) %collective-permute-start.8) | collective-permute-done | bytes 24608 | tf_op jit(solution)/shard_map/ppermute | solution.py:77
  68.0 2.1 %collective-permute-start.9 = (f32[4,12,128]{2,0,1:T(4,128)S(1)}, f32[4,12,128]{2,0,1:T(4,128)S(1)}, u32[]{:S(2)}, u32[]{:S(2)}) collective-permute-start(f32[4,12,128]{2,0,1:T(4,128)S(1)} %add.136), channel_id=1, source_target_pairs={{0,128},{16,144},{32,160},{48,176},{64,192},{80,208},{96,224},{112... | collective-permute-start | bytes 73736 | tf_op jit(solution)/shard_map/ppermute | solution.py:77
  70.3 6.5 %collective-permute-done.9 = f32[4,12,128]{2,0,1:T(4,128)S(1)} collective-permute-done((f32[4,12,128]{2,0,1:T(4,128)S(1)}, f32[4,12,128]{2,0,1:T(4,128)S(1)}, u32[]{:S(2)}, u32[]{:S(2)}) %collective-permute-start.9) | collective-permute-done | bytes 24608 | tf_op jit(solution)/shard_map/ppermute | solution.py:77
  76.8 15.5 %collective-permute-start.10 = (f32[4,12,128]{2,0,1:T(4,128)S(1)}, f32[4,12,128]{2,0,1:T(4,128)S(1)}, u32[]{:S(2)}, u32[]{:S(2)}) collective-permute-start(f32[4,12,128]{2,0,1:T(4,128)S(1)} %add.137), channel_id=1, source_target_pairs={{0,256},{16,272},{32,288},{48,304},{64,320},{80,336},{96,352},{112... | collective-permute-start | bytes 73736 | tf_op jit(solution)/shard_map/ppermute | solution.py:77
  92.3 1.0 fusion.8
  93.3 0.6 collective-permute-done.10
  93.9 12.2 %collective-permute-start.11 = (f32[4,12,128]{2,0,1:T(4,128)S(1)}, f32[4,12,128]{2,0,1:T(4,128)S(1)}, u32[]{:S(2)}, u32[]{:S(2)}) collective-permute-start(f32[4,12,128]{2,0,1:T(4,128)S(1)} %add.138), channel_id=1, source_target_pairs={{0,992},{16,1008},{32,960},{48,976},{64,928},{80,944},{96,896},{11... | collective-permute-start | bytes 73736 | tf_op jit(solution)/shard_map/ppermute | solution.py:80
  106.4 8.3 %collective-permute-done.11 = f32[4,12,128]{2,0,1:T(4,128)S(1)} collective-permute-done((f32[4,12,128]{2,0,1:T(4,128)S(1)}, f32[4,12,128]{2,0,1:T(4,128)S(1)}, u32[]{:S(2)}, u32[]{:S(2)}) %collective-permute-start.11) | collective-permute-done | bytes 24608 | tf_op jit(solution)/shard_map/ppermute | solution.py:80
  114.8 7.2 %collective-permute-start.12 = (f32[4,12,128]{2,0,1:T(4,128)S(1)}, f32[4,12,128]{2,0,1:T(4,128)S(1)}, u32[]{:S(2)}, u32[]{:S(2)}) collective-permute-start(f32[4,12,128]{2,0,1:T(4,128)S(1)} %add.139), channel_id=1, source_target_pairs={{0,16},{16,0},{32,48},{48,32},{64,80},{80,64},{96,112},{112,96},{1... | collective-permute-start | bytes 73736 | tf_op jit(solution)/shard_map/ppermute | solution.py:86
  122.0 1.0 fusion
  123.1 0.6 slice.194
  123.7 0.6 slice.195
  (64 shorter events, 5.9 us)
Async XLA Ops:
  0.6 5.5 %copy-start.1 = (f32[2,2,96,128]{3,2,1,0:T(8,128)S(1)}, f32[2,2,96,128]{3,2,1,0:T(8,128)}, u32[]{:S(2)}) copy-start(f32[2,2,96,128]{3,2,1,0:T(8,128)} %param.7) | copy-start | bytes 589828
  0.6 8.3 %copy-start.5 = (f32[3,128,128]{2,1,0:T(8,128)S(1)}, f32[3,128,128]{2,1,0:T(8,128)}, u32[]{:S(2)}) copy-start(f32[3,128,128]{2,1,0:T(8,128)} %param.6) | copy-start | bytes 589828
  1.7 7.7 %collective-permute-start = (f32[2,1,96,128]{3,2,1,0:T(8,128)S(1)}, f32[2,1,96,128]{3,2,1,0:T(8,128)S(1)}, u32[]{:S(2)}, u32[]{:S(2)}) collective-permute-start(f32[2,1,96,128]{3,2,1,0:T(8,128)S(1)} %get-tuple-element.10), channel_id=1, source_target_pairs={{0,1},{1,2},{2,3},{3,4},{4,5},{5,6},{6,7},{7,8},{8,9},{9,10},{10,1... | collective-permute-start | bytes 294920 | tf_op jit(solution)/shard_map/ppermute | solution.py:18
  4.8 6.0 %collective-permute-start.1 = (f32[2,1,96,128]{3,2,1,0:T(8,128)S(1)}, f32[2,1,96,128]{3,2,1,0:T(8,128)S(1)}, u32[]{:S(2)}, u32[]{:S(2)}) collective-permute-start(f32[2,1,96,128]{3,2,1,0:T(8,128)S(1)} %get-tuple-element.11), channel_id=1, source_target_pairs={{1,0},{2,1},{3,2},{4,3},{5,4},{6,5},{7,6},{8,7},{9,8},{10,9},{11,1... | collective-permute-start | bytes 294920 | tf_op jit(solution)/shard_map/ppermute | solution.py:19
  6.1 15.0 %collective-permute-start.3 = (f32[2,2,96,128]{3,2,1,0:T(8,128)S(1)}, f32[2,2,96,128]{3,2,1,0:T(8,128)S(1)}, u32[]{:S(2)}, u32[]{:S(2)}) collective-permute-start(f32[2,2,96,128]{3,2,1,0:T(8,128)S(1)} %copy-done.1), channel_id=1, source_target_pairs={{16,0},{32,16},{48,32},{64,48},{80,64},{96,80},{112,96},{128,112},... | collective-permute-start | bytes 589832 | tf_op jit(solution)/shard_map/ppermute | solution.py:27
  9.3 0.9 copy-start
  9.3 1.2 copy-start.2
  14.0 17.2 %collective-permute-start.2 = (f32[2,2,96,128]{3,2,1,0:T(8,128)S(1)}, f32[2,2,96,128]{3,2,1,0:T(8,128)S(1)}, u32[]{:S(2)}, u32[]{:S(2)}) collective-permute-start(f32[2,2,96,128]{3,2,1,0:T(8,128)S(1)} %get-tuple-element.12), channel_id=1, source_target_pairs={{0,16},{16,32},{32,48},{48,64},{64,80},{80,96},{96,112},{112,128},... | collective-permute-start | bytes 589832 | tf_op jit(solution)/shard_map/ppermute | solution.py:27
  26.3 8.4 %collective-permute-start.4 = (f32[2,1,96,128]{3,2,1,0:T(8,128)S(1)}, f32[2,1,96,128]{3,2,1,0:T(8,128)S(1)}, u32[]{:S(2)}, u32[]{:S(2)}) collective-permute-start(f32[2,1,96,128]{3,2,1,0:T(8,128)S(1)} %get-tuple-element.6), channel_id=1, source_target_pairs={{0,1},{1,2},{2,3},{3,4},{4,5},{5,6},{6,7},{7,8},{8,9},{9,10},{10,1... | collective-permute-start | bytes 294920 | tf_op jit(solution)/shard_map/ppermute | solution.py:18
  29.4 5.4 %collective-permute-start.5 = (f32[2,1,96,128]{3,2,1,0:T(8,128)S(1)}, f32[2,1,96,128]{3,2,1,0:T(8,128)S(1)}, u32[]{:S(2)}, u32[]{:S(2)}) collective-permute-start(f32[2,1,96,128]{3,2,1,0:T(8,128)S(1)} %get-tuple-element.7), channel_id=1, source_target_pairs={{1,0},{2,1},{3,2},{4,3},{5,4},{6,5},{7,6},{8,7},{9,8},{10,9},{11,1... | collective-permute-start | bytes 294920 | tf_op jit(solution)/shard_map/ppermute | solution.py:19
  32.7 3.6 %collective-permute-start.6 = (f32[16,4,12,128]{3,1,2,0:T(4,128)S(1)}, f32[16,4,12,128]{3,1,2,0:T(4,128)S(1)}, u32[]{:S(2)}, u32[]{:S(2)}) collective-permute-start(f32[16,4,12,128]{3,1,2,0:T(4,128)S(1)} %bitcast.205), channel_id=1, source_target_pairs={{0,16},{16,0},{32,48},{48,32},{64,80},{80,64},{96,112},{112,96},{1... | collective-permute-start | bytes 1179656 | tf_op jit(solution)/shard_map/ppermute | solution.py:139
  34.8 0.6 copy-start.3
  37.2 20.5 %all-to-all-start = ((f32[16,4,12,128]{3,1,2,0:T(4,128)}), f32[16,4,12,128]{3,1,2,0:T(4,128)S(1)}, u32[]{:S(2)}, u32[]{:S(2)}) async-start(f32[16,4,12,128]{3,1,2,0:T(4,128)} %bitcast_add_fusion), calls=%async_computation | async-start | bytes 786432 | tf_op jit(solution)/shard_map/all_to_all | solution.py:140
  57.8 4.6 %collective-permute-start.7 = (f32[4,12,128]{2,0,1:T(4,128)S(1)}, f32[4,12,128]{2,0,1:T(4,128)S(1)}, u32[]{:S(2)}, u32[]{:S(2)}) collective-permute-start(f32[4,12,128]{2,0,1:T(4,128)S(1)} %reduce_sum.9), channel_id=1, source_target_pairs={{0,32},{16,48},{32,0},{48,16},{64,96},{80,112},{96,64},{112,80},{1... | collective-permute-start | bytes 73736 | tf_op jit(solution)/shard_map/ppermute | solution.py:77
  59.7 4.7 %copy-start.4 = (f32[2,1,96,128]{3,2,1,0:T(8,128)S(1)}, f32[2,1,96,128]{3,2,1,0:T(8,128)}, u32[]{:S(2)}) copy-start(f32[2,1,96,128]{3,2,1,0:T(8,128)} %copy-done.3) | copy-start | bytes 294916
  62.3 7.7 %copy-start.6 = (f32[3,128,128]{2,1,0:T(8,128)S(1)}, f32[3,128,128]{2,1,0:T(8,128)}, u32[]{:S(2)}) copy-start(f32[3,128,128]{2,1,0:T(8,128)} %param.6) | copy-start | bytes 589828
  62.3 5.6 %collective-permute-start.8 = (f32[4,12,128]{2,0,1:T(4,128)S(1)}, f32[4,12,128]{2,0,1:T(4,128)S(1)}, u32[]{:S(2)}, u32[]{:S(2)}) collective-permute-start(f32[4,12,128]{2,0,1:T(4,128)S(1)} %add.135), channel_id=1, source_target_pairs={{0,64},{16,80},{32,96},{48,112},{64,0},{80,16},{96,32},{112,48},{1... | collective-permute-start | bytes 73736 | tf_op jit(solution)/shard_map/ppermute | solution.py:77
  68.0 24.4 %copy-start.7 = (f32[2,2,96,128]{3,2,1,0:T(8,128)S(1)}, f32[2,2,96,128]{3,2,1,0:T(8,128)}, u32[]{:S(2)}) copy-start(f32[2,2,96,128]{3,2,1,0:T(8,128)} %fusion.86) | copy-start | bytes 589828
  68.0 8.9 %collective-permute-start.9 = (f32[4,12,128]{2,0,1:T(4,128)S(1)}, f32[4,12,128]{2,0,1:T(4,128)S(1)}, u32[]{:S(2)}, u32[]{:S(2)}) collective-permute-start(f32[4,12,128]{2,0,1:T(4,128)S(1)} %add.136), channel_id=1, source_target_pairs={{0,128},{16,144},{32,160},{48,176},{64,192},{80,208},{96,224},{112... | collective-permute-start | bytes 73736 | tf_op jit(solution)/shard_map/ppermute | solution.py:77
  76.8 17.0 %collective-permute-start.10 = (f32[4,12,128]{2,0,1:T(4,128)S(1)}, f32[4,12,128]{2,0,1:T(4,128)S(1)}, u32[]{:S(2)}, u32[]{:S(2)}) collective-permute-start(f32[4,12,128]{2,0,1:T(4,128)S(1)} %add.137), channel_id=1, source_target_pairs={{0,256},{16,272},{32,288},{48,304},{64,320},{80,336},{96,352},{112... | collective-permute-start | bytes 73736 | tf_op jit(solution)/shard_map/ppermute | solution.py:77
  93.9 20.9 %collective-permute-start.11 = (f32[4,12,128]{2,0,1:T(4,128)S(1)}, f32[4,12,128]{2,0,1:T(4,128)S(1)}, u32[]{:S(2)}, u32[]{:S(2)}) collective-permute-start(f32[4,12,128]{2,0,1:T(4,128)S(1)} %add.138), channel_id=1, source_target_pairs={{0,992},{16,1008},{32,960},{48,976},{64,928},{80,944},{96,896},{11... | collective-permute-start | bytes 73736 | tf_op jit(solution)/shard_map/ppermute | solution.py:80
  114.8 8.3 %collective-permute-start.12 = (f32[4,12,128]{2,0,1:T(4,128)S(1)}, f32[4,12,128]{2,0,1:T(4,128)S(1)}, u32[]{:S(2)}, u32[]{:S(2)}) collective-permute-start(f32[4,12,128]{2,0,1:T(4,128)S(1)} %add.139), channel_id=1, source_target_pairs={{0,16},{16,0},{32,48},{48,32},{64,80},{80,64},{96,112},{112,96},{1... | collective-permute-start | bytes 73736 | tf_op jit(solution)/shard_map/ppermute | solution.py:86

commit v4 on v3

--- a/solution.py
+++ b/solution.py
@@ -76,8 +76,17 @@
         pairs = [(i, i ^ mask) for i in range(count)]
         value = value + lax.ppermute(value, axis, pairs)
         mask *= 2
-    pairs = [(i, count - first * (i // first + 1) + i % first) for i in range(count)]
+    ring = count // first
+    pairs = [(i, first * ring_partner(i // first, ring) + i % first) for i in range(count)]
     return value + lax.ppermute(value, axis, pairs)
+
+
+def ring_partner(z, ring):
+    if ring % 4:
+        return ring - 1 - z
+    quarter = ring // 4
+    shift = (3 * quarter, quarter, -quarter, -3 * quarter)
+    return z + shift[z // quarter]
 
 
 def pair_gather(value, axis):

time: 125 us -> 124 us (level)
  the two profiles are of different devices: /device:TPU:225 before, /device:TPU:1 now
where the time goes in v4:
time: 124 us; the launch traced here: 123 us
  starting transfers between devices  87 us (70%)
  matrix products  15.7 us (13%)
  waiting for transfers between devices  13.7 us (11%)
  local copies, waits for them, and re-layouts  4.42 us (4%)
  between operations  1.32 us (1%)
  other arithmetic  1.27 us (1%)
    ppermute x4, starting transfers between devices, doubling_sum(): value = value + lax.ppermute(value, axis, pairs)  31.1 us
    ppermute x2, starting transfers between devices, passed_along(): return lax.ppermute(value, axis, pairs)  15.3 us
    ppermute x1, starting transfers between devices, doubling_sum(): return value + lax.ppermute(value, axis, pairs)  13.7 us
    ppermute x1, starting transfers between devices, pair_gather(): other = lax.ppermute(value, axis, [(i, i ^ 1) for i in range(count)])  9.67 us
    all_to_all x1, waiting for transfers between devices, per_device(): terms = lax.all_to_all(terms, 'rows', 0, 0, tiled=True).sum(axis=0)  8.46 us
    ppermute x2, starting transfers between devices, padded_2(): before = lax.ppermute(last, axis, up)  8.22 us
    dot_general x9, matrix products, per_device(): jnp.einsum('frwc,frwd->dc', padded[:, i:i + strip, j:j + width], dpre, pr...  4.42 us
    ppermute x4, waiting for transfers between devices, doubling_sum(): value = value + lax.ppermute(value, axis, pairs)  4.2 us
  transfers between devices with their start and end apart: 14, of which 6 were waited for; matrix products, arithmetic and copies ran while one was open for 13% of the time, Pallas kernels for 0%

profile of v4, /device:TPU:1, one launch (start us, length us, event | category | flops | bytes accessed | tf_op | source)
XLA Modules:
  0.0 123.4 jit_solution(16577397733856200052)
XLA Ops:
  0.7 1.0 fusion.122
  1.7 4.0 %collective-permute-start = (f32[2,1,96,128]{3,2,1,0:T(8,128)S(1)}, f32[2,1,96,128]{3,2,1,0:T(8,128)S(1)}, u32[]{:S(2)}, u32[]{:S(2)}) collective-permute-start(f32[2,1,96,128]{3,2,1,0:T(8,128)S(1)} %get-tuple-element.10), channel_id=1, source_target_pairs={{0,1},{1,2},{2,3},{3,4},{4,5},{5,6},{6,7},{7,8},{8,9},{9,10},{10,1... | collective-permute-start | bytes 294920 | tf_op jit(solution)/shard_map/ppermute | solution.py:18
  5.6 1.3 %collective-permute-start.1 = (f32[2,1,96,128]{3,2,1,0:T(8,128)S(1)}, f32[2,1,96,128]{3,2,1,0:T(8,128)S(1)}, u32[]{:S(2)}, u32[]{:S(2)}) collective-permute-start(f32[2,1,96,128]{3,2,1,0:T(8,128)S(1)} %get-tuple-element.11), channel_id=1, source_target_pairs={{1,0},{2,1},{3,2},{4,3},{5,4},{6,5},{7,6},{8,7},{9,8},{10,9},{11,1... | collective-permute-start | bytes 294920 | tf_op jit(solution)/shard_map/ppermute | solution.py:19
  6.9 13.4 %collective-permute-start.3 = (f32[2,2,96,128]{3,2,1,0:T(8,128)S(1)}, f32[2,2,96,128]{3,2,1,0:T(8,128)S(1)}, u32[]{:S(2)}, u32[]{:S(2)}) collective-permute-start(f32[2,2,96,128]{3,2,1,0:T(8,128)S(1)} %copy-done.1), channel_id=1, source_target_pairs={{16,0},{32,16},{48,32},{64,48},{80,64},{96,80},{112,96},{128,112},... | collective-permute-start | bytes 589832 | tf_op jit(solution)/shard_map/ppermute | solution.py:27
  20.8 0.9 copy-done
  24.5 0.3 fusion.38
  24.9 0.5 fusion.118
  25.4 1.9 %collective-permute-start.2 = (f32[2,2,96,128]{3,2,1,0:T(8,128)S(1)}, f32[2,2,96,128]{3,2,1,0:T(8,128)S(1)}, u32[]{:S(2)}, u32[]{:S(2)}) collective-permute-start(f32[2,2,96,128]{3,2,1,0:T(8,128)S(1)} %get-tuple-element.12), channel_id=1, source_target_pairs={{0,16},{16,32},{32,48},{48,64},{64,80},{80,96},{96,112},{112,128},... | collective-permute-start | bytes 589832 | tf_op jit(solution)/shard_map/ppermute | solution.py:27
  27.3 1.0 fusion.86
  28.3 0.3 fusion.78
  28.6 0.3 fusion.6
  29.0 0.5 fusion.55
  29.5 0.5 fusion.25
  30.0 0.5 fusion.52
  30.5 0.5 fusion.49
  31.0 0.5 fusion.123
  31.5 0.5 fusion.46
  32.0 0.5 fusion.43
  32.5 0.5 fusion.23
  33.0 0.5 fusion.39
  33.5 4.3 %collective-permute-start.4 = (f32[2,1,96,128]{3,2,1,0:T(8,128)S(1)}, f32[2,1,96,128]{3,2,1,0:T(8,128)S(1)}, u32[]{:S(2)}, u32[]{:S(2)}) collective-permute-start(f32[2,1,96,128]{3,2,1,0:T(8,128)S(1)} %get-tuple-element.6), channel_id=1, source_target_pairs={{0,1},{1,2},{2,3},{3,4},{4,5},{5,6},{6,7},{7,8},{8,9},{9,10},{10,1... | collective-permute-start | bytes 294920 | tf_op jit(solution)/shard_map/ppermute | solution.py:18
  37.8 1.3 %collective-permute-start.5 = (f32[2,1,96,128]{3,2,1,0:T(8,128)S(1)}, f32[2,1,96,128]{3,2,1,0:T(8,128)S(1)}, u32[]{:S(2)}, u32[]{:S(2)}) collective-permute-start(f32[2,1,96,128]{3,2,1,0:T(8,128)S(1)} %get-tuple-element.7), channel_id=1, source_target_pairs={{1,0},{2,1},{3,2},{4,3},{5,4},{6,5},{7,6},{8,7},{9,8},{10,9},{11,1... | collective-permute-start | bytes 294920 | tf_op jit(solution)/shard_map/ppermute | solution.py:19
  39.3 0.3 fusion.66
  39.6 0.5 fusion.16
  40.1 0.5 fusion.124
  41.1 2.7 %collective-permute-start.6 = (f32[16,4,12,128]{3,1,2,0:T(4,128)S(1)}, f32[16,4,12,128]{3,1,2,0:T(4,128)S(1)}, u32[]{:S(2)}, u32[]{:S(2)}) collective-permute-start(f32[16,4,12,128]{3,1,2,0:T(4,128)S(1)} %bitcast.205), channel_id=1, source_target_pairs={{0,16},{16,0},{32,48},{48,32},{64,80},{80,64},{96,112},{112,96},{1... | collective-permute-start | bytes 1179656 | tf_op jit(solution)/shard_map/ppermute | solution.py:148
  43.8 0.6 copy-done.3
  44.8 0.3 fusion.31
  45.2 0.8 bitcast_add_fusion
  46.0 3.8 %all-to-all-start = ((f32[16,4,12,128]{3,1,2,0:T(4,128)}), f32[16,4,12,128]{3,1,2,0:T(4,128)S(1)}, u32[]{:S(2)}, u32[]{:S(2)}) async-start(f32[16,4,12,128]{3,1,2,0:T(4,128)} %bitcast_add_fusion), calls=%async_computation | async-start | bytes 786432 | tf_op jit(solution)/shard_map/all_to_all | solution.py:149
  50.2 0.3 convolution_add_fusion.5
  50.5 8.5 %all-to-all-done = f32[16,4,12,128]{3,1,2,0:T(4,128)S(1)} async-done(((f32[16,4,12,128]{3,1,2,0:T(4,128)}), f32[16,4,12,128]{3,1,2,0:T(4,128)S(1)}, u32[]{:S(2)}, u32[]{:S(2)}) %all-to-all-start) | async-done | bytes 393248 | tf_op jit(solution)/shard_map/all_to_all | solution.py:149
  59.0 1.9 %collective-permute-start.7 = (f32[4,12,128]{2,0,1:T(4,128)S(1)}, f32[4,12,128]{2,0,1:T(4,128)S(1)}, u32[]{:S(2)}, u32[]{:S(2)}) collective-permute-start(f32[4,12,128]{2,0,1:T(4,128)S(1)} %reduce_sum.9), channel_id=1, source_target_pairs={{0,32},{16,48},{32,0},{48,16},{64,96},{80,112},{96,64},{112,80},{1... | collective-permute-start | bytes 73736 | tf_op jit(solution)/shard_map/ppermute | solution.py:77
  61.0 0.3 fusion.35
  61.3 2.3 %collective-permute-done.7 = f32[4,12,128]{2,0,1:T(4,128)S(1)} collective-permute-done((f32[4,12,128]{2,0,1:T(4,128)S(1)}, f32[4,12,128]{2,0,1:T(4,128)S(1)}, u32[]{:S(2)}, u32[]{:S(2)}) %collective-permute-start.7) | collective-permute-done | bytes 24608 | tf_op jit(solution)/shard_map/ppermute | solution.py:77
  63.6 4.8 %collective-permute-start.8 = (f32[4,12,128]{2,0,1:T(4,128)S(1)}, f32[4,12,128]{2,0,1:T(4,128)S(1)}, u32[]{:S(2)}, u32[]{:S(2)}) collective-permute-start(f32[4,12,128]{2,0,1:T(4,128)S(1)} %add.135), channel_id=1, source_target_pairs={{0,64},{16,80},{32,96},{48,112},{64,0},{80,16},{96,32},{112,48},{1... | collective-permute-start | bytes 73736 | tf_op jit(solution)/shard_map/ppermute | solution.py:77
  68.4 0.3 fusion.11
  68.8 0.8 collective-permute-done.8
  69.6 8.9 %collective-permute-start.9 = (f32[4,12,128]{2,0,1:T(4,128)S(1)}, f32[4,12,128]{2,0,1:T(4,128)S(1)}, u32[]{:S(2)}, u32[]{:S(2)}) collective-permute-start(f32[4,12,128]{2,0,1:T(4,128)S(1)} %add.136), channel_id=1, source_target_pairs={{0,128},{16,144},{32,160},{48,176},{64,192},{80,208},{96,224},{112... | collective-permute-start | bytes 73736 | tf_op jit(solution)/shard_map/ppermute | solution.py:77
  78.9 0.9 collective-permute-done.9
  79.8 15.5 %collective-permute-start.10 = (f32[4,12,128]{2,0,1:T(4,128)S(1)}, f32[4,12,128]{2,0,1:T(4,128)S(1)}, u32[]{:S(2)}, u32[]{:S(2)}) collective-permute-start(f32[4,12,128]{2,0,1:T(4,128)S(1)} %add.137), channel_id=1, source_target_pairs={{0,256},{16,272},{32,288},{48,304},{64,320},{80,336},{96,352},{112... | collective-permute-start | bytes 73736 | tf_op jit(solution)/shard_map/ppermute | solution.py:77
  95.3 1.0 fusion.8
  96.5 13.7 %collective-permute-start.11 = (f32[4,12,128]{2,0,1:T(4,128)S(1)}, f32[4,12,128]{2,0,1:T(4,128)S(1)}, u32[]{:S(2)}, u32[]{:S(2)}) collective-permute-start(f32[4,12,128]{2,0,1:T(4,128)S(1)} %add.138), channel_id=1, source_target_pairs={{0,768},{16,784},{32,800},{48,816},{64,832},{80,848},{96,864},{112... | collective-permute-start | bytes 73736 | tf_op jit(solution)/shard_map/ppermute | solution.py:81
  110.5 1.0 collective-permute-done.11
  111.5 9.7 %collective-permute-start.12 = (f32[4,12,128]{2,0,1:T(4,128)S(1)}, f32[4,12,128]{2,0,1:T(4,128)S(1)}, u32[]{:S(2)}, u32[]{:S(2)}) collective-permute-start(f32[4,12,128]{2,0,1:T(4,128)S(1)} %add.139), channel_id=1, source_target_pairs={{0,16},{16,0},{32,48},{48,32},{64,80},{80,64},{96,112},{112,96},{1... | collective-permute-start | bytes 73736 | tf_op jit(solution)/shard_map/ppermute | solution.py:95
  121.1 1.0 fusion
  122.2 0.6 slice.194
  122.8 0.6 slice.195
  (64 shorter events, 5.4 us)
Async XLA Ops:
  0.6 6.3 %copy-start.1 = (f32[2,2,96,128]{3,2,1,0:T(8,128)S(1)}, f32[2,2,96,128]{3,2,1,0:T(8,128)}, u32[]{:S(2)}) copy-start(f32[2,2,96,128]{3,2,1,0:T(8,128)} %param.7) | copy-start | bytes 589828
  0.6 19.7 %copy-start.5 = (f32[3,128,128]{2,1,0:T(8,128)S(1)}, f32[3,128,128]{2,1,0:T(8,128)}, u32[]{:S(2)}) copy-start(f32[3,128,128]{2,1,0:T(8,128)} %param.6) | copy-start | bytes 589828
  1.7 19.1 %collective-permute-start = (f32[2,1,96,128]{3,2,1,0:T(8,128)S(1)}, f32[2,1,96,128]{3,2,1,0:T(8,128)S(1)}, u32[]{:S(2)}, u32[]{:S(2)}) collective-permute-start(f32[2,1,96,128]{3,2,1,0:T(8,128)S(1)} %get-tuple-element.10), channel_id=1, source_target_pairs={{0,1},{1,2},{2,3},{3,4},{4,5},{5,6},{6,7},{7,8},{8,9},{9,10},{10,1... | collective-permute-start | bytes 294920 | tf_op jit(solution)/shard_map/ppermute | solution.py:18
  5.6 16.6 %collective-permute-start.1 = (f32[2,1,96,128]{3,2,1,0:T(8,128)S(1)}, f32[2,1,96,128]{3,2,1,0:T(8,128)S(1)}, u32[]{:S(2)}, u32[]{:S(2)}) collective-permute-start(f32[2,1,96,128]{3,2,1,0:T(8,128)S(1)} %get-tuple-element.11), channel_id=1, source_target_pairs={{1,0},{2,1},{3,2},{4,3},{5,4},{6,5},{7,6},{8,7},{9,8},{10,9},{11,1... | collective-permute-start | bytes 294920 | tf_op jit(solution)/shard_map/ppermute | solution.py:19
  6.9 21.4 %collective-permute-start.3 = (f32[2,2,96,128]{3,2,1,0:T(8,128)S(1)}, f32[2,2,96,128]{3,2,1,0:T(8,128)S(1)}, u32[]{:S(2)}, u32[]{:S(2)}) collective-permute-start(f32[2,2,96,128]{3,2,1,0:T(8,128)S(1)} %copy-done.1), channel_id=1, source_target_pairs={{16,0},{32,16},{48,32},{64,48},{80,64},{96,80},{112,96},{128,112},... | collective-permute-start | bytes 589832 | tf_op jit(solution)/shard_map/ppermute | solution.py:27
  20.7 0.9 copy-start
  20.7 1.2 copy-start.2
  25.4 14.2 %collective-permute-start.2 = (f32[2,2,96,128]{3,2,1,0:T(8,128)S(1)}, f32[2,2,96,128]{3,2,1,0:T(8,128)S(1)}, u32[]{:S(2)}, u32[]{:S(2)}) collective-permute-start(f32[2,2,96,128]{3,2,1,0:T(8,128)S(1)} %get-tuple-element.12), channel_id=1, source_target_pairs={{0,16},{16,32},{32,48},{48,64},{64,80},{80,96},{96,112},{112,128},... | collective-permute-start | bytes 589832 | tf_op jit(solution)/shard_map/ppermute | solution.py:27
  33.5 10.3 %collective-permute-start.4 = (f32[2,1,96,128]{3,2,1,0:T(8,128)S(1)}, f32[2,1,96,128]{3,2,1,0:T(8,128)S(1)}, u32[]{:S(2)}, u32[]{:S(2)}) collective-permute-start(f32[2,1,96,128]{3,2,1,0:T(8,128)S(1)} %get-tuple-element.6), channel_id=1, source_target_pairs={{0,1},{1,2},{2,3},{3,4},{4,5},{5,6},{6,7},{7,8},{8,9},{9,10},{10,1... | collective-permute-start | bytes 294920 | tf_op jit(solution)/shard_map/ppermute | solution.py:18
  37.8 6.0 %collective-permute-start.5 = (f32[2,1,96,128]{3,2,1,0:T(8,128)S(1)}, f32[2,1,96,128]{3,2,1,0:T(8,128)S(1)}, u32[]{:S(2)}, u32[]{:S(2)}) collective-permute-start(f32[2,1,96,128]{3,2,1,0:T(8,128)S(1)} %get-tuple-element.7), channel_id=1, source_target_pairs={{1,0},{2,1},{3,2},{4,3},{5,4},{6,5},{7,6},{8,7},{9,8},{10,9},{11,1... | collective-permute-start | bytes 294920 | tf_op jit(solution)/shard_map/ppermute | solution.py:19
  41.1 4.1 %collective-permute-start.6 = (f32[16,4,12,128]{3,1,2,0:T(4,128)S(1)}, f32[16,4,12,128]{3,1,2,0:T(4,128)S(1)}, u32[]{:S(2)}, u32[]{:S(2)}) collective-permute-start(f32[16,4,12,128]{3,1,2,0:T(4,128)S(1)} %bitcast.205), channel_id=1, source_target_pairs={{0,16},{16,0},{32,48},{48,32},{64,80},{80,64},{96,112},{112,96},{1... | collective-permute-start | bytes 1179656 | tf_op jit(solution)/shard_map/ppermute | solution.py:148
  43.8 0.6 copy-start.3
  46.0 12.9 %all-to-all-start = ((f32[16,4,12,128]{3,1,2,0:T(4,128)}), f32[16,4,12,128]{3,1,2,0:T(4,128)S(1)}, u32[]{:S(2)}, u32[]{:S(2)}) async-start(f32[16,4,12,128]{3,1,2,0:T(4,128)} %bitcast_add_fusion), calls=%async_computation | async-start | bytes 786432 | tf_op jit(solution)/shard_map/all_to_all | solution.py:149
  59.0 4.6 %collective-permute-start.7 = (f32[4,12,128]{2,0,1:T(4,128)S(1)}, f32[4,12,128]{2,0,1:T(4,128)S(1)}, u32[]{:S(2)}, u32[]{:S(2)}) collective-permute-start(f32[4,12,128]{2,0,1:T(4,128)S(1)} %reduce_sum.9), channel_id=1, source_target_pairs={{0,32},{16,48},{32,0},{48,16},{64,96},{80,112},{96,64},{112,80},{1... | collective-permute-start | bytes 73736 | tf_op jit(solution)/shard_map/ppermute | solution.py:77
  60.9 7.4 %copy-start.4 = (f32[2,1,96,128]{3,2,1,0:T(8,128)S(1)}, f32[2,1,96,128]{3,2,1,0:T(8,128)}, u32[]{:S(2)}) copy-start(f32[2,1,96,128]{3,2,1,0:T(8,128)} %copy-done.3) | copy-start | bytes 294916
  63.6 15.0 %copy-start.6 = (f32[3,128,128]{2,1,0:T(8,128)S(1)}, f32[3,128,128]{2,1,0:T(8,128)}, u32[]{:S(2)}) copy-start(f32[3,128,128]{2,1,0:T(8,128)} %param.6) | copy-start | bytes 589828
  63.6 6.0 %collective-permute-start.8 = (f32[4,12,128]{2,0,1:T(4,128)S(1)}, f32[4,12,128]{2,0,1:T(4,128)S(1)}, u32[]{:S(2)}, u32[]{:S(2)}) collective-permute-start(f32[4,12,128]{2,0,1:T(4,128)S(1)} %add.135), channel_id=1, source_target_pairs={{0,64},{16,80},{32,96},{48,112},{64,0},{80,16},{96,32},{112,48},{1... | collective-permute-start | bytes 73736 | tf_op jit(solution)/shard_map/ppermute | solution.py:77
  69.6 25.6 %copy-start.7 = (f32[2,2,96,128]{3,2,1,0:T(8,128)S(1)}, f32[2,2,96,128]{3,2,1,0:T(8,128)}, u32[]{:S(2)}) copy-start(f32[2,2,96,128]{3,2,1,0:T(8,128)} %fusion.86) | copy-start | bytes 589828
  69.6 10.2 %collective-permute-start.9 = (f32[4,12,128]{2,0,1:T(4,128)S(1)}, f32[4,12,128]{2,0,1:T(4,128)S(1)}, u32[]{:S(2)}, u32[]{:S(2)}) collective-permute-start(f32[4,12,128]{2,0,1:T(4,128)S(1)} %add.136), channel_id=1, source_target_pairs={{0,128},{16,144},{32,160},{48,176},{64,192},{80,208},{96,224},{112... | collective-permute-start | bytes 73736 | tf_op jit(solution)/shard_map/ppermute | solution.py:77
  79.8 16.7 %collective-permute-start.10 = (f32[4,12,128]{2,0,1:T(4,128)S(1)}, f32[4,12,128]{2,0,1:T(4,128)S(1)}, u32[]{:S(2)}, u32[]{:S(2)}) collective-permute-start(f32[4,12,128]{2,0,1:T(4,128)S(1)} %add.137), channel_id=1, source_target_pairs={{0,256},{16,272},{32,288},{48,304},{64,320},{80,336},{96,352},{112... | collective-permute-start | bytes 73736 | tf_op jit(solution)/shard_map/ppermute | solution.py:77
  96.5 15.0 %collective-permute-start.11 = (f32[4,12,128]{2,0,1:T(4,128)S(1)}, f32[4,12,128]{2,0,1:T(4,128)S(1)}, u32[]{:S(2)}, u32[]{:S(2)}) collective-permute-start(f32[4,12,128]{2,0,1:T(4,128)S(1)} %add.138), channel_id=1, source_target_pairs={{0,768},{16,784},{32,800},{48,816},{64,832},{80,848},{96,864},{112... | collective-permute-start | bytes 73736 | tf_op jit(solution)/shard_map/ppermute | solution.py:81
  111.5 10.7 %collective-permute-start.12 = (f32[4,12,128]{2,0,1:T(4,128)S(1)}, f32[4,12,128]{2,0,1:T(4,128)S(1)}, u32[]{:S(2)}, u32[]{:S(2)}) collective-permute-start(f32[4,12,128]{2,0,1:T(4,128)S(1)} %add.139), channel_id=1, source_target_pairs={{0,16},{16,0},{32,48},{48,32},{64,80},{80,64},{96,112},{112,96},{1... | collective-permute-start | bytes 73736 | tf_op jit(solution)/shard_map/ppermute | solution.py:95

commit v5 on v4

--- a/solution.py
+++ b/solution.py
@@ -105,25 +105,9 @@
     grad_long = jnp.concatenate([cotangent, later], axis=0)
     dact = temporal_back(grad_long, temporal_weight, nframes)
     dpre = dact * sig * (1.0 + pre * (1.0 - sig))
-    dpre_wide = widen(padded_2(dpre, (("rows", 1),), 1))
     act = pre * sig
     earlier = passed_along(act, "frames", 1)
     longer = jnp.concatenate([earlier, act], axis=0)
-    mixed = jnp.zeros(images.shape, jnp.float32)
-    for k in range(3):
-        mixed = mixed + jnp.einsum(
-            "frwc,cd->frwd", longer[2 - k : 2 - k + nframes], temporal_weight[k], precision=HIGH
-        )
-    block_out = images + mixed
-    grad_images = cotangent
-    for i in range(3):
-        for j in range(3):
-            grad_images = grad_images + jnp.einsum(
-                "frwd,cd->frwc",
-                dpre_wide[:, 2 - i : 2 - i + strip, 2 - j : 2 - j + width],
-                spatial_weight[i, j],
-                precision=HIGH,
-            )
     total_cells = nframes * lax.axis_size("frames") * strip * lax.axis_size("rows") * width
     factor = 1.0 / math.sqrt(total_cells)
     taps = []
@@ -140,6 +124,23 @@
         )
     nrows = lax.axis_size("rows")
     terms = jnp.stack(taps, axis=1) * factor
+    terms, dpre_late = lax.optimization_barrier((terms, dpre))
+    dpre_wide = widen(padded_2(dpre_late, (("rows", 1),), 1))
+    mixed = jnp.zeros(images.shape, jnp.float32)
+    for k in range(3):
+        mixed = mixed + jnp.einsum(
+            "frwc,cd->frwd", longer[2 - k : 2 - k + nframes], temporal_weight[k], precision=HIGH
+        )
+    block_out = images + mixed
+    grad_images = cotangent
+    for i in range(3):
+        for j in range(3):
+            grad_images = grad_images + jnp.einsum(
+                "frwd,cd->frwc",
+                dpre_wide[:, 2 - i : 2 - i + strip, 2 - j : 2 - j + width],
+                spatial_weight[i, j],
+                precision=HIGH,
+            )
     terms = terms.reshape(nrows, 2, chans // nrows // 2, len(taps), chans)
     parity = lax.axis_index("frames") % 2
     keep = lax.dynamic_index_in_dim(terms, parity, axis=1, keepdims=False)

time: 124 us -> 126 us (1.016)
  waiting for transfers between devices: 13.7 us -> 19 us
  starting transfers between devices: 87 us -> 85.1 us
    ppermute x4, starting transfers between devices: 31.1 us -> 26.6 us  [doubling_sum(): value = value + lax.ppermute(value, axis, pairs)]
    ppermute x1, starting transfers between devices: 13.7 us -> 16.8 us  [doubling_sum(): return value + lax.ppermute(value, axis, pairs)]
    ppermute x2, waiting for transfers between devices: 0.01 us -> 3.04 us  [padded_2(): after = lax.ppermute(leading, axis, down)]
    ppermute x4, waiting for transfers between devices: 4.2 us -> 6.95 us  [doubling_sum(): value = value + lax.ppermute(value, axis, pairs)]
  transfers between devices with their start and end apart: 14 -> 14, of which waited for: 6 -> 7; matrix products, arithmetic and copies ran while one was open for 13% -> 11% of each run, Pallas kernels for 0% -> 0%
where the time goes in v5:
time: 126 us; the launch traced here: 125 us
  starting transfers between devices  85.1 us (68%)
  waiting for transfers between devices  19 us (15%)
  matrix products  15 us (12%)
  local copies, waits for them, and re-layouts  3.6 us (3%)
    ppermute x4, starting transfers between devices, doubling_sum(): value = value + lax.ppermute(value, axis, pairs)  26.6 us
    ppermute x1, starting transfers between devices, doubling_sum(): return value + lax.ppermute(value, axis, pairs)  16.8 us
    ppermute x2, starting transfers between devices, passed_along(): return lax.ppermute(value, axis, pairs)  15.3 us
    ppermute x1, starting transfers between devices, pair_gather(): other = lax.ppermute(value, axis, [(i, i ^ 1) for i in range(count)])  9.45 us
    all_to_all x1, waiting for transfers between devices, per_device(): terms = lax.all_to_all(terms, 'rows', 0, 0, tiled=True).sum(axis=0)  8.11 us
    ppermute x2, starting transfers between devices, padded_2(): before = lax.ppermute(last, axis, up)  7.91 us
    ppermute x4, waiting for transfers between devices, doubling_sum(): value = value + lax.ppermute(value, axis, pairs)  6.95 us
    dot_general x9, matrix products, per_device(): jnp.einsum('frwc,frwd->dc', padded[:, i:i + strip, j:j + width], dpre, pr...  4.43 us
  transfers between devices with their start and end apart: 14, of which 7 were waited for; matrix products, arithmetic and copies ran while one was open for 11% of the time, Pallas kernels for 0%

profile of v5, /device:TPU:1, one launch (start us, length us, event | category | flops | bytes accessed | tf_op | source)
XLA Modules:
  0.0 125.0 jit_solution(13410943783332101736)
XLA Ops:
  0.7 1.0 fusion.124
  1.7 4.0 %collective-permute-start = (f32[2,1,96,128]{3,2,1,0:T(8,128)S(1)}, f32[2,1,96,128]{3,2,1,0:T(8,128)S(1)}, u32[]{:S(2)}, u32[]{:S(2)}) collective-permute-start(f32[2,1,96,128]{3,2,1,0:T(8,128)S(1)} %get-tuple-element.14), channel_id=1, source_target_pairs={{0,1},{1,2},{2,3},{3,4},{4,5},{5,6},{6,7},{7,8},{8,9},{9,10},{10,1... | collective-permute-start | bytes 294920 | tf_op jit(solution)/shard_map/ppermute | solution.py:18
  5.6 1.3 %collective-permute-start.1 = (f32[2,1,96,128]{3,2,1,0:T(8,128)S(1)}, f32[2,1,96,128]{3,2,1,0:T(8,128)S(1)}, u32[]{:S(2)}, u32[]{:S(2)}) collective-permute-start(f32[2,1,96,128]{3,2,1,0:T(8,128)S(1)} %get-tuple-element.15), channel_id=1, source_target_pairs={{1,0},{2,1},{3,2},{4,3},{5,4},{6,5},{7,6},{8,7},{9,8},{10,9},{11,1... | collective-permute-start | bytes 294920 | tf_op jit(solution)/shard_map/ppermute | solution.py:19
  6.9 13.4 %collective-permute-start.3 = (f32[2,2,96,128]{3,2,1,0:T(8,128)S(1)}, f32[2,2,96,128]{3,2,1,0:T(8,128)S(1)}, u32[]{:S(2)}, u32[]{:S(2)}) collective-permute-start(f32[2,2,96,128]{3,2,1,0:T(8,128)S(1)} %copy-done.1), channel_id=1, source_target_pairs={{16,0},{32,16},{48,32},{64,48},{80,64},{96,80},{112,96},{128,112},... | collective-permute-start | bytes 589832 | tf_op jit(solution)/shard_map/ppermute | solution.py:27
  20.8 0.9 copy-done
  24.5 0.3 fusion.47
  24.9 1.9 %collective-permute-start.2 = (f32[2,2,96,128]{3,2,1,0:T(8,128)S(1)}, f32[2,2,96,128]{3,2,1,0:T(8,128)S(1)}, u32[]{:S(2)}, u32[]{:S(2)}) collective-permute-start(f32[2,2,96,128]{3,2,1,0:T(8,128)S(1)} %get-tuple-element.16), channel_id=1, source_target_pairs={{0,16},{16,32},{32,48},{48,64},{64,80},{80,96},{96,112},{112,128},... | collective-permute-start | bytes 589832 | tf_op jit(solution)/shard_map/ppermute | solution.py:27
  26.8 0.3 fusion.89
  27.5 0.3 fusion.6
  27.8 0.5 fusion.23
  28.3 0.5 fusion.22
  28.8 0.5 fusion.21
  29.3 0.5 fusion.20
  29.8 0.5 fusion.19
  30.3 0.5 fusion.18
  30.8 0.5 fusion.17
  31.3 0.5 fusion.16
  31.8 0.5 fusion.15
  32.3 0.5 fusion.14
  32.8 0.5 fusion.12
  33.3 0.5 fusion.13
  34.1 2.7 %collective-permute-start.6 = (f32[16,4,12,128]{3,1,2,0:T(4,128)S(1)}, f32[16,4,12,128]{3,1,2,0:T(4,128)S(1)}, u32[]{:S(2)}, u32[]{:S(2)}) collective-permute-start(f32[16,4,12,128]{3,1,2,0:T(4,128)S(1)} %bitcast.237), channel_id=1, source_target_pairs={{0,16},{16,0},{32,48},{48,32},{64,80},{80,64},{96,112},{112,96},{1... | collective-permute-start | bytes 1179656 | tf_op jit(solution)/shard_map/ppermute | solution.py:149
  36.9 4.0 %collective-permute-start.4 = (f32[2,1,96,128]{3,2,1,0:T(8,128)S(1)}, f32[2,1,96,128]{3,2,1,0:T(8,128)S(1)}, u32[]{:S(2)}, u32[]{:S(2)}) collective-permute-start(f32[2,1,96,128]{3,2,1,0:T(8,128)S(1)} %get-tuple-element.10), channel_id=1, source_target_pairs={{0,1},{1,2},{2,3},{3,4},{4,5},{5,6},{6,7},{7,8},{8,9},{9,10},{10,1... | collective-permute-start | bytes 294920 | tf_op jit(solution)/shard_map/ppermute | solution.py:18
  40.8 1.3 %collective-permute-start.5 = (f32[2,1,96,128]{3,2,1,0:T(8,128)S(1)}, f32[2,1,96,128]{3,2,1,0:T(8,128)S(1)}, u32[]{:S(2)}, u32[]{:S(2)}) collective-permute-start(f32[2,1,96,128]{3,2,1,0:T(8,128)S(1)} %get-tuple-element.11), channel_id=1, source_target_pairs={{1,0},{2,1},{3,2},{4,3},{5,4},{6,5},{7,6},{8,7},{9,8},{10,9},{11,1... | collective-permute-start | bytes 294920 | tf_op jit(solution)/shard_map/ppermute | solution.py:19
  42.5 1.0 fusion.8
  43.5 0.3 fusion.69
  43.8 3.0 %collective-permute-done.5 = f32[2,1,96,128]{3,2,1,0:T(8,128)S(1)} collective-permute-done((f32[2,1,96,128]{3,2,1,0:T(8,128)S(1)}, f32[2,1,96,128]{3,2,1,0:T(8,128)S(1)}, u32[]{:S(2)}, u32[]{:S(2)}) %collective-permute-start.5) | collective-permute-done | bytes 98336 | tf_op jit(solution)/shard_map/ppermute | solution.py:19
  46.9 0.9 bitcast_add_fusion
  47.7 3.7 %all-to-all-start = ((f32[16,4,12,128]{3,1,2,0:T(4,128)}), f32[16,4,12,128]{3,1,2,0:T(4,128)S(1)}, u32[]{:S(2)}, u32[]{:S(2)}) async-start(f32[16,4,12,128]{3,1,2,0:T(4,128)} %bitcast_add_fusion), calls=%async_computation | async-start | bytes 786432 | tf_op jit(solution)/shard_map/all_to_all | solution.py:150
  51.5 0.3 fusion.36
  51.8 0.3 convolution_add_fusion.5
  52.2 8.1 %all-to-all-done = f32[16,4,12,128]{3,1,2,0:T(4,128)S(1)} async-done(((f32[16,4,12,128]{3,1,2,0:T(4,128)}), f32[16,4,12,128]{3,1,2,0:T(4,128)S(1)}, u32[]{:S(2)}, u32[]{:S(2)}) %all-to-all-start) | async-done | bytes 393248 | tf_op jit(solution)/shard_map/all_to_all | solution.py:150
  60.3 1.9 %collective-permute-start.7 = (f32[4,12,128]{2,0,1:T(4,128)S(1)}, f32[4,12,128]{2,0,1:T(4,128)S(1)}, u32[]{:S(2)}, u32[]{:S(2)}) collective-permute-start(f32[4,12,128]{2,0,1:T(4,128)S(1)} %reduce_sum.9), channel_id=1, source_target_pairs={{0,32},{16,48},{32,0},{48,16},{64,96},{80,112},{96,64},{112,80},{1... | collective-permute-start | bytes 73736 | tf_op jit(solution)/shard_map/ppermute | solution.py:77
  62.6 2.3 %collective-permute-done.7 = f32[4,12,128]{2,0,1:T(4,128)S(1)} collective-permute-done((f32[4,12,128]{2,0,1:T(4,128)S(1)}, f32[4,12,128]{2,0,1:T(4,128)S(1)}, u32[]{:S(2)}, u32[]{:S(2)}) %collective-permute-start.7) | collective-permute-done | bytes 24608 | tf_op jit(solution)/shard_map/ppermute | solution.py:77
  64.9 2.5 %collective-permute-start.8 = (f32[4,12,128]{2,0,1:T(4,128)S(1)}, f32[4,12,128]{2,0,1:T(4,128)S(1)}, u32[]{:S(2)}, u32[]{:S(2)}) collective-permute-start(f32[4,12,128]{2,0,1:T(4,128)S(1)} %add.135), channel_id=1, source_target_pairs={{0,64},{16,80},{32,96},{48,112},{64,0},{80,16},{96,32},{112,48},{1... | collective-permute-start | bytes 73736 | tf_op jit(solution)/shard_map/ppermute | solution.py:77
  67.7 2.7 %collective-permute-done.8 = f32[4,12,128]{2,0,1:T(4,128)S(1)} collective-permute-done((f32[4,12,128]{2,0,1:T(4,128)S(1)}, f32[4,12,128]{2,0,1:T(4,128)S(1)}, u32[]{:S(2)}, u32[]{:S(2)}) %collective-permute-start.8) | collective-permute-done | bytes 24608 | tf_op jit(solution)/shard_map/ppermute | solution.py:77
  70.4 7.0 %collective-permute-start.9 = (f32[4,12,128]{2,0,1:T(4,128)S(1)}, f32[4,12,128]{2,0,1:T(4,128)S(1)}, u32[]{:S(2)}, u32[]{:S(2)}) collective-permute-start(f32[4,12,128]{2,0,1:T(4,128)S(1)} %add.136), channel_id=1, source_target_pairs={{0,128},{16,144},{32,160},{48,176},{64,192},{80,208},{96,224},{112... | collective-permute-start | bytes 73736 | tf_op jit(solution)/shard_map/ppermute | solution.py:77
  77.4 0.3 fusion.42
  77.8 1.1 collective-permute-done.9
  78.9 15.2 %collective-permute-start.10 = (f32[4,12,128]{2,0,1:T(4,128)S(1)}, f32[4,12,128]{2,0,1:T(4,128)S(1)}, u32[]{:S(2)}, u32[]{:S(2)}) collective-permute-start(f32[4,12,128]{2,0,1:T(4,128)S(1)} %add.137), channel_id=1, source_target_pairs={{0,256},{16,272},{32,288},{48,304},{64,320},{80,336},{96,352},{112... | collective-permute-start | bytes 73736 | tf_op jit(solution)/shard_map/ppermute | solution.py:77
  94.1 0.4 fusion.11
  94.4 0.8 collective-permute-done.10
  95.3 16.8 %collective-permute-start.11 = (f32[4,12,128]{2,0,1:T(4,128)S(1)}, f32[4,12,128]{2,0,1:T(4,128)S(1)}, u32[]{:S(2)}, u32[]{:S(2)}) collective-permute-start(f32[4,12,128]{2,0,1:T(4,128)S(1)} %add.138), channel_id=1, source_target_pairs={{0,768},{16,784},{32,800},{48,816},{64,832},{80,848},{96,864},{112... | collective-permute-start | bytes 73736 | tf_op jit(solution)/shard_map/ppermute | solution.py:81
  112.4 0.9 collective-permute-done.11
  113.3 9.4 %collective-permute-start.12 = (f32[4,12,128]{2,0,1:T(4,128)S(1)}, f32[4,12,128]{2,0,1:T(4,128)S(1)}, u32[]{:S(2)}, u32[]{:S(2)}) collective-permute-start(f32[4,12,128]{2,0,1:T(4,128)S(1)} %add.139), channel_id=1, source_target_pairs={{0,16},{16,0},{32,48},{48,32},{64,80},{80,64},{96,112},{112,96},{1... | collective-permute-start | bytes 73736 | tf_op jit(solution)/shard_map/ppermute | solution.py:95
  122.7 1.0 fusion
  123.8 0.6 slice.192
  124.4 0.6 slice.193
  (44 shorter events, 5.2 us)
Async XLA Ops:
  0.6 6.3 %copy-start.1 = (f32[2,2,96,128]{3,2,1,0:T(8,128)S(1)}, f32[2,2,96,128]{3,2,1,0:T(8,128)}, u32[]{:S(2)}) copy-start(f32[2,2,96,128]{3,2,1,0:T(8,128)} %param.7) | copy-start | bytes 589828
  0.6 19.7 %copy-start.3 = (f32[3,128,128]{2,1,0:T(8,128)S(1)}, f32[3,128,128]{2,1,0:T(8,128)}, u32[]{:S(2)}) copy-start(f32[3,128,128]{2,1,0:T(8,128)} %param.6) | copy-start | bytes 589828
  1.7 19.1 %collective-permute-start = (f32[2,1,96,128]{3,2,1,0:T(8,128)S(1)}, f32[2,1,96,128]{3,2,1,0:T(8,128)S(1)}, u32[]{:S(2)}, u32[]{:S(2)}) collective-permute-start(f32[2,1,96,128]{3,2,1,0:T(8,128)S(1)} %get-tuple-element.14), channel_id=1, source_target_pairs={{0,1},{1,2},{2,3},{3,4},{4,5},{5,6},{6,7},{7,8},{8,9},{9,10},{10,1... | collective-permute-start | bytes 294920 | tf_op jit(solution)/shard_map/ppermute | solution.py:18
  5.6 16.6 %collective-permute-start.1 = (f32[2,1,96,128]{3,2,1,0:T(8,128)S(1)}, f32[2,1,96,128]{3,2,1,0:T(8,128)S(1)}, u32[]{:S(2)}, u32[]{:S(2)}) collective-permute-start(f32[2,1,96,128]{3,2,1,0:T(8,128)S(1)} %get-tuple-element.15), channel_id=1, source_target_pairs={{1,0},{2,1},{3,2},{4,3},{5,4},{6,5},{7,6},{8,7},{9,8},{10,9},{11,1... | collective-permute-start | bytes 294920 | tf_op jit(solution)/shard_map/ppermute | solution.py:19
  6.9 20.2 %collective-permute-start.3 = (f32[2,2,96,128]{3,2,1,0:T(8,128)S(1)}, f32[2,2,96,128]{3,2,1,0:T(8,128)S(1)}, u32[]{:S(2)}, u32[]{:S(2)}) collective-permute-start(f32[2,2,96,128]{3,2,1,0:T(8,128)S(1)} %copy-done.1), channel_id=1, source_target_pairs={{16,0},{32,16},{48,32},{64,48},{80,64},{96,80},{112,96},{128,112},... | collective-permute-start | bytes 589832 | tf_op jit(solution)/shard_map/ppermute | solution.py:27
  20.7 0.9 copy-start
  20.7 1.2 copy-start.2
  24.9 8.0 %collective-permute-start.2 = (f32[2,2,96,128]{3,2,1,0:T(8,128)S(1)}, f32[2,2,96,128]{3,2,1,0:T(8,128)S(1)}, u32[]{:S(2)}, u32[]{:S(2)}) collective-permute-start(f32[2,2,96,128]{3,2,1,0:T(8,128)S(1)} %get-tuple-element.16), channel_id=1, source_target_pairs={{0,16},{16,32},{32,48},{48,64},{64,80},{80,96},{96,112},{112,128},... | collective-permute-start | bytes 589832 | tf_op jit(solution)/shard_map/ppermute | solution.py:27
  34.1 12.8 %collective-permute-start.6 = (f32[16,4,12,128]{3,1,2,0:T(4,128)S(1)}, f32[16,4,12,128]{3,1,2,0:T(4,128)S(1)}, u32[]{:S(2)}, u32[]{:S(2)}) collective-permute-start(f32[16,4,12,128]{3,1,2,0:T(4,128)S(1)} %bitcast.237), channel_id=1, source_target_pairs={{0,16},{16,0},{32,48},{48,32},{64,80},{80,64},{96,112},{112,96},{1... | collective-permute-start | bytes 1179656 | tf_op jit(solution)/shard_map/ppermute | solution.py:149
  36.9 6.9 %collective-permute-start.4 = (f32[2,1,96,128]{3,2,1,0:T(8,128)S(1)}, f32[2,1,96,128]{3,2,1,0:T(8,128)S(1)}, u32[]{:S(2)}, u32[]{:S(2)}) collective-permute-start(f32[2,1,96,128]{3,2,1,0:T(8,128)S(1)} %get-tuple-element.10), channel_id=1, source_target_pairs={{0,1},{1,2},{2,3},{3,4},{4,5},{5,6},{6,7},{7,8},{8,9},{9,10},{10,1... | collective-permute-start | bytes 294920 | tf_op jit(solution)/shard_map/ppermute | solution.py:18
  40.8 6.0 %collective-permute-start.5 = (f32[2,1,96,128]{3,2,1,0:T(8,128)S(1)}, f32[2,1,96,128]{3,2,1,0:T(8,128)S(1)}, u32[]{:S(2)}, u32[]{:S(2)}) collective-permute-start(f32[2,1,96,128]{3,2,1,0:T(8,128)S(1)} %get-tuple-element.11), channel_id=1, source_target_pairs={{1,0},{2,1},{3,2},{4,3},{5,4},{6,5},{7,6},{8,7},{9,8},{10,9},{11,1... | collective-permute-start | bytes 294920 | tf_op jit(solution)/shard_map/ppermute | solution.py:19
  47.7 12.5 %all-to-all-start = ((f32[16,4,12,128]{3,1,2,0:T(4,128)}), f32[16,4,12,128]{3,1,2,0:T(4,128)S(1)}, u32[]{:S(2)}, u32[]{:S(2)}) async-start(f32[16,4,12,128]{3,1,2,0:T(4,128)} %bitcast_add_fusion), calls=%async_computation | async-start | bytes 786432 | tf_op jit(solution)/shard_map/all_to_all | solution.py:150
  60.3 4.6 %collective-permute-start.7 = (f32[4,12,128]{2,0,1:T(4,128)S(1)}, f32[4,12,128]{2,0,1:T(4,128)S(1)}, u32[]{:S(2)}, u32[]{:S(2)}) collective-permute-start(f32[4,12,128]{2,0,1:T(4,128)S(1)} %reduce_sum.9), channel_id=1, source_target_pairs={{0,32},{16,48},{32,0},{48,16},{64,96},{80,112},{96,64},{112,80},{1... | collective-permute-start | bytes 73736 | tf_op jit(solution)/shard_map/ppermute | solution.py:77
  64.9 5.5 %collective-permute-start.8 = (f32[4,12,128]{2,0,1:T(4,128)S(1)}, f32[4,12,128]{2,0,1:T(4,128)S(1)}, u32[]{:S(2)}, u32[]{:S(2)}) collective-permute-start(f32[4,12,128]{2,0,1:T(4,128)S(1)} %add.135), channel_id=1, source_target_pairs={{0,64},{16,80},{32,96},{48,112},{64,0},{80,16},{96,32},{112,48},{1... | collective-permute-start | bytes 73736 | tf_op jit(solution)/shard_map/ppermute | solution.py:77
  70.4 8.5 %collective-permute-start.9 = (f32[4,12,128]{2,0,1:T(4,128)S(1)}, f32[4,12,128]{2,0,1:T(4,128)S(1)}, u32[]{:S(2)}, u32[]{:S(2)}) collective-permute-start(f32[4,12,128]{2,0,1:T(4,128)S(1)} %add.136), channel_id=1, source_target_pairs={{0,128},{16,144},{32,160},{48,176},{64,192},{80,208},{96,224},{112... | collective-permute-start | bytes 73736 | tf_op jit(solution)/shard_map/ppermute | solution.py:77
  78.9 16.4 %collective-permute-start.10 = (f32[4,12,128]{2,0,1:T(4,128)S(1)}, f32[4,12,128]{2,0,1:T(4,128)S(1)}, u32[]{:S(2)}, u32[]{:S(2)}) collective-permute-start(f32[4,12,128]{2,0,1:T(4,128)S(1)} %add.137), channel_id=1, source_target_pairs={{0,256},{16,272},{32,288},{48,304},{64,320},{80,336},{96,352},{112... | collective-permute-start | bytes 73736 | tf_op jit(solution)/shard_map/ppermute | solution.py:77
  95.3 18.0 %collective-permute-start.11 = (f32[4,12,128]{2,0,1:T(4,128)S(1)}, f32[4,12,128]{2,0,1:T(4,128)S(1)}, u32[]{:S(2)}, u32[]{:S(2)}) collective-permute-start(f32[4,12,128]{2,0,1:T(4,128)S(1)} %add.138), channel_id=1, source_target_pairs={{0,768},{16,784},{32,800},{48,816},{64,832},{80,848},{96,864},{112... | collective-permute-start | bytes 73736 | tf_op jit(solution)/shard_map/ppermute | solution.py:81
  113.3 10.5 %collective-permute-start.12 = (f32[4,12,128]{2,0,1:T(4,128)S(1)}, f32[4,12,128]{2,0,1:T(4,128)S(1)}, u32[]{:S(2)}, u32[]{:S(2)}) collective-permute-start(f32[4,12,128]{2,0,1:T(4,128)S(1)} %add.139), channel_id=1, source_target_pairs={{0,16},{16,0},{32,48},{48,32},{64,80},{80,64},{96,112},{112,96},{1... | collective-permute-start | bytes 73736 | tf_op jit(solution)/shard_map/ppermute | solution.py:95

commit v6 on v4

--- a/solution.py
+++ b/solution.py
@@ -31,26 +31,20 @@
     return jnp.pad(array, ((0, 0), (0, 0), (1, 1), (0, 0)))
 
 
+def shifted(source, offsets, height, width):
+    return jnp.stack([source[:, i : i + height, j : j + width] for i, j in offsets])
+
+
 def convolve(source, kernel, height, width):
-    total = jnp.zeros((source.shape[0], height, width, kernel.shape[3]), jnp.float32)
-    for i in range(3):
-        for j in range(3):
-            total = total + jnp.einsum(
-                "frwc,cd->frwd",
-                source[:, i : i + height, j : j + width],
-                kernel[i, j],
-                precision=HIGH,
-            )
-    return total
+    offsets = [(i, j) for i in range(3) for j in range(3)]
+    views = shifted(source, offsets, height, width)
+    taps = kernel.reshape(9, kernel.shape[2], kernel.shape[3])
+    return jnp.einsum("tfrwc,tcd->frwd", views, taps, precision=HIGH)
 
 
 def temporal_back(grad_long, temporal_weight, nframes):
-    dact = jnp.zeros((nframes,) + grad_long.shape[1:], jnp.float32)
-    for k in range(3):
-        dact = dact + jnp.einsum(
-            "frwd,cd->frwc", grad_long[k : k + nframes], temporal_weight[k], precision=HIGH
-        )
-    return dact
+    views = jnp.stack([grad_long[k : k + nframes] for k in range(3)])
+    return jnp.einsum("kfrwd,kcd->frwc", views, temporal_weight, precision=HIGH)
 
 
 def halving_scatter(blocks, axis, order):
@@ -109,38 +103,24 @@
     act = pre * sig
     earlier = passed_along(act, "frames", 1)
     longer = jnp.concatenate([earlier, act], axis=0)
-    mixed = jnp.zeros(images.shape, jnp.float32)
-    for k in range(3):
-        mixed = mixed + jnp.einsum(
-            "frwc,cd->frwd", longer[2 - k : 2 - k + nframes], temporal_weight[k], precision=HIGH
-        )
+    lagged = jnp.stack([longer[2 - k : 2 - k + nframes] for k in range(3)])
+    mixed = jnp.einsum("kfrwc,kcd->frwd", lagged, temporal_weight, precision=HIGH)
     block_out = images + mixed
-    grad_images = cotangent
-    for i in range(3):
-        for j in range(3):
-            grad_images = grad_images + jnp.einsum(
-                "frwd,cd->frwc",
-                dpre_wide[:, 2 - i : 2 - i + strip, 2 - j : 2 - j + width],
-                spatial_weight[i, j],
-                precision=HIGH,
-            )
+    back = [(2 - i, 2 - j) for i in range(3) for j in range(3)]
+    spatial_taps = spatial_weight.reshape(9, chans, chans)
+    grad_images = cotangent + jnp.einsum(
+        "tfrwd,tcd->frwc", shifted(dpre_wide, back, strip, width), spatial_taps, precision=HIGH
+    )
     total_cells = nframes * lax.axis_size("frames") * strip * lax.axis_size("rows") * width
     factor = 1.0 / math.sqrt(total_cells)
-    taps = []
-    for i in range(3):
-        for j in range(3):
-            taps.append(
-                jnp.einsum(
-                    "frwc,frwd->dc", padded[:, i : i + strip, j : j + width], dpre, precision=HIGH
-                )
-            )
-    for k in range(3):
-        taps.append(
-            jnp.einsum("frwc,frwd->dc", longer[2 - k : 2 - k + nframes], cotangent, precision=HIGH)
-        )
+    offsets = [(i, j) for i in range(3) for j in range(3)]
+    spatial_terms = jnp.einsum(
+        "tfrwc,frwd->dtc", shifted(padded, offsets, strip, width), dpre, precision=HIGH
+    )
+    temporal_terms = jnp.einsum("kfrwc,frwd->dkc", lagged, cotangent, precision=HIGH)
     nrows = lax.axis_size("rows")
-    terms = jnp.stack(taps, axis=1) * factor
-    terms = terms.reshape(nrows, 2, chans // nrows // 2, len(taps), chans)
+    terms = jnp.concatenate([spatial_terms, temporal_terms], axis=1) * factor
+    terms = terms.reshape(nrows, 2, chans // nrows // 2, terms.shape[1], chans)
     parity = lax.axis_index("frames") % 2
     keep = lax.dynamic_index_in_dim(terms, parity, axis=1, keepdims=False)
     give = lax.dynamic_index_in_dim(terms, 1 - parity, axis=1, keepdims=False)

time: 124 us -> 118 us (0.952)
  matrix products: 15.7 us -> 6.39 us
  other arithmetic: 1.27 us -> 4.25 us
  waiting for transfers between devices: 13.7 us -> 16.5 us
  local copies, waits for them, and re-layouts: 4.42 us -> 2.83 us
    dot_general x36 -> x6, matrix products: 15.7 us -> 6.39 us  [the longest x1 1.59 us: convolve(): return jnp.einsum('tfrwc,tcd->frwd', views, taps, precision=HIGH)]
    unnamed x29 -> x34, local copies, waits for them, and re-layouts: 1.93 us -> 0.3 us
  transfers between devices with their start and end apart: 14 -> 14, of which waited for: 6 -> 6; matrix products, arithmetic and copies ran while one was open for 13% -> 8% of each run, Pallas kernels for 0% -> 0%
where the time goes in v6:
time: 118 us
  starting transfers between devices  86.3 us (73%)
  waiting for transfers between devices  16.5 us (14%)
  matrix products  6.39 us (5%)
  other arithmetic  4.25 us (4%)
  local copies, waits for them, and re-layouts  2.83 us (2%)
  between operations  1.26 us (1%)
    ppermute x4, starting transfers between devices, doubling_sum(): value = value + lax.ppermute(value, axis, pairs)  29.9 us
    ppermute x2, starting transfers between devices, passed_along(): return lax.ppermute(value, axis, pairs)  15.3 us
    ppermute x1, starting transfers between devices, doubling_sum(): return value + lax.ppermute(value, axis, pairs)  14.5 us
    all_to_all x1, waiting for transfers between devices, per_device(): terms = lax.all_to_all(terms, 'rows', 0, 0, tiled=True).sum(axis=0)  9.51 us
    ppermute x1, starting transfers between devices, pair_gather(): other = lax.ppermute(value, axis, [(i, i ^ 1) for i in range(count)])  8.94 us
    ppermute x2, starting transfers between devices, padded_2(): before = lax.ppermute(last, axis, up)  8.22 us
    ppermute x4, waiting for transfers between devices, doubling_sum(): value = value + lax.ppermute(value, axis, pairs)  5.31 us
    all_to_all x1, starting transfers between devices, per_device(): terms = lax.all_to_all(terms, 'rows', 0, 0, tiled=True).sum(axis=0)  4.21 us
  transfers between devices with their start and end apart: 14, of which 6 were waited for; matrix products, arithmetic and copies ran while one was open for 8% of the time, Pallas kernels for 0%

profile of v6, /device:TPU:1, one launch (start us, length us, event | category | flops | bytes accessed | tf_op | source)
XLA Modules:
  0.0 117.6 jit_solution(8083035185578384036)
XLA Ops:
  0.6 0.0 copy-start
  0.6 0.0 copy-start.1
  0.7 1.0 fusion.45
  1.7 4.0 %collective-permute-start = (f32[2,1,96,128]{3,2,1,0:T(8,128)S(1)}, f32[2,1,96,128]{3,2,1,0:T(8,128)S(1)}, u32[]{:S(2)}, u32[]{:S(2)}) collective-permute-start(f32[2,1,96,128]{3,2,1,0:T(8,128)S(1)} %get-tuple-element.10), channel_id=1, source_target_pairs={{0,1},{1,2},{2,3},{3,4},{4,5},{5,6},{6,7},{7,8},{8,9},{9,10},{10,1... | collective-permute-start | bytes 294920 | tf_op jit(solution)/shard_map/ppermute | solution.py:18
  5.7 1.3 %collective-permute-start.1 = (f32[2,1,96,128]{3,2,1,0:T(8,128)S(1)}, f32[2,1,96,128]{3,2,1,0:T(8,128)S(1)}, u32[]{:S(2)}, u32[]{:S(2)}) collective-permute-start(f32[2,1,96,128]{3,2,1,0:T(8,128)S(1)} %get-tuple-element.11), channel_id=1, source_target_pairs={{1,0},{2,1},{3,2},{4,3},{5,4},{6,5},{7,6},{8,7},{9,8},{10,9},{11,1... | collective-permute-start | bytes 294920 | tf_op jit(solution)/shard_map/ppermute | solution.py:19
  7.0 13.4 %collective-permute-start.3 = (f32[2,2,96,128]{3,2,1,0:T(8,128)}, f32[2,2,96,128]{3,2,1,0:T(8,128)S(1)}, u32[]{:S(2)}, u32[]{:S(2)}) collective-permute-start(f32[2,2,96,128]{3,2,1,0:T(8,128)} %param.7), channel_id=1, source_target_pairs={{16,0},{32,16},{48,32},{64,48},{80,64},{96,80},{112,96},{128,112},... | collective-permute-start | bytes 589832 | tf_op jit(solution)/shard_map/ppermute | solution.py:27
  20.4 1.0 select_maximum_fusion.2
  21.6 0.0 copy-start.2
  21.7 0.0 copy-start.9
  21.7 1.6 %convolution_bitcast_fusion.1 = f32[2,2,96,128]{3,2,1,0:T(8,128)S(1)} fusion(f32[9,2,2,96,128]{4,3,0,2,1:T(8,128)S(1)} %fusion.24, f32[9,128,128,1,1]{2,1,0,4,3:T(8,128)S(1)} %bitcast.162), kind=kOutput, calls=%fused_computation.4 | convolution fusion | flops 679477248 | bytes 2555904 | tf_op jit(solution)/shard_map/tfrwc,tcd->frwd/dot_general | solution.py:42
  23.3 0.1 fusion.43
  23.3 1.9 %collective-permute-start.2 = (f32[2,2,96,128]{3,2,1,0:T(8,128)S(1)}, f32[2,2,96,128]{3,2,1,0:T(8,128)S(1)}, u32[]{:S(2)}, u32[]{:S(2)}) collective-permute-start(f32[2,2,96,128]{3,2,1,0:T(8,128)S(1)} %get-tuple-element.9), channel_id=1, source_target_pairs={{0,16},{16,32},{32,48},{48,64},{64,80},{80,96},{96,112},{112,128},... | collective-permute-start | bytes 589832 | tf_op jit(solution)/shard_map/ppermute | solution.py:27
  25.3 0.6 fusion.3
  26.0 4.3 %collective-permute-start.4 = (f32[2,1,96,128]{3,2,1,0:T(8,128)S(1)}, f32[2,1,96,128]{3,2,1,0:T(8,128)S(1)}, u32[]{:S(2)}, u32[]{:S(2)}) collective-permute-start(f32[2,1,96,128]{3,2,1,0:T(8,128)S(1)} %get-tuple-element.6), channel_id=1, source_target_pairs={{0,1},{1,2},{2,3},{3,4},{4,5},{5,6},{6,7},{7,8},{8,9},{9,10},{10,1... | collective-permute-start | bytes 294920 | tf_op jit(solution)/shard_map/ppermute | solution.py:18
  30.3 1.3 %collective-permute-start.5 = (f32[2,1,96,128]{3,2,1,0:T(8,128)S(1)}, f32[2,1,96,128]{3,2,1,0:T(8,128)S(1)}, u32[]{:S(2)}, u32[]{:S(2)}) collective-permute-start(f32[2,1,96,128]{3,2,1,0:T(8,128)S(1)} %get-tuple-element.7), channel_id=1, source_target_pairs={{1,0},{2,1},{3,2},{4,3},{5,4},{6,5},{7,6},{8,7},{9,8},{10,9},{11,1... | collective-permute-start | bytes 294920 | tf_op jit(solution)/shard_map/ppermute | solution.py:19
  31.6 1.3 %fusion.36 = f32[128,9,128,1,1]{2,0,1,4,3:T(8,128)S(1)} fusion(f32[9,2,2,96,128]{4,3,0,2,1:T(8,128)S(1)} %fusion.24, f32[2,2,96,128]{3,2,1,0:T(8,128)S(1)} %fusion.3), kind=kOutput, calls=%fused_computation.66 | convolution fusion | flops 679477248 | bytes 2555904 | tf_op jit(solution)/shard_map/tfrwc,frwd->dtc/dot_general | solution.py:117
  32.9 0.0 copy-start.5
  32.9 0.0 copy-start.7
  32.9 0.6 fusion.34
  33.6 0.0 copy-done.7
  33.6 0.3 maximum_multiply_fusion
  33.9 0.1 constant_dynamic-slice_fusion.1
  34.1 0.1 copy.55
  34.1 2.7 %collective-permute-start.6 = (f32[16,4,12,128]{3,1,2,0:T(4,128)S(1)}, f32[16,4,12,128]{3,1,2,0:T(4,128)S(1)}, u32[]{:S(2)}, u32[]{:S(2)}) collective-permute-start(f32[16,4,12,128]{3,1,2,0:T(4,128)S(1)} %bitcast.168), channel_id=1, source_target_pairs={{0,16},{16,0},{32,48},{48,32},{64,80},{80,64},{96,112},{112,96},{1... | collective-permute-start | bytes 1179656 | tf_op jit(solution)/shard_map/ppermute | solution.py:128
  37.0 1.2 collective-permute-done.6
  38.2 0.9 bitcast_add_fusion
  39.0 4.2 %all-to-all-start = ((f32[16,4,12,128]{3,1,2,0:T(4,128)}), f32[16,4,12,128]{3,1,2,0:T(4,128)}, u32[]{:S(2)}, u32[]{:S(2)}) async-start(f32[16,4,12,128]{3,1,2,0:T(4,128)} %bitcast_add_fusion), calls=%async_computation | async-start | bytes 786432 | tf_op jit(solution)/shard_map/all_to_all | solution.py:129
  43.3 9.5 %all-to-all-done = f32[16,4,12,128]{3,1,2,0:T(4,128)} async-done(((f32[16,4,12,128]{3,1,2,0:T(4,128)}), f32[16,4,12,128]{3,1,2,0:T(4,128)}, u32[]{:S(2)}, u32[]{:S(2)}) %all-to-all-start) | async-done | bytes 393248 | tf_op jit(solution)/shard_map/all_to_all | solution.py:129
  52.8 1.1 reduce_sum.9
  53.9 1.9 %collective-permute-start.7 = (f32[4,12,128]{2,0,1:T(4,128)S(1)}, f32[4,12,128]{2,0,1:T(4,128)S(1)}, u32[]{:S(2)}, u32[]{:S(2)}) collective-permute-start(f32[4,12,128]{2,0,1:T(4,128)S(1)} %reduce_sum.9), channel_id=1, source_target_pairs={{0,32},{16,48},{32,0},{48,16},{64,96},{80,112},{96,64},{112,80},{1... | collective-permute-start | bytes 73736 | tf_op jit(solution)/shard_map/ppermute | solution.py:71
  55.8 2.6 %collective-permute-done.7 = f32[4,12,128]{2,0,1:T(4,128)S(1)} collective-permute-done((f32[4,12,128]{2,0,1:T(4,128)S(1)}, f32[4,12,128]{2,0,1:T(4,128)S(1)}, u32[]{:S(2)}, u32[]{:S(2)}) %collective-permute-start.7) | collective-permute-done | bytes 24608 | tf_op jit(solution)/shard_map/ppermute | solution.py:71
  58.5 0.0 copy-start.6
  58.5 0.0 copy-start.8
  58.5 0.0 copy-start.10
  58.5 4.1 %collective-permute-start.8 = (f32[4,12,128]{2,0,1:T(4,128)S(1)}, f32[4,12,128]{2,0,1:T(4,128)S(1)}, u32[]{:S(2)}, u32[]{:S(2)}) collective-permute-start(f32[4,12,128]{2,0,1:T(4,128)S(1)} %add.55), channel_id=1, source_target_pairs={{0,64},{16,80},{32,96},{48,112},{64,0},{80,16},{96,32},{112,48},{1... | collective-permute-start | bytes 73736 | tf_op jit(solution)/shard_map/ppermute | solution.py:71
  62.6 1.5 %collective-permute-done.8 = f32[4,12,128]{2,0,1:T(4,128)S(1)} collective-permute-done((f32[4,12,128]{2,0,1:T(4,128)S(1)}, f32[4,12,128]{2,0,1:T(4,128)S(1)}, u32[]{:S(2)}, u32[]{:S(2)}) %collective-permute-start.8) | collective-permute-done | bytes 24608 | tf_op jit(solution)/shard_map/ppermute | solution.py:71
  64.1 8.5 %collective-permute-start.9 = (f32[4,12,128]{2,0,1:T(4,128)S(1)}, f32[4,12,128]{2,0,1:T(4,128)S(1)}, u32[]{:S(2)}, u32[]{:S(2)}) collective-permute-start(f32[4,12,128]{2,0,1:T(4,128)S(1)} %add.56), channel_id=1, source_target_pairs={{0,128},{16,144},{32,160},{48,176},{64,192},{80,208},{96,224},{112... | collective-permute-start | bytes 73736 | tf_op jit(solution)/shard_map/ppermute | solution.py:71
  72.6 1.2 %collective-permute-done.9 = f32[4,12,128]{2,0,1:T(4,128)S(1)} collective-permute-done((f32[4,12,128]{2,0,1:T(4,128)S(1)}, f32[4,12,128]{2,0,1:T(4,128)S(1)}, u32[]{:S(2)}, u32[]{:S(2)}) %collective-permute-start.9) | collective-permute-done | bytes 24608 | tf_op jit(solution)/shard_map/ppermute | solution.py:71
  73.8 15.4 %collective-permute-start.10 = (f32[4,12,128]{2,0,1:T(4,128)S(1)}, f32[4,12,128]{2,0,1:T(4,128)S(1)}, u32[]{:S(2)}, u32[]{:S(2)}) collective-permute-start(f32[4,12,128]{2,0,1:T(4,128)S(1)} %add.57), channel_id=1, source_target_pairs={{0,256},{16,272},{32,288},{48,304},{64,320},{80,336},{96,352},{112... | collective-permute-start | bytes 73736 | tf_op jit(solution)/shard_map/ppermute | solution.py:71
  89.3 1.6 %fusion = f32[2,2,96,128,1]{3,2,0,1,4:T(8,128)S(1)} fusion(f32[9,128,128,1,1]{2,1,3,4,0:T(8,128)S(1)} %bitcast.161, f32[9,2,2,96,128]{4,3,2,1,0:T(8,128)S(1)} %fusion.12), kind=kOutput, calls=%fused_computation | convolution fusion | flops 679477248 | bytes 2555904 | tf_op jit(solution)/shard_map/tfrwd,tcd->frwc/dot_general | solution.py:111
  90.9 14.5 %collective-permute-start.11 = (f32[4,12,128]{2,0,1:T(4,128)S(1)}, f32[4,12,128]{2,0,1:T(4,128)S(1)}, u32[]{:S(2)}, u32[]{:S(2)}) collective-permute-start(f32[4,12,128]{2,0,1:T(4,128)S(1)} %add.58), channel_id=1, source_target_pairs={{0,768},{16,784},{32,800},{48,816},{64,832},{80,848},{96,864},{112... | collective-permute-start | bytes 73736 | tf_op jit(solution)/shard_map/ppermute | solution.py:75
  105.4 0.6 fusion.9
  106.1 0.5 collective-permute-done.11
  106.6 8.9 %collective-permute-start.12 = (f32[4,12,128]{2,0,1:T(4,128)S(1)}, f32[4,12,128]{2,0,1:T(4,128)S(1)}, u32[]{:S(2)}, u32[]{:S(2)}) collective-permute-start(f32[4,12,128]{2,0,1:T(4,128)S(1)} %add.59), channel_id=1, source_target_pairs={{0,16},{16,0},{32,48},{48,32},{64,80},{80,64},{96,112},{112,96},{1... | collective-permute-start | bytes 73736 | tf_op jit(solution)/shard_map/ppermute | solution.py:89
  115.5 0.8 bitcast_add_fusion.1
  116.3 0.0 collective-permute-done.12
  116.4 0.6 slice.132
  117.0 0.6 slice.131
  (47 shorter events, 0.5 us)
Async XLA Ops:
  0.6 21.0 %copy-start = (f32[3,3,128,128]{3,2,1,0:T(8,128)S(1)}, f32[3,3,128,128]{3,2,1,0:T(8,128)}, u32[]{:S(2)}) copy-start(f32[3,3,128,128]{3,2,1,0:T(8,128)} %param.5) | copy-start | bytes 1769476
  0.6 20.8 %copy-start.1 = (f32[2,2,96,128]{3,2,1,0:T(8,128)S(1)}, f32[2,2,96,128]{3,2,1,0:T(8,128)}, u32[]{:S(2)}) copy-start(f32[2,2,96,128]{3,2,1,0:T(8,128)} %param.4) | copy-start | bytes 589828
  1.7 18.7 %collective-permute-start = (f32[2,1,96,128]{3,2,1,0:T(8,128)S(1)}, f32[2,1,96,128]{3,2,1,0:T(8,128)S(1)}, u32[]{:S(2)}, u32[]{:S(2)}) collective-permute-start(f32[2,1,96,128]{3,2,1,0:T(8,128)S(1)} %get-tuple-element.10), channel_id=1, source_target_pairs={{0,1},{1,2},{2,3},{3,4},{4,5},{5,6},{6,7},{7,8},{8,9},{9,10},{10,1... | collective-permute-start | bytes 294920 | tf_op jit(solution)/shard_map/ppermute | solution.py:18
  5.7 14.8 %collective-permute-start.1 = (f32[2,1,96,128]{3,2,1,0:T(8,128)S(1)}, f32[2,1,96,128]{3,2,1,0:T(8,128)S(1)}, u32[]{:S(2)}, u32[]{:S(2)}) collective-permute-start(f32[2,1,96,128]{3,2,1,0:T(8,128)S(1)} %get-tuple-element.11), channel_id=1, source_target_pairs={{1,0},{2,1},{3,2},{4,3},{5,4},{6,5},{7,6},{8,7},{9,8},{10,9},{11,1... | collective-permute-start | bytes 294920 | tf_op jit(solution)/shard_map/ppermute | solution.py:19
  7.0 18.3 %collective-permute-start.3 = (f32[2,2,96,128]{3,2,1,0:T(8,128)}, f32[2,2,96,128]{3,2,1,0:T(8,128)S(1)}, u32[]{:S(2)}, u32[]{:S(2)}) collective-permute-start(f32[2,2,96,128]{3,2,1,0:T(8,128)} %param.7), channel_id=1, source_target_pairs={{16,0},{32,16},{48,32},{64,48},{80,64},{96,80},{112,96},{128,112},... | collective-permute-start | bytes 589832 | tf_op jit(solution)/shard_map/ppermute | solution.py:27
  21.6 3.7 %copy-start.2 = (f32[2,2,96,128]{3,2,1,0:T(8,128)S(1)}, f32[2,2,96,128]{3,2,1,0:T(8,128)}, u32[]{:S(2)}) copy-start(f32[2,2,96,128]{3,2,1,0:T(8,128)} %param.7) | copy-start | bytes 589828
  21.7 3.7 %copy-start.9 = (f32[3,128,128]{2,1,0:T(8,128)S(1)}, f32[3,128,128]{2,1,0:T(8,128)}, u32[]{:S(2)}) copy-start(f32[3,128,128]{2,1,0:T(8,128)} %param.6) | copy-start | bytes 589828
  23.3 9.6 %copy-start.3 = (f32[1,2,2,96,128]{4,3,2,1,0:T(8,128)}, f32[1,2,2,96,128]{4,3,2,1,0:T(8,128)S(1)}, u32[]{:S(2)}) copy-start(f32[1,2,2,96,128]{4,3,2,1,0:T(8,128)S(1)} %get-tuple-element.8) | copy-start | bytes 589828
  23.3 9.5 %collective-permute-start.2 = (f32[2,2,96,128]{3,2,1,0:T(8,128)S(1)}, f32[2,2,96,128]{3,2,1,0:T(8,128)S(1)}, u32[]{:S(2)}, u32[]{:S(2)}) collective-permute-start(f32[2,2,96,128]{3,2,1,0:T(8,128)S(1)} %get-tuple-element.9), channel_id=1, source_target_pairs={{0,16},{16,32},{32,48},{48,64},{64,80},{80,96},{96,112},{112,128},... | collective-permute-start | bytes 589832 | tf_op jit(solution)/shard_map/ppermute | solution.py:27
  26.0 10.8 %collective-permute-start.4 = (f32[2,1,96,128]{3,2,1,0:T(8,128)S(1)}, f32[2,1,96,128]{3,2,1,0:T(8,128)S(1)}, u32[]{:S(2)}, u32[]{:S(2)}) collective-permute-start(f32[2,1,96,128]{3,2,1,0:T(8,128)S(1)} %get-tuple-element.6), channel_id=1, source_target_pairs={{0,1},{1,2},{2,3},{3,4},{4,5},{5,6},{6,7},{7,8},{8,9},{9,10},{10,1... | collective-permute-start | bytes 294920 | tf_op jit(solution)/shard_map/ppermute | solution.py:18
  30.3 6.6 %collective-permute-start.5 = (f32[2,1,96,128]{3,2,1,0:T(8,128)S(1)}, f32[2,1,96,128]{3,2,1,0:T(8,128)S(1)}, u32[]{:S(2)}, u32[]{:S(2)}) collective-permute-start(f32[2,1,96,128]{3,2,1,0:T(8,128)S(1)} %get-tuple-element.7), channel_id=1, source_target_pairs={{1,0},{2,1},{3,2},{4,3},{5,4},{6,5},{7,6},{8,7},{9,8},{10,9},{11,1... | collective-permute-start | bytes 294920 | tf_op jit(solution)/shard_map/ppermute | solution.py:19
  32.9 0.7 copy-start.5
  32.9 0.7 copy-start.7
  34.1 4.0 %collective-permute-start.6 = (f32[16,4,12,128]{3,1,2,0:T(4,128)S(1)}, f32[16,4,12,128]{3,1,2,0:T(4,128)S(1)}, u32[]{:S(2)}, u32[]{:S(2)}) collective-permute-start(f32[16,4,12,128]{3,1,2,0:T(4,128)S(1)} %bitcast.168), channel_id=1, source_target_pairs={{0,16},{16,0},{32,48},{48,32},{64,80},{80,64},{96,112},{112,96},{1... | collective-permute-start | bytes 1179656 | tf_op jit(solution)/shard_map/ppermute | solution.py:128
  39.0 13.8 %all-to-all-start = ((f32[16,4,12,128]{3,1,2,0:T(4,128)}), f32[16,4,12,128]{3,1,2,0:T(4,128)}, u32[]{:S(2)}, u32[]{:S(2)}) async-start(f32[16,4,12,128]{3,1,2,0:T(4,128)} %bitcast_add_fusion), calls=%async_computation | async-start | bytes 786432 | tf_op jit(solution)/shard_map/all_to_all | solution.py:129
  53.9 4.6 %collective-permute-start.7 = (f32[4,12,128]{2,0,1:T(4,128)S(1)}, f32[4,12,128]{2,0,1:T(4,128)S(1)}, u32[]{:S(2)}, u32[]{:S(2)}) collective-permute-start(f32[4,12,128]{2,0,1:T(4,128)S(1)} %reduce_sum.9), channel_id=1, source_target_pairs={{0,32},{16,48},{32,0},{48,16},{64,96},{80,112},{96,64},{112,80},{1... | collective-permute-start | bytes 73736 | tf_op jit(solution)/shard_map/ppermute | solution.py:71
  58.5 46.9 %copy-start.4 = (f32[1,2,2,96,128]{4,3,2,1,0:T(8,128)S(1)}, f32[1,2,2,96,128]{4,3,2,1,0:T(8,128)}, u32[]{:S(2)}) copy-start(f32[1,2,2,96,128]{4,3,2,1,0:T(8,128)} %copy-done.3) | copy-start | bytes 589828
  58.5 46.9 %copy-start.6 = (f32[2,2,96,128]{3,2,1,0:T(8,128)S(1)}, f32[2,2,96,128]{3,2,1,0:T(8,128)}, u32[]{:S(2)}) copy-start(f32[2,2,96,128]{3,2,1,0:T(8,128)} %copy-done.5) | copy-start | bytes 589828
  58.5 46.9 %copy-start.8 = (f32[1,2,2,96,128]{4,3,2,1,0:T(8,128)S(1)}, f32[1,2,2,96,128]{4,3,2,1,0:T(8,128)}, u32[]{:S(2)}) copy-start(f32[1,2,2,96,128]{4,3,2,1,0:T(8,128)} %copy-done.7) | copy-start | bytes 589828
  58.5 46.9 %copy-start.10 = (f32[3,128,128]{2,1,0:T(8,128)S(1)}, f32[3,128,128]{2,1,0:T(8,128)}, u32[]{:S(2)}) copy-start(f32[3,128,128]{2,1,0:T(8,128)} %param.6) | copy-start | bytes 589828
  58.5 5.6 %collective-permute-start.8 = (f32[4,12,128]{2,0,1:T(4,128)S(1)}, f32[4,12,128]{2,0,1:T(4,128)S(1)}, u32[]{:S(2)}, u32[]{:S(2)}) collective-permute-start(f32[4,12,128]{2,0,1:T(4,128)S(1)} %add.55), channel_id=1, source_target_pairs={{0,64},{16,80},{32,96},{48,112},{64,0},{80,16},{96,32},{112,48},{1... | collective-permute-start | bytes 73736 | tf_op jit(solution)/shard_map/ppermute | solution.py:71
  64.1 9.7 %collective-permute-start.9 = (f32[4,12,128]{2,0,1:T(4,128)S(1)}, f32[4,12,128]{2,0,1:T(4,128)S(1)}, u32[]{:S(2)}, u32[]{:S(2)}) collective-permute-start(f32[4,12,128]{2,0,1:T(4,128)S(1)} %add.56), channel_id=1, source_target_pairs={{0,128},{16,144},{32,160},{48,176},{64,192},{80,208},{96,224},{112... | collective-permute-start | bytes 73736 | tf_op jit(solution)/shard_map/ppermute | solution.py:71
  73.8 17.0 %collective-permute-start.10 = (f32[4,12,128]{2,0,1:T(4,128)S(1)}, f32[4,12,128]{2,0,1:T(4,128)S(1)}, u32[]{:S(2)}, u32[]{:S(2)}) collective-permute-start(f32[4,12,128]{2,0,1:T(4,128)S(1)} %add.57), channel_id=1, source_target_pairs={{0,256},{16,272},{32,288},{48,304},{64,320},{80,336},{96,352},{112... | collective-permute-start | bytes 73736 | tf_op jit(solution)/shard_map/ppermute | solution.py:71
  90.9 15.7 %collective-permute-start.11 = (f32[4,12,128]{2,0,1:T(4,128)S(1)}, f32[4,12,128]{2,0,1:T(4,128)S(1)}, u32[]{:S(2)}, u32[]{:S(2)}) collective-permute-start(f32[4,12,128]{2,0,1:T(4,128)S(1)} %add.58), channel_id=1, source_target_pairs={{0,768},{16,784},{32,800},{48,816},{64,832},{80,848},{96,864},{112... | collective-permute-start | bytes 73736 | tf_op jit(solution)/shard_map/ppermute | solution.py:75
  106.6 9.8 %collective-permute-start.12 = (f32[4,12,128]{2,0,1:T(4,128)S(1)}, f32[4,12,128]{2,0,1:T(4,128)S(1)}, u32[]{:S(2)}, u32[]{:S(2)}) collective-permute-start(f32[4,12,128]{2,0,1:T(4,128)S(1)} %add.59), channel_id=1, source_target_pairs={{0,16},{16,0},{32,48},{48,32},{64,80},{80,64},{96,112},{112,96},{1... | collective-permute-start | bytes 73736 | tf_op jit(solution)/shard_map/ppermute | solution.py:89

commit v7 on v6

--- a/solution.py
+++ b/solution.py
@@ -99,18 +99,12 @@
     grad_long = jnp.concatenate([cotangent, later], axis=0)
     dact = temporal_back(grad_long, temporal_weight, nframes)
     dpre = dact * sig * (1.0 + pre * (1.0 - sig))
-    dpre_wide = widen(padded_2(dpre, (("rows", 1),), 1))
     act = pre * sig
     earlier = passed_along(act, "frames", 1)
     longer = jnp.concatenate([earlier, act], axis=0)
     lagged = jnp.stack([longer[2 - k : 2 - k + nframes] for k in range(3)])
     mixed = jnp.einsum("kfrwc,kcd->frwd", lagged, temporal_weight, precision=HIGH)
     block_out = images + mixed
-    back = [(2 - i, 2 - j) for i in range(3) for j in range(3)]
-    spatial_taps = spatial_weight.reshape(9, chans, chans)
-    grad_images = cotangent + jnp.einsum(
-        "tfrwd,tcd->frwc", shifted(dpre_wide, back, strip, width), spatial_taps, precision=HIGH
-    )
     total_cells = nframes * lax.axis_size("frames") * strip * lax.axis_size("rows") * width
     factor = 1.0 / math.sqrt(total_cells)
     offsets = [(i, j) for i in range(3) for j in range(3)]
@@ -128,6 +122,13 @@
     terms = keep + lax.ppermute(give, "frames", [(i, i ^ 1) for i in range(nframes_all)])
     terms = lax.all_to_all(terms, "rows", 0, 0, tiled=True).sum(axis=0)
     summed = pair_gather(doubling_sum(terms, "frames", 2), "frames")
+    summed, dpre_late = lax.optimization_barrier((summed, dpre))
+    dpre_wide = widen(padded_2(dpre_late, (("rows", 1),), 1))
+    back = [(2 - i, 2 - j) for i in range(3) for j in range(3)]
+    spatial_taps = spatial_weight.reshape(9, chans, chans)
+    grad_images = cotangent + jnp.einsum(
+        "tfrwd,tcd->frwc", shifted(dpre_wide, back, strip, width), spatial_taps, precision=HIGH
+    )
     summed = jnp.transpose(summed, (1, 2, 0))
     grad_spatial = summed[:9].reshape(3, 3, chans, summed.shape[2])
     grad_temporal = summed[9:]

time: 118 us -> 124 us (1.051)
  blocking collectives: 0 us -> 12.2 us
  waiting for transfers between devices: 16.5 us -> 12.1 us
  other arithmetic: 4.25 us -> 2.48 us
    all_to_all x0 -> x1, blocking collectives: none -> 12.2 us  [per_device(): terms = lax.all_to_all(terms, 'rows', 0, 0, tiled=True).sum(axis=0)]
    all_to_all x1 -> x0, waiting for transfers between devices: 9.51 us -> none  [per_device(): terms = lax.all_to_all(terms, 'rows', 0, 0, tiled=True).sum(axis=0)]
    all_to_all x1 -> x0, starting transfers between devices: 4.21 us -> none  [per_device(): terms = lax.all_to_all(terms, 'rows', 0, 0, tiled=True).sum(axis=0)]
    ppermute x1, starting transfers between devices: 14.5 us -> 18.2 us  [doubling_sum(): return value + lax.ppermute(value, axis, pairs)]
    ppermute x2, waiting for transfers between devices: 0.01 us -> 2.2 us  [padded_2(): after = lax.ppermute(leading, axis, down)]
    ppermute x2, starting transfers between devices: 8.22 us -> 6.14 us  [padded_2(): before = lax.ppermute(last, axis, up)]
    ppermute x4, starting transfers between devices: 29.9 us -> 31.8 us  [doubling_sum(): value = value + lax.ppermute(value, axis, pairs)]
    ppermute x2, waiting for transfers between devices: 0.01 us -> 1.52 us  [passed_along(): return lax.ppermute(value, axis, pairs)]
  transfers between devices with their start and end apart: 14 -> 13, of which waited for: 6 -> 9; matrix products, arithmetic and copies ran while one was open for 8% -> 5% of each run, Pallas kernels for 0% -> 0%
where the time goes in v7:
time: 124 us; the launch traced here: 122 us
  starting transfers between devices  85.5 us (69%)
  blocking collectives  12.2 us (10%)
  waiting for transfers between devices  12.1 us (10%)
  matrix products  6.38 us (5%)
  local copies, waits for them, and re-layouts  2.76 us (2%)
  other arithmetic  2.48 us (2%)
    ppermute x4, starting transfers between devices, doubling_sum(): value = value + lax.ppermute(value, axis, pairs)  31.8 us
    ppermute x1, starting transfers between devices, doubling_sum(): return value + lax.ppermute(value, axis, pairs)  18.2 us
    ppermute x2, starting transfers between devices, passed_along(): return lax.ppermute(value, axis, pairs)  15.3 us
    all_to_all x1, blocking collectives, per_device(): terms = lax.all_to_all(terms, 'rows', 0, 0, tiled=True).sum(axis=0)  12.2 us
    ppermute x1, starting transfers between devices, pair_gather(): other = lax.ppermute(value, axis, [(i, i ^ 1) for i in range(count)])  8.32 us
    ppermute x2, starting transfers between devices, padded_2(): before = lax.ppermute(last, axis, up)  6.14 us
    ppermute x4, waiting for transfers between devices, doubling_sum(): value = value + lax.ppermute(value, axis, pairs)  4.84 us
    ppermute x1, starting transfers between devices, per_device(): lax.ppermute(give, 'frames', [(i, i ^ 1) for i in range(nframes_all)])  3.04 us
  transfers between devices with their start and end apart: 13, of which 9 were waited for; matrix products, arithmetic and copies ran while one was open for 5% of the time, Pallas kernels for 0%

profile of v7, /device:TPU:1, one launch (start us, length us, event | category | flops | bytes accessed | tf_op | source)
XLA Modules:
  0.0 122.5 jit_solution(7104879791870284188)
XLA Ops:
  0.6 0.0 copy-start
  0.6 0.0 copy-start.1
  0.7 1.0 fusion.44
  1.7 4.0 %collective-permute-start = (f32[2,1,96,128]{3,2,1,0:T(8,128)S(1)}, f32[2,1,96,128]{3,2,1,0:T(8,128)S(1)}, u32[]{:S(2)}, u32[]{:S(2)}) collective-permute-start(f32[2,1,96,128]{3,2,1,0:T(8,128)S(1)} %get-tuple-element.14), channel_id=1, source_target_pairs={{0,1},{1,2},{2,3},{3,4},{4,5},{5,6},{6,7},{7,8},{8,9},{9,10},{10,1... | collective-permute-start | bytes 294920 | tf_op jit(solution)/shard_map/ppermute | solution.py:18
  5.7 1.3 %collective-permute-start.1 = (f32[2,1,96,128]{3,2,1,0:T(8,128)S(1)}, f32[2,1,96,128]{3,2,1,0:T(8,128)S(1)}, u32[]{:S(2)}, u32[]{:S(2)}) collective-permute-start(f32[2,1,96,128]{3,2,1,0:T(8,128)S(1)} %get-tuple-element.15), channel_id=1, source_target_pairs={{1,0},{2,1},{3,2},{4,3},{5,4},{6,5},{7,6},{8,7},{9,8},{10,9},{11,1... | collective-permute-start | bytes 294920 | tf_op jit(solution)/shard_map/ppermute | solution.py:19
  7.0 13.4 %collective-permute-start.3 = (f32[2,2,96,128]{3,2,1,0:T(8,128)}, f32[2,2,96,128]{3,2,1,0:T(8,128)S(1)}, u32[]{:S(2)}, u32[]{:S(2)}) collective-permute-start(f32[2,2,96,128]{3,2,1,0:T(8,128)} %param.7), channel_id=1, source_target_pairs={{16,0},{32,16},{48,32},{64,48},{80,64},{96,80},{112,96},{128,112},... | collective-permute-start | bytes 589832 | tf_op jit(solution)/shard_map/ppermute | solution.py:27
  20.4 0.0 collective-permute-done
  20.4 0.0 collective-permute-done.1
  20.4 1.0 select_maximum_fusion.2
  21.6 0.0 copy-start.2
  21.7 0.0 copy-start.3
  21.7 1.6 %convolution_bitcast_fusion.1 = f32[2,2,96,128]{3,2,1,0:T(8,128)S(1)} fusion(f32[9,2,2,96,128]{4,3,0,2,1:T(8,128)S(1)} %fusion.24, f32[9,128,128,1,1]{2,1,0,4,3:T(8,128)S(1)} %bitcast.161), kind=kOutput, calls=%fused_computation.4 | convolution fusion | flops 679477248 | bytes 2555904 | tf_op jit(solution)/shard_map/tfrwc,tcd->frwd/dot_general | solution.py:42
  23.3 0.1 fusion.42
  23.3 1.9 %collective-permute-start.2 = (f32[2,2,96,128]{3,2,1,0:T(8,128)S(1)}, f32[2,2,96,128]{3,2,1,0:T(8,128)S(1)}, u32[]{:S(2)}, u32[]{:S(2)}) collective-permute-start(f32[2,2,96,128]{3,2,1,0:T(8,128)S(1)} %get-tuple-element.13), channel_id=1, source_target_pairs={{0,16},{16,32},{32,48},{48,64},{64,80},{80,96},{96,112},{112,128},... | collective-permute-start | bytes 589832 | tf_op jit(solution)/shard_map/ppermute | solution.py:27
  25.3 0.0 collective-permute-done.3
  25.3 0.6 fusion.3
  26.0 1.3 %fusion.36 = f32[128,9,128,1,1]{2,0,1,4,3:T(8,128)S(1)} fusion(f32[9,2,2,96,128]{4,3,0,2,1:T(8,128)S(1)} %fusion.24, f32[2,2,96,128]{3,2,1,0:T(8,128)S(1)} %fusion.3), kind=kOutput, calls=%fused_computation.66 | convolution fusion | flops 679477248 | bytes 2555904 | tf_op jit(solution)/shard_map/tfrwc,frwd->dtc/dot_general | solution.py:111
  27.3 1.5 %collective-permute-done.2 = f32[2,2,96,128]{3,2,1,0:T(8,128)S(1)} collective-permute-done((f32[2,2,96,128]{3,2,1,0:T(8,128)S(1)}, f32[2,2,96,128]{3,2,1,0:T(8,128)S(1)}, u32[]{:S(2)}, u32[]{:S(2)}) %collective-permute-start.2) | collective-permute-done | bytes 196640 | tf_op jit(solution)/shard_map/ppermute | solution.py:27
  28.8 0.6 fusion.34
  29.4 0.3 maximum_multiply_fusion
  29.7 0.1 constant_dynamic-slice_fusion.1
  29.9 0.1 copy.55
  29.9 3.0 %collective-permute-start.4 = (f32[16,4,12,128]{3,1,2,0:T(4,128)S(1)}, f32[16,4,12,128]{3,1,2,0:T(4,128)S(1)}, u32[]{:S(2)}, u32[]{:S(2)}) collective-permute-start(f32[16,4,12,128]{3,1,2,0:T(4,128)S(1)} %bitcast.167), channel_id=1, source_target_pairs={{0,16},{16,0},{32,48},{48,32},{64,80},{80,64},{96,112},{112,96},{1... | collective-permute-start | bytes 1179656 | tf_op jit(solution)/shard_map/ppermute | solution.py:122
  33.0 1.3 %collective-permute-done.4 = f32[16,4,12,128]{3,1,2,0:T(4,128)S(1)} collective-permute-done((f32[16,4,12,128]{3,1,2,0:T(4,128)S(1)}, f32[16,4,12,128]{3,1,2,0:T(4,128)S(1)}, u32[]{:S(2)}, u32[]{:S(2)}) %collective-permute-start.4) | collective-permute-done | bytes 393248 | tf_op jit(solution)/shard_map/ppermute | solution.py:122
  34.3 0.1 bitcast_add_fusion
  34.4 12.2 %all_to_all.5 = f32[16,4,12,128]{3,1,2,0:T(4,128)S(1)} all-to-all(f32[16,4,12,128]{3,1,2,0:T(4,128)S(1)} %bitcast_add_fusion), channel_id=1, replica_groups=mesh['frames'=64,'rows'=16] {'rows'}, dimensions={0} | all-to-all | bytes 786432 | tf_op jit(solution)/shard_map/all_to_all | solution.py:123
  46.6 0.1 reduce_sum.9
  46.7 3.3 %collective-permute-start.5 = (f32[4,12,128]{2,0,1:T(4,128)S(1)}, f32[4,12,128]{2,0,1:T(4,128)S(1)}, u32[]{:S(2)}, u32[]{:S(2)}) collective-permute-start(f32[4,12,128]{2,0,1:T(4,128)S(1)} %reduce_sum.9), channel_id=1, source_target_pairs={{0,32},{16,48},{32,0},{48,16},{64,96},{80,112},{96,64},{112,80},{1... | collective-permute-start | bytes 73736 | tf_op jit(solution)/shard_map/ppermute | solution.py:71
  50.0 1.2 collective-permute-done.5
  51.2 4.2 %collective-permute-start.6 = (f32[4,12,128]{2,0,1:T(4,128)S(1)}, f32[4,12,128]{2,0,1:T(4,128)S(1)}, u32[]{:S(2)}, u32[]{:S(2)}) collective-permute-start(f32[4,12,128]{2,0,1:T(4,128)S(1)} %add.54), channel_id=1, source_target_pairs={{0,64},{16,80},{32,96},{48,112},{64,0},{80,16},{96,32},{112,48},{1... | collective-permute-start | bytes 73736 | tf_op jit(solution)/shard_map/ppermute | solution.py:71
  55.5 1.2 collective-permute-done.6
  56.7 8.8 %collective-permute-start.7 = (f32[4,12,128]{2,0,1:T(4,128)S(1)}, f32[4,12,128]{2,0,1:T(4,128)S(1)}, u32[]{:S(2)}, u32[]{:S(2)}) collective-permute-start(f32[4,12,128]{2,0,1:T(4,128)S(1)} %add.55), channel_id=1, source_target_pairs={{0,128},{16,144},{32,160},{48,176},{64,192},{80,208},{96,224},{112... | collective-permute-start | bytes 73736 | tf_op jit(solution)/shard_map/ppermute | solution.py:71
  65.5 1.2 collective-permute-done.7
  66.7 15.4 %collective-permute-start.8 = (f32[4,12,128]{2,0,1:T(4,128)S(1)}, f32[4,12,128]{2,0,1:T(4,128)S(1)}, u32[]{:S(2)}, u32[]{:S(2)}) collective-permute-start(f32[4,12,128]{2,0,1:T(4,128)S(1)} %add.56), channel_id=1, source_target_pairs={{0,256},{16,272},{32,288},{48,304},{64,320},{80,336},{96,352},{112... | collective-permute-start | bytes 73736 | tf_op jit(solution)/shard_map/ppermute | solution.py:71
  82.2 1.2 collective-permute-done.8
  83.4 18.2 %collective-permute-start.9 = (f32[4,12,128]{2,0,1:T(4,128)S(1)}, f32[4,12,128]{2,0,1:T(4,128)S(1)}, u32[]{:S(2)}, u32[]{:S(2)}) collective-permute-start(f32[4,12,128]{2,0,1:T(4,128)S(1)} %add.57), channel_id=1, source_target_pairs={{0,768},{16,784},{32,800},{48,816},{64,832},{80,848},{96,864},{112... | collective-permute-start | bytes 73736 | tf_op jit(solution)/shard_map/ppermute | solution.py:75
  101.6 1.4 %collective-permute-done.9 = f32[4,12,128]{2,0,1:T(4,128)S(1)} collective-permute-done((f32[4,12,128]{2,0,1:T(4,128)S(1)}, f32[4,12,128]{2,0,1:T(4,128)S(1)}, u32[]{:S(2)}, u32[]{:S(2)}) %collective-permute-start.9) | collective-permute-done | bytes 24608 | tf_op jit(solution)/shard_map/ppermute | solution.py:75
  103.1 8.3 %collective-permute-start.10 = (f32[4,12,128]{2,0,1:T(4,128)S(1)}, f32[4,12,128]{2,0,1:T(4,128)S(1)}, u32[]{:S(2)}, u32[]{:S(2)}) collective-permute-start(f32[4,12,128]{2,0,1:T(4,128)S(1)} %add.58), channel_id=1, source_target_pairs={{0,16},{16,0},{32,48},{48,32},{64,80},{80,64},{96,112},{112,96},{1... | collective-permute-start | bytes 73736 | tf_op jit(solution)/shard_map/ppermute | solution.py:89
  111.4 0.8 collective-permute-done.10
  112.3 2.2 %collective-permute-start.11 = (f32[2,1,96,128]{3,2,1,0:T(8,128)S(1)}, f32[2,1,96,128]{3,2,1,0:T(8,128)S(1)}, u32[]{:S(2)}, u32[]{:S(2)}) collective-permute-start(f32[2,1,96,128]{3,2,1,0:T(8,128)S(1)} %get-tuple-element.10), channel_id=1, source_target_pairs={{0,1},{1,2},{2,3},{3,4},{4,5},{5,6},{6,7},{7,8},{8,9},{9,10},{10,1... | collective-permute-start | bytes 294920 | tf_op jit(solution)/shard_map/ppermute | solution.py:18
  114.5 1.3 %collective-permute-start.12 = (f32[2,1,96,128]{3,2,1,0:T(8,128)S(1)}, f32[2,1,96,128]{3,2,1,0:T(8,128)S(1)}, u32[]{:S(2)}, u32[]{:S(2)}) collective-permute-start(f32[2,1,96,128]{3,2,1,0:T(8,128)S(1)} %get-tuple-element.11), channel_id=1, source_target_pairs={{1,0},{2,1},{3,2},{4,3},{5,4},{6,5},{7,6},{8,7},{9,8},{10,9},{11,1... | collective-permute-start | bytes 294920 | tf_op jit(solution)/shard_map/ppermute | solution.py:19
  115.8 0.6 fusion.9
  116.4 0.6 slice.130
  117.0 0.6 slice.129
  117.6 0.0 collective-permute-done.11
  117.7 2.2 %collective-permute-done.12 = f32[2,1,96,128]{3,2,1,0:T(8,128)S(1)} collective-permute-done((f32[2,1,96,128]{3,2,1,0:T(8,128)S(1)}, f32[2,1,96,128]{3,2,1,0:T(8,128)S(1)}, u32[]{:S(2)}, u32[]{:S(2)}) %collective-permute-start.12) | collective-permute-done | bytes 98336 | tf_op jit(solution)/shard_map/ppermute | solution.py:19
  120.1 1.6 %fusion = f32[2,2,96,128,1]{3,2,0,1,4:T(8,128)S(1)} fusion(f32[9,128,128,1,1]{2,1,3,4,0:T(8,128)S(1)} %bitcast.160, f32[9,2,2,96,128]{4,3,2,1,0:T(8,128)S(1)} %fusion.12), kind=kOutput, calls=%fused_computation | convolution fusion | flops 679477248 | bytes 2555904 | tf_op jit(solution)/shard_map/tfrwd,tcd->frwc/dot_general | solution.py:129
  121.7 0.8 bitcast_add_fusion.1
  (32 shorter events, 0.5 us)
Async XLA Ops:
  0.6 21.0 %copy-start = (f32[3,3,128,128]{3,2,1,0:T(8,128)S(1)}, f32[3,3,128,128]{3,2,1,0:T(8,128)}, u32[]{:S(2)}) copy-start(f32[3,3,128,128]{3,2,1,0:T(8,128)} %param.5) | copy-start | bytes 1769476
  0.6 20.8 %copy-start.1 = (f32[2,2,96,128]{3,2,1,0:T(8,128)S(1)}, f32[2,2,96,128]{3,2,1,0:T(8,128)}, u32[]{:S(2)}) copy-start(f32[2,2,96,128]{3,2,1,0:T(8,128)} %param.4) | copy-start | bytes 589828
  1.7 18.7 %collective-permute-start = (f32[2,1,96,128]{3,2,1,0:T(8,128)S(1)}, f32[2,1,96,128]{3,2,1,0:T(8,128)S(1)}, u32[]{:S(2)}, u32[]{:S(2)}) collective-permute-start(f32[2,1,96,128]{3,2,1,0:T(8,128)S(1)} %get-tuple-element.14), channel_id=1, source_target_pairs={{0,1},{1,2},{2,3},{3,4},{4,5},{5,6},{6,7},{7,8},{8,9},{9,10},{10,1... | collective-permute-start | bytes 294920 | tf_op jit(solution)/shard_map/ppermute | solution.py:18
  5.7 14.8 %collective-permute-start.1 = (f32[2,1,96,128]{3,2,1,0:T(8,128)S(1)}, f32[2,1,96,128]{3,2,1,0:T(8,128)S(1)}, u32[]{:S(2)}, u32[]{:S(2)}) collective-permute-start(f32[2,1,96,128]{3,2,1,0:T(8,128)S(1)} %get-tuple-element.15), channel_id=1, source_target_pairs={{1,0},{2,1},{3,2},{4,3},{5,4},{6,5},{7,6},{8,7},{9,8},{10,9},{11,1... | collective-permute-start | bytes 294920 | tf_op jit(solution)/shard_map/ppermute | solution.py:19
  7.0 18.3 %collective-permute-start.3 = (f32[2,2,96,128]{3,2,1,0:T(8,128)}, f32[2,2,96,128]{3,2,1,0:T(8,128)S(1)}, u32[]{:S(2)}, u32[]{:S(2)}) collective-permute-start(f32[2,2,96,128]{3,2,1,0:T(8,128)} %param.7), channel_id=1, source_target_pairs={{16,0},{32,16},{48,32},{64,48},{80,64},{96,80},{112,96},{128,112},... | collective-permute-start | bytes 589832 | tf_op jit(solution)/shard_map/ppermute | solution.py:27
  21.6 3.7 %copy-start.2 = (f32[2,2,96,128]{3,2,1,0:T(8,128)S(1)}, f32[2,2,96,128]{3,2,1,0:T(8,128)}, u32[]{:S(2)}) copy-start(f32[2,2,96,128]{3,2,1,0:T(8,128)} %param.7) | copy-start | bytes 589828
  21.7 3.6 %copy-start.3 = (f32[3,128,128]{2,1,0:T(8,128)S(1)}, f32[3,128,128]{2,1,0:T(8,128)}, u32[]{:S(2)}) copy-start(f32[3,128,128]{2,1,0:T(8,128)} %param.6) | copy-start | bytes 589828
  23.3 5.5 %collective-permute-start.2 = (f32[2,2,96,128]{3,2,1,0:T(8,128)S(1)}, f32[2,2,96,128]{3,2,1,0:T(8,128)S(1)}, u32[]{:S(2)}, u32[]{:S(2)}) collective-permute-start(f32[2,2,96,128]{3,2,1,0:T(8,128)S(1)} %get-tuple-element.13), channel_id=1, source_target_pairs={{0,16},{16,32},{32,48},{48,64},{64,80},{80,96},{96,112},{112,128},... | collective-permute-start | bytes 589832 | tf_op jit(solution)/shard_map/ppermute | solution.py:27
  29.9 4.4 %collective-permute-start.4 = (f32[16,4,12,128]{3,1,2,0:T(4,128)S(1)}, f32[16,4,12,128]{3,1,2,0:T(4,128)S(1)}, u32[]{:S(2)}, u32[]{:S(2)}) collective-permute-start(f32[16,4,12,128]{3,1,2,0:T(4,128)S(1)} %bitcast.167), channel_id=1, source_target_pairs={{0,16},{16,0},{32,48},{48,32},{64,80},{80,64},{96,112},{112,96},{1... | collective-permute-start | bytes 1179656 | tf_op jit(solution)/shard_map/ppermute | solution.py:122
  46.7 4.6 %collective-permute-start.5 = (f32[4,12,128]{2,0,1:T(4,128)S(1)}, f32[4,12,128]{2,0,1:T(4,128)S(1)}, u32[]{:S(2)}, u32[]{:S(2)}) collective-permute-start(f32[4,12,128]{2,0,1:T(4,128)S(1)} %reduce_sum.9), channel_id=1, source_target_pairs={{0,32},{16,48},{32,0},{48,16},{64,96},{80,112},{96,64},{112,80},{1... | collective-permute-start | bytes 73736 | tf_op jit(solution)/shard_map/ppermute | solution.py:71
  51.2 5.5 %collective-permute-start.6 = (f32[4,12,128]{2,0,1:T(4,128)S(1)}, f32[4,12,128]{2,0,1:T(4,128)S(1)}, u32[]{:S(2)}, u32[]{:S(2)}) collective-permute-start(f32[4,12,128]{2,0,1:T(4,128)S(1)} %add.54), channel_id=1, source_target_pairs={{0,64},{16,80},{32,96},{48,112},{64,0},{80,16},{96,32},{112,48},{1... | collective-permute-start | bytes 73736 | tf_op jit(solution)/shard_map/ppermute | solution.py:71
  56.7 10.0 %collective-permute-start.7 = (f32[4,12,128]{2,0,1:T(4,128)S(1)}, f32[4,12,128]{2,0,1:T(4,128)S(1)}, u32[]{:S(2)}, u32[]{:S(2)}) collective-permute-start(f32[4,12,128]{2,0,1:T(4,128)S(1)} %add.55), channel_id=1, source_target_pairs={{0,128},{16,144},{32,160},{48,176},{64,192},{80,208},{96,224},{112... | collective-permute-start | bytes 73736 | tf_op jit(solution)/shard_map/ppermute | solution.py:71
  66.7 16.7 %collective-permute-start.8 = (f32[4,12,128]{2,0,1:T(4,128)S(1)}, f32[4,12,128]{2,0,1:T(4,128)S(1)}, u32[]{:S(2)}, u32[]{:S(2)}) collective-permute-start(f32[4,12,128]{2,0,1:T(4,128)S(1)} %add.56), channel_id=1, source_target_pairs={{0,256},{16,272},{32,288},{48,304},{64,320},{80,336},{96,352},{112... | collective-permute-start | bytes 73736 | tf_op jit(solution)/shard_map/ppermute | solution.py:71
  83.4 19.7 %collective-permute-start.9 = (f32[4,12,128]{2,0,1:T(4,128)S(1)}, f32[4,12,128]{2,0,1:T(4,128)S(1)}, u32[]{:S(2)}, u32[]{:S(2)}) collective-permute-start(f32[4,12,128]{2,0,1:T(4,128)S(1)} %add.57), channel_id=1, source_target_pairs={{0,768},{16,784},{32,800},{48,816},{64,832},{80,848},{96,864},{112... | collective-permute-start | bytes 73736 | tf_op jit(solution)/shard_map/ppermute | solution.py:75
  103.1 9.2 %collective-permute-start.10 = (f32[4,12,128]{2,0,1:T(4,128)S(1)}, f32[4,12,128]{2,0,1:T(4,128)S(1)}, u32[]{:S(2)}, u32[]{:S(2)}) collective-permute-start(f32[4,12,128]{2,0,1:T(4,128)S(1)} %add.58), channel_id=1, source_target_pairs={{0,16},{16,0},{32,48},{48,32},{64,80},{80,64},{96,112},{112,96},{1... | collective-permute-start | bytes 73736 | tf_op jit(solution)/shard_map/ppermute | solution.py:89
  112.3 5.4 %collective-permute-start.11 = (f32[2,1,96,128]{3,2,1,0:T(8,128)S(1)}, f32[2,1,96,128]{3,2,1,0:T(8,128)S(1)}, u32[]{:S(2)}, u32[]{:S(2)}) collective-permute-start(f32[2,1,96,128]{3,2,1,0:T(8,128)S(1)} %get-tuple-element.10), channel_id=1, source_target_pairs={{0,1},{1,2},{2,3},{3,4},{4,5},{5,6},{6,7},{7,8},{8,9},{9,10},{10,1... | collective-permute-start | bytes 294920 | tf_op jit(solution)/shard_map/ppermute | solution.py:18
  114.5 5.4 %collective-permute-start.12 = (f32[2,1,96,128]{3,2,1,0:T(8,128)S(1)}, f32[2,1,96,128]{3,2,1,0:T(8,128)S(1)}, u32[]{:S(2)}, u32[]{:S(2)}) collective-permute-start(f32[2,1,96,128]{3,2,1,0:T(8,128)S(1)} %get-tuple-element.11), channel_id=1, source_target_pairs={{1,0},{2,1},{3,2},{4,3},{5,4},{6,5},{7,6},{8,7},{9,8},{10,9},{11,1... | collective-permute-start | bytes 294920 | tf_op jit(solution)/shard_map/ppermute | solution.py:19

commit v8 on v6

--- a/solution.py
+++ b/solution.py
@@ -90,6 +90,18 @@
     return jnp.where(low, jnp.concatenate([value, other]), jnp.concatenate([other, value]))
 
 
+def reduce_terms(terms, nrows):
+    chans, taps = terms.shape[0], terms.shape[1]
+    terms = terms.reshape(nrows, 2, chans // nrows // 2, taps, terms.shape[2])
+    parity = lax.axis_index("frames") % 2
+    keep = lax.dynamic_index_in_dim(terms, parity, axis=1, keepdims=False)
+    give = lax.dynamic_index_in_dim(terms, 1 - parity, axis=1, keepdims=False)
+    nframes_all = lax.axis_size("frames")
+    terms = keep + lax.ppermute(give, "frames", [(i, i ^ 1) for i in range(nframes_all)])
+    terms = lax.all_to_all(terms, "rows", 0, 0, tiled=True).sum(axis=0)
+    return pair_gather(doubling_sum(terms, "frames", 2), "frames")
+
+
 def per_device(images, spatial_weight, temporal_weight, cotangent):
     nframes, strip, width, chans = images.shape
     padded = widen(padded_2(images, (("rows", 1),), 1))
@@ -120,14 +132,10 @@
     temporal_terms = jnp.einsum("kfrwc,frwd->dkc", lagged, cotangent, precision=HIGH)
     nrows = lax.axis_size("rows")
     terms = jnp.concatenate([spatial_terms, temporal_terms], axis=1) * factor
-    terms = terms.reshape(nrows, 2, chans // nrows // 2, terms.shape[1], chans)
-    parity = lax.axis_index("frames") % 2
-    keep = lax.dynamic_index_in_dim(terms, parity, axis=1, keepdims=False)
-    give = lax.dynamic_index_in_dim(terms, 1 - parity, axis=1, keepdims=False)
-    nframes_all = lax.axis_size("frames")
-    terms = keep + lax.ppermute(give, "frames", [(i, i ^ 1) for i in range(nframes_all)])
-    terms = lax.all_to_all(terms, "rows", 0, 0, tiled=True).sum(axis=0)
-    summed = pair_gather(doubling_sum(terms, "frames", 2), "frames")
+    half = terms.shape[1] // 2
+    summed = jnp.concatenate(
+        [reduce_terms(terms[:, :half], nrows), reduce_terms(terms[:, half:], nrows)], axis=1
+    )
     summed = jnp.transpose(summed, (1, 2, 0))
     grad_spatial = summed[:9].reshape(3, 3, chans, summed.shape[2])
     grad_temporal = summed[9:]

time: 118 us -> 144 us (1.22)
  starting transfers between devices: 86.3 us -> 113 us
  waiting for transfers between devices: 16.5 us -> 10.9 us
  other arithmetic: 4.25 us -> 6.57 us
  local copies, waits for them, and re-layouts: 2.83 us -> 4.91 us
    ppermute x4 -> x8, starting transfers between devices: 29.9 us -> 42.7 us  [doubling_sum(): value = value + lax.ppermute(value, axis, pairs)]
    ppermute x4 -> x8, waiting for transfers between devices: 5.31 us -> 0.02 us  [doubling_sum(): value = value + lax.ppermute(value, axis, pairs)]
    ppermute x1 -> x2, starting transfers between devices: 8.94 us -> 13.2 us  [pair_gather(): other = lax.ppermute(value, axis, [(i, i ^ 1) for i in range(count)])]
    all_to_all x1 -> x2, starting transfers between devices: 4.21 us -> 8.35 us  [reduce_terms(): terms = lax.all_to_all(terms, 'rows', 0, 0, tiled=True).sum(axis=0)]
    ppermute x1 -> x2, starting transfers between devices: 14.5 us -> 17.9 us  [doubling_sum(): return value + lax.ppermute(value, axis, pairs)]
    ppermute x1 -> x2, starting transfers between devices: 2.69 us -> 4.62 us  [reduce_terms(): lax.ppermute(give, 'frames', [(i, i ^ 1) for i in range(nframes_all)])]
    add x1 -> x2, other arithmetic: 0.88 us -> 2.49 us  [reduce_terms(): keep + lax.ppermute(give, 'frames', [(i, i ^ 1) for i in range(nframes_al...]
    all_to_all x1 -> x2, waiting for transfers between devices: 9.51 us -> 10.1 us  [reduce_terms(): terms = lax.all_to_all(terms, 'rows', 0, 0, tiled=True).sum(axis=0)]
  transfers between devices with their start and end apart: 14 -> 22, of which waited for: 6 -> 3; matrix products, arithmetic and copies ran while one was open for 8% -> 10% of each run, Pallas kernels for 0% -> 0%
where the time goes in v8:
time: 144 us; the launch traced here: 143 us
  starting transfers between devices  113 us (78%)
  waiting for transfers between devices  10.9 us (8%)
  other arithmetic  6.57 us (5%)
  matrix products  6.39 us (4%)
  local copies, waits for them, and re-layouts  4.91 us (3%)
  between operations  1.47 us (1%)
    ppermute x8, starting transfers between devices, doubling_sum(): value = value + lax.ppermute(value, axis, pairs)  42.7 us
    ppermute x2, starting transfers between devices, doubling_sum(): return value + lax.ppermute(value, axis, pairs)  17.9 us
    ppermute x2, starting transfers between devices, passed_along(): return lax.ppermute(value, axis, pairs)  15.3 us
    ppermute x2, starting transfers between devices, pair_gather(): other = lax.ppermute(value, axis, [(i, i ^ 1) for i in range(count)])  13.2 us
    all_to_all x2, waiting for transfers between devices, reduce_terms(): terms = lax.all_to_all(terms, 'rows', 0, 0, tiled=True).sum(axis=0)  10.1 us
    all_to_all x2, starting transfers between devices, reduce_terms(): terms = lax.all_to_all(terms, 'rows', 0, 0, tiled=True).sum(axis=0)  8.35 us
    ppermute x2, starting transfers between devices, padded_2(): before = lax.ppermute(last, axis, up)  8.22 us
    ppermute x2, starting transfers between devices, reduce_terms(): lax.ppermute(give, 'frames', [(i, i ^ 1) for i in range(nframes_all)])  4.62 us
  transfers between devices with their start and end apart: 22, of which 3 were waited for; matrix products, arithmetic and copies ran while one was open for 10% of the time, Pallas kernels for 0%

profile of v8, /device:TPU:1, one launch (start us, length us, event | category | flops | bytes accessed | tf_op | source)
XLA Modules:
  0.0 143.2 jit_solution(7451734302475558829)
XLA Ops:
  0.6 0.0 copy-start
  0.7 1.0 fusion.43
  1.7 4.0 %collective-permute-start = (f32[2,1,96,128]{3,2,1,0:T(8,128)S(1)}, f32[2,1,96,128]{3,2,1,0:T(8,128)S(1)}, u32[]{:S(2)}, u32[]{:S(2)}) collective-permute-start(f32[2,1,96,128]{3,2,1,0:T(8,128)S(1)} %get-tuple-element.14), channel_id=1, source_target_pairs={{0,1},{1,2},{2,3},{3,4},{4,5},{5,6},{6,7},{7,8},{8,9},{9,10},{10,1... | collective-permute-start | bytes 294920 | tf_op jit(solution)/shard_map/ppermute | solution.py:18
  5.7 1.3 collective-permute-start.1
  7.0 13.4 %collective-permute-start.3 = (f32[2,2,96,128]{3,2,1,0:T(8,128)}, f32[2,2,96,128]{3,2,1,0:T(8,128)S(1)}, u32[]{:S(2)}, u32[]{:S(2)}) collective-permute-start(f32[2,2,96,128]{3,2,1,0:T(8,128)} %param.7), channel_id=1, source_target_pairs={{16,0},{32,16},{48,32},{64,48},{80,64},{96,80},{112,96},{128,112},... | collective-permute-start | bytes 589832 | tf_op jit(solution)/shard_map/ppermute | solution.py:27
  20.4 1.0 select_maximum_fusion.2
  21.7 1.6 %convolution_bitcast_fusion.3 = f32[2,2,96,128]{3,2,1,0:T(8,128)S(1)} fusion(f32[9,2,2,96,128]{4,3,0,2,1:T(8,128)S(1)} %fusion.24, f32[9,128,128,1,1]{2,1,0,4,3:T(8,128)S(1)} %bitcast.167), kind=kOutput, calls=%fused_computation.6 | convolution fusion | flops 679477248 | bytes 2555904 | tf_op jit(solution)/shard_map/tfrwc,tcd->frwd/dot_general | solution.py:42
  23.3 0.1 fusion.40
  23.3 1.9 %collective-permute-start.2 = (f32[2,2,96,128]{3,2,1,0:T(8,128)S(1)}, f32[2,2,96,128]{3,2,1,0:T(8,128)S(1)}, u32[]{:S(2)}, u32[]{:S(2)}) collective-permute-start(f32[2,2,96,128]{3,2,1,0:T(8,128)S(1)} %get-tuple-element.13), channel_id=1, source_target_pairs={{0,16},{16,32},{32,48},{48,64},{64,80},{80,96},{96,112},{112,128},... | collective-permute-start | bytes 589832 | tf_op jit(solution)/shard_map/ppermute | solution.py:27
  25.3 0.6 fusion.3
  26.0 4.3 %collective-permute-start.4 = (f32[2,1,96,128]{3,2,1,0:T(8,128)S(1)}, f32[2,1,96,128]{3,2,1,0:T(8,128)S(1)}, u32[]{:S(2)}, u32[]{:S(2)}) collective-permute-start(f32[2,1,96,128]{3,2,1,0:T(8,128)S(1)} %get-tuple-element.10), channel_id=1, source_target_pairs={{0,1},{1,2},{2,3},{3,4},{4,5},{5,6},{6,7},{7,8},{8,9},{9,10},{10,1... | collective-permute-start | bytes 294920 | tf_op jit(solution)/shard_map/ppermute | solution.py:18
  30.3 1.3 collective-permute-start.5
  31.6 1.3 convolution_bitcast_fusion
  32.9 0.6 copy-done.5
  33.6 0.1 copy-done.7
  33.6 0.6 convolution_bitcast_fusion.1
  34.3 0.1 maximum_multiply_fusion
  34.3 0.1 fusion.41
  34.4 0.8 constant_dynamic-slice_fusion.1
  35.2 0.7 copy.59
  36.0 2.7 %collective-permute-start.6 = (f32[16,4,6,128]{3,1,2,0:T(4,128)S(1)}, f32[16,4,6,128]{3,1,2,0:T(4,128)S(1)}, u32[]{:S(2)}, u32[]{:S(2)}) collective-permute-start(f32[16,4,6,128]{3,1,2,0:T(4,128)S(1)} %bitcast.173), channel_id=1, source_target_pairs={{0,16},{16,0},{32,48},{48,32},{64,80},{80,64},{96,112},{112,96},{1... | collective-permute-start | bytes 589832 | tf_op jit(solution)/shard_map/ppermute | solution.py:100
  38.7 1.9 %collective-permute-start.13 = (f32[16,4,6,128]{3,1,2,0:T(4,128)}, f32[16,4,6,128]{3,1,2,0:T(4,128)}, u32[]{:S(2)}, u32[]{:S(2)}) collective-permute-start(f32[16,4,6,128]{3,1,2,0:T(4,128)} %bitcast.164), channel_id=1, source_target_pairs={{0,16},{16,0},{32,48},{48,32},{64,80},{80,64},{96,112},{112,96},{1... | collective-permute-start | bytes 589832 | tf_op jit(solution)/shard_map/ppermute | solution.py:100
  40.9 0.7 bitcast_add_fusion.1
  41.6 4.2 %all-to-all-start = ((f32[16,4,6,128]{3,1,2,0:T(4,128)}), f32[16,4,6,128]{3,1,2,0:T(4,128)}, u32[]{:S(2)}, u32[]{:S(2)}) async-start(f32[16,4,6,128]{3,1,2,0:T(4,128)} %bitcast_add_fusion.1), calls=%async_computation | async-start | bytes 393216 | tf_op jit(solution)/shard_map/all_to_all | solution.py:101
  45.8 1.8 %bitcast_add_fusion = f32[16,4,6,128]{3,1,2,0:T(4,128)} fusion(f32[16,4,6,128]{3,1,2,0:T(4,128)} %collective-permute-done.13, f32[16,1,4,6,128]{4,2,1,0,3:T(4,128)} %get-tuple-element.8), kind=kLoop, calls=%fused_computation.68 | loop fusion | flops 49152 | bytes 589824 | tf_op jit(solution)/shard_map/add | solution.py:100
  47.5 5.8 %all-to-all-done = f32[16,4,6,128]{3,1,2,0:T(4,128)} async-done(((f32[16,4,6,128]{3,1,2,0:T(4,128)}), f32[16,4,6,128]{3,1,2,0:T(4,128)}, u32[]{:S(2)}, u32[]{:S(2)}) %all-to-all-start) | async-done | bytes 196640 | tf_op jit(solution)/shard_map/all_to_all | solution.py:101
  53.4 4.2 %all-to-all-start.1 = ((f32[16,4,6,128]{3,1,2,0:T(4,128)}), f32[16,4,6,128]{3,1,2,0:T(4,128)}, u32[]{:S(2)}, u32[]{:S(2)}) async-start(f32[16,4,6,128]{3,1,2,0:T(4,128)} %bitcast_add_fusion), calls=%async_computation.1 | async-start | bytes 393216 | tf_op jit(solution)/shard_map/all_to_all | solution.py:101
  57.5 1.0 reduce_sum.18
  58.5 1.9 %collective-permute-start.7 = (f32[4,6,128]{2,0,1:T(4,128)S(1)}, f32[4,6,128]{2,0,1:T(4,128)S(1)}, u32[]{:S(2)}, u32[]{:S(2)}) collective-permute-start(f32[4,6,128]{2,0,1:T(4,128)S(1)} %reduce_sum.18), channel_id=1, source_target_pairs={{0,32},{16,48},{32,0},{48,16},{64,96},{80,112},{96,64},{112,80},{1... | collective-permute-start | bytes 36872 | tf_op jit(solution)/shard_map/ppermute | solution.py:71
  60.5 4.3 %all-to-all-done.1 = f32[16,4,6,128]{3,1,2,0:T(4,128)} async-done(((f32[16,4,6,128]{3,1,2,0:T(4,128)}), f32[16,4,6,128]{3,1,2,0:T(4,128)}, u32[]{:S(2)}, u32[]{:S(2)}) %all-to-all-start.1) | async-done | bytes 196640 | tf_op jit(solution)/shard_map/all_to_all | solution.py:101
  64.8 1.0 reduce_sum.19
  65.7 1.9 %collective-permute-start.14 = (f32[4,6,128]{2,0,1:T(4,128)S(1)}, f32[4,6,128]{2,0,1:T(4,128)S(1)}, u32[]{:S(2)}, u32[]{:S(2)}) collective-permute-start(f32[4,6,128]{2,0,1:T(4,128)S(1)} %reduce_sum.19), channel_id=1, source_target_pairs={{0,32},{16,48},{32,0},{48,16},{64,96},{80,112},{96,64},{112,80},{1... | collective-permute-start | bytes 36872 | tf_op jit(solution)/shard_map/ppermute | solution.py:71
  67.7 6.0 %collective-permute-start.8 = (f32[4,6,128]{2,0,1:T(4,128)S(1)}, f32[4,6,128]{2,0,1:T(4,128)S(1)}, u32[]{:S(2)}, u32[]{:S(2)}) collective-permute-start(f32[4,6,128]{2,0,1:T(4,128)S(1)} %add.77), channel_id=1, source_target_pairs={{0,64},{16,80},{32,96},{48,112},{64,0},{80,16},{96,32},{112,48},{1... | collective-permute-start | bytes 36872 | tf_op jit(solution)/shard_map/ppermute | solution.py:71
  73.8 1.9 %collective-permute-start.15 = (f32[4,6,128]{2,0,1:T(4,128)S(1)}, f32[4,6,128]{2,0,1:T(4,128)S(1)}, u32[]{:S(2)}, u32[]{:S(2)}) collective-permute-start(f32[4,6,128]{2,0,1:T(4,128)S(1)} %add.83), channel_id=1, source_target_pairs={{0,64},{16,80},{32,96},{48,112},{64,0},{80,16},{96,32},{112,48},{1... | collective-permute-start | bytes 36872 | tf_op jit(solution)/shard_map/ppermute | solution.py:71
  75.8 8.8 %collective-permute-start.9 = (f32[4,6,128]{2,0,1:T(4,128)S(1)}, f32[4,6,128]{2,0,1:T(4,128)S(1)}, u32[]{:S(2)}, u32[]{:S(2)}) collective-permute-start(f32[4,6,128]{2,0,1:T(4,128)S(1)} %add.78), channel_id=1, source_target_pairs={{0,128},{16,144},{32,160},{48,176},{64,192},{80,208},{96,224},{112... | collective-permute-start | bytes 36872 | tf_op jit(solution)/shard_map/ppermute | solution.py:71
  84.6 3.4 %collective-permute-start.16 = (f32[4,6,128]{2,0,1:T(4,128)S(1)}, f32[4,6,128]{2,0,1:T(4,128)S(1)}, u32[]{:S(2)}, u32[]{:S(2)}) collective-permute-start(f32[4,6,128]{2,0,1:T(4,128)S(1)} %add.84), channel_id=1, source_target_pairs={{0,128},{16,144},{32,160},{48,176},{64,192},{80,208},{96,224},{112... | collective-permute-start | bytes 36872 | tf_op jit(solution)/shard_map/ppermute | solution.py:71
  88.1 15.4 %collective-permute-start.10 = (f32[4,6,128]{2,0,1:T(4,128)S(1)}, f32[4,6,128]{2,0,1:T(4,128)S(1)}, u32[]{:S(2)}, u32[]{:S(2)}) collective-permute-start(f32[4,6,128]{2,0,1:T(4,128)S(1)} %add.79), channel_id=1, source_target_pairs={{0,256},{16,272},{32,288},{48,304},{64,320},{80,336},{96,352},{112... | collective-permute-start | bytes 36872 | tf_op jit(solution)/shard_map/ppermute | solution.py:71
  103.5 1.6 %fusion = f32[2,2,96,128,1]{3,2,0,1,4:T(8,128)S(1)} fusion(f32[9,128,128,1,1]{2,1,3,4,0:T(8,128)S(1)} %bitcast.166, f32[9,2,2,96,128]{4,3,2,1,0:T(8,128)S(1)} %fusion.12), kind=kOutput, calls=%fused_computation | convolution fusion | flops 679477248 | bytes 2555904 | tf_op jit(solution)/shard_map/tfrwd,tcd->frwc/dot_general | solution.py:123
  105.1 3.3 %collective-permute-start.17 = (f32[4,6,128]{2,0,1:T(4,128)S(1)}, f32[4,6,128]{2,0,1:T(4,128)S(1)}, u32[]{:S(2)}, u32[]{:S(2)}) collective-permute-start(f32[4,6,128]{2,0,1:T(4,128)S(1)} %add.85), channel_id=1, source_target_pairs={{0,256},{16,272},{32,288},{48,304},{64,320},{80,336},{96,352},{112... | collective-permute-start | bytes 36872 | tf_op jit(solution)/shard_map/ppermute | solution.py:71
  108.5 11.3 %collective-permute-start.11 = (f32[4,6,128]{2,0,1:T(4,128)S(1)}, f32[4,6,128]{2,0,1:T(4,128)S(1)}, u32[]{:S(2)}, u32[]{:S(2)}) collective-permute-start(f32[4,6,128]{2,0,1:T(4,128)S(1)} %add.80), channel_id=1, source_target_pairs={{0,768},{16,784},{32,800},{48,816},{64,832},{80,848},{96,864},{112... | collective-permute-start | bytes 36872 | tf_op jit(solution)/shard_map/ppermute | solution.py:75
  119.8 0.6 fusion.9
  120.5 6.6 %collective-permute-start.18 = (f32[4,6,128]{2,0,1:T(4,128)S(1)}, f32[4,6,128]{2,0,1:T(4,128)S(1)}, u32[]{:S(2)}, u32[]{:S(2)}) collective-permute-start(f32[4,6,128]{2,0,1:T(4,128)S(1)} %add.86), channel_id=1, source_target_pairs={{0,768},{16,784},{32,800},{48,816},{64,832},{80,848},{96,864},{112... | collective-permute-start | bytes 36872 | tf_op jit(solution)/shard_map/ppermute | solution.py:75
  127.1 7.2 %collective-permute-start.12 = (f32[4,6,128]{2,0,1:T(4,128)S(1)}, f32[4,6,128]{2,0,1:T(4,128)S(1)}, u32[]{:S(2)}, u32[]{:S(2)}) collective-permute-start(f32[4,6,128]{2,0,1:T(4,128)S(1)} %add.81), channel_id=1, source_target_pairs={{0,16},{16,0},{32,48},{48,32},{64,80},{80,64},{96,112},{112,96},{1... | collective-permute-start | bytes 36872 | tf_op jit(solution)/shard_map/ppermute | solution.py:89
  134.3 0.8 bitcast_add_fusion.2
  135.1 6.0 %collective-permute-start.19 = (f32[4,6,128]{2,0,1:T(4,128)S(1)}, f32[4,6,128]{2,0,1:T(4,128)S(1)}, u32[]{:S(2)}, u32[]{:S(2)}) collective-permute-start(f32[4,6,128]{2,0,1:T(4,128)S(1)} %add.87), channel_id=1, source_target_pairs={{0,16},{16,0},{32,48},{48,32},{64,80},{80,64},{96,112},{112,96},{1... | collective-permute-start | bytes 36872 | tf_op jit(solution)/shard_map/ppermute | solution.py:89
  141.2 0.8 collective-permute-done.19
  142.0 0.6 slice.142
  142.6 0.6 slice.141
  (74 shorter events, 0.6 us)
Async XLA Ops:
  0.6 21.0 %copy-start = (f32[3,3,128,128]{3,2,1,0:T(8,128)S(1)}, f32[3,3,128,128]{3,2,1,0:T(8,128)}, u32[]{:S(2)}) copy-start(f32[3,3,128,128]{3,2,1,0:T(8,128)} %param.5) | copy-start | bytes 1769476
  0.6 20.8 %copy-start.1 = (f32[2,2,96,128]{3,2,1,0:T(8,128)S(1)}, f32[2,2,96,128]{3,2,1,0:T(8,128)}, u32[]{:S(2)}) copy-start(f32[2,2,96,128]{3,2,1,0:T(8,128)} %param.4) | copy-start | bytes 589828
  1.7 18.7 %collective-permute-start = (f32[2,1,96,128]{3,2,1,0:T(8,128)S(1)}, f32[2,1,96,128]{3,2,1,0:T(8,128)S(1)}, u32[]{:S(2)}, u32[]{:S(2)}) collective-permute-start(f32[2,1,96,128]{3,2,1,0:T(8,128)S(1)} %get-tuple-element.14), channel_id=1, source_target_pairs={{0,1},{1,2},{2,3},{3,4},{4,5},{5,6},{6,7},{7,8},{8,9},{9,10},{10,1... | collective-permute-start | bytes 294920 | tf_op jit(solution)/shard_map/ppermute | solution.py:18
  5.7 14.8 %collective-permute-start.1 = (f32[2,1,96,128]{3,2,1,0:T(8,128)S(1)}, f32[2,1,96,128]{3,2,1,0:T(8,128)S(1)}, u32[]{:S(2)}, u32[]{:S(2)}) collective-permute-start(f32[2,1,96,128]{3,2,1,0:T(8,128)S(1)} %get-tuple-element.15), channel_id=1, source_target_pairs={{1,0},{2,1},{3,2},{4,3},{5,4},{6,5},{7,6},{8,7},{9,8},{10,9},{11,1... | collective-permute-start | bytes 294920 | tf_op jit(solution)/shard_map/ppermute | solution.py:19
  7.0 18.3 %collective-permute-start.3 = (f32[2,2,96,128]{3,2,1,0:T(8,128)}, f32[2,2,96,128]{3,2,1,0:T(8,128)S(1)}, u32[]{:S(2)}, u32[]{:S(2)}) collective-permute-start(f32[2,2,96,128]{3,2,1,0:T(8,128)} %param.7), channel_id=1, source_target_pairs={{16,0},{32,16},{48,32},{64,48},{80,64},{96,80},{112,96},{128,112},... | collective-permute-start | bytes 589832 | tf_op jit(solution)/shard_map/ppermute | solution.py:27
  21.6 3.7 %copy-start.2 = (f32[2,2,96,128]{3,2,1,0:T(8,128)S(1)}, f32[2,2,96,128]{3,2,1,0:T(8,128)}, u32[]{:S(2)}) copy-start(f32[2,2,96,128]{3,2,1,0:T(8,128)} %param.7) | copy-start | bytes 589828
  21.7 3.7 %copy-start.9 = (f32[3,128,128]{2,1,0:T(8,128)S(1)}, f32[3,128,128]{2,1,0:T(8,128)}, u32[]{:S(2)}) copy-start(f32[3,128,128]{2,1,0:T(8,128)} %param.6) | copy-start | bytes 589828
  23.3 9.6 %copy-start.3 = (f32[1,2,2,96,128]{4,3,2,1,0:T(8,128)}, f32[1,2,2,96,128]{4,3,2,1,0:T(8,128)S(1)}, u32[]{:S(2)}) copy-start(f32[1,2,2,96,128]{4,3,2,1,0:T(8,128)S(1)} %get-tuple-element.12) | copy-start | bytes 589828
  23.3 9.5 %collective-permute-start.2 = (f32[2,2,96,128]{3,2,1,0:T(8,128)S(1)}, f32[2,2,96,128]{3,2,1,0:T(8,128)S(1)}, u32[]{:S(2)}, u32[]{:S(2)}) collective-permute-start(f32[2,2,96,128]{3,2,1,0:T(8,128)S(1)} %get-tuple-element.13), channel_id=1, source_target_pairs={{0,16},{16,32},{32,48},{48,64},{64,80},{80,96},{96,112},{112,128},... | collective-permute-start | bytes 589832 | tf_op jit(solution)/shard_map/ppermute | solution.py:27
  26.0 14.6 %collective-permute-start.4 = (f32[2,1,96,128]{3,2,1,0:T(8,128)S(1)}, f32[2,1,96,128]{3,2,1,0:T(8,128)S(1)}, u32[]{:S(2)}, u32[]{:S(2)}) collective-permute-start(f32[2,1,96,128]{3,2,1,0:T(8,128)S(1)} %get-tuple-element.10), channel_id=1, source_target_pairs={{0,1},{1,2},{2,3},{3,4},{4,5},{5,6},{6,7},{7,8},{8,9},{9,10},{10,1... | collective-permute-start | bytes 294920 | tf_op jit(solution)/shard_map/ppermute | solution.py:18
  30.3 10.4 %collective-permute-start.5 = (f32[2,1,96,128]{3,2,1,0:T(8,128)S(1)}, f32[2,1,96,128]{3,2,1,0:T(8,128)S(1)}, u32[]{:S(2)}, u32[]{:S(2)}) collective-permute-start(f32[2,1,96,128]{3,2,1,0:T(8,128)S(1)} %get-tuple-element.11), channel_id=1, source_target_pairs={{1,0},{2,1},{3,2},{4,3},{5,4},{6,5},{7,6},{8,7},{9,8},{10,9},{11,1... | collective-permute-start | bytes 294920 | tf_op jit(solution)/shard_map/ppermute | solution.py:19
  32.9 0.7 copy-start.5
  32.9 0.7 copy-start.7
  36.0 4.9 %collective-permute-start.6 = (f32[16,4,6,128]{3,1,2,0:T(4,128)S(1)}, f32[16,4,6,128]{3,1,2,0:T(4,128)S(1)}, u32[]{:S(2)}, u32[]{:S(2)}) collective-permute-start(f32[16,4,6,128]{3,1,2,0:T(4,128)S(1)} %bitcast.173), channel_id=1, source_target_pairs={{0,16},{16,0},{32,48},{48,32},{64,80},{80,64},{96,112},{112,96},{1... | collective-permute-start | bytes 589832 | tf_op jit(solution)/shard_map/ppermute | solution.py:100
  38.7 7.1 %collective-permute-start.13 = (f32[16,4,6,128]{3,1,2,0:T(4,128)}, f32[16,4,6,128]{3,1,2,0:T(4,128)}, u32[]{:S(2)}, u32[]{:S(2)}) collective-permute-start(f32[16,4,6,128]{3,1,2,0:T(4,128)} %bitcast.164), channel_id=1, source_target_pairs={{0,16},{16,0},{32,48},{48,32},{64,80},{80,64},{96,112},{112,96},{1... | collective-permute-start | bytes 589832 | tf_op jit(solution)/shard_map/ppermute | solution.py:100
  41.6 11.8 %all-to-all-start = ((f32[16,4,6,128]{3,1,2,0:T(4,128)}), f32[16,4,6,128]{3,1,2,0:T(4,128)}, u32[]{:S(2)}, u32[]{:S(2)}) async-start(f32[16,4,6,128]{3,1,2,0:T(4,128)} %bitcast_add_fusion.1), calls=%async_computation | async-start | bytes 393216 | tf_op jit(solution)/shard_map/all_to_all | solution.py:101
  53.4 11.4 %all-to-all-start.1 = ((f32[16,4,6,128]{3,1,2,0:T(4,128)}), f32[16,4,6,128]{3,1,2,0:T(4,128)}, u32[]{:S(2)}, u32[]{:S(2)}) async-start(f32[16,4,6,128]{3,1,2,0:T(4,128)} %bitcast_add_fusion), calls=%async_computation.1 | async-start | bytes 393216 | tf_op jit(solution)/shard_map/all_to_all | solution.py:101
  58.5 9.1 %collective-permute-start.7 = (f32[4,6,128]{2,0,1:T(4,128)S(1)}, f32[4,6,128]{2,0,1:T(4,128)S(1)}, u32[]{:S(2)}, u32[]{:S(2)}) collective-permute-start(f32[4,6,128]{2,0,1:T(4,128)S(1)} %reduce_sum.18), channel_id=1, source_target_pairs={{0,32},{16,48},{32,0},{48,16},{64,96},{80,112},{96,64},{112,80},{1... | collective-permute-start | bytes 36872 | tf_op jit(solution)/shard_map/ppermute | solution.py:71
  65.7 8.1 %collective-permute-start.14 = (f32[4,6,128]{2,0,1:T(4,128)S(1)}, f32[4,6,128]{2,0,1:T(4,128)S(1)}, u32[]{:S(2)}, u32[]{:S(2)}) collective-permute-start(f32[4,6,128]{2,0,1:T(4,128)S(1)} %reduce_sum.19), channel_id=1, source_target_pairs={{0,32},{16,48},{32,0},{48,16},{64,96},{80,112},{96,64},{112,80},{1... | collective-permute-start | bytes 36872 | tf_op jit(solution)/shard_map/ppermute | solution.py:71
  67.7 52.1 %copy-start.4 = (f32[1,2,2,96,128]{4,3,2,1,0:T(8,128)S(1)}, f32[1,2,2,96,128]{4,3,2,1,0:T(8,128)}, u32[]{:S(2)}) copy-start(f32[1,2,2,96,128]{4,3,2,1,0:T(8,128)} %copy-done.3) | copy-start | bytes 589828
  67.7 52.1 %copy-start.6 = (f32[2,2,96,128]{3,2,1,0:T(8,128)S(1)}, f32[2,2,96,128]{3,2,1,0:T(8,128)}, u32[]{:S(2)}) copy-start(f32[2,2,96,128]{3,2,1,0:T(8,128)} %copy-done.5) | copy-start | bytes 589828
  67.7 52.1 %copy-start.8 = (f32[1,2,2,96,128]{4,3,2,1,0:T(8,128)S(1)}, f32[1,2,2,96,128]{4,3,2,1,0:T(8,128)}, u32[]{:S(2)}) copy-start(f32[1,2,2,96,128]{4,3,2,1,0:T(8,128)} %copy-done.7) | copy-start | bytes 589828
  67.7 52.1 %copy-start.10 = (f32[3,128,128]{2,1,0:T(8,128)S(1)}, f32[3,128,128]{2,1,0:T(8,128)}, u32[]{:S(2)}) copy-start(f32[3,128,128]{2,1,0:T(8,128)} %param.6) | copy-start | bytes 589828
  67.7 8.0 %collective-permute-start.8 = (f32[4,6,128]{2,0,1:T(4,128)S(1)}, f32[4,6,128]{2,0,1:T(4,128)S(1)}, u32[]{:S(2)}, u32[]{:S(2)}) collective-permute-start(f32[4,6,128]{2,0,1:T(4,128)S(1)} %add.77), channel_id=1, source_target_pairs={{0,64},{16,80},{32,96},{48,112},{64,0},{80,16},{96,32},{112,48},{1... | collective-permute-start | bytes 36872 | tf_op jit(solution)/shard_map/ppermute | solution.py:71
  73.8 10.8 %collective-permute-start.15 = (f32[4,6,128]{2,0,1:T(4,128)S(1)}, f32[4,6,128]{2,0,1:T(4,128)S(1)}, u32[]{:S(2)}, u32[]{:S(2)}) collective-permute-start(f32[4,6,128]{2,0,1:T(4,128)S(1)} %add.83), channel_id=1, source_target_pairs={{0,64},{16,80},{32,96},{48,112},{64,0},{80,16},{96,32},{112,48},{1... | collective-permute-start | bytes 36872 | tf_op jit(solution)/shard_map/ppermute | solution.py:71
  75.8 12.3 %collective-permute-start.9 = (f32[4,6,128]{2,0,1:T(4,128)S(1)}, f32[4,6,128]{2,0,1:T(4,128)S(1)}, u32[]{:S(2)}, u32[]{:S(2)}) collective-permute-start(f32[4,6,128]{2,0,1:T(4,128)S(1)} %add.78), channel_id=1, source_target_pairs={{0,128},{16,144},{32,160},{48,176},{64,192},{80,208},{96,224},{112... | collective-permute-start | bytes 36872 | tf_op jit(solution)/shard_map/ppermute | solution.py:71
  84.6 20.5 %collective-permute-start.16 = (f32[4,6,128]{2,0,1:T(4,128)S(1)}, f32[4,6,128]{2,0,1:T(4,128)S(1)}, u32[]{:S(2)}, u32[]{:S(2)}) collective-permute-start(f32[4,6,128]{2,0,1:T(4,128)S(1)} %add.84), channel_id=1, source_target_pairs={{0,128},{16,144},{32,160},{48,176},{64,192},{80,208},{96,224},{112... | collective-permute-start | bytes 36872 | tf_op jit(solution)/shard_map/ppermute | solution.py:71
  88.1 20.4 %collective-permute-start.10 = (f32[4,6,128]{2,0,1:T(4,128)S(1)}, f32[4,6,128]{2,0,1:T(4,128)S(1)}, u32[]{:S(2)}, u32[]{:S(2)}) collective-permute-start(f32[4,6,128]{2,0,1:T(4,128)S(1)} %add.79), channel_id=1, source_target_pairs={{0,256},{16,272},{32,288},{48,304},{64,320},{80,336},{96,352},{112... | collective-permute-start | bytes 36872 | tf_op jit(solution)/shard_map/ppermute | solution.py:71
  105.1 15.3 %collective-permute-start.17 = (f32[4,6,128]{2,0,1:T(4,128)S(1)}, f32[4,6,128]{2,0,1:T(4,128)S(1)}, u32[]{:S(2)}, u32[]{:S(2)}) collective-permute-start(f32[4,6,128]{2,0,1:T(4,128)S(1)} %add.85), channel_id=1, source_target_pairs={{0,256},{16,272},{32,288},{48,304},{64,320},{80,336},{96,352},{112... | collective-permute-start | bytes 36872 | tf_op jit(solution)/shard_map/ppermute | solution.py:71
  108.5 18.6 %collective-permute-start.11 = (f32[4,6,128]{2,0,1:T(4,128)S(1)}, f32[4,6,128]{2,0,1:T(4,128)S(1)}, u32[]{:S(2)}, u32[]{:S(2)}) collective-permute-start(f32[4,6,128]{2,0,1:T(4,128)S(1)} %add.80), channel_id=1, source_target_pairs={{0,768},{16,784},{32,800},{48,816},{64,832},{80,848},{96,864},{112... | collective-permute-start | bytes 36872 | tf_op jit(solution)/shard_map/ppermute | solution.py:75
  120.5 14.6 %collective-permute-start.18 = (f32[4,6,128]{2,0,1:T(4,128)S(1)}, f32[4,6,128]{2,0,1:T(4,128)S(1)}, u32[]{:S(2)}, u32[]{:S(2)}) collective-permute-start(f32[4,6,128]{2,0,1:T(4,128)S(1)} %add.86), channel_id=1, source_target_pairs={{0,768},{16,784},{32,800},{48,816},{64,832},{80,848},{96,864},{112... | collective-permute-start | bytes 36872 | tf_op jit(solution)/shard_map/ppermute | solution.py:75
  127.1 14.0 %collective-permute-start.12 = (f32[4,6,128]{2,0,1:T(4,128)S(1)}, f32[4,6,128]{2,0,1:T(4,128)S(1)}, u32[]{:S(2)}, u32[]{:S(2)}) collective-permute-start(f32[4,6,128]{2,0,1:T(4,128)S(1)} %add.81), channel_id=1, source_target_pairs={{0,16},{16,0},{32,48},{48,32},{64,80},{80,64},{96,112},{112,96},{1... | collective-permute-start | bytes 36872 | tf_op jit(solution)/shard_map/ppermute | solution.py:89
  135.1 6.8 %collective-permute-start.19 = (f32[4,6,128]{2,0,1:T(4,128)S(1)}, f32[4,6,128]{2,0,1:T(4,128)S(1)}, u32[]{:S(2)}, u32[]{:S(2)}) collective-permute-start(f32[4,6,128]{2,0,1:T(4,128)S(1)} %add.87), channel_id=1, source_target_pairs={{0,16},{16,0},{32,48},{48,32},{64,80},{80,64},{96,112},{112,96},{1... | collective-permute-start | bytes 36872 | tf_op jit(solution)/shard_map/ppermute | solution.py:89

commit v9 on v6

--- a/solution.py
+++ b/solution.py
@@ -5,7 +5,7 @@
 from jax import lax
 from jax.sharding import PartitionSpec as P
 
-HIGH = lax.Precision.HIGHEST
+HIGH = lax.Precision.HIGH
 
 
 def padded_2(value, sides, width):

time: 118 us -> 117 us (level)
  matrix products: 6.39 us -> 3.69 us
  transfers between devices with their start and end apart: 14 -> 14, of which waited for: 6 -> 7; matrix products, arithmetic and copies ran while one was open for 8% -> 5% of each run, Pallas kernels for 0% -> 0%
where the time goes in v9:
time: 117 us; the launch traced here: 116 us
  starting transfers between devices  86.7 us (74%)
  waiting for transfers between devices  17.1 us (15%)
  other arithmetic  4.24 us (4%)
  matrix products  3.69 us (3%)
  local copies, waits for them, and re-layouts  3.06 us (3%)
  between operations  1.25 us (1%)
    ppermute x4, starting transfers between devices, doubling_sum(): value = value + lax.ppermute(value, axis, pairs)  29.9 us
    ppermute x2, starting transfers between devices, passed_along(): return lax.ppermute(value, axis, pairs)  15.3 us
    ppermute x1, starting transfers between devices, doubling_sum(): return value + lax.ppermute(value, axis, pairs)  14.9 us
    all_to_all x1, waiting for transfers between devices, per_device(): terms = lax.all_to_all(terms, 'rows', 0, 0, tiled=True).sum(axis=0)  9.51 us
    ppermute x1, starting transfers between devices, pair_gather(): other = lax.ppermute(value, axis, [(i, i ^ 1) for i in range(count)])  8.87 us
    ppermute x2, starting transfers between devices, padded_2(): before = lax.ppermute(last, axis, up)  8.23 us
    ppermute x4, waiting for transfers between devices, doubling_sum(): value = value + lax.ppermute(value, axis, pairs)  5.65 us
    all_to_all x1, starting transfers between devices, per_device(): terms = lax.all_to_all(terms, 'rows', 0, 0, tiled=True).sum(axis=0)  4.21 us
  transfers between devices with their start and end apart: 14, of which 7 were waited for; matrix products, arithmetic and copies ran while one was open for 5% of the time, Pallas kernels for 0%

profile of v9, /device:TPU:1, one launch (start us, length us, event | category | flops | bytes accessed | tf_op | source)
XLA Modules:
  0.0 116.1 jit_solution(311789526461769969)
XLA Ops:
  0.6 0.0 copy-start
  0.6 0.0 copy-start.1
  0.7 1.0 fusion.45
  1.7 4.0 %collective-permute-start = (f32[2,1,96,128]{3,2,1,0:T(8,128)S(1)}, f32[2,1,96,128]{3,2,1,0:T(8,128)S(1)}, u32[]{:S(2)}, u32[]{:S(2)}) collective-permute-start(f32[2,1,96,128]{3,2,1,0:T(8,128)S(1)} %get-tuple-element.10), channel_id=1, source_target_pairs={{0,1},{1,2},{2,3},{3,4},{4,5},{5,6},{6,7},{7,8},{8,9},{9,10},{10,1... | collective-permute-start | bytes 294920 | tf_op jit(solution)/shard_map/ppermute | solution.py:18
  5.7 1.3 %collective-permute-start.1 = (f32[2,1,96,128]{3,2,1,0:T(8,128)S(1)}, f32[2,1,96,128]{3,2,1,0:T(8,128)S(1)}, u32[]{:S(2)}, u32[]{:S(2)}) collective-permute-start(f32[2,1,96,128]{3,2,1,0:T(8,128)S(1)} %get-tuple-element.11), channel_id=1, source_target_pairs={{1,0},{2,1},{3,2},{4,3},{5,4},{6,5},{7,6},{8,7},{9,8},{10,9},{11,1... | collective-permute-start | bytes 294920 | tf_op jit(solution)/shard_map/ppermute | solution.py:19
  7.0 13.4 %collective-permute-start.3 = (f32[2,2,96,128]{3,2,1,0:T(8,128)}, f32[2,2,96,128]{3,2,1,0:T(8,128)S(1)}, u32[]{:S(2)}, u32[]{:S(2)}) collective-permute-start(f32[2,2,96,128]{3,2,1,0:T(8,128)} %param.7), channel_id=1, source_target_pairs={{16,0},{32,16},{48,32},{64,48},{80,64},{96,80},{112,96},{128,112},... | collective-permute-start | bytes 589832 | tf_op jit(solution)/shard_map/ppermute | solution.py:27
  20.4 1.0 select_maximum_fusion.2
  21.6 0.0 copy-start.2
  21.7 0.0 copy-start.9
  21.7 0.8 convolution_bitcast_fusion.1
  22.5 0.1 fusion.43
  22.6 1.9 %collective-permute-start.2 = (f32[2,2,96,128]{3,2,1,0:T(8,128)S(1)}, f32[2,2,96,128]{3,2,1,0:T(8,128)S(1)}, u32[]{:S(2)}, u32[]{:S(2)}) collective-permute-start(f32[2,2,96,128]{3,2,1,0:T(8,128)S(1)} %get-tuple-element.9), channel_id=1, source_target_pairs={{0,16},{16,32},{32,48},{48,64},{64,80},{80,96},{96,112},{112,128},... | collective-permute-start | bytes 589832 | tf_op jit(solution)/shard_map/ppermute | solution.py:27
  24.6 0.4 fusion.3
  25.0 4.3 %collective-permute-start.4 = (f32[2,1,96,128]{3,2,1,0:T(8,128)S(1)}, f32[2,1,96,128]{3,2,1,0:T(8,128)S(1)}, u32[]{:S(2)}, u32[]{:S(2)}) collective-permute-start(f32[2,1,96,128]{3,2,1,0:T(8,128)S(1)} %get-tuple-element.6), channel_id=1, source_target_pairs={{0,1},{1,2},{2,3},{3,4},{4,5},{5,6},{6,7},{7,8},{8,9},{9,10},{10,1... | collective-permute-start | bytes 294920 | tf_op jit(solution)/shard_map/ppermute | solution.py:18
  29.3 1.3 %collective-permute-start.5 = (f32[2,1,96,128]{3,2,1,0:T(8,128)S(1)}, f32[2,1,96,128]{3,2,1,0:T(8,128)S(1)}, u32[]{:S(2)}, u32[]{:S(2)}) collective-permute-start(f32[2,1,96,128]{3,2,1,0:T(8,128)S(1)} %get-tuple-element.7), channel_id=1, source_target_pairs={{1,0},{2,1},{3,2},{4,3},{5,4},{6,5},{7,6},{8,7},{9,8},{10,9},{11,1... | collective-permute-start | bytes 294920 | tf_op jit(solution)/shard_map/ppermute | solution.py:19
  30.6 0.8 fusion.36
  31.4 0.0 copy-start.7
  31.5 0.4 fusion.34
  31.9 0.2 copy-done.5
  32.1 0.1 copy-done.7
  32.1 0.3 maximum_multiply_fusion
  32.4 0.1 constant_dynamic-slice_fusion.1
  32.6 0.1 copy.55
  32.6 2.7 %collective-permute-start.6 = (f32[16,4,12,128]{3,1,2,0:T(4,128)S(1)}, f32[16,4,12,128]{3,1,2,0:T(4,128)S(1)}, u32[]{:S(2)}, u32[]{:S(2)}) collective-permute-start(f32[16,4,12,128]{3,1,2,0:T(4,128)S(1)} %bitcast.168), channel_id=1, source_target_pairs={{0,16},{16,0},{32,48},{48,32},{64,80},{80,64},{96,112},{112,96},{1... | collective-permute-start | bytes 1179656 | tf_op jit(solution)/shard_map/ppermute | solution.py:128
  35.5 1.2 collective-permute-done.6
  36.7 0.9 bitcast_add_fusion
  37.6 4.2 %all-to-all-start = ((f32[16,4,12,128]{3,1,2,0:T(4,128)}), f32[16,4,12,128]{3,1,2,0:T(4,128)}, u32[]{:S(2)}, u32[]{:S(2)}) async-start(f32[16,4,12,128]{3,1,2,0:T(4,128)} %bitcast_add_fusion), calls=%async_computation | async-start | bytes 786432 | tf_op jit(solution)/shard_map/all_to_all | solution.py:129
  41.8 9.5 %all-to-all-done = f32[16,4,12,128]{3,1,2,0:T(4,128)} async-done(((f32[16,4,12,128]{3,1,2,0:T(4,128)}), f32[16,4,12,128]{3,1,2,0:T(4,128)}, u32[]{:S(2)}, u32[]{:S(2)}) %all-to-all-start) | async-done | bytes 393248 | tf_op jit(solution)/shard_map/all_to_all | solution.py:129
  51.3 1.1 reduce_sum.9
  52.4 1.9 %collective-permute-start.7 = (f32[4,12,128]{2,0,1:T(4,128)S(1)}, f32[4,12,128]{2,0,1:T(4,128)S(1)}, u32[]{:S(2)}, u32[]{:S(2)}) collective-permute-start(f32[4,12,128]{2,0,1:T(4,128)S(1)} %reduce_sum.9), channel_id=1, source_target_pairs={{0,32},{16,48},{32,0},{48,16},{64,96},{80,112},{96,64},{112,80},{1... | collective-permute-start | bytes 73736 | tf_op jit(solution)/shard_map/ppermute | solution.py:71
  54.3 2.6 %collective-permute-done.7 = f32[4,12,128]{2,0,1:T(4,128)S(1)} collective-permute-done((f32[4,12,128]{2,0,1:T(4,128)S(1)}, f32[4,12,128]{2,0,1:T(4,128)S(1)}, u32[]{:S(2)}, u32[]{:S(2)}) %collective-permute-start.7) | collective-permute-done | bytes 24608 | tf_op jit(solution)/shard_map/ppermute | solution.py:71
  57.0 0.0 copy-start.8
  57.0 0.0 copy-start.10
  57.0 4.0 %collective-permute-start.8 = (f32[4,12,128]{2,0,1:T(4,128)S(1)}, f32[4,12,128]{2,0,1:T(4,128)S(1)}, u32[]{:S(2)}, u32[]{:S(2)}) collective-permute-start(f32[4,12,128]{2,0,1:T(4,128)S(1)} %add.55), channel_id=1, source_target_pairs={{0,64},{16,80},{32,96},{48,112},{64,0},{80,16},{96,32},{112,48},{1... | collective-permute-start | bytes 73736 | tf_op jit(solution)/shard_map/ppermute | solution.py:71
  61.1 1.5 %collective-permute-done.8 = f32[4,12,128]{2,0,1:T(4,128)S(1)} collective-permute-done((f32[4,12,128]{2,0,1:T(4,128)S(1)}, f32[4,12,128]{2,0,1:T(4,128)S(1)}, u32[]{:S(2)}, u32[]{:S(2)}) %collective-permute-start.8) | collective-permute-done | bytes 24608 | tf_op jit(solution)/shard_map/ppermute | solution.py:71
  62.6 8.5 %collective-permute-start.9 = (f32[4,12,128]{2,0,1:T(4,128)S(1)}, f32[4,12,128]{2,0,1:T(4,128)S(1)}, u32[]{:S(2)}, u32[]{:S(2)}) collective-permute-start(f32[4,12,128]{2,0,1:T(4,128)S(1)} %add.56), channel_id=1, source_target_pairs={{0,128},{16,144},{32,160},{48,176},{64,192},{80,208},{96,224},{112... | collective-permute-start | bytes 73736 | tf_op jit(solution)/shard_map/ppermute | solution.py:71
  71.1 1.2 %collective-permute-done.9 = f32[4,12,128]{2,0,1:T(4,128)S(1)} collective-permute-done((f32[4,12,128]{2,0,1:T(4,128)S(1)}, f32[4,12,128]{2,0,1:T(4,128)S(1)}, u32[]{:S(2)}, u32[]{:S(2)}) %collective-permute-start.9) | collective-permute-done | bytes 24608 | tf_op jit(solution)/shard_map/ppermute | solution.py:71
  72.3 15.4 %collective-permute-start.10 = (f32[4,12,128]{2,0,1:T(4,128)S(1)}, f32[4,12,128]{2,0,1:T(4,128)S(1)}, u32[]{:S(2)}, u32[]{:S(2)}) collective-permute-start(f32[4,12,128]{2,0,1:T(4,128)S(1)} %add.57), channel_id=1, source_target_pairs={{0,256},{16,272},{32,288},{48,304},{64,320},{80,336},{96,352},{112... | collective-permute-start | bytes 73736 | tf_op jit(solution)/shard_map/ppermute | solution.py:71
  87.8 0.9 fusion
  88.6 0.3 collective-permute-done.10
  89.0 14.9 %collective-permute-start.11 = (f32[4,12,128]{2,0,1:T(4,128)S(1)}, f32[4,12,128]{2,0,1:T(4,128)S(1)}, u32[]{:S(2)}, u32[]{:S(2)}) collective-permute-start(f32[4,12,128]{2,0,1:T(4,128)S(1)} %add.58), channel_id=1, source_target_pairs={{0,768},{16,784},{32,800},{48,816},{64,832},{80,848},{96,864},{112... | collective-permute-start | bytes 73736 | tf_op jit(solution)/shard_map/ppermute | solution.py:75
  104.0 0.4 fusion.9
  104.4 0.8 collective-permute-done.11
  105.2 8.9 %collective-permute-start.12 = (f32[4,12,128]{2,0,1:T(4,128)S(1)}, f32[4,12,128]{2,0,1:T(4,128)S(1)}, u32[]{:S(2)}, u32[]{:S(2)}) collective-permute-start(f32[4,12,128]{2,0,1:T(4,128)S(1)} %add.59), channel_id=1, source_target_pairs={{0,16},{16,0},{32,48},{48,32},{64,80},{80,64},{96,112},{112,96},{1... | collective-permute-start | bytes 73736 | tf_op jit(solution)/shard_map/ppermute | solution.py:89
  114.0 0.8 bitcast_add_fusion.1
  114.8 0.0 collective-permute-done.12
  114.9 0.6 slice.132
  115.5 0.6 slice.131
  (47 shorter events, 0.5 us)
Async XLA Ops:
  0.6 21.0 %copy-start = (f32[3,3,128,128]{3,2,1,0:T(8,128)S(1)}, f32[3,3,128,128]{3,2,1,0:T(8,128)}, u32[]{:S(2)}) copy-start(f32[3,3,128,128]{3,2,1,0:T(8,128)} %param.5) | copy-start | bytes 1769476
  0.6 20.8 %copy-start.1 = (f32[2,2,96,128]{3,2,1,0:T(8,128)S(1)}, f32[2,2,96,128]{3,2,1,0:T(8,128)}, u32[]{:S(2)}) copy-start(f32[2,2,96,128]{3,2,1,0:T(8,128)} %param.4) | copy-start | bytes 589828
  1.7 18.7 %collective-permute-start = (f32[2,1,96,128]{3,2,1,0:T(8,128)S(1)}, f32[2,1,96,128]{3,2,1,0:T(8,128)S(1)}, u32[]{:S(2)}, u32[]{:S(2)}) collective-permute-start(f32[2,1,96,128]{3,2,1,0:T(8,128)S(1)} %get-tuple-element.10), channel_id=1, source_target_pairs={{0,1},{1,2},{2,3},{3,4},{4,5},{5,6},{6,7},{7,8},{8,9},{9,10},{10,1... | collective-permute-start | bytes 294920 | tf_op jit(solution)/shard_map/ppermute | solution.py:18
  5.7 14.8 %collective-permute-start.1 = (f32[2,1,96,128]{3,2,1,0:T(8,128)S(1)}, f32[2,1,96,128]{3,2,1,0:T(8,128)S(1)}, u32[]{:S(2)}, u32[]{:S(2)}) collective-permute-start(f32[2,1,96,128]{3,2,1,0:T(8,128)S(1)} %get-tuple-element.11), channel_id=1, source_target_pairs={{1,0},{2,1},{3,2},{4,3},{5,4},{6,5},{7,6},{8,7},{9,8},{10,9},{11,1... | collective-permute-start | bytes 294920 | tf_op jit(solution)/shard_map/ppermute | solution.py:19
  7.0 17.6 %collective-permute-start.3 = (f32[2,2,96,128]{3,2,1,0:T(8,128)}, f32[2,2,96,128]{3,2,1,0:T(8,128)S(1)}, u32[]{:S(2)}, u32[]{:S(2)}) collective-permute-start(f32[2,2,96,128]{3,2,1,0:T(8,128)} %param.7), channel_id=1, source_target_pairs={{16,0},{32,16},{48,32},{64,48},{80,64},{96,80},{112,96},{128,112},... | collective-permute-start | bytes 589832 | tf_op jit(solution)/shard_map/ppermute | solution.py:27
  21.6 2.9 %copy-start.2 = (f32[2,2,96,128]{3,2,1,0:T(8,128)S(1)}, f32[2,2,96,128]{3,2,1,0:T(8,128)}, u32[]{:S(2)}) copy-start(f32[2,2,96,128]{3,2,1,0:T(8,128)} %param.7) | copy-start | bytes 589828
  21.7 2.9 %copy-start.9 = (f32[3,128,128]{2,1,0:T(8,128)S(1)}, f32[3,128,128]{2,1,0:T(8,128)}, u32[]{:S(2)}) copy-start(f32[3,128,128]{2,1,0:T(8,128)} %param.6) | copy-start | bytes 589828
  22.6 8.9 %copy-start.3 = (f32[1,2,2,96,128]{4,3,2,1,0:T(8,128)}, f32[1,2,2,96,128]{4,3,2,1,0:T(8,128)S(1)}, u32[]{:S(2)}) copy-start(f32[1,2,2,96,128]{4,3,2,1,0:T(8,128)S(1)} %get-tuple-element.8) | copy-start | bytes 589828
  22.6 8.8 %collective-permute-start.2 = (f32[2,2,96,128]{3,2,1,0:T(8,128)S(1)}, f32[2,2,96,128]{3,2,1,0:T(8,128)S(1)}, u32[]{:S(2)}, u32[]{:S(2)}) collective-permute-start(f32[2,2,96,128]{3,2,1,0:T(8,128)S(1)} %get-tuple-element.9), channel_id=1, source_target_pairs={{0,16},{16,32},{32,48},{48,64},{64,80},{80,96},{96,112},{112,128},... | collective-permute-start | bytes 589832 | tf_op jit(solution)/shard_map/ppermute | solution.py:27
  25.0 10.3 %collective-permute-start.4 = (f32[2,1,96,128]{3,2,1,0:T(8,128)S(1)}, f32[2,1,96,128]{3,2,1,0:T(8,128)S(1)}, u32[]{:S(2)}, u32[]{:S(2)}) collective-permute-start(f32[2,1,96,128]{3,2,1,0:T(8,128)S(1)} %get-tuple-element.6), channel_id=1, source_target_pairs={{0,1},{1,2},{2,3},{3,4},{4,5},{5,6},{6,7},{7,8},{8,9},{9,10},{10,1... | collective-permute-start | bytes 294920 | tf_op jit(solution)/shard_map/ppermute | solution.py:18
  29.3 6.0 %collective-permute-start.5 = (f32[2,1,96,128]{3,2,1,0:T(8,128)S(1)}, f32[2,1,96,128]{3,2,1,0:T(8,128)S(1)}, u32[]{:S(2)}, u32[]{:S(2)}) collective-permute-start(f32[2,1,96,128]{3,2,1,0:T(8,128)S(1)} %get-tuple-element.7), channel_id=1, source_target_pairs={{1,0},{2,1},{3,2},{4,3},{5,4},{6,5},{7,6},{8,7},{9,8},{10,9},{11,1... | collective-permute-start | bytes 294920 | tf_op jit(solution)/shard_map/ppermute | solution.py:19
  31.4 0.7 copy-start.5
  31.4 0.7 copy-start.7
  32.6 4.0 %collective-permute-start.6 = (f32[16,4,12,128]{3,1,2,0:T(4,128)S(1)}, f32[16,4,12,128]{3,1,2,0:T(4,128)S(1)}, u32[]{:S(2)}, u32[]{:S(2)}) collective-permute-start(f32[16,4,12,128]{3,1,2,0:T(4,128)S(1)} %bitcast.168), channel_id=1, source_target_pairs={{0,16},{16,0},{32,48},{48,32},{64,80},{80,64},{96,112},{112,96},{1... | collective-permute-start | bytes 1179656 | tf_op jit(solution)/shard_map/ppermute | solution.py:128
  37.6 13.8 %all-to-all-start = ((f32[16,4,12,128]{3,1,2,0:T(4,128)}), f32[16,4,12,128]{3,1,2,0:T(4,128)}, u32[]{:S(2)}, u32[]{:S(2)}) async-start(f32[16,4,12,128]{3,1,2,0:T(4,128)} %bitcast_add_fusion), calls=%async_computation | async-start | bytes 786432 | tf_op jit(solution)/shard_map/all_to_all | solution.py:129
  52.4 4.6 %collective-permute-start.7 = (f32[4,12,128]{2,0,1:T(4,128)S(1)}, f32[4,12,128]{2,0,1:T(4,128)S(1)}, u32[]{:S(2)}, u32[]{:S(2)}) collective-permute-start(f32[4,12,128]{2,0,1:T(4,128)S(1)} %reduce_sum.9), channel_id=1, source_target_pairs={{0,32},{16,48},{32,0},{48,16},{64,96},{80,112},{96,64},{112,80},{1... | collective-permute-start | bytes 73736 | tf_op jit(solution)/shard_map/ppermute | solution.py:71
  57.0 47.0 %copy-start.4 = (f32[1,2,2,96,128]{4,3,2,1,0:T(8,128)S(1)}, f32[1,2,2,96,128]{4,3,2,1,0:T(8,128)}, u32[]{:S(2)}) copy-start(f32[1,2,2,96,128]{4,3,2,1,0:T(8,128)} %copy-done.3) | copy-start | bytes 589828
  57.0 47.0 %copy-start.6 = (f32[2,2,96,128]{3,2,1,0:T(8,128)S(1)}, f32[2,2,96,128]{3,2,1,0:T(8,128)}, u32[]{:S(2)}) copy-start(f32[2,2,96,128]{3,2,1,0:T(8,128)} %copy-done.5) | copy-start | bytes 589828
  57.0 47.0 %copy-start.8 = (f32[1,2,2,96,128]{4,3,2,1,0:T(8,128)S(1)}, f32[1,2,2,96,128]{4,3,2,1,0:T(8,128)}, u32[]{:S(2)}) copy-start(f32[1,2,2,96,128]{4,3,2,1,0:T(8,128)} %copy-done.7) | copy-start | bytes 589828
  57.0 47.0 %copy-start.10 = (f32[3,128,128]{2,1,0:T(8,128)S(1)}, f32[3,128,128]{2,1,0:T(8,128)}, u32[]{:S(2)}) copy-start(f32[3,128,128]{2,1,0:T(8,128)} %param.6) | copy-start | bytes 589828
  57.0 5.6 %collective-permute-start.8 = (f32[4,12,128]{2,0,1:T(4,128)S(1)}, f32[4,12,128]{2,0,1:T(4,128)S(1)}, u32[]{:S(2)}, u32[]{:S(2)}) collective-permute-start(f32[4,12,128]{2,0,1:T(4,128)S(1)} %add.55), channel_id=1, source_target_pairs={{0,64},{16,80},{32,96},{48,112},{64,0},{80,16},{96,32},{112,48},{1... | collective-permute-start | bytes 73736 | tf_op jit(solution)/shard_map/ppermute | solution.py:71
  62.6 9.7 %collective-permute-start.9 = (f32[4,12,128]{2,0,1:T(4,128)S(1)}, f32[4,12,128]{2,0,1:T(4,128)S(1)}, u32[]{:S(2)}, u32[]{:S(2)}) collective-permute-start(f32[4,12,128]{2,0,1:T(4,128)S(1)} %add.56), channel_id=1, source_target_pairs={{0,128},{16,144},{32,160},{48,176},{64,192},{80,208},{96,224},{112... | collective-permute-start | bytes 73736 | tf_op jit(solution)/shard_map/ppermute | solution.py:71
  72.3 16.7 %collective-permute-start.10 = (f32[4,12,128]{2,0,1:T(4,128)S(1)}, f32[4,12,128]{2,0,1:T(4,128)S(1)}, u32[]{:S(2)}, u32[]{:S(2)}) collective-permute-start(f32[4,12,128]{2,0,1:T(4,128)S(1)} %add.57), channel_id=1, source_target_pairs={{0,256},{16,272},{32,288},{48,304},{64,320},{80,336},{96,352},{112... | collective-permute-start | bytes 73736 | tf_op jit(solution)/shard_map/ppermute | solution.py:71
  89.0 16.2 %collective-permute-start.11 = (f32[4,12,128]{2,0,1:T(4,128)S(1)}, f32[4,12,128]{2,0,1:T(4,128)S(1)}, u32[]{:S(2)}, u32[]{:S(2)}) collective-permute-start(f32[4,12,128]{2,0,1:T(4,128)S(1)} %add.58), channel_id=1, source_target_pairs={{0,768},{16,784},{32,800},{48,816},{64,832},{80,848},{96,864},{112... | collective-permute-start | bytes 73736 | tf_op jit(solution)/shard_map/ppermute | solution.py:75
  105.2 9.7 %collective-permute-start.12 = (f32[4,12,128]{2,0,1:T(4,128)S(1)}, f32[4,12,128]{2,0,1:T(4,128)S(1)}, u32[]{:S(2)}, u32[]{:S(2)}) collective-permute-start(f32[4,12,128]{2,0,1:T(4,128)S(1)} %add.59), channel_id=1, source_target_pairs={{0,16},{16,0},{32,48},{48,32},{64,80},{80,64},{96,112},{112,96},{1... | collective-permute-start | bytes 73736 | tf_op jit(solution)/shard_map/ppermute | solution.py:89

commit v10 on v9

--- a/solution.py
+++ b/solution.py
@@ -65,14 +65,22 @@
 
 def doubling_sum(value, axis, first):
     count = lax.axis_size(axis)
-    mask = first
-    while mask < count // 2:
-        pairs = [(i, i ^ mask) for i in range(count)]
-        value = value + lax.ppermute(value, axis, pairs)
+    ring = count // first
+    turn = [(ring // 4) * (c % 2) for c in range(first)]
+
+    def pairs_of(partner):
+        pairs = []
+        for i in range(count):
+            c = i % first
+            place = (partner((i // first + turn[c]) % ring) - turn[c]) % ring
+            pairs.append((i, first * place + c))
+        return pairs
+
+    mask = 1
+    while mask < ring // 2:
+        value = value + lax.ppermute(value, axis, pairs_of(lambda z, m=mask: z ^ m))
         mask *= 2
-    ring = count // first
-    pairs = [(i, first * ring_partner(i // first, ring) + i % first) for i in range(count)]
-    return value + lax.ppermute(value, axis, pairs)
+    return value + lax.ppermute(value, axis, pairs_of(lambda z: ring_partner(z, ring)))
 
 
 def ring_partner(z, ring):

time: 117 us -> 118 us (level)
  waiting for transfers between devices: 17.1 us -> 19.9 us
  starting transfers between devices: 86.7 us -> 85 us
    ppermute x5, starting transfers between devices: 44.8 us -> 42 us  [the longest x4 32.8 us: doubling_sum(): value = value + lax.ppermute(value, axis, pairs_of(lambda z, m=mask: z ^ m))]
    ppermute x5, waiting for transfers between devices: 6.42 us -> 9.2 us  [the longest x4 5.65 us: doubling_sum(): value = value + lax.ppermute(value, axis, pairs_of(lambda z, m=mask: z ^ m))]
where the time goes in v10:
time: 118 us; the launch traced here: 117 us
  starting transfers between devices  85 us (72%)
  waiting for transfers between devices  19.9 us (17%)
  other arithmetic  4.24 us (4%)
  matrix products  3.69 us (3%)
  local copies, waits for them, and re-layouts  3.06 us (3%)
  between operations  1.25 us (1%)
    ppermute x4, starting transfers between devices, doubling_sum(): value = value + lax.ppermute(value, axis, pairs_of(lambda z, m=mask: z ^ m))  32.8 us
    ppermute x2, starting transfers between devices, passed_along(): return lax.ppermute(value, axis, pairs)  15.3 us
    ppermute x1, starting transfers between devices, pair_gather(): other = lax.ppermute(value, axis, [(i, i ^ 1) for i in range(count)])  9.86 us
    all_to_all x1, waiting for transfers between devices, per_device(): terms = lax.all_to_all(terms, 'rows', 0, 0, tiled=True).sum(axis=0)  9.51 us
    ppermute x1, starting transfers between devices, doubling_sum(): lax.ppermute(value, axis, pairs_of(lambda z: ring_partner(z, ring)))  9.3 us
    ppermute x2, starting transfers between devices, padded_2(): before = lax.ppermute(last, axis, up)  8.23 us
    ppermute x4, waiting for transfers between devices, doubling_sum(): value = value + lax.ppermute(value, axis, pairs_of(lambda z, m=mask: z ^ m))  5.65 us
    all_to_all x1, starting transfers between devices, per_device(): terms = lax.all_to_all(terms, 'rows', 0, 0, tiled=True).sum(axis=0)  4.21 us
  transfers between devices with their start and end apart: 14, of which 7 were waited for; matrix products, arithmetic and copies ran while one was open for 5% of the time, Pallas kernels for 0%

profile of v10, /device:TPU:1, one launch (start us, length us, event | category | flops | bytes accessed | tf_op | source)
XLA Modules:
  0.0 117.1 jit_solution(10562625853195642438)
XLA Ops:
  0.6 0.0 copy-start
  0.6 0.0 copy-start.1
  0.7 1.0 fusion.45
  1.7 4.0 %collective-permute-start = (f32[2,1,96,128]{3,2,1,0:T(8,128)S(1)}, f32[2,1,96,128]{3,2,1,0:T(8,128)S(1)}, u32[]{:S(2)}, u32[]{:S(2)}) collective-permute-start(f32[2,1,96,128]{3,2,1,0:T(8,128)S(1)} %get-tuple-element.10), channel_id=1, source_target_pairs={{0,1},{1,2},{2,3},{3,4},{4,5},{5,6},{6,7},{7,8},{8,9},{9,10},{10,1... | collective-permute-start | bytes 294920 | tf_op jit(solution)/shard_map/ppermute | solution.py:18
  5.7 1.3 %collective-permute-start.1 = (f32[2,1,96,128]{3,2,1,0:T(8,128)S(1)}, f32[2,1,96,128]{3,2,1,0:T(8,128)S(1)}, u32[]{:S(2)}, u32[]{:S(2)}) collective-permute-start(f32[2,1,96,128]{3,2,1,0:T(8,128)S(1)} %get-tuple-element.11), channel_id=1, source_target_pairs={{1,0},{2,1},{3,2},{4,3},{5,4},{6,5},{7,6},{8,7},{9,8},{10,9},{11,1... | collective-permute-start | bytes 294920 | tf_op jit(solution)/shard_map/ppermute | solution.py:19
  7.0 13.4 %collective-permute-start.3 = (f32[2,2,96,128]{3,2,1,0:T(8,128)}, f32[2,2,96,128]{3,2,1,0:T(8,128)S(1)}, u32[]{:S(2)}, u32[]{:S(2)}) collective-permute-start(f32[2,2,96,128]{3,2,1,0:T(8,128)} %param.7), channel_id=1, source_target_pairs={{16,0},{32,16},{48,32},{64,48},{80,64},{96,80},{112,96},{128,112},... | collective-permute-start | bytes 589832 | tf_op jit(solution)/shard_map/ppermute | solution.py:27
  20.4 1.0 select_maximum_fusion.2
  21.6 0.0 copy-start.2
  21.7 0.0 copy-start.9
  21.7 0.8 convolution_bitcast_fusion.1
  22.5 0.1 fusion.43
  22.6 1.9 %collective-permute-start.2 = (f32[2,2,96,128]{3,2,1,0:T(8,128)S(1)}, f32[2,2,96,128]{3,2,1,0:T(8,128)S(1)}, u32[]{:S(2)}, u32[]{:S(2)}) collective-permute-start(f32[2,2,96,128]{3,2,1,0:T(8,128)S(1)} %get-tuple-element.9), channel_id=1, source_target_pairs={{0,16},{16,32},{32,48},{48,64},{64,80},{80,96},{96,112},{112,128},... | collective-permute-start | bytes 589832 | tf_op jit(solution)/shard_map/ppermute | solution.py:27
  24.6 0.4 fusion.3
  25.0 4.3 %collective-permute-start.4 = (f32[2,1,96,128]{3,2,1,0:T(8,128)S(1)}, f32[2,1,96,128]{3,2,1,0:T(8,128)S(1)}, u32[]{:S(2)}, u32[]{:S(2)}) collective-permute-start(f32[2,1,96,128]{3,2,1,0:T(8,128)S(1)} %get-tuple-element.6), channel_id=1, source_target_pairs={{0,1},{1,2},{2,3},{3,4},{4,5},{5,6},{6,7},{7,8},{8,9},{9,10},{10,1... | collective-permute-start | bytes 294920 | tf_op jit(solution)/shard_map/ppermute | solution.py:18
  29.3 1.3 %collective-permute-start.5 = (f32[2,1,96,128]{3,2,1,0:T(8,128)S(1)}, f32[2,1,96,128]{3,2,1,0:T(8,128)S(1)}, u32[]{:S(2)}, u32[]{:S(2)}) collective-permute-start(f32[2,1,96,128]{3,2,1,0:T(8,128)S(1)} %get-tuple-element.7), channel_id=1, source_target_pairs={{1,0},{2,1},{3,2},{4,3},{5,4},{6,5},{7,6},{8,7},{9,8},{10,9},{11,1... | collective-permute-start | bytes 294920 | tf_op jit(solution)/shard_map/ppermute | solution.py:19
  30.6 0.8 fusion.36
  31.4 0.0 copy-start.7
  31.5 0.4 fusion.34
  31.9 0.2 copy-done.5
  32.1 0.1 copy-done.7
  32.1 0.3 maximum_multiply_fusion
  32.4 0.1 constant_dynamic-slice_fusion.1
  32.6 0.1 copy.55
  32.6 2.7 %collective-permute-start.6 = (f32[16,4,12,128]{3,1,2,0:T(4,128)S(1)}, f32[16,4,12,128]{3,1,2,0:T(4,128)S(1)}, u32[]{:S(2)}, u32[]{:S(2)}) collective-permute-start(f32[16,4,12,128]{3,1,2,0:T(4,128)S(1)} %bitcast.168), channel_id=1, source_target_pairs={{0,16},{16,0},{32,48},{48,32},{64,80},{80,64},{96,112},{112,96},{1... | collective-permute-start | bytes 1179656 | tf_op jit(solution)/shard_map/ppermute | solution.py:136
  35.5 1.2 collective-permute-done.6
  36.7 0.9 bitcast_add_fusion
  37.6 4.2 %all-to-all-start = ((f32[16,4,12,128]{3,1,2,0:T(4,128)}), f32[16,4,12,128]{3,1,2,0:T(4,128)}, u32[]{:S(2)}, u32[]{:S(2)}) async-start(f32[16,4,12,128]{3,1,2,0:T(4,128)} %bitcast_add_fusion), calls=%async_computation | async-start | bytes 786432 | tf_op jit(solution)/shard_map/all_to_all | solution.py:137
  41.8 9.5 %all-to-all-done = f32[16,4,12,128]{3,1,2,0:T(4,128)} async-done(((f32[16,4,12,128]{3,1,2,0:T(4,128)}), f32[16,4,12,128]{3,1,2,0:T(4,128)}, u32[]{:S(2)}, u32[]{:S(2)}) %all-to-all-start) | async-done | bytes 393248 | tf_op jit(solution)/shard_map/all_to_all | solution.py:137
  51.3 1.1 reduce_sum.9
  52.4 1.9 %collective-permute-start.7 = (f32[4,12,128]{2,0,1:T(4,128)S(1)}, f32[4,12,128]{2,0,1:T(4,128)S(1)}, u32[]{:S(2)}, u32[]{:S(2)}) collective-permute-start(f32[4,12,128]{2,0,1:T(4,128)S(1)} %reduce_sum.9), channel_id=1, source_target_pairs={{0,32},{16,48},{32,0},{48,16},{64,96},{80,112},{96,64},{112,80},{1... | collective-permute-start | bytes 73736 | tf_op jit(solution)/shard_map/ppermute | solution.py:81
  54.3 2.6 %collective-permute-done.7 = f32[4,12,128]{2,0,1:T(4,128)S(1)} collective-permute-done((f32[4,12,128]{2,0,1:T(4,128)S(1)}, f32[4,12,128]{2,0,1:T(4,128)S(1)}, u32[]{:S(2)}, u32[]{:S(2)}) %collective-permute-start.7) | collective-permute-done | bytes 24608 | tf_op jit(solution)/shard_map/ppermute | solution.py:81
  57.0 0.0 copy-start.8
  57.0 0.0 copy-start.10
  57.0 4.0 %collective-permute-start.8 = (f32[4,12,128]{2,0,1:T(4,128)S(1)}, f32[4,12,128]{2,0,1:T(4,128)S(1)}, u32[]{:S(2)}, u32[]{:S(2)}) collective-permute-start(f32[4,12,128]{2,0,1:T(4,128)S(1)} %add.55), channel_id=1, source_target_pairs={{0,64},{16,80},{32,96},{48,112},{64,0},{80,16},{96,32},{112,48},{1... | collective-permute-start | bytes 73736 | tf_op jit(solution)/shard_map/ppermute | solution.py:81
  61.1 1.5 %collective-permute-done.8 = f32[4,12,128]{2,0,1:T(4,128)S(1)} collective-permute-done((f32[4,12,128]{2,0,1:T(4,128)S(1)}, f32[4,12,128]{2,0,1:T(4,128)S(1)}, u32[]{:S(2)}, u32[]{:S(2)}) %collective-permute-start.8) | collective-permute-done | bytes 24608 | tf_op jit(solution)/shard_map/ppermute | solution.py:81
  62.6 8.5 %collective-permute-start.9 = (f32[4,12,128]{2,0,1:T(4,128)S(1)}, f32[4,12,128]{2,0,1:T(4,128)S(1)}, u32[]{:S(2)}, u32[]{:S(2)}) collective-permute-start(f32[4,12,128]{2,0,1:T(4,128)S(1)} %add.56), channel_id=1, source_target_pairs={{0,128},{16,144},{32,160},{48,176},{64,192},{80,208},{96,224},{112... | collective-permute-start | bytes 73736 | tf_op jit(solution)/shard_map/ppermute | solution.py:81
  71.1 1.2 %collective-permute-done.9 = f32[4,12,128]{2,0,1:T(4,128)S(1)} collective-permute-done((f32[4,12,128]{2,0,1:T(4,128)S(1)}, f32[4,12,128]{2,0,1:T(4,128)S(1)}, u32[]{:S(2)}, u32[]{:S(2)}) %collective-permute-start.9) | collective-permute-done | bytes 24608 | tf_op jit(solution)/shard_map/ppermute | solution.py:81
  72.3 18.3 %collective-permute-start.10 = (f32[4,12,128]{2,0,1:T(4,128)S(1)}, f32[4,12,128]{2,0,1:T(4,128)S(1)}, u32[]{:S(2)}, u32[]{:S(2)}) collective-permute-start(f32[4,12,128]{2,0,1:T(4,128)S(1)} %add.57), channel_id=1, source_target_pairs={{0,256},{16,784},{32,288},{48,816},{64,320},{80,848},{96,352},{112... | collective-permute-start | bytes 73736 | tf_op jit(solution)/shard_map/ppermute | solution.py:81
  90.7 0.9 fusion
  91.5 0.3 collective-permute-done.10
  91.9 9.3 %collective-permute-start.11 = (f32[4,12,128]{2,0,1:T(4,128)S(1)}, f32[4,12,128]{2,0,1:T(4,128)S(1)}, u32[]{:S(2)}, u32[]{:S(2)}) collective-permute-start(f32[4,12,128]{2,0,1:T(4,128)S(1)} %add.58), channel_id=1, source_target_pairs={{0,768},{16,272},{32,800},{48,304},{64,832},{80,336},{96,864},{112... | collective-permute-start | bytes 73736 | tf_op jit(solution)/shard_map/ppermute | solution.py:83
  101.2 0.4 fusion.9
  101.6 3.6 %collective-permute-done.11 = f32[4,12,128]{2,0,1:T(4,128)S(1)} collective-permute-done((f32[4,12,128]{2,0,1:T(4,128)S(1)}, f32[4,12,128]{2,0,1:T(4,128)S(1)}, u32[]{:S(2)}, u32[]{:S(2)}) %collective-permute-start.11) | collective-permute-done | bytes 24608 | tf_op jit(solution)/shard_map/ppermute | solution.py:83
  105.2 9.9 %collective-permute-start.12 = (f32[4,12,128]{2,0,1:T(4,128)S(1)}, f32[4,12,128]{2,0,1:T(4,128)S(1)}, u32[]{:S(2)}, u32[]{:S(2)}) collective-permute-start(f32[4,12,128]{2,0,1:T(4,128)S(1)} %add.59), channel_id=1, source_target_pairs={{0,16},{16,0},{32,48},{48,32},{64,80},{80,64},{96,112},{112,96},{1... | collective-permute-start | bytes 73736 | tf_op jit(solution)/shard_map/ppermute | solution.py:97
  115.0 0.8 bitcast_add_fusion.1
  115.8 0.0 collective-permute-done.12
  115.9 0.6 slice.132
  116.5 0.6 slice.131
  (47 shorter events, 0.5 us)
Async XLA Ops:
  0.6 21.0 %copy-start = (f32[3,3,128,128]{3,2,1,0:T(8,128)S(1)}, f32[3,3,128,128]{3,2,1,0:T(8,128)}, u32[]{:S(2)}) copy-start(f32[3,3,128,128]{3,2,1,0:T(8,128)} %param.5) | copy-start | bytes 1769476
  0.6 20.8 %copy-start.1 = (f32[2,2,96,128]{3,2,1,0:T(8,128)S(1)}, f32[2,2,96,128]{3,2,1,0:T(8,128)}, u32[]{:S(2)}) copy-start(f32[2,2,96,128]{3,2,1,0:T(8,128)} %param.4) | copy-start | bytes 589828
  1.7 18.7 %collective-permute-start = (f32[2,1,96,128]{3,2,1,0:T(8,128)S(1)}, f32[2,1,96,128]{3,2,1,0:T(8,128)S(1)}, u32[]{:S(2)}, u32[]{:S(2)}) collective-permute-start(f32[2,1,96,128]{3,2,1,0:T(8,128)S(1)} %get-tuple-element.10), channel_id=1, source_target_pairs={{0,1},{1,2},{2,3},{3,4},{4,5},{5,6},{6,7},{7,8},{8,9},{9,10},{10,1... | collective-permute-start | bytes 294920 | tf_op jit(solution)/shard_map/ppermute | solution.py:18
  5.7 14.8 %collective-permute-start.1 = (f32[2,1,96,128]{3,2,1,0:T(8,128)S(1)}, f32[2,1,96,128]{3,2,1,0:T(8,128)S(1)}, u32[]{:S(2)}, u32[]{:S(2)}) collective-permute-start(f32[2,1,96,128]{3,2,1,0:T(8,128)S(1)} %get-tuple-element.11), channel_id=1, source_target_pairs={{1,0},{2,1},{3,2},{4,3},{5,4},{6,5},{7,6},{8,7},{9,8},{10,9},{11,1... | collective-permute-start | bytes 294920 | tf_op jit(solution)/shard_map/ppermute | solution.py:19
  7.0 17.6 %collective-permute-start.3 = (f32[2,2,96,128]{3,2,1,0:T(8,128)}, f32[2,2,96,128]{3,2,1,0:T(8,128)S(1)}, u32[]{:S(2)}, u32[]{:S(2)}) collective-permute-start(f32[2,2,96,128]{3,2,1,0:T(8,128)} %param.7), channel_id=1, source_target_pairs={{16,0},{32,16},{48,32},{64,48},{80,64},{96,80},{112,96},{128,112},... | collective-permute-start | bytes 589832 | tf_op jit(solution)/shard_map/ppermute | solution.py:27
  21.6 2.9 %copy-start.2 = (f32[2,2,96,128]{3,2,1,0:T(8,128)S(1)}, f32[2,2,96,128]{3,2,1,0:T(8,128)}, u32[]{:S(2)}) copy-start(f32[2,2,96,128]{3,2,1,0:T(8,128)} %param.7) | copy-start | bytes 589828
  21.7 2.9 %copy-start.9 = (f32[3,128,128]{2,1,0:T(8,128)S(1)}, f32[3,128,128]{2,1,0:T(8,128)}, u32[]{:S(2)}) copy-start(f32[3,128,128]{2,1,0:T(8,128)} %param.6) | copy-start | bytes 589828
  22.6 8.9 %copy-start.3 = (f32[1,2,2,96,128]{4,3,2,1,0:T(8,128)}, f32[1,2,2,96,128]{4,3,2,1,0:T(8,128)S(1)}, u32[]{:S(2)}) copy-start(f32[1,2,2,96,128]{4,3,2,1,0:T(8,128)S(1)} %get-tuple-element.8) | copy-start | bytes 589828
  22.6 8.8 %collective-permute-start.2 = (f32[2,2,96,128]{3,2,1,0:T(8,128)S(1)}, f32[2,2,96,128]{3,2,1,0:T(8,128)S(1)}, u32[]{:S(2)}, u32[]{:S(2)}) collective-permute-start(f32[2,2,96,128]{3,2,1,0:T(8,128)S(1)} %get-tuple-element.9), channel_id=1, source_target_pairs={{0,16},{16,32},{32,48},{48,64},{64,80},{80,96},{96,112},{112,128},... | collective-permute-start | bytes 589832 | tf_op jit(solution)/shard_map/ppermute | solution.py:27
  25.0 10.3 %collective-permute-start.4 = (f32[2,1,96,128]{3,2,1,0:T(8,128)S(1)}, f32[2,1,96,128]{3,2,1,0:T(8,128)S(1)}, u32[]{:S(2)}, u32[]{:S(2)}) collective-permute-start(f32[2,1,96,128]{3,2,1,0:T(8,128)S(1)} %get-tuple-element.6), channel_id=1, source_target_pairs={{0,1},{1,2},{2,3},{3,4},{4,5},{5,6},{6,7},{7,8},{8,9},{9,10},{10,1... | collective-permute-start | bytes 294920 | tf_op jit(solution)/shard_map/ppermute | solution.py:18
  29.3 6.0 %collective-permute-start.5 = (f32[2,1,96,128]{3,2,1,0:T(8,128)S(1)}, f32[2,1,96,128]{3,2,1,0:T(8,128)S(1)}, u32[]{:S(2)}, u32[]{:S(2)}) collective-permute-start(f32[2,1,96,128]{3,2,1,0:T(8,128)S(1)} %get-tuple-element.7), channel_id=1, source_target_pairs={{1,0},{2,1},{3,2},{4,3},{5,4},{6,5},{7,6},{8,7},{9,8},{10,9},{11,1... | collective-permute-start | bytes 294920 | tf_op jit(solution)/shard_map/ppermute | solution.py:19
  31.4 0.7 copy-start.5
  31.4 0.7 copy-start.7
  32.6 4.0 %collective-permute-start.6 = (f32[16,4,12,128]{3,1,2,0:T(4,128)S(1)}, f32[16,4,12,128]{3,1,2,0:T(4,128)S(1)}, u32[]{:S(2)}, u32[]{:S(2)}) collective-permute-start(f32[16,4,12,128]{3,1,2,0:T(4,128)S(1)} %bitcast.168), channel_id=1, source_target_pairs={{0,16},{16,0},{32,48},{48,32},{64,80},{80,64},{96,112},{112,96},{1... | collective-permute-start | bytes 1179656 | tf_op jit(solution)/shard_map/ppermute | solution.py:136
  37.6 13.8 %all-to-all-start = ((f32[16,4,12,128]{3,1,2,0:T(4,128)}), f32[16,4,12,128]{3,1,2,0:T(4,128)}, u32[]{:S(2)}, u32[]{:S(2)}) async-start(f32[16,4,12,128]{3,1,2,0:T(4,128)} %bitcast_add_fusion), calls=%async_computation | async-start | bytes 786432 | tf_op jit(solution)/shard_map/all_to_all | solution.py:137
  52.4 4.6 %collective-permute-start.7 = (f32[4,12,128]{2,0,1:T(4,128)S(1)}, f32[4,12,128]{2,0,1:T(4,128)S(1)}, u32[]{:S(2)}, u32[]{:S(2)}) collective-permute-start(f32[4,12,128]{2,0,1:T(4,128)S(1)} %reduce_sum.9), channel_id=1, source_target_pairs={{0,32},{16,48},{32,0},{48,16},{64,96},{80,112},{96,64},{112,80},{1... | collective-permute-start | bytes 73736 | tf_op jit(solution)/shard_map/ppermute | solution.py:81
  57.0 44.2 %copy-start.4 = (f32[1,2,2,96,128]{4,3,2,1,0:T(8,128)S(1)}, f32[1,2,2,96,128]{4,3,2,1,0:T(8,128)}, u32[]{:S(2)}) copy-start(f32[1,2,2,96,128]{4,3,2,1,0:T(8,128)} %copy-done.3) | copy-start | bytes 589828
  57.0 44.2 %copy-start.6 = (f32[2,2,96,128]{3,2,1,0:T(8,128)S(1)}, f32[2,2,96,128]{3,2,1,0:T(8,128)}, u32[]{:S(2)}) copy-start(f32[2,2,96,128]{3,2,1,0:T(8,128)} %copy-done.5) | copy-start | bytes 589828
  57.0 44.2 %copy-start.8 = (f32[1,2,2,96,128]{4,3,2,1,0:T(8,128)S(1)}, f32[1,2,2,96,128]{4,3,2,1,0:T(8,128)}, u32[]{:S(2)}) copy-start(f32[1,2,2,96,128]{4,3,2,1,0:T(8,128)} %copy-done.7) | copy-start | bytes 589828
  57.0 44.2 %copy-start.10 = (f32[3,128,128]{2,1,0:T(8,128)S(1)}, f32[3,128,128]{2,1,0:T(8,128)}, u32[]{:S(2)}) copy-start(f32[3,128,128]{2,1,0:T(8,128)} %param.6) | copy-start | bytes 589828
  57.0 5.6 %collective-permute-start.8 = (f32[4,12,128]{2,0,1:T(4,128)S(1)}, f32[4,12,128]{2,0,1:T(4,128)S(1)}, u32[]{:S(2)}, u32[]{:S(2)}) collective-permute-start(f32[4,12,128]{2,0,1:T(4,128)S(1)} %add.55), channel_id=1, source_target_pairs={{0,64},{16,80},{32,96},{48,112},{64,0},{80,16},{96,32},{112,48},{1... | collective-permute-start | bytes 73736 | tf_op jit(solution)/shard_map/ppermute | solution.py:81
  62.6 9.7 %collective-permute-start.9 = (f32[4,12,128]{2,0,1:T(4,128)S(1)}, f32[4,12,128]{2,0,1:T(4,128)S(1)}, u32[]{:S(2)}, u32[]{:S(2)}) collective-permute-start(f32[4,12,128]{2,0,1:T(4,128)S(1)} %add.56), channel_id=1, source_target_pairs={{0,128},{16,144},{32,160},{48,176},{64,192},{80,208},{96,224},{112... | collective-permute-start | bytes 73736 | tf_op jit(solution)/shard_map/ppermute | solution.py:81
  72.3 19.5 %collective-permute-start.10 = (f32[4,12,128]{2,0,1:T(4,128)S(1)}, f32[4,12,128]{2,0,1:T(4,128)S(1)}, u32[]{:S(2)}, u32[]{:S(2)}) collective-permute-start(f32[4,12,128]{2,0,1:T(4,128)S(1)} %add.57), channel_id=1, source_target_pairs={{0,256},{16,784},{32,288},{48,816},{64,320},{80,848},{96,352},{112... | collective-permute-start | bytes 73736 | tf_op jit(solution)/shard_map/ppermute | solution.py:81
  91.9 13.3 %collective-permute-start.11 = (f32[4,12,128]{2,0,1:T(4,128)S(1)}, f32[4,12,128]{2,0,1:T(4,128)S(1)}, u32[]{:S(2)}, u32[]{:S(2)}) collective-permute-start(f32[4,12,128]{2,0,1:T(4,128)S(1)} %add.58), channel_id=1, source_target_pairs={{0,768},{16,272},{32,800},{48,304},{64,832},{80,336},{96,864},{112... | collective-permute-start | bytes 73736 | tf_op jit(solution)/shard_map/ppermute | solution.py:83
  105.2 10.7 %collective-permute-start.12 = (f32[4,12,128]{2,0,1:T(4,128)S(1)}, f32[4,12,128]{2,0,1:T(4,128)S(1)}, u32[]{:S(2)}, u32[]{:S(2)}) collective-permute-start(f32[4,12,128]{2,0,1:T(4,128)S(1)} %add.59), channel_id=1, source_target_pairs={{0,16},{16,0},{32,48},{48,32},{64,80},{80,64},{96,112},{112,96},{1... | collective-permute-start | bytes 73736 | tf_op jit(solution)/shard_map/ppermute | solution.py:97

commit v11 on v9

--- a/solution.py
+++ b/solution.py
@@ -92,14 +92,29 @@
 
 def per_device(images, spatial_weight, temporal_weight, cotangent):
     nframes, strip, width, chans = images.shape
-    padded = widen(padded_2(images, (("rows", 1),), 1))
-    pre = convolve(padded, spatial_weight, strip, width)
-    sig = jax.nn.sigmoid(pre)
     later = passed_along(cotangent, "frames", -1)
-    grad_long = jnp.concatenate([cotangent, later], axis=0)
-    dact = temporal_back(grad_long, temporal_weight, nframes)
-    dpre = dact * sig * (1.0 + pre * (1.0 - sig))
-    dpre_wide = widen(padded_2(dpre, (("rows", 1),), 1))
+    count = lax.axis_size("rows")
+    up = jnp.concatenate(
+        [images[:, strip - 2 :], jnp.concatenate([cotangent[:, -1:], later[:, -1:]], axis=1)], axis=3
+    )
+    down = jnp.concatenate(
+        [images[:, :2], jnp.concatenate([cotangent[:, :1], later[:, :1]], axis=1)], axis=3
+    )
+    before = lax.ppermute(up, "rows", [(i, i + 1) for i in range(count - 1)])
+    after = lax.ppermute(down, "rows", [(i + 1, i) for i in range(count - 1)])
+    padded_all = widen(jnp.concatenate([before[..., :chans], images, after[..., :chans]], axis=1))
+    cot_wide = jnp.concatenate([before[:, :1, :, chans:], cotangent, after[:, :1, :, chans:]], axis=1)
+    later_wide = jnp.concatenate([before[:, 1:, :, chans:], later, after[:, 1:, :, chans:]], axis=1)
+    pre_wide = convolve(padded_all, spatial_weight, strip + 2, width)
+    sig_wide = jax.nn.sigmoid(pre_wide)
+    grad_long = jnp.concatenate([cot_wide, later_wide], axis=0)
+    dact_wide = temporal_back(grad_long, temporal_weight, nframes)
+    dpre_full = dact_wide * sig_wide * (1.0 + pre_wide * (1.0 - sig_wide))
+    dpre_wide = widen(dpre_full)
+    padded = padded_all[:, 1:-1]
+    pre = pre_wide[:, 1:-1]
+    sig = sig_wide[:, 1:-1]
+    dpre = dpre_full[:, 1:-1]
     act = pre * sig
     earlier = passed_along(act, "frames", 1)
     longer = jnp.concatenate([earlier, act], axis=0)

time: 117 us -> 131 us (1.12)
  waiting for transfers between devices: 17.1 us -> 26.4 us
  starting transfers between devices: 86.7 us -> 88.3 us
  other arithmetic: 4.24 us -> 5.67 us
    ppermute x4 -> x2, waiting for transfers between devices: 0.01 us -> 7.73 us  [the longest x1 6.88 us: per_device(): after = lax.ppermute(down, 'rows', [(i + 1, i) for i in range(count - 1)])]
    ppermute x4 -> x2, starting transfers between devices: 10.8 us -> 5.3 us  [the longest x1 4.01 us: per_device(): before = lax.ppermute(up, 'rows', [(i, i + 1) for i in range(count - 1)])]
    ppermute x1, starting transfers between devices: 14.9 us -> 18.6 us  [doubling_sum(): return value + lax.ppermute(value, axis, pairs)]
    ppermute x2, starting transfers between devices: 15.3 us -> 18.1 us  [passed_along(): return lax.ppermute(value, axis, pairs)]
    ppermute x2, waiting for transfers between devices: 0.01 us -> 1.84 us  [passed_along(): return lax.ppermute(value, axis, pairs)]
    ppermute x4, starting transfers between devices: 29.9 us -> 31.5 us  [doubling_sum(): value = value + lax.ppermute(value, axis, pairs)]
  transfers between devices with their start and end apart: 14 -> 12, of which waited for: 7 -> 11; matrix products, arithmetic and copies ran while one was open for 5% -> 3% of each run, Pallas kernels for 0% -> 0%
where the time goes in v11:
time: 131 us; the launch traced here: 130 us
  starting transfers between devices  88.3 us (67%)
  waiting for transfers between devices  26.4 us (20%)
  other arithmetic  5.67 us (4%)
  matrix products  4.78 us (4%)
  local copies, waits for them, and re-layouts  3.75 us (3%)
    ppermute x4, starting transfers between devices, doubling_sum(): value = value + lax.ppermute(value, axis, pairs)  31.5 us
    ppermute x1, starting transfers between devices, doubling_sum(): return value + lax.ppermute(value, axis, pairs)  18.6 us
    ppermute x2, starting transfers between devices, passed_along(): return lax.ppermute(value, axis, pairs)  18.1 us
    all_to_all x1, waiting for transfers between devices, per_device(): terms = lax.all_to_all(terms, 'rows', 0, 0, tiled=True).sum(axis=0)  9.46 us
    ppermute x1, starting transfers between devices, pair_gather(): other = lax.ppermute(value, axis, [(i, i ^ 1) for i in range(count)])  8.63 us
    ppermute x1, waiting for transfers between devices, per_device(): after = lax.ppermute(down, 'rows', [(i + 1, i) for i in range(count - 1)])  6.88 us
    ppermute x4, waiting for transfers between devices, doubling_sum(): value = value + lax.ppermute(value, axis, pairs)  4.9 us
    all_to_all x1, starting transfers between devices, per_device(): terms = lax.all_to_all(terms, 'rows', 0, 0, tiled=True).sum(axis=0)  4.28 us
  transfers between devices with their start and end apart: 12, of which 11 were waited for; matrix products, arithmetic and copies ran while one was open for 3% of the time, Pallas kernels for 0%

profile of v11, /device:TPU:1, one launch (start us, length us, event | category | flops | bytes accessed | tf_op | source)
XLA Modules:
  0.0 130.1 jit_solution(1121684260596569720)
XLA Ops:
  0.6 0.0 copy-start
  0.6 0.0 copy-start.1
  0.7 16.2 %collective-permute-start = (f32[2,2,96,128]{3,2,1,0:T(8,128)}, f32[2,2,96,128]{3,2,1,0:T(8,128)S(1)}, u32[]{:S(2)}, u32[]{:S(2)}) collective-permute-start(f32[2,2,96,128]{3,2,1,0:T(8,128)} %param.7), channel_id=1, source_target_pairs={{16,0},{32,16},{48,32},{64,48},{80,64},{96,80},{112,96},{128,112},... | collective-permute-start | bytes 589832 | tf_op jit(solution)/shard_map/ppermute | solution.py:27
  16.9 1.0 fusion.69
  17.8 0.3 collective-permute-done
  18.1 1.0 pad_maximum_fusion.4
  19.1 1.3 collective-permute-start.2
  20.4 4.0 %collective-permute-start.1 = (f32[2,2,96,256]{3,2,1,0:T(8,128)S(1)}, f32[2,2,96,256]{3,2,1,0:T(8,128)S(1)}, u32[]{:S(2)}, u32[]{:S(2)}) collective-permute-start(f32[2,2,96,256]{3,2,1,0:T(8,128)S(1)} %get-tuple-element.15), channel_id=1, source_target_pairs={{0,1},{1,2},{2,3},{3,4},{4,5},{5,6},{6,7},{7,8},{8,9},{9,10},{10,1... | collective-permute-start | bytes 1179656 | tf_op jit(solution)/shard_map/ppermute | solution.py:103
  24.5 6.9 %collective-permute-done.2 = f32[2,2,96,256]{3,2,1,0:T(8,128)S(1)} collective-permute-done((f32[2,2,96,256]{3,2,1,0:T(8,128)S(1)}, f32[2,2,96,256]{3,2,1,0:T(8,128)S(1)}, u32[]{:S(2)}, u32[]{:S(2)}) %collective-permute-start.2) | collective-permute-done | bytes 393248 | tf_op jit(solution)/shard_map/ppermute | solution.py:104
  31.4 0.8 collective-permute-done.1
  32.7 0.7 copy-done.2
  33.5 0.1 maximum_bitcast_fusion
  33.6 0.6 fusion.2
  34.3 1.7 %fusion.25 = (f32[2,4,96,128]{3,2,1,0:T(8,128)S(1)}, f32[2,4,96,128]{3,2,1,0:T(8,128)S(1)}, f32[2,4,96,128]{3,2,1,0:T(8,128)S(1)}) fusion(f32[2,4,96,128,1]{3,2,0,1,4:T(8,128)S(1)} %fusion.2, f32[9,2,4,96,128]{4,3,0,2,1:T(8,128)S(1)} %fusion.21, f32[9,128,128,1,1]{2,1,0,4,3:T(8,128)S(1)} %bitcast.198), kind=kOutput, calls=%fused_computation.59 | convolution fusion | flops 680263680 | bytes 5701632 | tf_op jit(solution)/shard_map/tfrwc,tcd->frwd/dot_general | solution.py:42
  36.0 1.9 %collective-permute-start.3 = (f32[2,2,96,128]{3,2,1,0:T(8,128)S(1)}, f32[2,2,96,128]{3,2,1,0:T(8,128)S(1)}, u32[]{:S(2)}, u32[]{:S(2)}) collective-permute-start(f32[2,2,96,128]{3,2,1,0:T(8,128)S(1)} %slice_multiply_fusion), channel_id=1, source_target_pairs={{0,16},{16,32},{32,48},{48,64},{64,80},{80,96},{96,112},{112,128},... | collective-permute-start | bytes 589832 | tf_op jit(solution)/shard_map/ppermute | solution.py:27
  38.1 0.8 fusion.61
  38.9 1.5 %collective-permute-done.3 = f32[2,2,96,128]{3,2,1,0:T(8,128)S(1)} collective-permute-done((f32[2,2,96,128]{3,2,1,0:T(8,128)S(1)}, f32[2,2,96,128]{3,2,1,0:T(8,128)S(1)}, u32[]{:S(2)}, u32[]{:S(2)}) %collective-permute-start.3) | collective-permute-done | bytes 196640 | tf_op jit(solution)/shard_map/ppermute | solution.py:27
  40.5 0.0 copy-start.3
  40.5 0.4 fusion.59
  40.9 0.3 maximum_multiply_fusion
  41.2 0.1 constant_dynamic-slice_fusion.1
  41.4 0.1 copy.62
  41.5 1.9 %collective-permute-start.4 = (f32[16,4,12,128]{3,1,2,0:T(4,128)S(1)}, f32[16,4,12,128]{3,1,2,0:T(4,128)S(1)}, u32[]{:S(2)}, u32[]{:S(2)}) collective-permute-start(f32[16,4,12,128]{3,1,2,0:T(4,128)S(1)} %bitcast.205), channel_id=1, source_target_pairs={{0,16},{16,0},{32,48},{48,32},{64,80},{80,64},{96,112},{112,96},{1... | collective-permute-start | bytes 1179656 | tf_op jit(solution)/shard_map/ppermute | solution.py:143
  43.5 1.6 %collective-permute-done.4 = f32[16,4,12,128]{3,1,2,0:T(4,128)S(1)} collective-permute-done((f32[16,4,12,128]{3,1,2,0:T(4,128)S(1)}, f32[16,4,12,128]{3,1,2,0:T(4,128)S(1)}, u32[]{:S(2)}, u32[]{:S(2)}) %collective-permute-start.4) | collective-permute-done | bytes 393248 | tf_op jit(solution)/shard_map/ppermute | solution.py:143
  45.1 0.9 bitcast_add_fusion
  45.9 4.3 %all-to-all-start = ((f32[16,4,12,128]{3,1,2,0:T(4,128)}), f32[16,4,12,128]{3,1,2,0:T(4,128)}, u32[]{:S(2)}, u32[]{:S(2)}) async-start(f32[16,4,12,128]{3,1,2,0:T(4,128)} %bitcast_add_fusion), calls=%async_computation | async-start | bytes 786432 | tf_op jit(solution)/shard_map/all_to_all | solution.py:144
  50.3 9.5 %all-to-all-done = f32[16,4,12,128]{3,1,2,0:T(4,128)} async-done(((f32[16,4,12,128]{3,1,2,0:T(4,128)}), f32[16,4,12,128]{3,1,2,0:T(4,128)}, u32[]{:S(2)}, u32[]{:S(2)}) %all-to-all-start) | async-done | bytes 393248 | tf_op jit(solution)/shard_map/all_to_all | solution.py:144
  59.7 1.7 %reduce_sum.9 = f32[4,12,128]{2,0,1:T(4,128)} reduce(f32[16,4,12,128]{3,1,2,0:T(4,128)} %all-to-all-done, f32[]{:T(128)} %constant.29.clone.1), dimensions={0}, to_apply=%region_0.1 | reduce | flops 92160 | bytes 417796 | tf_op jit(solution)/shard_map/reduce_sum | solution.py:144
  61.4 4.2 %collective-permute-start.5 = (f32[4,12,128]{2,0,1:T(4,128)}, f32[4,12,128]{2,0,1:T(4,128)S(1)}, u32[]{:S(2)}, u32[]{:S(2)}) collective-permute-start(f32[4,12,128]{2,0,1:T(4,128)} %reduce_sum.9), channel_id=1, source_target_pairs={{0,32},{16,48},{32,0},{48,16},{64,96},{80,112},{96,64},{112,80},{1... | collective-permute-start | bytes 73736 | tf_op jit(solution)/shard_map/ppermute | solution.py:71
  65.6 1.4 %collective-permute-done.5 = f32[4,12,128]{2,0,1:T(4,128)S(1)} collective-permute-done((f32[4,12,128]{2,0,1:T(4,128)}, f32[4,12,128]{2,0,1:T(4,128)S(1)}, u32[]{:S(2)}, u32[]{:S(2)}) %collective-permute-start.5) | collective-permute-done | bytes 24608 | tf_op jit(solution)/shard_map/ppermute | solution.py:71
  67.0 0.7 add.55
  67.7 3.4 %collective-permute-start.6 = (f32[4,12,128]{2,0,1:T(4,128)S(1)}, f32[4,12,128]{2,0,1:T(4,128)S(1)}, u32[]{:S(2)}, u32[]{:S(2)}) collective-permute-start(f32[4,12,128]{2,0,1:T(4,128)S(1)} %add.55), channel_id=1, source_target_pairs={{0,64},{16,80},{32,96},{48,112},{64,0},{80,16},{96,32},{112,48},{1... | collective-permute-start | bytes 73736 | tf_op jit(solution)/shard_map/ppermute | solution.py:71
  71.2 0.0 copy-start.4
  71.2 0.0 copy-start.6
  71.2 2.0 %collective-permute-done.6 = f32[4,12,128]{2,0,1:T(4,128)S(1)} collective-permute-done((f32[4,12,128]{2,0,1:T(4,128)S(1)}, f32[4,12,128]{2,0,1:T(4,128)S(1)}, u32[]{:S(2)}, u32[]{:S(2)}) %collective-permute-start.6) | collective-permute-done | bytes 24608 | tf_op jit(solution)/shard_map/ppermute | solution.py:71
  73.2 8.0 %collective-permute-start.7 = (f32[4,12,128]{2,0,1:T(4,128)S(1)}, f32[4,12,128]{2,0,1:T(4,128)S(1)}, u32[]{:S(2)}, u32[]{:S(2)}) collective-permute-start(f32[4,12,128]{2,0,1:T(4,128)S(1)} %add.56), channel_id=1, source_target_pairs={{0,128},{16,144},{32,160},{48,176},{64,192},{80,208},{96,224},{112... | collective-permute-start | bytes 73736 | tf_op jit(solution)/shard_map/ppermute | solution.py:71
  81.2 1.2 collective-permute-done.7
  82.4 16.0 %collective-permute-start.8 = (f32[4,12,128]{2,0,1:T(4,128)S(1)}, f32[4,12,128]{2,0,1:T(4,128)S(1)}, u32[]{:S(2)}, u32[]{:S(2)}) collective-permute-start(f32[4,12,128]{2,0,1:T(4,128)S(1)} %add.57), channel_id=1, source_target_pairs={{0,256},{16,272},{32,288},{48,304},{64,320},{80,336},{96,352},{112... | collective-permute-start | bytes 73736 | tf_op jit(solution)/shard_map/ppermute | solution.py:71
  98.4 0.9 fusion
  99.2 0.3 collective-permute-done.8
  99.6 18.6 %collective-permute-start.9 = (f32[4,12,128]{2,0,1:T(4,128)S(1)}, f32[4,12,128]{2,0,1:T(4,128)S(1)}, u32[]{:S(2)}, u32[]{:S(2)}) collective-permute-start(f32[4,12,128]{2,0,1:T(4,128)S(1)} %add.58), channel_id=1, source_target_pairs={{0,768},{16,784},{32,800},{48,816},{64,832},{80,848},{96,864},{112... | collective-permute-start | bytes 73736 | tf_op jit(solution)/shard_map/ppermute | solution.py:75
  118.2 0.4 fusion.4
  118.5 0.8 collective-permute-done.9
  119.4 8.6 %collective-permute-start.10 = (f32[4,12,128]{2,0,1:T(4,128)S(1)}, f32[4,12,128]{2,0,1:T(4,128)S(1)}, u32[]{:S(2)}, u32[]{:S(2)}) collective-permute-start(f32[4,12,128]{2,0,1:T(4,128)S(1)} %add.59), channel_id=1, source_target_pairs={{0,16},{16,0},{32,48},{48,32},{64,80},{80,64},{96,112},{112,96},{1... | collective-permute-start | bytes 73736 | tf_op jit(solution)/shard_map/ppermute | solution.py:89
  128.0 0.8 bitcast_add_fusion.1
  128.8 0.0 collective-permute-done.10
  128.8 0.6 slice.205
  129.5 0.6 slice.206
  (48 shorter events, 0.8 us)
Async XLA Ops:
  0.6 33.6 %copy-start = (f32[3,3,128,128]{3,2,1,0:T(8,128)S(1)}, f32[3,3,128,128]{3,2,1,0:T(8,128)}, u32[]{:S(2)}) copy-start(f32[3,3,128,128]{3,2,1,0:T(8,128)} %param.5) | copy-start | bytes 1769476
  0.6 31.6 %copy-start.1 = (f32[2,2,96,128]{3,2,1,0:T(8,128)S(1)}, f32[2,2,96,128]{3,2,1,0:T(8,128)}, u32[]{:S(2)}) copy-start(f32[2,2,96,128]{3,2,1,0:T(8,128)} %param.4) | copy-start | bytes 589828
  0.7 17.5 %collective-permute-start = (f32[2,2,96,128]{3,2,1,0:T(8,128)}, f32[2,2,96,128]{3,2,1,0:T(8,128)S(1)}, u32[]{:S(2)}, u32[]{:S(2)}) collective-permute-start(f32[2,2,96,128]{3,2,1,0:T(8,128)} %param.7), channel_id=1, source_target_pairs={{16,0},{32,16},{48,32},{64,48},{80,64},{96,80},{112,96},{128,112},... | collective-permute-start | bytes 589832 | tf_op jit(solution)/shard_map/ppermute | solution.py:27
  19.1 12.2 %collective-permute-start.2 = (f32[2,2,96,256]{3,2,1,0:T(8,128)S(1)}, f32[2,2,96,256]{3,2,1,0:T(8,128)S(1)}, u32[]{:S(2)}, u32[]{:S(2)}) collective-permute-start(f32[2,2,96,256]{3,2,1,0:T(8,128)S(1)} %get-tuple-element.16), channel_id=1, source_target_pairs={{1,0},{2,1},{3,2},{4,3},{5,4},{6,5},{7,6},{8,7},{9,8},{10,9},{11,1... | collective-permute-start | bytes 1179656 | tf_op jit(solution)/shard_map/ppermute | solution.py:104
  20.4 11.8 %collective-permute-start.1 = (f32[2,2,96,256]{3,2,1,0:T(8,128)S(1)}, f32[2,2,96,256]{3,2,1,0:T(8,128)S(1)}, u32[]{:S(2)}, u32[]{:S(2)}) collective-permute-start(f32[2,2,96,256]{3,2,1,0:T(8,128)S(1)} %get-tuple-element.15), channel_id=1, source_target_pairs={{0,1},{1,2},{2,3},{3,4},{4,5},{5,6},{6,7},{7,8},{8,9},{9,10},{10,1... | collective-permute-start | bytes 1179656 | tf_op jit(solution)/shard_map/ppermute | solution.py:103
  32.5 0.9 copy-start.2
  32.6 1.0 copy-start.5
  36.0 4.5 %collective-permute-start.3 = (f32[2,2,96,128]{3,2,1,0:T(8,128)S(1)}, f32[2,2,96,128]{3,2,1,0:T(8,128)S(1)}, u32[]{:S(2)}, u32[]{:S(2)}) collective-permute-start(f32[2,2,96,128]{3,2,1,0:T(8,128)S(1)} %slice_multiply_fusion), channel_id=1, source_target_pairs={{0,16},{16,32},{32,48},{48,64},{64,80},{80,96},{96,112},{112,128},... | collective-permute-start | bytes 589832 | tf_op jit(solution)/shard_map/ppermute | solution.py:27
  40.5 0.9 copy-start.3
  41.5 3.6 %collective-permute-start.4 = (f32[16,4,12,128]{3,1,2,0:T(4,128)S(1)}, f32[16,4,12,128]{3,1,2,0:T(4,128)S(1)}, u32[]{:S(2)}, u32[]{:S(2)}) collective-permute-start(f32[16,4,12,128]{3,1,2,0:T(4,128)S(1)} %bitcast.205), channel_id=1, source_target_pairs={{0,16},{16,0},{32,48},{48,32},{64,80},{80,64},{96,112},{112,96},{1... | collective-permute-start | bytes 1179656 | tf_op jit(solution)/shard_map/ppermute | solution.py:143
  45.9 13.8 %all-to-all-start = ((f32[16,4,12,128]{3,1,2,0:T(4,128)}), f32[16,4,12,128]{3,1,2,0:T(4,128)}, u32[]{:S(2)}, u32[]{:S(2)}) async-start(f32[16,4,12,128]{3,1,2,0:T(4,128)} %bitcast_add_fusion), calls=%async_computation | async-start | bytes 786432 | tf_op jit(solution)/shard_map/all_to_all | solution.py:144
  61.4 5.6 %collective-permute-start.5 = (f32[4,12,128]{2,0,1:T(4,128)}, f32[4,12,128]{2,0,1:T(4,128)S(1)}, u32[]{:S(2)}, u32[]{:S(2)}) collective-permute-start(f32[4,12,128]{2,0,1:T(4,128)} %reduce_sum.9), channel_id=1, source_target_pairs={{0,32},{16,48},{32,0},{48,16},{64,96},{80,112},{96,64},{112,80},{1... | collective-permute-start | bytes 73736 | tf_op jit(solution)/shard_map/ppermute | solution.py:71
  67.7 5.5 %collective-permute-start.6 = (f32[4,12,128]{2,0,1:T(4,128)S(1)}, f32[4,12,128]{2,0,1:T(4,128)S(1)}, u32[]{:S(2)}, u32[]{:S(2)}) collective-permute-start(f32[4,12,128]{2,0,1:T(4,128)S(1)} %add.55), channel_id=1, source_target_pairs={{0,64},{16,80},{32,96},{48,112},{64,0},{80,16},{96,32},{112,48},{1... | collective-permute-start | bytes 73736 | tf_op jit(solution)/shard_map/ppermute | solution.py:71
  71.2 47.0 %copy-start.4 = (f32[1,2,2,96,128]{4,3,2,1,0:T(8,128)S(1)}, f32[1,2,2,96,128]{4,3,2,1,0:T(8,128)}, u32[]{:S(2)}) copy-start(f32[1,2,2,96,128]{4,3,2,1,0:T(8,128)} %copy-done.3) | copy-start | bytes 589828
  71.2 47.0 %copy-start.6 = (f32[3,128,128]{2,1,0:T(8,128)S(1)}, f32[3,128,128]{2,1,0:T(8,128)}, u32[]{:S(2)}) copy-start(f32[3,128,128]{2,1,0:T(8,128)} %param.6) | copy-start | bytes 589828
  73.2 9.2 %collective-permute-start.7 = (f32[4,12,128]{2,0,1:T(4,128)S(1)}, f32[4,12,128]{2,0,1:T(4,128)S(1)}, u32[]{:S(2)}, u32[]{:S(2)}) collective-permute-start(f32[4,12,128]{2,0,1:T(4,128)S(1)} %add.56), channel_id=1, source_target_pairs={{0,128},{16,144},{32,160},{48,176},{64,192},{80,208},{96,224},{112... | collective-permute-start | bytes 73736 | tf_op jit(solution)/shard_map/ppermute | solution.py:71
  82.4 17.2 %collective-permute-start.8 = (f32[4,12,128]{2,0,1:T(4,128)S(1)}, f32[4,12,128]{2,0,1:T(4,128)S(1)}, u32[]{:S(2)}, u32[]{:S(2)}) collective-permute-start(f32[4,12,128]{2,0,1:T(4,128)S(1)} %add.57), channel_id=1, source_target_pairs={{0,256},{16,272},{32,288},{48,304},{64,320},{80,336},{96,352},{112... | collective-permute-start | bytes 73736 | tf_op jit(solution)/shard_map/ppermute | solution.py:71
  99.6 19.8 %collective-permute-start.9 = (f32[4,12,128]{2,0,1:T(4,128)S(1)}, f32[4,12,128]{2,0,1:T(4,128)S(1)}, u32[]{:S(2)}, u32[]{:S(2)}) collective-permute-start(f32[4,12,128]{2,0,1:T(4,128)S(1)} %add.58), channel_id=1, source_target_pairs={{0,768},{16,784},{32,800},{48,816},{64,832},{80,848},{96,864},{112... | collective-permute-start | bytes 73736 | tf_op jit(solution)/shard_map/ppermute | solution.py:75
  119.4 9.5 %collective-permute-start.10 = (f32[4,12,128]{2,0,1:T(4,128)S(1)}, f32[4,12,128]{2,0,1:T(4,128)S(1)}, u32[]{:S(2)}, u32[]{:S(2)}) collective-permute-start(f32[4,12,128]{2,0,1:T(4,128)S(1)} %add.59), channel_id=1, source_target_pairs={{0,16},{16,0},{32,48},{48,32},{64,80},{80,64},{96,112},{112,96},{1... | collective-permute-start | bytes 73736 | tf_op jit(solution)/shard_map/ppermute | solution.py:89

commit v12 on v9

--- a/solution.py
+++ b/solution.py
@@ -117,7 +117,8 @@
     spatial_terms = jnp.einsum(
         "tfrwc,frwd->dtc", shifted(padded, offsets, strip, width), dpre, precision=HIGH
     )
-    temporal_terms = jnp.einsum("kfrwc,frwd->dkc", lagged, cotangent, precision=HIGH)
+    leading = jnp.stack([grad_long[k : k + nframes] for k in range(3)])
+    temporal_terms = jnp.einsum("frwc,kfrwd->dkc", act, leading, precision=HIGH)
     nrows = lax.axis_size("rows")
     terms = jnp.concatenate([spatial_terms, temporal_terms], axis=1) * factor
     terms = terms.reshape(nrows, 2, chans // nrows // 2, terms.shape[1], chans)

time: 117 us -> 118 us (level)
  waiting for transfers between devices: 17.1 us -> 13.8 us
  starting transfers between devices: 86.7 us -> 89.2 us
  other arithmetic: 4.24 us -> 5.92 us
    another operation x2, other arithmetic: 0.08 us -> 1.76 us  [per_device(): lagged = jnp.stack([longer[2 - k:2 - k + nframes] for k in range(3)])]
    ppermute x4, waiting for transfers between devices: 5.65 us -> 4.24 us  [doubling_sum(): value = value + lax.ppermute(value, axis, pairs)]
  transfers between devices with their start and end apart: 14 -> 14, of which waited for: 7 -> 7; matrix products, arithmetic and copies ran while one was open for 5% -> 10% of each run, Pallas kernels for 0% -> 0%
where the time goes in v12:
time: 118 us
  starting transfers between devices  89.2 us (76%)
  waiting for transfers between devices  13.8 us (12%)
  other arithmetic  5.92 us (5%)
  matrix products  4.86 us (4%)
  local copies, waits for them, and re-layouts  2.77 us (2%)
    ppermute x4, starting transfers between devices, doubling_sum(): value = value + lax.ppermute(value, axis, pairs)  31 us
    ppermute x1, starting transfers between devices, doubling_sum(): return value + lax.ppermute(value, axis, pairs)  15.5 us
    ppermute x2, starting transfers between devices, passed_along(): return lax.ppermute(value, axis, pairs)  15.3 us
    ppermute x1, starting transfers between devices, pair_gather(): other = lax.ppermute(value, axis, [(i, i ^ 1) for i in range(count)])  9.05 us
    all_to_all x1, waiting for transfers between devices, per_device(): terms = lax.all_to_all(terms, 'rows', 0, 0, tiled=True).sum(axis=0)  8.39 us
    ppermute x2, starting transfers between devices, padded_2(): before = lax.ppermute(last, axis, up)  8.22 us
    ppermute x4, waiting for transfers between devices, doubling_sum(): value = value + lax.ppermute(value, axis, pairs)  4.24 us
    all_to_all x1, starting transfers between devices, per_device(): terms = lax.all_to_all(terms, 'rows', 0, 0, tiled=True).sum(axis=0)  4.21 us
  transfers between devices with their start and end apart: 14, of which 7 were waited for; matrix products, arithmetic and copies ran while one was open for 10% of the time, Pallas kernels for 0%

profile of v12, /device:TPU:1, one launch (start us, length us, event | category | flops | bytes accessed | tf_op | source)
XLA Modules:
  0.0 117.7 jit_solution(4331140265356494723)
XLA Ops:
  0.6 0.0 copy-start
  0.6 0.0 copy-start.1
  0.7 1.0 fusion.42
  1.7 4.0 %collective-permute-start = (f32[2,1,96,128]{3,2,1,0:T(8,128)S(1)}, f32[2,1,96,128]{3,2,1,0:T(8,128)S(1)}, u32[]{:S(2)}, u32[]{:S(2)}) collective-permute-start(f32[2,1,96,128]{3,2,1,0:T(8,128)S(1)} %get-tuple-element.10), channel_id=1, source_target_pairs={{0,1},{1,2},{2,3},{3,4},{4,5},{5,6},{6,7},{7,8},{8,9},{9,10},{10,1... | collective-permute-start | bytes 294920 | tf_op jit(solution)/shard_map/ppermute | solution.py:18
  5.7 1.3 %collective-permute-start.1 = (f32[2,1,96,128]{3,2,1,0:T(8,128)S(1)}, f32[2,1,96,128]{3,2,1,0:T(8,128)S(1)}, u32[]{:S(2)}, u32[]{:S(2)}) collective-permute-start(f32[2,1,96,128]{3,2,1,0:T(8,128)S(1)} %get-tuple-element.11), channel_id=1, source_target_pairs={{1,0},{2,1},{3,2},{4,3},{5,4},{6,5},{7,6},{8,7},{9,8},{10,9},{11,1... | collective-permute-start | bytes 294920 | tf_op jit(solution)/shard_map/ppermute | solution.py:19
  7.0 13.4 %collective-permute-start.3 = (f32[2,2,96,128]{3,2,1,0:T(8,128)}, f32[2,2,96,128]{3,2,1,0:T(8,128)S(1)}, u32[]{:S(2)}, u32[]{:S(2)}) collective-permute-start(f32[2,2,96,128]{3,2,1,0:T(8,128)} %param.7), channel_id=1, source_target_pairs={{16,0},{32,16},{48,32},{64,48},{80,64},{96,80},{112,96},{128,112},... | collective-permute-start | bytes 589832 | tf_op jit(solution)/shard_map/ppermute | solution.py:27
  20.4 0.0 collective-permute-done.1
  20.4 1.0 select_maximum_fusion.2
  21.6 0.0 copy-start.2
  21.7 0.8 convolution_bitcast_fusion.1
  22.5 0.0 copy-start.4
  22.5 0.8 fusion.40
  23.3 1.9 %collective-permute-start.2 = (f32[2,2,96,128]{3,2,1,0:T(8,128)}, f32[2,2,96,128]{3,2,1,0:T(8,128)}, u32[]{:S(2)}, u32[]{:S(2)}) collective-permute-start(f32[2,2,96,128]{3,2,1,0:T(8,128)} %get-tuple-element.9), channel_id=1, source_target_pairs={{0,16},{16,32},{32,48},{48,64},{64,80},{80,96},{96,112},{112,128},... | collective-permute-start | bytes 589832 | tf_op jit(solution)/shard_map/ppermute | solution.py:27
  25.3 0.7 fusion.7
  26.0 0.4 fusion.3
  26.4 0.8 fusion.30
  27.2 4.3 %collective-permute-start.4 = (f32[2,1,96,128]{3,2,1,0:T(8,128)S(1)}, f32[2,1,96,128]{3,2,1,0:T(8,128)S(1)}, u32[]{:S(2)}, u32[]{:S(2)}) collective-permute-start(f32[2,1,96,128]{3,2,1,0:T(8,128)S(1)} %get-tuple-element.6), channel_id=1, source_target_pairs={{0,1},{1,2},{2,3},{3,4},{4,5},{5,6},{6,7},{7,8},{8,9},{9,10},{10,1... | collective-permute-start | bytes 294920 | tf_op jit(solution)/shard_map/ppermute | solution.py:18
  31.5 1.3 %collective-permute-start.5 = (f32[2,1,96,128]{3,2,1,0:T(8,128)S(1)}, f32[2,1,96,128]{3,2,1,0:T(8,128)S(1)}, u32[]{:S(2)}, u32[]{:S(2)}) collective-permute-start(f32[2,1,96,128]{3,2,1,0:T(8,128)S(1)} %get-tuple-element.7), channel_id=1, source_target_pairs={{1,0},{2,1},{3,2},{4,3},{5,4},{6,5},{7,6},{8,7},{9,8},{10,9},{11,1... | collective-permute-start | bytes 294920 | tf_op jit(solution)/shard_map/ppermute | solution.py:19
  32.8 0.3 maximum_multiply_fusion
  33.0 0.1 constant_dynamic-slice_fusion.1
  33.2 0.1 copy.57
  33.3 3.3 %collective-permute-start.6 = (f32[16,4,12,128]{3,1,2,0:T(4,128)S(1)}, f32[16,4,12,128]{3,1,2,0:T(4,128)S(1)}, u32[]{:S(2)}, u32[]{:S(2)}) collective-permute-start(f32[16,4,12,128]{3,1,2,0:T(4,128)S(1)} %bitcast.162), channel_id=1, source_target_pairs={{0,16},{16,0},{32,48},{48,32},{64,80},{80,64},{96,112},{112,96},{1... | collective-permute-start | bytes 1179656 | tf_op jit(solution)/shard_map/ppermute | solution.py:129
  36.6 0.0 collective-permute-done.4
  36.6 0.2 collective-permute-done.5
  37.0 1.0 collective-permute-done.6
  37.9 0.9 bitcast_add_fusion
  38.8 4.2 %all-to-all-start = ((f32[16,4,12,128]{3,1,2,0:T(4,128)}), f32[16,4,12,128]{3,1,2,0:T(4,128)}, u32[]{:S(2)}, u32[]{:S(2)}) async-start(f32[16,4,12,128]{3,1,2,0:T(4,128)} %bitcast_add_fusion), calls=%async_computation | async-start | bytes 786432 | tf_op jit(solution)/shard_map/all_to_all | solution.py:130
  43.1 8.4 %all-to-all-done = f32[16,4,12,128]{3,1,2,0:T(4,128)} async-done(((f32[16,4,12,128]{3,1,2,0:T(4,128)}), f32[16,4,12,128]{3,1,2,0:T(4,128)}, u32[]{:S(2)}, u32[]{:S(2)}) %all-to-all-start) | async-done | bytes 393248 | tf_op jit(solution)/shard_map/all_to_all | solution.py:130
  51.5 1.1 reduce_sum.9
  52.5 2.0 %collective-permute-start.7 = (f32[4,12,128]{2,0,1:T(4,128)S(1)}, f32[4,12,128]{2,0,1:T(4,128)S(1)}, u32[]{:S(2)}, u32[]{:S(2)}) collective-permute-start(f32[4,12,128]{2,0,1:T(4,128)S(1)} %reduce_sum.9), channel_id=1, source_target_pairs={{0,32},{16,48},{32,0},{48,16},{64,96},{80,112},{96,64},{112,80},{1... | collective-permute-start | bytes 73736 | tf_op jit(solution)/shard_map/ppermute | solution.py:71
  54.6 2.5 %collective-permute-done.7 = f32[4,12,128]{2,0,1:T(4,128)S(1)} collective-permute-done((f32[4,12,128]{2,0,1:T(4,128)S(1)}, f32[4,12,128]{2,0,1:T(4,128)S(1)}, u32[]{:S(2)}, u32[]{:S(2)}) %collective-permute-start.7) | collective-permute-done | bytes 24608 | tf_op jit(solution)/shard_map/ppermute | solution.py:71
  57.1 4.7 %collective-permute-start.8 = (f32[4,12,128]{2,0,1:T(4,128)S(1)}, f32[4,12,128]{2,0,1:T(4,128)S(1)}, u32[]{:S(2)}, u32[]{:S(2)}) collective-permute-start(f32[4,12,128]{2,0,1:T(4,128)S(1)} %add.55), channel_id=1, source_target_pairs={{0,64},{16,80},{32,96},{48,112},{64,0},{80,16},{96,32},{112,48},{1... | collective-permute-start | bytes 73736 | tf_op jit(solution)/shard_map/ppermute | solution.py:71
  61.9 0.0 copy-start.3
  61.9 0.0 copy-start.5
  61.9 1.2 collective-permute-done.8
  63.1 8.8 %collective-permute-start.9 = (f32[4,12,128]{2,0,1:T(4,128)S(1)}, f32[4,12,128]{2,0,1:T(4,128)S(1)}, u32[]{:S(2)}, u32[]{:S(2)}) collective-permute-start(f32[4,12,128]{2,0,1:T(4,128)S(1)} %add.56), channel_id=1, source_target_pairs={{0,128},{16,144},{32,160},{48,176},{64,192},{80,208},{96,224},{112... | collective-permute-start | bytes 73736 | tf_op jit(solution)/shard_map/ppermute | solution.py:71
  71.9 0.9 fusion
  72.8 0.3 collective-permute-done.9
  73.1 15.4 %collective-permute-start.10 = (f32[4,12,128]{2,0,1:T(4,128)S(1)}, f32[4,12,128]{2,0,1:T(4,128)S(1)}, u32[]{:S(2)}, u32[]{:S(2)}) collective-permute-start(f32[4,12,128]{2,0,1:T(4,128)S(1)} %add.57), channel_id=1, source_target_pairs={{0,256},{16,272},{32,288},{48,304},{64,320},{80,336},{96,352},{112... | collective-permute-start | bytes 73736 | tf_op jit(solution)/shard_map/ppermute | solution.py:71
  88.6 1.0 fusion.19
  89.5 0.2 collective-permute-done.10
  89.8 15.5 %collective-permute-start.11 = (f32[4,12,128]{2,0,1:T(4,128)S(1)}, f32[4,12,128]{2,0,1:T(4,128)S(1)}, u32[]{:S(2)}, u32[]{:S(2)}) collective-permute-start(f32[4,12,128]{2,0,1:T(4,128)S(1)} %add.58), channel_id=1, source_target_pairs={{0,768},{16,784},{32,800},{48,816},{64,832},{80,848},{96,864},{112... | collective-permute-start | bytes 73736 | tf_op jit(solution)/shard_map/ppermute | solution.py:75
  105.2 1.3 %fusion.4 = f32[2,2,96,128,1]{3,2,0,1,4:T(8,128)S(1)} fusion(f32[3,128,128]{2,1,0:T(8,128)S(1)} %copy-done.5, f32[1,2,2,96,128]{4,3,2,1,0:T(8,128)} %bitcast.21, f32[1,2,2,96,128]{4,3,2,1,0:T(8,128)S(1)} %fusion.19, f32[1,2,2,96,128]{4,3,2,1,0:T(8,128)S(1)} %copy-done.3), kind=kOutput, calls=%fused_computation.11 | convolution fusion | flops 113541120 | bytes 983040 | tf_op jit(solution)/shard_map/kfrwc,kcd->frwd/dot_general | solution.py:107
  106.6 9.0 %collective-permute-start.12 = (f32[4,12,128]{2,0,1:T(4,128)S(1)}, f32[4,12,128]{2,0,1:T(4,128)S(1)}, u32[]{:S(2)}, u32[]{:S(2)}) collective-permute-start(f32[4,12,128]{2,0,1:T(4,128)S(1)} %add.59), channel_id=1, source_target_pairs={{0,16},{16,0},{32,48},{48,32},{64,80},{80,64},{96,112},{112,96},{1... | collective-permute-start | bytes 73736 | tf_op jit(solution)/shard_map/ppermute | solution.py:89
  115.6 0.8 bitcast_add_fusion.1
  116.4 0.0 collective-permute-done.12
  116.5 0.6 slice.133
  117.1 0.6 slice.132
  (37 shorter events, 0.5 us)
Async XLA Ops:
  0.6 21.0 %copy-start = (f32[3,3,128,128]{3,2,1,0:T(8,128)S(1)}, f32[3,3,128,128]{3,2,1,0:T(8,128)}, u32[]{:S(2)}) copy-start(f32[3,3,128,128]{3,2,1,0:T(8,128)} %param.5) | copy-start | bytes 1769476
  0.6 20.8 %copy-start.1 = (f32[2,2,96,128]{3,2,1,0:T(8,128)S(1)}, f32[2,2,96,128]{3,2,1,0:T(8,128)}, u32[]{:S(2)}) copy-start(f32[2,2,96,128]{3,2,1,0:T(8,128)} %param.4) | copy-start | bytes 589828
  1.7 18.7 %collective-permute-start = (f32[2,1,96,128]{3,2,1,0:T(8,128)S(1)}, f32[2,1,96,128]{3,2,1,0:T(8,128)S(1)}, u32[]{:S(2)}, u32[]{:S(2)}) collective-permute-start(f32[2,1,96,128]{3,2,1,0:T(8,128)S(1)} %get-tuple-element.10), channel_id=1, source_target_pairs={{0,1},{1,2},{2,3},{3,4},{4,5},{5,6},{6,7},{7,8},{8,9},{9,10},{10,1... | collective-permute-start | bytes 294920 | tf_op jit(solution)/shard_map/ppermute | solution.py:18
  5.7 14.8 %collective-permute-start.1 = (f32[2,1,96,128]{3,2,1,0:T(8,128)S(1)}, f32[2,1,96,128]{3,2,1,0:T(8,128)S(1)}, u32[]{:S(2)}, u32[]{:S(2)}) collective-permute-start(f32[2,1,96,128]{3,2,1,0:T(8,128)S(1)} %get-tuple-element.11), channel_id=1, source_target_pairs={{1,0},{2,1},{3,2},{4,3},{5,4},{6,5},{7,6},{8,7},{9,8},{10,9},{11,1... | collective-permute-start | bytes 294920 | tf_op jit(solution)/shard_map/ppermute | solution.py:19
  7.0 18.3 %collective-permute-start.3 = (f32[2,2,96,128]{3,2,1,0:T(8,128)}, f32[2,2,96,128]{3,2,1,0:T(8,128)S(1)}, u32[]{:S(2)}, u32[]{:S(2)}) collective-permute-start(f32[2,2,96,128]{3,2,1,0:T(8,128)} %param.7), channel_id=1, source_target_pairs={{16,0},{32,16},{48,32},{64,48},{80,64},{96,80},{112,96},{128,112},... | collective-permute-start | bytes 589832 | tf_op jit(solution)/shard_map/ppermute | solution.py:27
  21.6 3.7 %copy-start.2 = (f32[2,2,96,128]{3,2,1,0:T(8,128)S(1)}, f32[2,2,96,128]{3,2,1,0:T(8,128)}, u32[]{:S(2)}) copy-start(f32[2,2,96,128]{3,2,1,0:T(8,128)} %param.7) | copy-start | bytes 589828
  22.5 3.4 %copy-start.4 = (f32[3,128,128]{2,1,0:T(8,128)S(1)}, f32[3,128,128]{2,1,0:T(8,128)}, u32[]{:S(2)}) copy-start(f32[3,128,128]{2,1,0:T(8,128)} %param.6) | copy-start | bytes 589828
  23.3 65.2 %collective-permute-start.2 = (f32[2,2,96,128]{3,2,1,0:T(8,128)}, f32[2,2,96,128]{3,2,1,0:T(8,128)}, u32[]{:S(2)}, u32[]{:S(2)}) collective-permute-start(f32[2,2,96,128]{3,2,1,0:T(8,128)} %get-tuple-element.9), channel_id=1, source_target_pairs={{0,16},{16,32},{32,48},{48,64},{64,80},{80,96},{96,112},{112,128},... | collective-permute-start | bytes 589832 | tf_op jit(solution)/shard_map/ppermute | solution.py:27
  27.2 9.4 %collective-permute-start.4 = (f32[2,1,96,128]{3,2,1,0:T(8,128)S(1)}, f32[2,1,96,128]{3,2,1,0:T(8,128)S(1)}, u32[]{:S(2)}, u32[]{:S(2)}) collective-permute-start(f32[2,1,96,128]{3,2,1,0:T(8,128)S(1)} %get-tuple-element.6), channel_id=1, source_target_pairs={{0,1},{1,2},{2,3},{3,4},{4,5},{5,6},{6,7},{7,8},{8,9},{9,10},{10,1... | collective-permute-start | bytes 294920 | tf_op jit(solution)/shard_map/ppermute | solution.py:18
  31.5 5.4 %collective-permute-start.5 = (f32[2,1,96,128]{3,2,1,0:T(8,128)S(1)}, f32[2,1,96,128]{3,2,1,0:T(8,128)S(1)}, u32[]{:S(2)}, u32[]{:S(2)}) collective-permute-start(f32[2,1,96,128]{3,2,1,0:T(8,128)S(1)} %get-tuple-element.7), channel_id=1, source_target_pairs={{1,0},{2,1},{3,2},{4,3},{5,4},{6,5},{7,6},{8,7},{9,8},{10,9},{11,1... | collective-permute-start | bytes 294920 | tf_op jit(solution)/shard_map/ppermute | solution.py:19
  33.3 4.7 %collective-permute-start.6 = (f32[16,4,12,128]{3,1,2,0:T(4,128)S(1)}, f32[16,4,12,128]{3,1,2,0:T(4,128)S(1)}, u32[]{:S(2)}, u32[]{:S(2)}) collective-permute-start(f32[16,4,12,128]{3,1,2,0:T(4,128)S(1)} %bitcast.162), channel_id=1, source_target_pairs={{0,16},{16,0},{32,48},{48,32},{64,80},{80,64},{96,112},{112,96},{1... | collective-permute-start | bytes 1179656 | tf_op jit(solution)/shard_map/ppermute | solution.py:129
  38.8 12.7 %all-to-all-start = ((f32[16,4,12,128]{3,1,2,0:T(4,128)}), f32[16,4,12,128]{3,1,2,0:T(4,128)}, u32[]{:S(2)}, u32[]{:S(2)}) async-start(f32[16,4,12,128]{3,1,2,0:T(4,128)} %bitcast_add_fusion), calls=%async_computation | async-start | bytes 786432 | tf_op jit(solution)/shard_map/all_to_all | solution.py:130
  52.5 4.6 %collective-permute-start.7 = (f32[4,12,128]{2,0,1:T(4,128)S(1)}, f32[4,12,128]{2,0,1:T(4,128)S(1)}, u32[]{:S(2)}, u32[]{:S(2)}) collective-permute-start(f32[4,12,128]{2,0,1:T(4,128)S(1)} %reduce_sum.9), channel_id=1, source_target_pairs={{0,32},{16,48},{32,0},{48,16},{64,96},{80,112},{96,64},{112,80},{1... | collective-permute-start | bytes 73736 | tf_op jit(solution)/shard_map/ppermute | solution.py:71
  57.1 5.9 %collective-permute-start.8 = (f32[4,12,128]{2,0,1:T(4,128)S(1)}, f32[4,12,128]{2,0,1:T(4,128)S(1)}, u32[]{:S(2)}, u32[]{:S(2)}) collective-permute-start(f32[4,12,128]{2,0,1:T(4,128)S(1)} %add.55), channel_id=1, source_target_pairs={{0,64},{16,80},{32,96},{48,112},{64,0},{80,16},{96,32},{112,48},{1... | collective-permute-start | bytes 73736 | tf_op jit(solution)/shard_map/ppermute | solution.py:71
  61.9 43.4 %copy-start.3 = (f32[1,2,2,96,128]{4,3,2,1,0:T(8,128)S(1)}, f32[1,2,2,96,128]{4,3,2,1,0:T(8,128)}, u32[]{:S(2)}) copy-start(f32[1,2,2,96,128]{4,3,2,1,0:T(8,128)} %get-tuple-element.8) | copy-start | bytes 589828
  61.9 43.4 %copy-start.5 = (f32[3,128,128]{2,1,0:T(8,128)S(1)}, f32[3,128,128]{2,1,0:T(8,128)}, u32[]{:S(2)}) copy-start(f32[3,128,128]{2,1,0:T(8,128)} %param.6) | copy-start | bytes 589828
  63.1 10.0 %collective-permute-start.9 = (f32[4,12,128]{2,0,1:T(4,128)S(1)}, f32[4,12,128]{2,0,1:T(4,128)S(1)}, u32[]{:S(2)}, u32[]{:S(2)}) collective-permute-start(f32[4,12,128]{2,0,1:T(4,128)S(1)} %add.56), channel_id=1, source_target_pairs={{0,128},{16,144},{32,160},{48,176},{64,192},{80,208},{96,224},{112... | collective-permute-start | bytes 73736 | tf_op jit(solution)/shard_map/ppermute | solution.py:71
  73.1 16.7 %collective-permute-start.10 = (f32[4,12,128]{2,0,1:T(4,128)S(1)}, f32[4,12,128]{2,0,1:T(4,128)S(1)}, u32[]{:S(2)}, u32[]{:S(2)}) collective-permute-start(f32[4,12,128]{2,0,1:T(4,128)S(1)} %add.57), channel_id=1, source_target_pairs={{0,256},{16,272},{32,288},{48,304},{64,320},{80,336},{96,352},{112... | collective-permute-start | bytes 73736 | tf_op jit(solution)/shard_map/ppermute | solution.py:71
  89.8 16.8 %collective-permute-start.11 = (f32[4,12,128]{2,0,1:T(4,128)S(1)}, f32[4,12,128]{2,0,1:T(4,128)S(1)}, u32[]{:S(2)}, u32[]{:S(2)}) collective-permute-start(f32[4,12,128]{2,0,1:T(4,128)S(1)} %add.58), channel_id=1, source_target_pairs={{0,768},{16,784},{32,800},{48,816},{64,832},{80,848},{96,864},{112... | collective-permute-start | bytes 73736 | tf_op jit(solution)/shard_map/ppermute | solution.py:75
  106.6 9.9 %collective-permute-start.12 = (f32[4,12,128]{2,0,1:T(4,128)S(1)}, f32[4,12,128]{2,0,1:T(4,128)S(1)}, u32[]{:S(2)}, u32[]{:S(2)}) collective-permute-start(f32[4,12,128]{2,0,1:T(4,128)S(1)} %add.59), channel_id=1, source_target_pairs={{0,16},{16,0},{32,48},{48,32},{64,80},{80,64},{96,112},{112,96},{1... | collective-permute-start | bytes 73736 | tf_op jit(solution)/shard_map/ppermute | solution.py:89

commit v13 on v9

--- a/solution.py
+++ b/solution.py
@@ -121,12 +121,12 @@
     nrows = lax.axis_size("rows")
     terms = jnp.concatenate([spatial_terms, temporal_terms], axis=1) * factor
     terms = terms.reshape(nrows, 2, chans // nrows // 2, terms.shape[1], chans)
+    terms = lax.all_to_all(terms, "rows", 0, 0, tiled=True).sum(axis=0)
     parity = lax.axis_index("frames") % 2
-    keep = lax.dynamic_index_in_dim(terms, parity, axis=1, keepdims=False)
-    give = lax.dynamic_index_in_dim(terms, 1 - parity, axis=1, keepdims=False)
+    keep = lax.dynamic_index_in_dim(terms, parity, axis=0, keepdims=False)
+    give = lax.dynamic_index_in_dim(terms, 1 - parity, axis=0, keepdims=False)
     nframes_all = lax.axis_size("frames")
     terms = keep + lax.ppermute(give, "frames", [(i, i ^ 1) for i in range(nframes_all)])
-    terms = lax.all_to_all(terms, "rows", 0, 0, tiled=True).sum(axis=0)
     summed = pair_gather(doubling_sum(terms, "frames", 2), "frames")
     summed = jnp.transpose(summed, (1, 2, 0))
     grad_spatial = summed[:9].reshape(3, 3, chans, summed.shape[2])

time: 117 us -> 119 us (1.017)
  local copies, waits for them, and re-layouts: 3.06 us -> 7.93 us
  waiting for transfers between devices: 17.1 us -> 14 us
  matrix products: 3.69 us -> 5.16 us
    unnamed x34 -> x20, local copies, waits for them, and re-layouts: 0.52 us -> 4.29 us
    ppermute x4, waiting for transfers between devices: 5.65 us -> 3 us  [doubling_sum(): value = value + lax.ppermute(value, axis, pairs)]
    ppermute x1, starting transfers between devices: 8.87 us -> 7.24 us  [pair_gather(): other = lax.ppermute(value, axis, [(i, i ^ 1) for i in range(count)])]
    ppermute x1, starting transfers between devices: 2.69 us -> 4.27 us  [per_device(): lax.ppermute(give, 'frames', [(i, i ^ 1) for i in range(nframes_all)])]
    dot_general x1, matrix products: 0.86 us -> 2.34 us  [per_device(): jnp.einsum('tfrwd,tcd->frwc', shifted(dpre_wide, back, strip, width), spa...]
    unnamed x4, other arithmetic: 0.06 us -> 1.42 us
  transfers between devices with their start and end apart: 14 -> 14, of which waited for: 7 -> 6; matrix products, arithmetic and copies ran while one was open for 5% -> 13% of each run, Pallas kernels for 0% -> 0%
where the time goes in v13:
time: 119 us
  starting transfers between devices  86 us (72%)
  waiting for transfers between devices  14 us (12%)
  local copies, waits for them, and re-layouts  7.93 us (7%)
  matrix products  5.16 us (4%)
  other arithmetic  4.68 us (4%)
    ppermute x4, starting transfers between devices, doubling_sum(): value = value + lax.ppermute(value, axis, pairs)  29.9 us
    ppermute x2, starting transfers between devices, passed_along(): return lax.ppermute(value, axis, pairs)  15.3 us
    ppermute x1, starting transfers between devices, doubling_sum(): return value + lax.ppermute(value, axis, pairs)  14.7 us
    all_to_all x1, waiting for transfers between devices, per_device(): terms = lax.all_to_all(terms, 'rows', 0, 0, tiled=True).sum(axis=0)  9.53 us
    ppermute x2, starting transfers between devices, padded_2(): before = lax.ppermute(last, axis, up)  8.2 us
    ppermute x1, starting transfers between devices, pair_gather(): other = lax.ppermute(value, axis, [(i, i ^ 1) for i in range(count)])  7.24 us
    unnamed x20, local copies, waits for them, and re-layouts  4.29 us
    ppermute x1, starting transfers between devices, per_device(): lax.ppermute(give, 'frames', [(i, i ^ 1) for i in range(nframes_all)])  4.27 us
  transfers between devices with their start and end apart: 14, of which 6 were waited for; matrix products, arithmetic and copies ran while one was open for 13% of the time, Pallas kernels for 0%

profile of v13, /device:TPU:1, one launch (start us, length us, event | category | flops | bytes accessed | tf_op | source)
XLA Modules:
  0.0 118.8 jit_solution(11418238565311799986)
XLA Ops:
  0.6 0.0 copy-start
  0.6 0.0 copy-start.1
  0.7 1.0 fusion.45
  1.7 4.0 %collective-permute-start = (f32[2,1,96,128]{3,2,1,0:T(8,128)S(1)}, f32[2,1,96,128]{3,2,1,0:T(8,128)S(1)}, u32[]{:S(2)}, u32[]{:S(2)}) collective-permute-start(f32[2,1,96,128]{3,2,1,0:T(8,128)S(1)} %get-tuple-element.8), channel_id=1, source_target_pairs={{0,1},{1,2},{2,3},{3,4},{4,5},{5,6},{6,7},{7,8},{8,9},{9,10},{10,1... | collective-permute-start | bytes 294920 | tf_op jit(solution)/shard_map/ppermute | solution.py:18
  5.7 1.3 %collective-permute-start.1 = (f32[2,1,96,128]{3,2,1,0:T(8,128)S(1)}, f32[2,1,96,128]{3,2,1,0:T(8,128)S(1)}, u32[]{:S(2)}, u32[]{:S(2)}) collective-permute-start(f32[2,1,96,128]{3,2,1,0:T(8,128)S(1)} %get-tuple-element.9), channel_id=1, source_target_pairs={{1,0},{2,1},{3,2},{4,3},{5,4},{6,5},{7,6},{8,7},{9,8},{10,9},{11,1... | collective-permute-start | bytes 294920 | tf_op jit(solution)/shard_map/ppermute | solution.py:19
  7.0 13.4 %collective-permute-start.3 = (f32[2,2,96,128]{3,2,1,0:T(8,128)}, f32[2,2,96,128]{3,2,1,0:T(8,128)S(1)}, u32[]{:S(2)}, u32[]{:S(2)}) collective-permute-start(f32[2,2,96,128]{3,2,1,0:T(8,128)} %param.7), channel_id=1, source_target_pairs={{16,0},{32,16},{48,32},{64,48},{80,64},{96,80},{112,96},{128,112},... | collective-permute-start | bytes 589832 | tf_op jit(solution)/shard_map/ppermute | solution.py:27
  20.4 1.0 select_maximum_fusion.2
  21.6 0.0 copy-start.2
  21.7 0.8 convolution_bitcast_fusion.1
  22.5 0.1 fusion.43
  22.6 1.9 %collective-permute-start.2 = (f32[2,2,96,128]{3,2,1,0:T(8,128)S(1)}, f32[2,2,96,128]{3,2,1,0:T(8,128)S(1)}, u32[]{:S(2)}, u32[]{:S(2)}) collective-permute-start(f32[2,2,96,128]{3,2,1,0:T(8,128)S(1)} %get-tuple-element.7), channel_id=1, source_target_pairs={{0,16},{16,32},{32,48},{48,64},{64,80},{80,96},{96,112},{112,128},... | collective-permute-start | bytes 589832 | tf_op jit(solution)/shard_map/ppermute | solution.py:27
  24.6 0.4 fusion.3
  25.0 0.7 fusion.44
  25.7 4.3 %collective-permute-start.4 = (f32[2,1,96,128]{3,2,1,0:T(8,128)}, f32[2,1,96,128]{3,2,1,0:T(8,128)S(1)}, u32[]{:S(2)}, u32[]{:S(2)}) collective-permute-start(f32[2,1,96,128]{3,2,1,0:T(8,128)} %get-tuple-element.4), channel_id=1, source_target_pairs={{0,1},{1,2},{2,3},{3,4},{4,5},{5,6},{6,7},{7,8},{8,9},{9,10},{10,1... | collective-permute-start | bytes 294920 | tf_op jit(solution)/shard_map/ppermute | solution.py:18
  29.9 1.3 %collective-permute-start.5 = (f32[2,1,96,128]{3,2,1,0:T(8,128)S(1)}, f32[2,1,96,128]{3,2,1,0:T(8,128)S(1)}, u32[]{:S(2)}, u32[]{:S(2)}) collective-permute-start(f32[2,1,96,128]{3,2,1,0:T(8,128)S(1)} %get-tuple-element.5), channel_id=1, source_target_pairs={{1,0},{2,1},{3,2},{4,3},{5,4},{6,5},{7,6},{8,7},{9,8},{10,9},{11,1... | collective-permute-start | bytes 294920 | tf_op jit(solution)/shard_map/ppermute | solution.py:19
  31.2 0.8 fusion.36
  32.0 0.4 fusion.34
  32.4 1.2 copy_multiply_fusion
  33.6 3.8 %all-to-all-start = ((f32[16,2,4,12,128]{4,2,1,3,0:T(4,128)}), f32[16,2,4,12,128]{4,2,1,3,0:T(4,128)S(1)}, u32[]{:S(2)}, u32[]{:S(2)}) async-start(f32[16,2,4,12,128]{4,2,1,3,0:T(4,128)} %copy_multiply_fusion), calls=%async_computation | async-start | bytes 1572864 | tf_op jit(solution)/shard_map/all_to_all | solution.py:124
  37.5 0.7 fusion.21
  38.2 0.7 fusion.20
  38.9 0.7 fusion.18
  39.6 0.7 fusion.17
  40.3 0.7 bitcast_dynamic-update-slice_fusion
  40.9 9.5 %all-to-all-done = f32[16,2,4,12,128]{4,2,1,3,0:T(4,128)S(1)} async-done(((f32[16,2,4,12,128]{4,2,1,3,0:T(4,128)}), f32[16,2,4,12,128]{4,2,1,3,0:T(4,128)S(1)}, u32[]{:S(2)}, u32[]{:S(2)}) %all-to-all-start) | async-done | bytes 786464 | tf_op jit(solution)/shard_map/all_to_all | solution.py:124
  50.5 0.1 reduce_sum.9
  50.6 4.3 %collective-permute-start.6 = (f32[4,12,128]{2,0,1:T(4,128)S(1)}, f32[4,12,128]{2,0,1:T(4,128)S(1)}, u32[]{:S(2)}, u32[]{:S(2)}) collective-permute-start(f32[4,12,128]{2,0,1:T(4,128)S(1)} %dynamic-slice_bitcast_fusion), channel_id=1, source_target_pairs={{0,16},{16,0},{32,48},{48,32},{64,80},{80,64},{96,112},{112,96},{1... | collective-permute-start | bytes 73736 | tf_op jit(solution)/shard_map/ppermute | solution.py:129
  54.9 0.7 fusion.16
  55.6 0.1 collective-permute-done.6
  55.7 2.4 %collective-permute-start.7 = (f32[4,12,128]{2,0,1:T(4,128)S(1)}, f32[4,12,128]{2,0,1:T(4,128)S(1)}, u32[]{:S(2)}, u32[]{:S(2)}) collective-permute-start(f32[4,12,128]{2,0,1:T(4,128)S(1)} %bitcast_add_fusion.2), channel_id=1, source_target_pairs={{0,32},{16,48},{32,0},{48,16},{64,96},{80,112},{96,64},{112,80},{1... | collective-permute-start | bytes 73736 | tf_op jit(solution)/shard_map/ppermute | solution.py:71
  58.2 0.7 fusion.15
  58.9 1.5 %collective-permute-done.7 = f32[4,12,128]{2,0,1:T(4,128)S(1)} collective-permute-done((f32[4,12,128]{2,0,1:T(4,128)S(1)}, f32[4,12,128]{2,0,1:T(4,128)S(1)}, u32[]{:S(2)}, u32[]{:S(2)}) %collective-permute-start.7) | collective-permute-done | bytes 24608 | tf_op jit(solution)/shard_map/ppermute | solution.py:71
  60.3 3.7 %collective-permute-start.8 = (f32[4,12,128]{2,0,1:T(4,128)S(1)}, f32[4,12,128]{2,0,1:T(4,128)S(1)}, u32[]{:S(2)}, u32[]{:S(2)}) collective-permute-start(f32[4,12,128]{2,0,1:T(4,128)S(1)} %add.55), channel_id=1, source_target_pairs={{0,64},{16,80},{32,96},{48,112},{64,0},{80,16},{96,32},{112,48},{1... | collective-permute-start | bytes 73736 | tf_op jit(solution)/shard_map/ppermute | solution.py:71
  64.1 0.7 fusion.14
  64.8 1.0 collective-permute-done.8
  65.8 8.4 %collective-permute-start.9 = (f32[4,12,128]{2,0,1:T(4,128)S(1)}, f32[4,12,128]{2,0,1:T(4,128)S(1)}, u32[]{:S(2)}, u32[]{:S(2)}) collective-permute-start(f32[4,12,128]{2,0,1:T(4,128)S(1)} %add.56), channel_id=1, source_target_pairs={{0,128},{16,144},{32,160},{48,176},{64,192},{80,208},{96,224},{112... | collective-permute-start | bytes 73736 | tf_op jit(solution)/shard_map/ppermute | solution.py:71
  74.2 0.7 fusion.12
  74.9 0.5 collective-permute-done.9
  75.4 15.4 %collective-permute-start.10 = (f32[4,12,128]{2,0,1:T(4,128)S(1)}, f32[4,12,128]{2,0,1:T(4,128)S(1)}, u32[]{:S(2)}, u32[]{:S(2)}) collective-permute-start(f32[4,12,128]{2,0,1:T(4,128)S(1)} %add.57), channel_id=1, source_target_pairs={{0,256},{16,272},{32,288},{48,304},{64,320},{80,336},{96,352},{112... | collective-permute-start | bytes 73736 | tf_op jit(solution)/shard_map/ppermute | solution.py:71
  90.8 2.3 %fusion = f32[2,2,96,128,1]{3,2,0,1,4:T(8,128)S(1)} fusion(f32[9,128,128,1,1]{2,1,3,4,0:T(8,128)S(1)} %bitcast.160, f32[9,2,2,96,128]{4,3,2,1,0:T(8,128)} %fusion.12), kind=kOutput, calls=%fused_computation | convolution fusion | flops 339738624 | bytes 2555904 | tf_op jit(solution)/shard_map/tfrwd,tcd->frwc/dot_general | solution.py:111
  93.1 14.7 %collective-permute-start.11 = (f32[4,12,128]{2,0,1:T(4,128)S(1)}, f32[4,12,128]{2,0,1:T(4,128)S(1)}, u32[]{:S(2)}, u32[]{:S(2)}) collective-permute-start(f32[4,12,128]{2,0,1:T(4,128)S(1)} %add.58), channel_id=1, source_target_pairs={{0,768},{16,784},{32,800},{48,816},{64,832},{80,848},{96,864},{112... | collective-permute-start | bytes 73736 | tf_op jit(solution)/shard_map/ppermute | solution.py:75
  107.8 0.4 fusion.9
  108.2 1.3 %collective-permute-done.11 = f32[4,12,128]{2,0,1:T(4,128)S(1)} collective-permute-done((f32[4,12,128]{2,0,1:T(4,128)S(1)}, f32[4,12,128]{2,0,1:T(4,128)S(1)}, u32[]{:S(2)}, u32[]{:S(2)}) %collective-permute-start.11) | collective-permute-done | bytes 24608 | tf_op jit(solution)/shard_map/ppermute | solution.py:75
  109.5 7.2 %collective-permute-start.12 = (f32[4,12,128]{2,0,1:T(4,128)S(1)}, f32[4,12,128]{2,0,1:T(4,128)S(1)}, u32[]{:S(2)}, u32[]{:S(2)}) collective-permute-start(f32[4,12,128]{2,0,1:T(4,128)S(1)} %add.59), channel_id=1, source_target_pairs={{0,16},{16,0},{32,48},{48,32},{64,80},{80,64},{96,112},{112,96},{1... | collective-permute-start | bytes 73736 | tf_op jit(solution)/shard_map/ppermute | solution.py:89
  116.8 0.8 bitcast_add_fusion
  117.6 0.0 collective-permute-done.12
  117.6 0.6 slice.132
  118.2 0.6 slice.131
  (32 shorter events, 0.3 us)
Async XLA Ops:
  0.6 21.0 %copy-start = (f32[3,3,128,128]{3,2,1,0:T(8,128)S(1)}, f32[3,3,128,128]{3,2,1,0:T(8,128)}, u32[]{:S(2)}) copy-start(f32[3,3,128,128]{3,2,1,0:T(8,128)} %param.5) | copy-start | bytes 1769476
  0.6 20.8 %copy-start.1 = (f32[2,2,96,128]{3,2,1,0:T(8,128)S(1)}, f32[2,2,96,128]{3,2,1,0:T(8,128)}, u32[]{:S(2)}) copy-start(f32[2,2,96,128]{3,2,1,0:T(8,128)} %param.4) | copy-start | bytes 589828
  1.7 18.7 %collective-permute-start = (f32[2,1,96,128]{3,2,1,0:T(8,128)S(1)}, f32[2,1,96,128]{3,2,1,0:T(8,128)S(1)}, u32[]{:S(2)}, u32[]{:S(2)}) collective-permute-start(f32[2,1,96,128]{3,2,1,0:T(8,128)S(1)} %get-tuple-element.8), channel_id=1, source_target_pairs={{0,1},{1,2},{2,3},{3,4},{4,5},{5,6},{6,7},{7,8},{8,9},{9,10},{10,1... | collective-permute-start | bytes 294920 | tf_op jit(solution)/shard_map/ppermute | solution.py:18
  5.7 14.8 %collective-permute-start.1 = (f32[2,1,96,128]{3,2,1,0:T(8,128)S(1)}, f32[2,1,96,128]{3,2,1,0:T(8,128)S(1)}, u32[]{:S(2)}, u32[]{:S(2)}) collective-permute-start(f32[2,1,96,128]{3,2,1,0:T(8,128)S(1)} %get-tuple-element.9), channel_id=1, source_target_pairs={{1,0},{2,1},{3,2},{4,3},{5,4},{6,5},{7,6},{8,7},{9,8},{10,9},{11,1... | collective-permute-start | bytes 294920 | tf_op jit(solution)/shard_map/ppermute | solution.py:19
  7.0 17.6 %collective-permute-start.3 = (f32[2,2,96,128]{3,2,1,0:T(8,128)}, f32[2,2,96,128]{3,2,1,0:T(8,128)S(1)}, u32[]{:S(2)}, u32[]{:S(2)}) collective-permute-start(f32[2,2,96,128]{3,2,1,0:T(8,128)} %param.7), channel_id=1, source_target_pairs={{16,0},{32,16},{48,32},{64,48},{80,64},{96,80},{112,96},{128,112},... | collective-permute-start | bytes 589832 | tf_op jit(solution)/shard_map/ppermute | solution.py:27
  21.6 2.9 %copy-start.2 = (f32[2,2,96,128]{3,2,1,0:T(8,128)S(1)}, f32[2,2,96,128]{3,2,1,0:T(8,128)}, u32[]{:S(2)}) copy-start(f32[2,2,96,128]{3,2,1,0:T(8,128)} %param.7) | copy-start | bytes 589828
  21.7 2.9 %copy-start.3 = (f32[3,128,128]{2,1,0:T(8,128)S(1)}, f32[3,128,128]{2,1,0:T(8,128)}, u32[]{:S(2)}) copy-start(f32[3,128,128]{2,1,0:T(8,128)} %param.6) | copy-start | bytes 589828
  22.6 9.4 %collective-permute-start.2 = (f32[2,2,96,128]{3,2,1,0:T(8,128)S(1)}, f32[2,2,96,128]{3,2,1,0:T(8,128)S(1)}, u32[]{:S(2)}, u32[]{:S(2)}) collective-permute-start(f32[2,2,96,128]{3,2,1,0:T(8,128)S(1)} %get-tuple-element.7), channel_id=1, source_target_pairs={{0,16},{16,32},{32,48},{48,64},{64,80},{80,96},{96,112},{112,128},... | collective-permute-start | bytes 589832 | tf_op jit(solution)/shard_map/ppermute | solution.py:27
  25.7 11.8 %collective-permute-start.4 = (f32[2,1,96,128]{3,2,1,0:T(8,128)}, f32[2,1,96,128]{3,2,1,0:T(8,128)S(1)}, u32[]{:S(2)}, u32[]{:S(2)}) collective-permute-start(f32[2,1,96,128]{3,2,1,0:T(8,128)} %get-tuple-element.4), channel_id=1, source_target_pairs={{0,1},{1,2},{2,3},{3,4},{4,5},{5,6},{6,7},{7,8},{8,9},{9,10},{10,1... | collective-permute-start | bytes 294920 | tf_op jit(solution)/shard_map/ppermute | solution.py:18
  29.9 7.5 %collective-permute-start.5 = (f32[2,1,96,128]{3,2,1,0:T(8,128)S(1)}, f32[2,1,96,128]{3,2,1,0:T(8,128)S(1)}, u32[]{:S(2)}, u32[]{:S(2)}) collective-permute-start(f32[2,1,96,128]{3,2,1,0:T(8,128)S(1)} %get-tuple-element.5), channel_id=1, source_target_pairs={{1,0},{2,1},{3,2},{4,3},{5,4},{6,5},{7,6},{8,7},{9,8},{10,9},{11,1... | collective-permute-start | bytes 294920 | tf_op jit(solution)/shard_map/ppermute | solution.py:19
  33.6 16.9 %all-to-all-start = ((f32[16,2,4,12,128]{4,2,1,3,0:T(4,128)}), f32[16,2,4,12,128]{4,2,1,3,0:T(4,128)S(1)}, u32[]{:S(2)}, u32[]{:S(2)}) async-start(f32[16,2,4,12,128]{4,2,1,3,0:T(4,128)} %copy_multiply_fusion), calls=%async_computation | async-start | bytes 1572864 | tf_op jit(solution)/shard_map/all_to_all | solution.py:124
  50.6 5.1 %collective-permute-start.6 = (f32[4,12,128]{2,0,1:T(4,128)S(1)}, f32[4,12,128]{2,0,1:T(4,128)S(1)}, u32[]{:S(2)}, u32[]{:S(2)}) collective-permute-start(f32[4,12,128]{2,0,1:T(4,128)S(1)} %dynamic-slice_bitcast_fusion), channel_id=1, source_target_pairs={{0,16},{16,0},{32,48},{48,32},{64,80},{80,64},{96,112},{112,96},{1... | collective-permute-start | bytes 73736 | tf_op jit(solution)/shard_map/ppermute | solution.py:129
  55.7 4.6 %collective-permute-start.7 = (f32[4,12,128]{2,0,1:T(4,128)S(1)}, f32[4,12,128]{2,0,1:T(4,128)S(1)}, u32[]{:S(2)}, u32[]{:S(2)}) collective-permute-start(f32[4,12,128]{2,0,1:T(4,128)S(1)} %bitcast_add_fusion.2), channel_id=1, source_target_pairs={{0,32},{16,48},{32,0},{48,16},{64,96},{80,112},{96,64},{112,80},{1... | collective-permute-start | bytes 73736 | tf_op jit(solution)/shard_map/ppermute | solution.py:71
  60.3 5.5 %collective-permute-start.8 = (f32[4,12,128]{2,0,1:T(4,128)S(1)}, f32[4,12,128]{2,0,1:T(4,128)S(1)}, u32[]{:S(2)}, u32[]{:S(2)}) collective-permute-start(f32[4,12,128]{2,0,1:T(4,128)S(1)} %add.55), channel_id=1, source_target_pairs={{0,64},{16,80},{32,96},{48,112},{64,0},{80,16},{96,32},{112,48},{1... | collective-permute-start | bytes 73736 | tf_op jit(solution)/shard_map/ppermute | solution.py:71
  65.8 9.6 %collective-permute-start.9 = (f32[4,12,128]{2,0,1:T(4,128)S(1)}, f32[4,12,128]{2,0,1:T(4,128)S(1)}, u32[]{:S(2)}, u32[]{:S(2)}) collective-permute-start(f32[4,12,128]{2,0,1:T(4,128)S(1)} %add.56), channel_id=1, source_target_pairs={{0,128},{16,144},{32,160},{48,176},{64,192},{80,208},{96,224},{112... | collective-permute-start | bytes 73736 | tf_op jit(solution)/shard_map/ppermute | solution.py:71
  75.4 17.7 %collective-permute-start.10 = (f32[4,12,128]{2,0,1:T(4,128)S(1)}, f32[4,12,128]{2,0,1:T(4,128)S(1)}, u32[]{:S(2)}, u32[]{:S(2)}) collective-permute-start(f32[4,12,128]{2,0,1:T(4,128)S(1)} %add.57), channel_id=1, source_target_pairs={{0,256},{16,272},{32,288},{48,304},{64,320},{80,336},{96,352},{112... | collective-permute-start | bytes 73736 | tf_op jit(solution)/shard_map/ppermute | solution.py:71
  93.1 16.4 %collective-permute-start.11 = (f32[4,12,128]{2,0,1:T(4,128)S(1)}, f32[4,12,128]{2,0,1:T(4,128)S(1)}, u32[]{:S(2)}, u32[]{:S(2)}) collective-permute-start(f32[4,12,128]{2,0,1:T(4,128)S(1)} %add.58), channel_id=1, source_target_pairs={{0,768},{16,784},{32,800},{48,816},{64,832},{80,848},{96,864},{112... | collective-permute-start | bytes 73736 | tf_op jit(solution)/shard_map/ppermute | solution.py:75
  109.5 8.1 %collective-permute-start.12 = (f32[4,12,128]{2,0,1:T(4,128)S(1)}, f32[4,12,128]{2,0,1:T(4,128)S(1)}, u32[]{:S(2)}, u32[]{:S(2)}) collective-permute-start(f32[4,12,128]{2,0,1:T(4,128)S(1)} %add.59), channel_id=1, source_target_pairs={{0,16},{16,0},{32,48},{48,32},{64,80},{80,64},{96,112},{112,96},{1... | collective-permute-start | bytes 73736 | tf_op jit(solution)/shard_map/ppermute | solution.py:89

commit v14 on v7

--- a/solution.py
+++ b/solution.py
@@ -5,7 +5,7 @@
 from jax import lax
 from jax.sharding import PartitionSpec as P
 
-HIGH = lax.Precision.HIGHEST
+HIGH = lax.Precision.HIGH
 
 
 def padded_2(value, sides, width):
@@ -120,15 +120,16 @@
     give = lax.dynamic_index_in_dim(terms, 1 - parity, axis=1, keepdims=False)
     nframes_all = lax.axis_size("frames")
     terms = keep + lax.ppermute(give, "frames", [(i, i ^ 1) for i in range(nframes_all)])
-    terms = lax.all_to_all(terms, "rows", 0, 0, tiled=True).sum(axis=0)
-    summed = pair_gather(doubling_sum(terms, "frames", 2), "frames")
-    summed, dpre_late = lax.optimization_barrier((summed, dpre))
+    terms = lax.all_to_all(terms, "rows", 0, 0, tiled=True)
+    terms, dpre_late = lax.optimization_barrier((terms, dpre))
+    terms = terms.sum(axis=0)
     dpre_wide = widen(padded_2(dpre_late, (("rows", 1),), 1))
     back = [(2 - i, 2 - j) for i in range(3) for j in range(3)]
     spatial_taps = spatial_weight.reshape(9, chans, chans)
     grad_images = cotangent + jnp.einsum(
         "tfrwd,tcd->frwc", shifted(dpre_wide, back, strip, width), spatial_taps, precision=HIGH
     )
+    summed = pair_gather(doubling_sum(terms, "frames", 2), "frames")
     summed = jnp.transpose(summed, (1, 2, 0))
     grad_spatial = summed[:9].reshape(3, 3, chans, summed.shape[2])
     grad_temporal = summed[9:]

time: 124 us -> 113 us (0.911)
  waiting for transfers between devices: 12.1 us -> 7.18 us
  matrix products: 6.38 us -> 3.68 us
  starting transfers between devices: 85.5 us -> 83.2 us
    ppermute x1, starting transfers between devices: 18.2 us -> 15.9 us  [doubling_sum(): return value + lax.ppermute(value, axis, pairs)]
    ppermute x2, waiting for transfers between devices: 2.2 us -> 0.01 us  [padded_2(): after = lax.ppermute(leading, axis, down)]
    ppermute x4, waiting for transfers between devices: 4.84 us -> 3.22 us  [doubling_sum(): value = value + lax.ppermute(value, axis, pairs)]
  transfers between devices with their start and end apart: 13 -> 13, of which waited for: 9 -> 6; matrix products, arithmetic and copies ran while one was open for 5% -> 5% of each run, Pallas kernels for 0% -> 0%
where the time goes in v14:
time: 113 us
  starting transfers between devices  83.2 us (74%)
  blocking collectives  12.1 us (11%)
  waiting for transfers between devices  7.18 us (6%)
  matrix products  3.68 us (3%)
  local copies, waits for them, and re-layouts  2.76 us (2%)
  other arithmetic  2.49 us (2%)
  between operations  1.15 us (1%)
    ppermute x4, starting transfers between devices, doubling_sum(): value = value + lax.ppermute(value, axis, pairs)  32.7 us
    ppermute x1, starting transfers between devices, doubling_sum(): return value + lax.ppermute(value, axis, pairs)  15.9 us
    ppermute x2, starting transfers between devices, passed_along(): return lax.ppermute(value, axis, pairs)  15.3 us
    all_to_all x1, blocking collectives, per_device(): terms = lax.all_to_all(terms, 'rows', 0, 0, tiled=True)  12.1 us
    ppermute x1, starting transfers between devices, pair_gather(): other = lax.ppermute(value, axis, [(i, i ^ 1) for i in range(count)])  8.32 us
    ppermute x2, starting transfers between devices, padded_2(): before = lax.ppermute(last, axis, up)  6.14 us
    ppermute x4, waiting for transfers between devices, doubling_sum(): value = value + lax.ppermute(value, axis, pairs)  3.22 us
    ppermute x2, starting transfers between devices, padded_2(): after = lax.ppermute(leading, axis, down)  2.58 us
  transfers between devices with their start and end apart: 13, of which 6 were waited for; matrix products, arithmetic and copies ran while one was open for 5% of the time, Pallas kernels for 0%

profile of v14, /device:TPU:1, one launch (start us, length us, event | category | flops | bytes accessed | tf_op | source)
XLA Modules:
  0.0 112.5 jit_solution(2833343736356356947)
XLA Ops:
  0.6 0.0 copy-start
  0.6 0.0 copy-start.1
  0.7 1.0 fusion.45
  1.7 4.0 %collective-permute-start = (f32[2,1,96,128]{3,2,1,0:T(8,128)S(1)}, f32[2,1,96,128]{3,2,1,0:T(8,128)S(1)}, u32[]{:S(2)}, u32[]{:S(2)}) collective-permute-start(f32[2,1,96,128]{3,2,1,0:T(8,128)S(1)} %get-tuple-element.14), channel_id=1, source_target_pairs={{0,1},{1,2},{2,3},{3,4},{4,5},{5,6},{6,7},{7,8},{8,9},{9,10},{10,1... | collective-permute-start | bytes 294920 | tf_op jit(solution)/shard_map/ppermute | solution.py:18
  5.7 1.3 %collective-permute-start.1 = (f32[2,1,96,128]{3,2,1,0:T(8,128)S(1)}, f32[2,1,96,128]{3,2,1,0:T(8,128)S(1)}, u32[]{:S(2)}, u32[]{:S(2)}) collective-permute-start(f32[2,1,96,128]{3,2,1,0:T(8,128)S(1)} %get-tuple-element.15), channel_id=1, source_target_pairs={{1,0},{2,1},{3,2},{4,3},{5,4},{6,5},{7,6},{8,7},{9,8},{10,9},{11,1... | collective-permute-start | bytes 294920 | tf_op jit(solution)/shard_map/ppermute | solution.py:19
  7.0 13.4 %collective-permute-start.3 = (f32[2,2,96,128]{3,2,1,0:T(8,128)}, f32[2,2,96,128]{3,2,1,0:T(8,128)S(1)}, u32[]{:S(2)}, u32[]{:S(2)}) collective-permute-start(f32[2,2,96,128]{3,2,1,0:T(8,128)} %param.7), channel_id=1, source_target_pairs={{16,0},{32,16},{48,32},{64,48},{80,64},{96,80},{112,96},{128,112},... | collective-permute-start | bytes 589832 | tf_op jit(solution)/shard_map/ppermute | solution.py:27
  20.4 0.0 collective-permute-done
  20.4 0.0 collective-permute-done.1
  20.4 1.0 select_maximum_fusion.2
  21.6 0.0 copy-start.2
  21.7 0.0 copy-start.3
  21.7 0.8 convolution_bitcast_fusion.1
  22.5 0.1 fusion.43
  22.6 1.9 %collective-permute-start.2 = (f32[2,2,96,128]{3,2,1,0:T(8,128)S(1)}, f32[2,2,96,128]{3,2,1,0:T(8,128)S(1)}, u32[]{:S(2)}, u32[]{:S(2)}) collective-permute-start(f32[2,2,96,128]{3,2,1,0:T(8,128)S(1)} %get-tuple-element.13), channel_id=1, source_target_pairs={{0,16},{16,32},{32,48},{48,64},{64,80},{80,96},{96,112},{112,128},... | collective-permute-start | bytes 589832 | tf_op jit(solution)/shard_map/ppermute | solution.py:27
  24.5 0.0 collective-permute-done.3
  24.6 0.4 fusion.3
  25.0 0.8 fusion.36
  25.8 2.3 %collective-permute-done.2 = f32[2,2,96,128]{3,2,1,0:T(8,128)S(1)} collective-permute-done((f32[2,2,96,128]{3,2,1,0:T(8,128)S(1)}, f32[2,2,96,128]{3,2,1,0:T(8,128)S(1)}, u32[]{:S(2)}, u32[]{:S(2)}) %collective-permute-start.2) | collective-permute-done | bytes 196640 | tf_op jit(solution)/shard_map/ppermute | solution.py:27
  28.1 0.4 fusion.34
  28.5 0.3 maximum_multiply_fusion
  28.8 0.1 constant_dynamic-slice_fusion.1
  28.9 0.1 copy.55
  29.0 2.3 %collective-permute-start.4 = (f32[16,4,12,128]{3,1,2,0:T(4,128)S(1)}, f32[16,4,12,128]{3,1,2,0:T(4,128)S(1)}, u32[]{:S(2)}, u32[]{:S(2)}) collective-permute-start(f32[16,4,12,128]{3,1,2,0:T(4,128)S(1)} %bitcast.168), channel_id=1, source_target_pairs={{0,16},{16,0},{32,48},{48,32},{64,80},{80,64},{96,112},{112,96},{1... | collective-permute-start | bytes 1179656 | tf_op jit(solution)/shard_map/ppermute | solution.py:122
  31.3 1.3 %collective-permute-done.4 = f32[16,4,12,128]{3,1,2,0:T(4,128)S(1)} collective-permute-done((f32[16,4,12,128]{3,1,2,0:T(4,128)S(1)}, f32[16,4,12,128]{3,1,2,0:T(4,128)S(1)}, u32[]{:S(2)}, u32[]{:S(2)}) %collective-permute-start.4) | collective-permute-done | bytes 393248 | tf_op jit(solution)/shard_map/ppermute | solution.py:122
  32.6 0.1 bitcast_add_fusion
  32.7 12.1 %all_to_all.5 = f32[16,4,12,128]{3,1,2,0:T(4,128)S(1)} all-to-all(f32[16,4,12,128]{3,1,2,0:T(4,128)S(1)} %bitcast_add_fusion), channel_id=1, replica_groups=mesh['frames'=64,'rows'=16] {'rows'}, dimensions={0} | all-to-all | bytes 786432 | tf_op jit(solution)/shard_map/all_to_all | solution.py:123
  44.8 0.1 reduce_sum.9
  44.9 4.2 %collective-permute-start.7 = (f32[4,12,128]{2,0,1:T(4,128)S(1)}, f32[4,12,128]{2,0,1:T(4,128)S(1)}, u32[]{:S(2)}, u32[]{:S(2)}) collective-permute-start(f32[4,12,128]{2,0,1:T(4,128)S(1)} %reduce_sum.9), channel_id=1, source_target_pairs={{0,32},{16,48},{32,0},{48,16},{64,96},{80,112},{96,64},{112,80},{1... | collective-permute-start | bytes 73736 | tf_op jit(solution)/shard_map/ppermute | solution.py:71
  49.1 1.2 %collective-permute-done.7 = f32[4,12,128]{2,0,1:T(4,128)S(1)} collective-permute-done((f32[4,12,128]{2,0,1:T(4,128)S(1)}, f32[4,12,128]{2,0,1:T(4,128)S(1)}, u32[]{:S(2)}, u32[]{:S(2)}) %collective-permute-start.7) | collective-permute-done | bytes 24608 | tf_op jit(solution)/shard_map/ppermute | solution.py:71
  50.3 4.3 %collective-permute-start.8 = (f32[4,12,128]{2,0,1:T(4,128)S(1)}, f32[4,12,128]{2,0,1:T(4,128)S(1)}, u32[]{:S(2)}, u32[]{:S(2)}) collective-permute-start(f32[4,12,128]{2,0,1:T(4,128)S(1)} %add.55), channel_id=1, source_target_pairs={{0,64},{16,80},{32,96},{48,112},{64,0},{80,16},{96,32},{112,48},{1... | collective-permute-start | bytes 73736 | tf_op jit(solution)/shard_map/ppermute | solution.py:71
  54.5 1.2 %collective-permute-done.8 = f32[4,12,128]{2,0,1:T(4,128)S(1)} collective-permute-done((f32[4,12,128]{2,0,1:T(4,128)S(1)}, f32[4,12,128]{2,0,1:T(4,128)S(1)}, u32[]{:S(2)}, u32[]{:S(2)}) %collective-permute-start.8) | collective-permute-done | bytes 24608 | tf_op jit(solution)/shard_map/ppermute | solution.py:71
  55.8 8.8 %collective-permute-start.9 = (f32[4,12,128]{2,0,1:T(4,128)S(1)}, f32[4,12,128]{2,0,1:T(4,128)S(1)}, u32[]{:S(2)}, u32[]{:S(2)}) collective-permute-start(f32[4,12,128]{2,0,1:T(4,128)S(1)} %add.56), channel_id=1, source_target_pairs={{0,128},{16,144},{32,160},{48,176},{64,192},{80,208},{96,224},{112... | collective-permute-start | bytes 73736 | tf_op jit(solution)/shard_map/ppermute | solution.py:71
  64.6 2.2 %collective-permute-start.5 = (f32[2,1,96,128]{3,2,1,0:T(8,128)S(1)}, f32[2,1,96,128]{3,2,1,0:T(8,128)S(1)}, u32[]{:S(2)}, u32[]{:S(2)}) collective-permute-start(f32[2,1,96,128]{3,2,1,0:T(8,128)S(1)} %get-tuple-element.10), channel_id=1, source_target_pairs={{0,1},{1,2},{2,3},{3,4},{4,5},{5,6},{6,7},{7,8},{8,9},{9,10},{10,1... | collective-permute-start | bytes 294920 | tf_op jit(solution)/shard_map/ppermute | solution.py:18
  66.8 1.3 %collective-permute-start.6 = (f32[2,1,96,128]{3,2,1,0:T(8,128)S(1)}, f32[2,1,96,128]{3,2,1,0:T(8,128)S(1)}, u32[]{:S(2)}, u32[]{:S(2)}) collective-permute-start(f32[2,1,96,128]{3,2,1,0:T(8,128)S(1)} %get-tuple-element.11), channel_id=1, source_target_pairs={{1,0},{2,1},{3,2},{4,3},{5,4},{6,5},{7,6},{8,7},{9,8},{10,9},{11,1... | collective-permute-start | bytes 294920 | tf_op jit(solution)/shard_map/ppermute | solution.py:19
  68.1 0.0 collective-permute-done.9
  68.1 15.4 %collective-permute-start.10 = (f32[4,12,128]{2,0,1:T(4,128)S(1)}, f32[4,12,128]{2,0,1:T(4,128)S(1)}, u32[]{:S(2)}, u32[]{:S(2)}) collective-permute-start(f32[4,12,128]{2,0,1:T(4,128)S(1)} %add.57), channel_id=1, source_target_pairs={{0,256},{16,272},{32,288},{48,304},{64,320},{80,336},{96,352},{112... | collective-permute-start | bytes 73736 | tf_op jit(solution)/shard_map/ppermute | solution.py:71
  83.6 0.4 fusion.9
  84.0 0.8 collective-permute-done.10
  84.8 15.9 %collective-permute-start.11 = (f32[4,12,128]{2,0,1:T(4,128)S(1)}, f32[4,12,128]{2,0,1:T(4,128)S(1)}, u32[]{:S(2)}, u32[]{:S(2)}) collective-permute-start(f32[4,12,128]{2,0,1:T(4,128)S(1)} %add.58), channel_id=1, source_target_pairs={{0,768},{16,784},{32,800},{48,816},{64,832},{80,848},{96,864},{112... | collective-permute-start | bytes 73736 | tf_op jit(solution)/shard_map/ppermute | solution.py:75
  100.7 0.0 collective-permute-done.5
  100.7 0.0 collective-permute-done.6
  101.0 0.9 fusion
  101.8 0.3 collective-permute-done.11
  102.1 8.3 %collective-permute-start.12 = (f32[4,12,128]{2,0,1:T(4,128)S(1)}, f32[4,12,128]{2,0,1:T(4,128)S(1)}, u32[]{:S(2)}, u32[]{:S(2)}) collective-permute-start(f32[4,12,128]{2,0,1:T(4,128)S(1)} %add.59), channel_id=1, source_target_pairs={{0,16},{16,0},{32,48},{48,32},{64,80},{80,64},{96,112},{112,96},{1... | collective-permute-start | bytes 73736 | tf_op jit(solution)/shard_map/ppermute | solution.py:89
  110.5 0.8 bitcast_add_fusion.1
  111.2 0.0 collective-permute-done.12
  111.3 0.6 slice.130
  111.9 0.6 slice.129
  (32 shorter events, 0.5 us)
Async XLA Ops:
  0.6 21.0 %copy-start = (f32[3,3,128,128]{3,2,1,0:T(8,128)S(1)}, f32[3,3,128,128]{3,2,1,0:T(8,128)}, u32[]{:S(2)}) copy-start(f32[3,3,128,128]{3,2,1,0:T(8,128)} %param.5) | copy-start | bytes 1769476
  0.6 20.8 %copy-start.1 = (f32[2,2,96,128]{3,2,1,0:T(8,128)S(1)}, f32[2,2,96,128]{3,2,1,0:T(8,128)}, u32[]{:S(2)}) copy-start(f32[2,2,96,128]{3,2,1,0:T(8,128)} %param.4) | copy-start | bytes 589828
  1.7 18.7 %collective-permute-start = (f32[2,1,96,128]{3,2,1,0:T(8,128)S(1)}, f32[2,1,96,128]{3,2,1,0:T(8,128)S(1)}, u32[]{:S(2)}, u32[]{:S(2)}) collective-permute-start(f32[2,1,96,128]{3,2,1,0:T(8,128)S(1)} %get-tuple-element.14), channel_id=1, source_target_pairs={{0,1},{1,2},{2,3},{3,4},{4,5},{5,6},{6,7},{7,8},{8,9},{9,10},{10,1... | collective-permute-start | bytes 294920 | tf_op jit(solution)/shard_map/ppermute | solution.py:18
  5.7 14.8 %collective-permute-start.1 = (f32[2,1,96,128]{3,2,1,0:T(8,128)S(1)}, f32[2,1,96,128]{3,2,1,0:T(8,128)S(1)}, u32[]{:S(2)}, u32[]{:S(2)}) collective-permute-start(f32[2,1,96,128]{3,2,1,0:T(8,128)S(1)} %get-tuple-element.15), channel_id=1, source_target_pairs={{1,0},{2,1},{3,2},{4,3},{5,4},{6,5},{7,6},{8,7},{9,8},{10,9},{11,1... | collective-permute-start | bytes 294920 | tf_op jit(solution)/shard_map/ppermute | solution.py:19
  7.0 17.6 %collective-permute-start.3 = (f32[2,2,96,128]{3,2,1,0:T(8,128)}, f32[2,2,96,128]{3,2,1,0:T(8,128)S(1)}, u32[]{:S(2)}, u32[]{:S(2)}) collective-permute-start(f32[2,2,96,128]{3,2,1,0:T(8,128)} %param.7), channel_id=1, source_target_pairs={{16,0},{32,16},{48,32},{64,48},{80,64},{96,80},{112,96},{128,112},... | collective-permute-start | bytes 589832 | tf_op jit(solution)/shard_map/ppermute | solution.py:27
  21.6 2.9 %copy-start.2 = (f32[2,2,96,128]{3,2,1,0:T(8,128)S(1)}, f32[2,2,96,128]{3,2,1,0:T(8,128)}, u32[]{:S(2)}) copy-start(f32[2,2,96,128]{3,2,1,0:T(8,128)} %param.7) | copy-start | bytes 589828
  21.7 2.9 %copy-start.3 = (f32[3,128,128]{2,1,0:T(8,128)S(1)}, f32[3,128,128]{2,1,0:T(8,128)}, u32[]{:S(2)}) copy-start(f32[3,128,128]{2,1,0:T(8,128)} %param.6) | copy-start | bytes 589828
  22.6 5.5 %collective-permute-start.2 = (f32[2,2,96,128]{3,2,1,0:T(8,128)S(1)}, f32[2,2,96,128]{3,2,1,0:T(8,128)S(1)}, u32[]{:S(2)}, u32[]{:S(2)}) collective-permute-start(f32[2,2,96,128]{3,2,1,0:T(8,128)S(1)} %get-tuple-element.13), channel_id=1, source_target_pairs={{0,16},{16,32},{32,48},{48,64},{64,80},{80,96},{96,112},{112,128},... | collective-permute-start | bytes 589832 | tf_op jit(solution)/shard_map/ppermute | solution.py:27
  29.0 3.6 %collective-permute-start.4 = (f32[16,4,12,128]{3,1,2,0:T(4,128)S(1)}, f32[16,4,12,128]{3,1,2,0:T(4,128)S(1)}, u32[]{:S(2)}, u32[]{:S(2)}) collective-permute-start(f32[16,4,12,128]{3,1,2,0:T(4,128)S(1)} %bitcast.168), channel_id=1, source_target_pairs={{0,16},{16,0},{32,48},{48,32},{64,80},{80,64},{96,112},{112,96},{1... | collective-permute-start | bytes 1179656 | tf_op jit(solution)/shard_map/ppermute | solution.py:122
  44.9 5.4 %collective-permute-start.7 = (f32[4,12,128]{2,0,1:T(4,128)S(1)}, f32[4,12,128]{2,0,1:T(4,128)S(1)}, u32[]{:S(2)}, u32[]{:S(2)}) collective-permute-start(f32[4,12,128]{2,0,1:T(4,128)S(1)} %reduce_sum.9), channel_id=1, source_target_pairs={{0,32},{16,48},{32,0},{48,16},{64,96},{80,112},{96,64},{112,80},{1... | collective-permute-start | bytes 73736 | tf_op jit(solution)/shard_map/ppermute | solution.py:71
  50.3 5.5 %collective-permute-start.8 = (f32[4,12,128]{2,0,1:T(4,128)S(1)}, f32[4,12,128]{2,0,1:T(4,128)S(1)}, u32[]{:S(2)}, u32[]{:S(2)}) collective-permute-start(f32[4,12,128]{2,0,1:T(4,128)S(1)} %add.55), channel_id=1, source_target_pairs={{0,64},{16,80},{32,96},{48,112},{64,0},{80,16},{96,32},{112,48},{1... | collective-permute-start | bytes 73736 | tf_op jit(solution)/shard_map/ppermute | solution.py:71
  55.8 12.3 %collective-permute-start.9 = (f32[4,12,128]{2,0,1:T(4,128)S(1)}, f32[4,12,128]{2,0,1:T(4,128)S(1)}, u32[]{:S(2)}, u32[]{:S(2)}) collective-permute-start(f32[4,12,128]{2,0,1:T(4,128)S(1)} %add.56), channel_id=1, source_target_pairs={{0,128},{16,144},{32,160},{48,176},{64,192},{80,208},{96,224},{112... | collective-permute-start | bytes 73736 | tf_op jit(solution)/shard_map/ppermute | solution.py:71
  64.6 36.1 %collective-permute-start.5 = (f32[2,1,96,128]{3,2,1,0:T(8,128)S(1)}, f32[2,1,96,128]{3,2,1,0:T(8,128)S(1)}, u32[]{:S(2)}, u32[]{:S(2)}) collective-permute-start(f32[2,1,96,128]{3,2,1,0:T(8,128)S(1)} %get-tuple-element.10), channel_id=1, source_target_pairs={{0,1},{1,2},{2,3},{3,4},{4,5},{5,6},{6,7},{7,8},{8,9},{9,10},{10,1... | collective-permute-start | bytes 294920 | tf_op jit(solution)/shard_map/ppermute | solution.py:18
  66.8 33.9 %collective-permute-start.6 = (f32[2,1,96,128]{3,2,1,0:T(8,128)S(1)}, f32[2,1,96,128]{3,2,1,0:T(8,128)S(1)}, u32[]{:S(2)}, u32[]{:S(2)}) collective-permute-start(f32[2,1,96,128]{3,2,1,0:T(8,128)S(1)} %get-tuple-element.11), channel_id=1, source_target_pairs={{1,0},{2,1},{3,2},{4,3},{5,4},{6,5},{7,6},{8,7},{9,8},{10,9},{11,1... | collective-permute-start | bytes 294920 | tf_op jit(solution)/shard_map/ppermute | solution.py:19
  68.1 16.6 %collective-permute-start.10 = (f32[4,12,128]{2,0,1:T(4,128)S(1)}, f32[4,12,128]{2,0,1:T(4,128)S(1)}, u32[]{:S(2)}, u32[]{:S(2)}) collective-permute-start(f32[4,12,128]{2,0,1:T(4,128)S(1)} %add.57), channel_id=1, source_target_pairs={{0,256},{16,272},{32,288},{48,304},{64,320},{80,336},{96,352},{112... | collective-permute-start | bytes 73736 | tf_op jit(solution)/shard_map/ppermute | solution.py:71
  84.8 17.3 %collective-permute-start.11 = (f32[4,12,128]{2,0,1:T(4,128)S(1)}, f32[4,12,128]{2,0,1:T(4,128)S(1)}, u32[]{:S(2)}, u32[]{:S(2)}) collective-permute-start(f32[4,12,128]{2,0,1:T(4,128)S(1)} %add.58), channel_id=1, source_target_pairs={{0,768},{16,784},{32,800},{48,816},{64,832},{80,848},{96,864},{112... | collective-permute-start | bytes 73736 | tf_op jit(solution)/shard_map/ppermute | solution.py:75
  102.1 9.2 %collective-permute-start.12 = (f32[4,12,128]{2,0,1:T(4,128)S(1)}, f32[4,12,128]{2,0,1:T(4,128)S(1)}, u32[]{:S(2)}, u32[]{:S(2)}) collective-permute-start(f32[4,12,128]{2,0,1:T(4,128)S(1)} %add.59), channel_id=1, source_target_pairs={{0,16},{16,0},{32,48},{48,32},{64,80},{80,64},{96,112},{112,96},{1... | collective-permute-start | bytes 73736 | tf_op jit(solution)/shard_map/ppermute | solution.py:89

commit v15 on v14

--- a/solution.py
+++ b/solution.py
@@ -100,18 +100,14 @@
     dact = temporal_back(grad_long, temporal_weight, nframes)
     dpre = dact * sig * (1.0 + pre * (1.0 - sig))
     act = pre * sig
-    earlier = passed_along(act, "frames", 1)
-    longer = jnp.concatenate([earlier, act], axis=0)
-    lagged = jnp.stack([longer[2 - k : 2 - k + nframes] for k in range(3)])
-    mixed = jnp.einsum("kfrwc,kcd->frwd", lagged, temporal_weight, precision=HIGH)
-    block_out = images + mixed
     total_cells = nframes * lax.axis_size("frames") * strip * lax.axis_size("rows") * width
     factor = 1.0 / math.sqrt(total_cells)
     offsets = [(i, j) for i in range(3) for j in range(3)]
     spatial_terms = jnp.einsum(
         "tfrwc,frwd->dtc", shifted(padded, offsets, strip, width), dpre, precision=HIGH
     )
-    temporal_terms = jnp.einsum("kfrwc,frwd->dkc", lagged, cotangent, precision=HIGH)
+    leading = jnp.stack([grad_long[k : k + nframes] for k in range(3)])
+    temporal_terms = jnp.einsum("frwc,kfrwd->dkc", act, leading, precision=HIGH)
     nrows = lax.axis_size("rows")
     terms = jnp.concatenate([spatial_terms, temporal_terms], axis=1) * factor
     terms = terms.reshape(nrows, 2, chans // nrows // 2, terms.shape[1], chans)
@@ -121,7 +117,12 @@
     nframes_all = lax.axis_size("frames")
     terms = keep + lax.ppermute(give, "frames", [(i, i ^ 1) for i in range(nframes_all)])
     terms = lax.all_to_all(terms, "rows", 0, 0, tiled=True)
-    terms, dpre_late = lax.optimization_barrier((terms, dpre))
+    terms, dpre_late, act = lax.optimization_barrier((terms, dpre, act))
+    earlier = passed_along(act, "frames", 1)
+    longer = jnp.concatenate([earlier, act], axis=0)
+    lagged = jnp.stack([longer[2 - k : 2 - k + nframes] for k in range(3)])
+    mixed = jnp.einsum("kfrwc,kcd->frwd", lagged, temporal_weight, precision=HIGH)
+    block_out = images + mixed
     terms = terms.sum(axis=0)
     dpre_wide = widen(padded_2(dpre_late, (("rows", 1),), 1))
     back = [(2 - i, 2 - j) for i in range(3) for j in range(3)]

time: 113 us -> 110 us (0.973); the launches traced: 113 us -> 108 us
  starting transfers between devices: 83.2 us -> 76.7 us
  waiting for transfers between devices: 7.18 us -> 8.71 us
    ppermute x4, starting transfers between devices: 32.7 us -> 25.3 us  [doubling_sum(): value = value + lax.ppermute(value, axis, pairs)]
    ppermute x2, starting transfers between devices: 15.3 us -> 19.1 us  [passed_along(): return lax.ppermute(value, axis, pairs)]
    ppermute x1, starting transfers between devices: 8.32 us -> 5.08 us  [pair_gather(): other = lax.ppermute(value, axis, [(i, i ^ 1) for i in range(count)])]
    ppermute x1, starting transfers between devices: 2.27 us -> 5.15 us  [per_device(): lax.ppermute(give, 'frames', [(i, i ^ 1) for i in range(nframes_all)])]
    ppermute x1, starting transfers between devices: 15.9 us -> 13.3 us  [doubling_sum(): return value + lax.ppermute(value, axis, pairs)]
    ppermute x2, waiting for transfers between devices: 2.29 us -> 0.01 us  [passed_along(): return lax.ppermute(value, axis, pairs)]
    ppermute x4, waiting for transfers between devices: 3.22 us -> 5.28 us  [doubling_sum(): value = value + lax.ppermute(value, axis, pairs)]
    ppermute x1, waiting for transfers between devices: 0.28 us -> 2.08 us  [doubling_sum(): return value + lax.ppermute(value, axis, pairs)]
  transfers between devices with their start and end apart: 13 -> 13, of which waited for: 6 -> 4; matrix products, arithmetic and copies ran while one was open for 5% -> 4% of each run, Pallas kernels for 0% -> 0%
where the time goes in v15:
time: 110 us; the launch traced here: 108 us
  starting transfers between devices  76.7 us (70%)
  blocking collectives  12.2 us (11%)
  waiting for transfers between devices  8.71 us (8%)
  matrix products  3.94 us (4%)
  local copies, waits for them, and re-layouts  2.96 us (3%)
  other arithmetic  2.42 us (2%)
  between operations  1.16 us (1%)
    ppermute x4, starting transfers between devices, doubling_sum(): value = value + lax.ppermute(value, axis, pairs)  25.3 us
    ppermute x2, starting transfers between devices, passed_along(): return lax.ppermute(value, axis, pairs)  19.1 us
    ppermute x1, starting transfers between devices, doubling_sum(): return value + lax.ppermute(value, axis, pairs)  13.3 us
    all_to_all x1, blocking collectives, per_device(): terms = lax.all_to_all(terms, 'rows', 0, 0, tiled=True)  12.2 us
    ppermute x2, starting transfers between devices, padded_2(): before = lax.ppermute(last, axis, up)  6.15 us
    ppermute x4, waiting for transfers between devices, doubling_sum(): value = value + lax.ppermute(value, axis, pairs)  5.28 us
    ppermute x1, starting transfers between devices, per_device(): lax.ppermute(give, 'frames', [(i, i ^ 1) for i in range(nframes_all)])  5.15 us
    ppermute x1, starting transfers between devices, pair_gather(): other = lax.ppermute(value, axis, [(i, i ^ 1) for i in range(count)])  5.08 us
  transfers between devices with their start and end apart: 13, of which 4 were waited for; matrix products, arithmetic and copies ran while one was open for 4% of the time, Pallas kernels for 0%

profile of v15, /device:TPU:1, one launch (start us, length us, event | category | flops | bytes accessed | tf_op | source)
XLA Modules:
  0.0 108.0 jit_solution(17880814051530878602)
XLA Ops:
  0.6 0.0 copy-start
  0.6 0.0 copy-start.1
  0.7 1.0 fusion.41
  1.7 4.0 %collective-permute-start.1 = (f32[2,1,96,128]{3,2,1,0:T(8,128)S(1)}, f32[2,1,96,128]{3,2,1,0:T(8,128)S(1)}, u32[]{:S(2)}, u32[]{:S(2)}) collective-permute-start(f32[2,1,96,128]{3,2,1,0:T(8,128)S(1)} %get-tuple-element.14), channel_id=1, source_target_pairs={{0,1},{1,2},{2,3},{3,4},{4,5},{5,6},{6,7},{7,8},{8,9},{9,10},{10,1... | collective-permute-start | bytes 294920 | tf_op jit(solution)/shard_map/ppermute | solution.py:18
  5.7 1.3 %collective-permute-start.2 = (f32[2,1,96,128]{3,2,1,0:T(8,128)S(1)}, f32[2,1,96,128]{3,2,1,0:T(8,128)S(1)}, u32[]{:S(2)}, u32[]{:S(2)}) collective-permute-start(f32[2,1,96,128]{3,2,1,0:T(8,128)S(1)} %get-tuple-element.15), channel_id=1, source_target_pairs={{1,0},{2,1},{3,2},{4,3},{5,4},{6,5},{7,6},{8,7},{9,8},{10,9},{11,1... | collective-permute-start | bytes 294920 | tf_op jit(solution)/shard_map/ppermute | solution.py:19
  7.0 13.4 %collective-permute-start = (f32[2,2,96,128]{3,2,1,0:T(8,128)}, f32[2,2,96,128]{3,2,1,0:T(8,128)S(1)}, u32[]{:S(2)}, u32[]{:S(2)}) collective-permute-start(f32[2,2,96,128]{3,2,1,0:T(8,128)} %param.7), channel_id=1, source_target_pairs={{16,0},{32,16},{48,32},{64,48},{80,64},{96,80},{112,96},{128,112},... | collective-permute-start | bytes 589832 | tf_op jit(solution)/shard_map/ppermute | solution.py:27
  20.4 0.0 collective-permute-done.1
  20.4 0.0 collective-permute-done.2
  20.4 1.0 select_maximum_fusion.2
  21.6 0.0 copy-start.2
  21.7 0.9 fusion.35
  22.5 0.0 copy-start.3
  22.5 0.0 collective-permute-done
  22.6 0.7 fusion.7
  23.2 0.2 copy-done.3
  23.5 0.4 fusion.3
  23.9 0.8 fusion.30
  24.6 0.3 maximum_multiply_fusion
  24.9 0.1 constant_dynamic-slice_fusion.1
  25.1 0.1 copy.57
  25.2 5.2 %collective-permute-start.3 = (f32[16,4,12,128]{3,1,2,0:T(4,128)S(1)}, f32[16,4,12,128]{3,1,2,0:T(4,128)S(1)}, u32[]{:S(2)}, u32[]{:S(2)}) collective-permute-start(f32[16,4,12,128]{3,1,2,0:T(4,128)S(1)} %bitcast.163), channel_id=1, source_target_pairs={{0,16},{16,0},{32,48},{48,32},{64,80},{80,64},{96,112},{112,96},{1... | collective-permute-start | bytes 1179656 | tf_op jit(solution)/shard_map/ppermute | solution.py:118
  30.3 1.3 %collective-permute-done.3 = f32[16,4,12,128]{3,1,2,0:T(4,128)S(1)} collective-permute-done((f32[16,4,12,128]{3,1,2,0:T(4,128)S(1)}, f32[16,4,12,128]{3,1,2,0:T(4,128)S(1)}, u32[]{:S(2)}, u32[]{:S(2)}) %collective-permute-start.3) | collective-permute-done | bytes 393248 | tf_op jit(solution)/shard_map/ppermute | solution.py:118
  31.6 0.1 bitcast_add_fusion
  31.8 12.2 %all_to_all.5 = f32[16,4,12,128]{3,1,2,0:T(4,128)S(1)} all-to-all(f32[16,4,12,128]{3,1,2,0:T(4,128)S(1)} %bitcast_add_fusion), channel_id=1, replica_groups=mesh['frames'=64,'rows'=16] {'rows'}, dimensions={0} | all-to-all | bytes 786432 | tf_op jit(solution)/shard_map/all_to_all | solution.py:119
  43.9 0.1 reduce_sum.9
  44.0 1.9 %collective-permute-start.7 = (f32[4,12,128]{2,0,1:T(4,128)S(1)}, f32[4,12,128]{2,0,1:T(4,128)S(1)}, u32[]{:S(2)}, u32[]{:S(2)}) collective-permute-start(f32[4,12,128]{2,0,1:T(4,128)S(1)} %reduce_sum.9), channel_id=1, source_target_pairs={{0,32},{16,48},{32,0},{48,16},{64,96},{80,112},{96,64},{112,80},{1... | collective-permute-start | bytes 73736 | tf_op jit(solution)/shard_map/ppermute | solution.py:71
  45.9 2.2 %collective-permute-start.5 = (f32[2,1,96,128]{3,2,1,0:T(8,128)S(1)}, f32[2,1,96,128]{3,2,1,0:T(8,128)S(1)}, u32[]{:S(2)}, u32[]{:S(2)}) collective-permute-start(f32[2,1,96,128]{3,2,1,0:T(8,128)S(1)} %get-tuple-element.12), channel_id=1, source_target_pairs={{0,1},{1,2},{2,3},{3,4},{4,5},{5,6},{6,7},{7,8},{8,9},{9,10},{10,1... | collective-permute-start | bytes 294920 | tf_op jit(solution)/shard_map/ppermute | solution.py:18
  48.1 1.3 %collective-permute-start.6 = (f32[2,1,96,128]{3,2,1,0:T(8,128)S(1)}, f32[2,1,96,128]{3,2,1,0:T(8,128)S(1)}, u32[]{:S(2)}, u32[]{:S(2)}) collective-permute-start(f32[2,1,96,128]{3,2,1,0:T(8,128)S(1)} %get-tuple-element.13), channel_id=1, source_target_pairs={{1,0},{2,1},{3,2},{4,3},{5,4},{6,5},{7,6},{8,7},{9,8},{10,9},{11,1... | collective-permute-start | bytes 294920 | tf_op jit(solution)/shard_map/ppermute | solution.py:19
  49.4 0.0 collective-permute-done.7
  49.5 2.0 %collective-permute-start.8 = (f32[4,12,128]{2,0,1:T(4,128)S(1)}, f32[4,12,128]{2,0,1:T(4,128)S(1)}, u32[]{:S(2)}, u32[]{:S(2)}) collective-permute-start(f32[4,12,128]{2,0,1:T(4,128)S(1)} %add.55), channel_id=1, source_target_pairs={{0,64},{16,80},{32,96},{48,112},{64,0},{80,16},{96,32},{112,48},{1... | collective-permute-start | bytes 73736 | tf_op jit(solution)/shard_map/ppermute | solution.py:71
  51.5 3.4 %collective-permute-done.8 = f32[4,12,128]{2,0,1:T(4,128)S(1)} collective-permute-done((f32[4,12,128]{2,0,1:T(4,128)S(1)}, f32[4,12,128]{2,0,1:T(4,128)S(1)}, u32[]{:S(2)}, u32[]{:S(2)}) %collective-permute-start.8) | collective-permute-done | bytes 24608 | tf_op jit(solution)/shard_map/ppermute | solution.py:71
  55.0 6.6 %collective-permute-start.9 = (f32[4,12,128]{2,0,1:T(4,128)S(1)}, f32[4,12,128]{2,0,1:T(4,128)S(1)}, u32[]{:S(2)}, u32[]{:S(2)}) collective-permute-start(f32[4,12,128]{2,0,1:T(4,128)S(1)} %add.56), channel_id=1, source_target_pairs={{0,128},{16,144},{32,160},{48,176},{64,192},{80,208},{96,224},{112... | collective-permute-start | bytes 73736 | tf_op jit(solution)/shard_map/ppermute | solution.py:71
  61.6 1.9 %collective-permute-done.9 = f32[4,12,128]{2,0,1:T(4,128)S(1)} collective-permute-done((f32[4,12,128]{2,0,1:T(4,128)S(1)}, f32[4,12,128]{2,0,1:T(4,128)S(1)}, u32[]{:S(2)}, u32[]{:S(2)}) %collective-permute-start.9) | collective-permute-done | bytes 24608 | tf_op jit(solution)/shard_map/ppermute | solution.py:71
  63.4 14.8 %collective-permute-start.10 = (f32[4,12,128]{2,0,1:T(4,128)S(1)}, f32[4,12,128]{2,0,1:T(4,128)S(1)}, u32[]{:S(2)}, u32[]{:S(2)}) collective-permute-start(f32[4,12,128]{2,0,1:T(4,128)S(1)} %add.57), channel_id=1, source_target_pairs={{0,256},{16,272},{32,288},{48,304},{64,320},{80,336},{96,352},{112... | collective-permute-start | bytes 73736 | tf_op jit(solution)/shard_map/ppermute | solution.py:71
  78.2 5.7 %collective-permute-start.4 = (f32[2,2,96,128]{3,2,1,0:T(8,128)S(1)}, f32[2,2,96,128]{3,2,1,0:T(8,128)S(1)}, u32[]{:S(2)}, u32[]{:S(2)}) collective-permute-start(f32[2,2,96,128]{3,2,1,0:T(8,128)S(1)} %get-tuple-element.7), channel_id=1, source_target_pairs={{0,16},{16,32},{32,48},{48,64},{64,80},{80,96},{96,112},{112,128},... | collective-permute-start | bytes 589832 | tf_op jit(solution)/shard_map/ppermute | solution.py:27
  83.9 0.0 collective-permute-done.10
  83.9 13.3 %collective-permute-start.11 = (f32[4,12,128]{2,0,1:T(4,128)S(1)}, f32[4,12,128]{2,0,1:T(4,128)S(1)}, u32[]{:S(2)}, u32[]{:S(2)}) collective-permute-start(f32[4,12,128]{2,0,1:T(4,128)S(1)} %add.58), channel_id=1, source_target_pairs={{0,768},{16,784},{32,800},{48,816},{64,832},{80,848},{96,864},{112... | collective-permute-start | bytes 73736 | tf_op jit(solution)/shard_map/ppermute | solution.py:75
  97.2 0.0 collective-permute-done.5
  97.2 0.0 collective-permute-done.6
  97.5 2.1 %collective-permute-done.11 = f32[4,12,128]{2,0,1:T(4,128)S(1)} collective-permute-done((f32[4,12,128]{2,0,1:T(4,128)S(1)}, f32[4,12,128]{2,0,1:T(4,128)S(1)}, u32[]{:S(2)}, u32[]{:S(2)}) %collective-permute-start.11) | collective-permute-done | bytes 24608 | tf_op jit(solution)/shard_map/ppermute | solution.py:75
  99.6 5.1 %collective-permute-start.12 = (f32[4,12,128]{2,0,1:T(4,128)S(1)}, f32[4,12,128]{2,0,1:T(4,128)S(1)}, u32[]{:S(2)}, u32[]{:S(2)}) collective-permute-start(f32[4,12,128]{2,0,1:T(4,128)S(1)} %add.59), channel_id=1, source_target_pairs={{0,16},{16,0},{32,48},{48,32},{64,80},{80,64},{96,112},{112,96},{1... | collective-permute-start | bytes 73736 | tf_op jit(solution)/shard_map/ppermute | solution.py:89
  104.7 0.9 fusion
  105.5 0.0 collective-permute-done.12
  105.6 0.6 slice.131
  106.2 0.6 slice.130
  106.8 0.0 collective-permute-done.4
  106.8 0.4 fusion.4
  107.2 0.8 bitcast_add_fusion.1
  (31 shorter events, 0.5 us)
Async XLA Ops:
  0.6 21.0 %copy-start = (f32[3,3,128,128]{3,2,1,0:T(8,128)S(1)}, f32[3,3,128,128]{3,2,1,0:T(8,128)}, u32[]{:S(2)}) copy-start(f32[3,3,128,128]{3,2,1,0:T(8,128)} %param.5) | copy-start | bytes 1769476
  0.6 20.8 %copy-start.1 = (f32[2,2,96,128]{3,2,1,0:T(8,128)S(1)}, f32[2,2,96,128]{3,2,1,0:T(8,128)}, u32[]{:S(2)}) copy-start(f32[2,2,96,128]{3,2,1,0:T(8,128)} %param.4) | copy-start | bytes 589828
  1.7 18.7 %collective-permute-start.1 = (f32[2,1,96,128]{3,2,1,0:T(8,128)S(1)}, f32[2,1,96,128]{3,2,1,0:T(8,128)S(1)}, u32[]{:S(2)}, u32[]{:S(2)}) collective-permute-start(f32[2,1,96,128]{3,2,1,0:T(8,128)S(1)} %get-tuple-element.14), channel_id=1, source_target_pairs={{0,1},{1,2},{2,3},{3,4},{4,5},{5,6},{6,7},{7,8},{8,9},{9,10},{10,1... | collective-permute-start | bytes 294920 | tf_op jit(solution)/shard_map/ppermute | solution.py:18
  5.7 14.8 %collective-permute-start.2 = (f32[2,1,96,128]{3,2,1,0:T(8,128)S(1)}, f32[2,1,96,128]{3,2,1,0:T(8,128)S(1)}, u32[]{:S(2)}, u32[]{:S(2)}) collective-permute-start(f32[2,1,96,128]{3,2,1,0:T(8,128)S(1)} %get-tuple-element.15), channel_id=1, source_target_pairs={{1,0},{2,1},{3,2},{4,3},{5,4},{6,5},{7,6},{8,7},{9,8},{10,9},{11,1... | collective-permute-start | bytes 294920 | tf_op jit(solution)/shard_map/ppermute | solution.py:19
  7.0 15.6 %collective-permute-start = (f32[2,2,96,128]{3,2,1,0:T(8,128)}, f32[2,2,96,128]{3,2,1,0:T(8,128)S(1)}, u32[]{:S(2)}, u32[]{:S(2)}) collective-permute-start(f32[2,2,96,128]{3,2,1,0:T(8,128)} %param.7), channel_id=1, source_target_pairs={{16,0},{32,16},{48,32},{64,48},{80,64},{96,80},{112,96},{128,112},... | collective-permute-start | bytes 589832 | tf_op jit(solution)/shard_map/ppermute | solution.py:27
  21.6 1.0 copy-start.2
  22.5 0.9 copy-start.3
  25.2 6.5 %collective-permute-start.3 = (f32[16,4,12,128]{3,1,2,0:T(4,128)S(1)}, f32[16,4,12,128]{3,1,2,0:T(4,128)S(1)}, u32[]{:S(2)}, u32[]{:S(2)}) collective-permute-start(f32[16,4,12,128]{3,1,2,0:T(4,128)S(1)} %bitcast.163), channel_id=1, source_target_pairs={{0,16},{16,0},{32,48},{48,32},{64,80},{80,64},{96,112},{112,96},{1... | collective-permute-start | bytes 1179656 | tf_op jit(solution)/shard_map/ppermute | solution.py:118
  44.0 5.5 %collective-permute-start.7 = (f32[4,12,128]{2,0,1:T(4,128)S(1)}, f32[4,12,128]{2,0,1:T(4,128)S(1)}, u32[]{:S(2)}, u32[]{:S(2)}) collective-permute-start(f32[4,12,128]{2,0,1:T(4,128)S(1)} %reduce_sum.9), channel_id=1, source_target_pairs={{0,32},{16,48},{32,0},{48,16},{64,96},{80,112},{96,64},{112,80},{1... | collective-permute-start | bytes 73736 | tf_op jit(solution)/shard_map/ppermute | solution.py:71
  45.9 51.3 %collective-permute-start.5 = (f32[2,1,96,128]{3,2,1,0:T(8,128)S(1)}, f32[2,1,96,128]{3,2,1,0:T(8,128)S(1)}, u32[]{:S(2)}, u32[]{:S(2)}) collective-permute-start(f32[2,1,96,128]{3,2,1,0:T(8,128)S(1)} %get-tuple-element.12), channel_id=1, source_target_pairs={{0,1},{1,2},{2,3},{3,4},{4,5},{5,6},{6,7},{7,8},{8,9},{9,10},{10,1... | collective-permute-start | bytes 294920 | tf_op jit(solution)/shard_map/ppermute | solution.py:18
  48.1 49.1 %collective-permute-start.6 = (f32[2,1,96,128]{3,2,1,0:T(8,128)S(1)}, f32[2,1,96,128]{3,2,1,0:T(8,128)S(1)}, u32[]{:S(2)}, u32[]{:S(2)}) collective-permute-start(f32[2,1,96,128]{3,2,1,0:T(8,128)S(1)} %get-tuple-element.13), channel_id=1, source_target_pairs={{1,0},{2,1},{3,2},{4,3},{5,4},{6,5},{7,6},{8,7},{9,8},{10,9},{11,1... | collective-permute-start | bytes 294920 | tf_op jit(solution)/shard_map/ppermute | solution.py:19
  49.5 5.5 %collective-permute-start.8 = (f32[4,12,128]{2,0,1:T(4,128)S(1)}, f32[4,12,128]{2,0,1:T(4,128)S(1)}, u32[]{:S(2)}, u32[]{:S(2)}) collective-permute-start(f32[4,12,128]{2,0,1:T(4,128)S(1)} %add.55), channel_id=1, source_target_pairs={{0,64},{16,80},{32,96},{48,112},{64,0},{80,16},{96,32},{112,48},{1... | collective-permute-start | bytes 73736 | tf_op jit(solution)/shard_map/ppermute | solution.py:71
  55.0 8.5 %collective-permute-start.9 = (f32[4,12,128]{2,0,1:T(4,128)S(1)}, f32[4,12,128]{2,0,1:T(4,128)S(1)}, u32[]{:S(2)}, u32[]{:S(2)}) collective-permute-start(f32[4,12,128]{2,0,1:T(4,128)S(1)} %add.56), channel_id=1, source_target_pairs={{0,128},{16,144},{32,160},{48,176},{64,192},{80,208},{96,224},{112... | collective-permute-start | bytes 73736 | tf_op jit(solution)/shard_map/ppermute | solution.py:71
  63.4 20.5 %collective-permute-start.10 = (f32[4,12,128]{2,0,1:T(4,128)S(1)}, f32[4,12,128]{2,0,1:T(4,128)S(1)}, u32[]{:S(2)}, u32[]{:S(2)}) collective-permute-start(f32[4,12,128]{2,0,1:T(4,128)S(1)} %add.57), channel_id=1, source_target_pairs={{0,256},{16,272},{32,288},{48,304},{64,320},{80,336},{96,352},{112... | collective-permute-start | bytes 73736 | tf_op jit(solution)/shard_map/ppermute | solution.py:71
  78.2 28.6 %collective-permute-start.4 = (f32[2,2,96,128]{3,2,1,0:T(8,128)S(1)}, f32[2,2,96,128]{3,2,1,0:T(8,128)S(1)}, u32[]{:S(2)}, u32[]{:S(2)}) collective-permute-start(f32[2,2,96,128]{3,2,1,0:T(8,128)S(1)} %get-tuple-element.7), channel_id=1, source_target_pairs={{0,16},{16,32},{32,48},{48,64},{64,80},{80,96},{96,112},{112,128},... | collective-permute-start | bytes 589832 | tf_op jit(solution)/shard_map/ppermute | solution.py:27
  83.9 15.6 %collective-permute-start.11 = (f32[4,12,128]{2,0,1:T(4,128)S(1)}, f32[4,12,128]{2,0,1:T(4,128)S(1)}, u32[]{:S(2)}, u32[]{:S(2)}) collective-permute-start(f32[4,12,128]{2,0,1:T(4,128)S(1)} %add.58), channel_id=1, source_target_pairs={{0,768},{16,784},{32,800},{48,816},{64,832},{80,848},{96,864},{112... | collective-permute-start | bytes 73736 | tf_op jit(solution)/shard_map/ppermute | solution.py:75
  99.6 6.0 %collective-permute-start.12 = (f32[4,12,128]{2,0,1:T(4,128)S(1)}, f32[4,12,128]{2,0,1:T(4,128)S(1)}, u32[]{:S(2)}, u32[]{:S(2)}) collective-permute-start(f32[4,12,128]{2,0,1:T(4,128)S(1)} %add.59), channel_id=1, source_target_pairs={{0,16},{16,0},{32,48},{48,32},{64,80},{80,64},{96,112},{112,96},{1... | collective-permute-start | bytes 73736 | tf_op jit(solution)/shard_map/ppermute | solution.py:89
